TPU v7x, 32 devices: a whole 2x2x4 slice. The times are simulated.
32 devices in a mesh: row: 4 (over z), col: 8 (over y, x, core).
Axes of the slice: x: 2, y: 2, z: 4, core: 2. Of those that a mesh axis runs over, the one named last changes fastest.
Arguments:
- image: float32 [224, 32, 2048], P(None, 'row', 'col'), may hold values from -24 to 24
- start_basis: float32 [224, 16], replicated, may hold values from -4 to 4
Outputs:
- smoothed: float32 [224, 32, 2048], P(None, 'row', 'col')
- lowrank: float32 [224, 32, 2048], P(None, 'row', 'col')
All inputs are finite; a program needn't handle non-finite values.
Results may differ from a plain program's by a relative error of at most 0.0003.
Values sent between devices are 32-bit elements; how exact they have to be, the bound alone decides.
No kernel may reach another device: no remote copies, remote signals or barrier semaphores. Data moves between devices by JAX's collectives and lax.ppermute only.
A program may use at most 64 MiB of HBM per device.

v0:
```python
import jax
import jax.numpy as jnp
from jax import lax
from jax.sharding import PartitionSpec as P

SWEEPS = 4
SUBIT = 2


tau_step = 0.22
fidelity = 0.1


def padded_2(cells, sides, width):
    for axis, dim in sides:
        count = lax.axis_size(axis)
        ends = count - 1
        head = lax.slice_in_dim(cells, 0, width, axis=dim)
        tail = lax.slice_in_dim(cells, cells.shape[dim] - width, cells.shape[dim], axis=dim)
        cells = jnp.concatenate(
            [
                lax.ppermute(tail, axis, [(i, (i + 1) % count) for i in range(ends)]),
                cells,
                lax.ppermute(head, axis, [((i + 1) % count, i) for i in range(ends)]),
            ],
            axis=dim,
        )
    return cells


def forward_diffs(padded):
    diff_col = padded[..., :-1, 1:] - padded[..., :-1, :-1]
    diff_row = padded[..., 1:, :-1] - padded[..., :-1, :-1]
    return (diff_col, diff_row)


def smooth_step(padded, source):
    diff_col, diff_row = forward_diffs(padded)
    energy_sum = jnp.sum(diff_col * diff_col + diff_row * diff_row, axis=0)
    weight = 1.0 / jnp.sqrt(1.0 + energy_sum / padded.shape[0])
    flux_col = weight * diff_col
    flux_row = weight * diff_row
    spread = (
        flux_col[..., 1:, 1:]
        - flux_col[..., 1:, :-1]
        + flux_row[..., 1:, 1:]
        - flux_row[..., :-1, 1:]
    )
    centre = padded[..., 1:-1, 1:-1]
    return centre + tau_step * spread + tau_step * fidelity * (source - centre)


def orthonormal(block):
    inner = jnp.dot(block.T, block, precision=lax.Precision.HIGHEST)
    lower = jnp.linalg.cholesky(inner)
    return lax.linalg.triangular_solve(lower, block, left_side=False, lower=True, transpose_a=True)


def shards(image, start_basis):
    band_count, tile_rows, tile_cols = image.shape
    field = image
    for sweep_no in range(SWEEPS):
        extended = padded_2(field, (("row", 1), ("col", 2)), 1)
        field = smooth_step(extended, image)
    flat_field = field.reshape(band_count, tile_rows * tile_cols)
    basis_now = start_basis
    local_gram = lax.dot_general(
        flat_field,
        flat_field,
        (((1,), (1,)), ((), ())),
        precision=lax.Precision.HIGHEST,
        preferred_element_type=jnp.float32,
    )
    gram_full = lax.psum(local_gram, ("row", "col"))
    for turn in range(SUBIT):
        product = jnp.dot(gram_full, basis_now, precision=lax.Precision.HIGHEST)
        basis_now = orthonormal(orthonormal(product))
    coeffs = jnp.dot(basis_now.T, flat_field, precision=lax.Precision.HIGHEST)
    lowrank = jnp.dot(basis_now, coeffs, precision=lax.Precision.HIGHEST)
    return (field, lowrank.reshape(band_count, tile_rows, tile_cols))


def solution(mesh):
    in_specs = (P(None, "row", "col"), P())
    out_specs = (P(None, "row", "col"), P(None, "row", "col"))
    return jax.shard_map(shards, mesh=mesh, in_specs=in_specs, out_specs=out_specs, check_vma=False)
```

profile of v0, /device:TPU:0, one launch (start us, length us, event | category | flops | bytes accessed | tf_op | source)
XLA Modules:
  0.0 324.9 jit_solution(15934660971049037170)
XLA Ops:
  7.2 2.4 fusion.42
  10.9 5.6 %collective-permute-start = (f32[224,1,256]{2,0,1:T(8,128)S(1)}, f32[224,1,256]{2,0,1:T(8,128)S(1)}, u32[]{:S(2)}, u32[]{:S(2)}) collective-permute-start(f32[224,1,256]{2,0,1:T(8,128)S(1)} %copy.216), channel_id=1, source_target_pairs={{0,8},{8,16},{16,24},{1,9},{9,17},{17,25},{2,10},{10,18},{18,26},{... | collective-permute-start | bytes 688136 | tf_op jit(solution)/shard_map/ppermute | solution.py:22
  16.5 2.2 copy.184
  25.0 2.8 collective-permute-done.2
  27.8 2.7 add_reduce_fusion.3
  30.8 6.5 %broadcast_multiply_fusion.7 = (f32[224,9,257]{0,1,2:T(8,128)S(1)}, f32[224,9,257]{0,1,2:T(8,128)S(1)}) fusion(f32[9,257]{0,1:T(8,128)S(1)} %copy.183, f32[224,10,257]{0,1,2:T(8,128)} %copy-done.1, f32[224,10,1]{0,1,2:T(8,128)S(1)} %collective-permute-done.2, f32[224,1,256]{0,1,2:T(1,128)S(1)} %copy.181, f32[224,8,256]{0,1,2:T(8,128)S(1)} %copy.184, ...), kind=kLoop, calls=%fused_computation.35 | loop fusion | flops 3626784 | bytes 10601764 | tf_op jit(solution)/shard_map/mul | solution.py:41
  41.6 5.0 %collective-permute-start.4 = (f32[224,1,256]{2,0,1:T(8,128)S(1)}, f32[224,1,256]{2,0,1:T(8,128)S(1)}, u32[]{:S(2)}, u32[]{:S(2)}) collective-permute-start(f32[224,1,256]{2,0,1:T(8,128)S(1)} %copy.187), channel_id=1, source_target_pairs={{0,8},{8,16},{16,24},{1,9},{9,17},{17,25},{2,10},{10,18},{18,26},{... | collective-permute-start | bytes 688136 | tf_op jit(solution)/shard_map/ppermute | solution.py:22
  46.6 2.5 collective-permute-done.5
  52.0 3.6 %collective-permute-start.7 = (f32[224,10,1]{0,1,2:T(8,128)S(1)}, f32[224,10,1]{0,1,2:T(8,128)S(1)}, u32[]{:S(2)}, u32[]{:S(2)}) collective-permute-start(f32[224,10,1]{0,1,2:T(8,128)S(1)} %get-tuple-element.27), channel_id=1, source_target_pairs={{0,1},{1,2},{2,3},{3,4},{4,5},{5,6},{6,7},{8,9},{9,10},{10,11},{11... | collective-permute-start | bytes 26888 | tf_op jit(solution)/shard_map/ppermute | solution.py:22
  57.1 2.4 maximum_maximum_fusion.1
  59.6 2.3 collective-permute-done.6
  61.9 2.8 add_reduce_fusion.2
  64.9 8.4 %broadcast_multiply_fusion.5 = (f32[224,9,257]{0,1,2:T(8,128)S(1)}, f32[224,9,257]{0,1,2:T(8,128)}) fusion(f32[9,257]{0,1:T(8,128)S(1)} %copy.192, f32[224,10,257]{0,1,2:T(8,128)} %copy-done.2, f32[224,10,1]{0,1,2:T(8,128)S(1)} %collective-permute-done.6, f32[224,1,256]{0,1,2:T(1,128)S(1)} %copy.190, f32[224,8,256]{0,1,2:T(8,128)} %copy-done.11, ...), kind=kLoop, calls=%fused_computation.33 | loop fusion | flops 3626784 | bytes 10601764 | tf_op jit(solution)/shard_map/mul | solution.py:41
  73.3 3.8 %fusion.12 = f32[224,8,256]{0,1,2:T(8,128)S(1)} fusion(f32[224,8,256]{0,1,2:T(8,128)S(1)} %copy-done.13, f32[224,9,257]{0,1,2:T(8,128)} %get-tuple-element.19, f32[224,9,257]{0,1,2:T(8,128)S(1)} %get-tuple-element.18, f32[224,8,256]{0,1,2:T(8,128)S(1)} %copy.184), kind=kLoop, calls=%fused_computation.51 | loop fusion | flops 3670016 | bytes 12845056 | tf_op jit(solution)/shard_map/add | solution.py:50
  80.3 5.0 %collective-permute-start.8 = (f32[224,1,256]{2,0,1:T(8,128)S(1)}, f32[224,1,256]{2,0,1:T(8,128)S(1)}, u32[]{:S(2)}, u32[]{:S(2)}) collective-permute-start(f32[224,1,256]{2,0,1:T(8,128)S(1)} %copy.194), channel_id=1, source_target_pairs={{0,8},{8,16},{16,24},{1,9},{9,17},{17,25},{2,10},{10,18},{18,26},{... | collective-permute-start | bytes 688136 | tf_op jit(solution)/shard_map/ppermute | solution.py:22
  89.9 5.0 %collective-permute-start.11 = (f32[224,10,1]{0,1,2:T(8,128)S(1)}, f32[224,10,1]{0,1,2:T(8,128)S(1)}, u32[]{:S(2)}, u32[]{:S(2)}) collective-permute-start(f32[224,10,1]{0,1,2:T(8,128)S(1)} %get-tuple-element.25), channel_id=1, source_target_pairs={{0,1},{1,2},{2,3},{3,4},{4,5},{5,6},{6,7},{8,9},{9,10},{10,11},{11... | collective-permute-start | bytes 26888 | tf_op jit(solution)/shard_map/ppermute | solution.py:22
  96.2 2.4 maximum_maximum_fusion.2
  98.7 2.2 collective-permute-done.10
  100.8 2.8 add_reduce_fusion.1
  103.8 8.4 %broadcast_multiply_fusion.3 = (f32[224,9,257]{0,1,2:T(8,128)S(1)}, f32[224,9,257]{0,1,2:T(8,128)}) fusion(f32[9,257]{0,1:T(8,128)S(1)} %copy.199, f32[224,10,257]{0,1,2:T(8,128)} %copy-done.3, f32[224,10,1]{0,1,2:T(8,128)S(1)} %collective-permute-done.10, f32[224,1,256]{0,1,2:T(1,128)S(1)} %copy.197, f32[224,8,256]{0,1,2:T(8,128)} %copy-done.8, ...), kind=kLoop, calls=%fused_computation.31 | loop fusion | flops 3626784 | bytes 10601764 | tf_op jit(solution)/shard_map/mul | solution.py:41
  112.2 3.8 %fusion.9 = f32[224,8,256]{0,1,2:T(8,128)S(1)} fusion(f32[224,8,256]{0,1,2:T(8,128)S(1)} %copy-done.10, f32[224,9,257]{0,1,2:T(8,128)} %get-tuple-element.17, f32[224,9,257]{0,1,2:T(8,128)S(1)} %get-tuple-element.16, f32[224,8,256]{0,1,2:T(8,128)S(1)} %copy.184), kind=kLoop, calls=%fused_computation.45 | loop fusion | flops 3670016 | bytes 12845056 | tf_op jit(solution)/shard_map/add | solution.py:50
  119.3 5.2 %collective-permute-start.12 = (f32[224,1,256]{2,0,1:T(8,128)S(1)}, f32[224,1,256]{2,0,1:T(8,128)S(1)}, u32[]{:S(2)}, u32[]{:S(2)}) collective-permute-start(f32[224,1,256]{2,0,1:T(8,128)S(1)} %copy.201), channel_id=1, source_target_pairs={{0,8},{8,16},{16,24},{1,9},{9,17},{17,25},{2,10},{10,18},{18,26},{... | collective-permute-start | bytes 688136 | tf_op jit(solution)/shard_map/ppermute | solution.py:22
  128.9 4.8 %collective-permute-start.15 = (f32[224,10,1]{0,1,2:T(8,128)S(1)}, f32[224,10,1]{0,1,2:T(8,128)S(1)}, u32[]{:S(2)}, u32[]{:S(2)}) collective-permute-start(f32[224,10,1]{0,1,2:T(8,128)S(1)} %get-tuple-element.23), channel_id=1, source_target_pairs={{0,1},{1,2},{2,3},{3,4},{4,5},{5,6},{6,7},{8,9},{9,10},{10,11},{11... | collective-permute-start | bytes 26888 | tf_op jit(solution)/shard_map/ppermute | solution.py:22
  135.0 2.4 maximum_maximum_fusion.3
  137.5 2.3 collective-permute-done.14
  139.8 2.8 add_reduce_fusion
  142.8 8.4 %broadcast_multiply_fusion.1 = (f32[224,9,257]{0,1,2:T(8,128)S(1)}, f32[224,9,257]{0,1,2:T(8,128)}) fusion(f32[9,257]{0,1:T(8,128)S(1)} %copy.206, f32[224,10,257]{0,1,2:T(8,128)} %copy-done.4, f32[224,10,1]{0,1,2:T(8,128)S(1)} %collective-permute-done.14, f32[224,1,256]{0,1,2:T(1,128)S(1)} %copy.204, f32[224,8,256]{0,1,2:T(8,128)} %copy-done.5, ...), kind=kLoop, calls=%fused_computation.29 | loop fusion | flops 3626784 | bytes 10601764 | tf_op jit(solution)/shard_map/mul | solution.py:41
  151.2 3.8 %fusion.6 = f32[224,8,256]{0,1,2:T(8,128)S(1)} fusion(f32[224,8,256]{0,1,2:T(8,128)S(1)} %copy-done.7, f32[224,9,257]{0,1,2:T(8,128)} %get-tuple-element.15, f32[224,9,257]{0,1,2:T(8,128)S(1)} %get-tuple-element.14, f32[224,8,256]{0,1,2:T(8,128)S(1)} %copy.184), kind=kLoop, calls=%fused_computation.39 | loop fusion | flops 3670016 | bytes 12845056 | tf_op jit(solution)/shard_map/add | solution.py:50
  156.4 5.0 %fusion.18 = f32[224,224]{1,0:T(8,128)} fusion(f32[224,8,256]{0,1,2:T(8,128)S(1)} %fusion.6), kind=kOutput, calls=%fused_computation.62 | convolution fusion | flops 1233125376 | bytes 2035712 | tf_op jit(solution)/shard_map/dot_general | solution.py:67
  161.4 2.6 copy.215
  166.0 125.2 %all-reduce.2.cloned.1.call-done = f32[224,224]{1,0:T(8,128)} async-done(((f32[224,224]{1,0:T(8,128)}), f32[224,224]{1,0:T(8,128)}) %all-reduce.2.cloned.1.call-update) | async-done | bytes 200720 | tf_op jit(solution)/shard_map/psum | solution.py:74
  311.9 2.5 fusion.49
  (132 shorter events, 62.6 us)
Async XLA Ops:
  7.2 284.0 %copy-start = (f32[224,16]{0,1:T(8,128)S(1)}, f32[224,16]{0,1:T(8,128)}, u32[]{:S(2)}) copy-start(f32[224,16]{0,1:T(8,128)} %param.6) | copy-start | bytes 43012
  7.2 284.0 %all-reduce.2.cloned.1.call-start = ((), (), s32[]{:S(2)}) async-start(), calls=%async_computation | async-start | bytes 458752 | tf_op jit(solution)/shard_map/psum | solution.py:74
  9.6 10.5 %collective-permute-start.1 = (f32[224,1,256]{2,0,1:T(8,128)S(1)}, f32[224,1,256]{2,0,1:T(8,128)S(1)}, u32[]{:S(2)}, u32[]{:S(2)}) collective-permute-start(f32[224,1,256]{2,0,1:T(8,128)S(1)} %copy.217), channel_id=1, source_target_pairs={{8,0},{16,8},{24,16},{9,1},{17,9},{25,17},{10,2},{18,10},{26,18},{... | collective-permute-start | bytes 688136 | tf_op jit(solution)/shard_map/ppermute | solution.py:24
  10.9 10.4 %collective-permute-start = (f32[224,1,256]{2,0,1:T(8,128)S(1)}, f32[224,1,256]{2,0,1:T(8,128)S(1)}, u32[]{:S(2)}, u32[]{:S(2)}) collective-permute-start(f32[224,1,256]{2,0,1:T(8,128)S(1)} %copy.216), channel_id=1, source_target_pairs={{0,8},{8,16},{16,24},{1,9},{9,17},{17,25},{2,10},{10,18},{18,26},{... | collective-permute-start | bytes 688136 | tf_op jit(solution)/shard_map/ppermute | solution.py:22
  21.5 2.6 collective-permute-start.3
  22.8 5.0 %collective-permute-start.2 = (f32[224,10,1]{0,1,2:T(8,128)S(1)}, f32[224,10,1]{0,1,2:T(8,128)S(1)}, u32[]{:S(2)}, u32[]{:S(2)}) collective-permute-start(f32[224,10,1]{0,1,2:T(8,128)S(1)} %get-tuple-element.28), channel_id=1, source_target_pairs={{1,0},{2,1},{3,2},{4,3},{5,4},{6,5},{7,6},{9,8},{10,9},{11,10},{12... | collective-permute-start | bytes 26888 | tf_op jit(solution)/shard_map/ppermute | solution.py:24
  25.0 2.8 copy-start.1
  38.3 1.4 copy-start.11
  40.1 9.0 %collective-permute-start.5 = (f32[224,1,256]{2,0,1:T(8,128)S(1)}, f32[224,1,256]{2,0,1:T(8,128)S(1)}, u32[]{:S(2)}, u32[]{:S(2)}) collective-permute-start(f32[224,1,256]{2,0,1:T(8,128)S(1)} %copy.188), channel_id=1, source_target_pairs={{8,0},{16,8},{24,16},{9,1},{17,9},{25,17},{10,2},{18,10},{26,18},{... | collective-permute-start | bytes 688136 | tf_op jit(solution)/shard_map/ppermute | solution.py:24
  41.6 9.4 %collective-permute-start.4 = (f32[224,1,256]{2,0,1:T(8,128)S(1)}, f32[224,1,256]{2,0,1:T(8,128)S(1)}, u32[]{:S(2)}, u32[]{:S(2)}) collective-permute-start(f32[224,1,256]{2,0,1:T(8,128)S(1)} %copy.187), channel_id=1, source_target_pairs={{0,8},{8,16},{16,24},{1,9},{9,17},{17,25},{2,10},{10,18},{18,26},{... | collective-permute-start | bytes 688136 | tf_op jit(solution)/shard_map/ppermute | solution.py:22
  51.1 10.7 %copy-start.12 = (f32[224,8,256]{0,1,2:T(8,128)S(1)}, f32[224,8,256]{0,1,2:T(8,128)}, u32[]{:S(2)}) copy-start(f32[224,8,256]{0,1,2:T(8,128)} %copy-done.11) | copy-start | bytes 5505028
  52.0 5.1 %collective-permute-start.7 = (f32[224,10,1]{0,1,2:T(8,128)S(1)}, f32[224,10,1]{0,1,2:T(8,128)S(1)}, u32[]{:S(2)}, u32[]{:S(2)}) collective-permute-start(f32[224,10,1]{0,1,2:T(8,128)S(1)} %get-tuple-element.27), channel_id=1, source_target_pairs={{0,1},{1,2},{2,3},{3,4},{4,5},{5,6},{6,7},{8,9},{9,10},{10,11},{11... | collective-permute-start | bytes 26888 | tf_op jit(solution)/shard_map/ppermute | solution.py:22
  55.6 6.2 %collective-permute-start.6 = (f32[224,10,1]{0,1,2:T(8,128)S(1)}, f32[224,10,1]{0,1,2:T(8,128)S(1)}, u32[]{:S(2)}, u32[]{:S(2)}) collective-permute-start(f32[224,10,1]{0,1,2:T(8,128)S(1)} %get-tuple-element.26), channel_id=1, source_target_pairs={{1,0},{2,1},{3,2},{4,3},{5,4},{6,5},{7,6},{9,8},{10,9},{11,10},{12... | collective-permute-start | bytes 26888 | tf_op jit(solution)/shard_map/ppermute | solution.py:24
  59.6 2.3 copy-start.2
  64.9 8.4 %copy-start.13 = (f32[224,8,256]{0,1,2:T(8,128)S(1)}, f32[224,8,256]{0,1,2:T(8,128)}, u32[]{:S(2)}) copy-start(f32[224,8,256]{0,1,2:T(8,128)} %copy-done.11) | copy-start | bytes 5505028
  77.1 1.4 copy-start.8
  78.9 8.4 %collective-permute-start.9 = (f32[224,1,256]{2,0,1:T(8,128)S(1)}, f32[224,1,256]{2,0,1:T(8,128)S(1)}, u32[]{:S(2)}, u32[]{:S(2)}) collective-permute-start(f32[224,1,256]{2,0,1:T(8,128)S(1)} %copy.195), channel_id=1, source_target_pairs={{8,0},{16,8},{24,16},{9,1},{17,9},{25,17},{10,2},{18,10},{26,18},{... | collective-permute-start | bytes 688136 | tf_op jit(solution)/shard_map/ppermute | solution.py:24
  80.3 8.5 %collective-permute-start.8 = (f32[224,1,256]{2,0,1:T(8,128)S(1)}, f32[224,1,256]{2,0,1:T(8,128)S(1)}, u32[]{:S(2)}, u32[]{:S(2)}) collective-permute-start(f32[224,1,256]{2,0,1:T(8,128)S(1)} %copy.194), channel_id=1, source_target_pairs={{0,8},{8,16},{16,24},{1,9},{9,17},{17,25},{2,10},{10,18},{18,26},{... | collective-permute-start | bytes 688136 | tf_op jit(solution)/shard_map/ppermute | solution.py:22
  89.0 11.8 %copy-start.9 = (f32[224,8,256]{0,1,2:T(8,128)S(1)}, f32[224,8,256]{0,1,2:T(8,128)}, u32[]{:S(2)}) copy-start(f32[224,8,256]{0,1,2:T(8,128)} %copy-done.8) | copy-start | bytes 5505028
  89.9 6.3 %collective-permute-start.11 = (f32[224,10,1]{0,1,2:T(8,128)S(1)}, f32[224,10,1]{0,1,2:T(8,128)S(1)}, u32[]{:S(2)}, u32[]{:S(2)}) collective-permute-start(f32[224,10,1]{0,1,2:T(8,128)S(1)} %get-tuple-element.25), channel_id=1, source_target_pairs={{0,1},{1,2},{2,3},{3,4},{4,5},{5,6},{6,7},{8,9},{9,10},{10,11},{11... | collective-permute-start | bytes 26888 | tf_op jit(solution)/shard_map/ppermute | solution.py:22
  94.9 5.9 %collective-permute-start.10 = (f32[224,10,1]{0,1,2:T(8,128)S(1)}, f32[224,10,1]{0,1,2:T(8,128)S(1)}, u32[]{:S(2)}, u32[]{:S(2)}) collective-permute-start(f32[224,10,1]{0,1,2:T(8,128)S(1)} %get-tuple-element.24), channel_id=1, source_target_pairs={{1,0},{2,1},{3,2},{4,3},{5,4},{6,5},{7,6},{9,8},{10,9},{11,10},{12... | collective-permute-start | bytes 26888 | tf_op jit(solution)/shard_map/ppermute | solution.py:24
  98.7 2.2 copy-start.3
  103.8 8.4 %copy-start.10 = (f32[224,8,256]{0,1,2:T(8,128)S(1)}, f32[224,8,256]{0,1,2:T(8,128)}, u32[]{:S(2)}) copy-start(f32[224,8,256]{0,1,2:T(8,128)} %copy-done.8) | copy-start | bytes 5505028
  116.1 1.4 copy-start.5
  117.9 8.4 %collective-permute-start.13 = (f32[224,1,256]{2,0,1:T(8,128)S(1)}, f32[224,1,256]{2,0,1:T(8,128)S(1)}, u32[]{:S(2)}, u32[]{:S(2)}) collective-permute-start(f32[224,1,256]{2,0,1:T(8,128)S(1)} %copy.202), channel_id=1, source_target_pairs={{8,0},{16,8},{24,16},{9,1},{17,9},{25,17},{10,2},{18,10},{26,18},{... | collective-permute-start | bytes 688136 | tf_op jit(solution)/shard_map/ppermute | solution.py:24
  119.3 8.5 %collective-permute-start.12 = (f32[224,1,256]{2,0,1:T(8,128)S(1)}, f32[224,1,256]{2,0,1:T(8,128)S(1)}, u32[]{:S(2)}, u32[]{:S(2)}) collective-permute-start(f32[224,1,256]{2,0,1:T(8,128)S(1)} %copy.201), channel_id=1, source_target_pairs={{0,8},{8,16},{16,24},{1,9},{9,17},{17,25},{2,10},{10,18},{18,26},{... | collective-permute-start | bytes 688136 | tf_op jit(solution)/shard_map/ppermute | solution.py:22
  128.0 11.8 %copy-start.6 = (f32[224,8,256]{0,1,2:T(8,128)S(1)}, f32[224,8,256]{0,1,2:T(8,128)}, u32[]{:S(2)}) copy-start(f32[224,8,256]{0,1,2:T(8,128)} %copy-done.5) | copy-start | bytes 5505028
  128.9 6.1 %collective-permute-start.15 = (f32[224,10,1]{0,1,2:T(8,128)S(1)}, f32[224,10,1]{0,1,2:T(8,128)S(1)}, u32[]{:S(2)}, u32[]{:S(2)}) collective-permute-start(f32[224,10,1]{0,1,2:T(8,128)S(1)} %get-tuple-element.23), channel_id=1, source_target_pairs={{0,1},{1,2},{2,3},{3,4},{4,5},{5,6},{6,7},{8,9},{9,10},{10,11},{11... | collective-permute-start | bytes 26888 | tf_op jit(solution)/shard_map/ppermute | solution.py:22
  133.7 6.1 %collective-permute-start.14 = (f32[224,10,1]{0,1,2:T(8,128)S(1)}, f32[224,10,1]{0,1,2:T(8,128)S(1)}, u32[]{:S(2)}, u32[]{:S(2)}) collective-permute-start(f32[224,10,1]{0,1,2:T(8,128)S(1)} %get-tuple-element.22), channel_id=1, source_target_pairs={{1,0},{2,1},{3,2},{4,3},{5,4},{6,5},{7,6},{9,8},{10,9},{11,10},{12... | collective-permute-start | bytes 26888 | tf_op jit(solution)/shard_map/ppermute | solution.py:24
  137.5 2.3 copy-start.4
  142.8 8.4 %copy-start.7 = (f32[224,8,256]{0,1,2:T(8,128)S(1)}, f32[224,8,256]{0,1,2:T(8,128)}, u32[]{:S(2)}) copy-start(f32[224,8,256]{0,1,2:T(8,128)} %copy-done.5) | copy-start | bytes 5505028
  164.0 152.1 %copy-start.15 = (f32[224,8,256]{2,1,0:T(8,128)}, f32[224,8,256]{2,1,0:T(8,128)S(1)}, u32[]{:S(2)}) copy-start(f32[224,8,256]{2,1,0:T(8,128)S(1)} %copy.215) | copy-start | bytes 5505028
  (1 other events, 1.3 us)
Sparse Core Ops, SparseCore 0:
  161.5 129.5 all-reduce.1
where the time goes:
time: 326 us; the launch traced here: 325 us
  waiting for transfers between devices  148 us (45%)
  other arithmetic  82.5 us (25%)
  starting transfers between devices  46.1 us (14%)
  local copies, waits for them, and re-layouts  20.7 us (6%)
  between operations  14.7 us (5%)
  matrix products  13 us (4%)
    psum x1, waiting for transfers between devices, shards(): gram_full = lax.psum(local_gram, ('row', 'col'))  125 us
    ppermute x8, starting transfers between devices, padded_2(): lax.ppermute(tail, axis, [(i, (i + 1) % count) for i in range(ends)])  35.6 us
    mul x4, other arithmetic, smooth_step(): flux_col = weight * diff_col  31.7 us
    ppermute x8, waiting for transfers between devices, padded_2(): lax.ppermute(head, axis, [((i + 1) % count, i) for i in range(ends)])  17 us
    unnamed x38, local copies, waits for them, and re-layouts  14.2 us
    add x4, other arithmetic, smooth_step(): return centre + tau_step * spread + tau_step * fidelity * (source - centre)  12.4 us
    reduce_sum x4, other arithmetic, smooth_step(): energy_sum = jnp.sum(diff_col * diff_col + diff_row * diff_row, axis=0)  11 us
    ppermute x8, starting transfers between devices, padded_2(): lax.ppermute(head, axis, [((i + 1) % count, i) for i in range(ends)])  10.5 us
  transfers between devices with their start and end apart: 17, of which 13 were waited for; matrix products, arithmetic and copies ran while one was open for 5% of the time, Pallas kernels for 0%

commit v1 on v0

--- a/solution.py
+++ b/solution.py
@@ -50,6 +50,20 @@
     return centre + tau_step * spread + tau_step * fidelity * (source - centre)
 
 
+def butterfly_sum(value, axes):
+    for axis in axes:
+        count = lax.axis_size(axis)
+        if count & (count - 1):
+            value = lax.psum(value, axis)
+            continue
+        step = 1
+        while step < count:
+            partner = lax.ppermute(value, axis, [(i, i ^ step) for i in range(count)])
+            value = value + partner
+            step *= 2
+    return value
+
+
 def orthonormal(block):
     inner = jnp.dot(block.T, block, precision=lax.Precision.HIGHEST)
     lower = jnp.linalg.cholesky(inner)
@@ -71,7 +85,7 @@
         precision=lax.Precision.HIGHEST,
         preferred_element_type=jnp.float32,
     )
-    gram_full = lax.psum(local_gram, ("row", "col"))
+    gram_full = butterfly_sum(local_gram, ("col", "row"))
     for turn in range(SUBIT):
         product = jnp.dot(gram_full, basis_now, precision=lax.Precision.HIGHEST)
         basis_now = orthonormal(orthonormal(product))

time: 326 us -> 219 us (0.67)
  waiting for transfers between devices: 148 us -> 43.4 us
  starting transfers between devices: 46.1 us -> 60.3 us
  between operations: 14.7 us -> 1.32 us
    psum x1 -> x0, waiting for transfers between devices: 125 us -> none  [shards(): gram_full = lax.psum(local_gram, ('row', 'col'))]
    ppermute x0 -> x5, waiting for transfers between devices: none -> 20.7 us  [butterfly_sum(): partner = lax.ppermute(value, axis, [(i, i ^ step) for i in range(count)])]
    ppermute x0 -> x5, starting transfers between devices: none -> 14.2 us  [butterfly_sum(): partner = lax.ppermute(value, axis, [(i, i ^ step) for i in range(count)])]
  transfers between devices with their start and end apart: 17 -> 21, of which waited for: 13 -> 17; matrix products, arithmetic and copies ran while one was open for 5% -> 7% of each run, Pallas kernels for 0% -> 0%
where the time goes in v1:
time: 219 us; the launch traced here: 218 us
  other arithmetic  81.9 us (37%)
  starting transfers between devices  60.3 us (28%)
  waiting for transfers between devices  43.4 us (20%)
  local copies, waits for them, and re-layouts  20.8 us (9%)
  matrix products  10.4 us (5%)
    ppermute x8, starting transfers between devices, padded_2(): lax.ppermute(tail, axis, [(i, (i + 1) % count) for i in range(ends)])  35.5 us
    mul x4, other arithmetic, smooth_step(): flux_col = weight * diff_col  31.7 us
    ppermute x5, waiting for transfers between devices, butterfly_sum(): partner = lax.ppermute(value, axis, [(i, i ^ step) for i in range(count)])  20.7 us
    ppermute x8, waiting for transfers between devices, padded_2(): lax.ppermute(head, axis, [((i + 1) % count, i) for i in range(ends)])  17.1 us
    unnamed x38, local copies, waits for them, and re-layouts  14.3 us
    ppermute x5, starting transfers between devices, butterfly_sum(): partner = lax.ppermute(value, axis, [(i, i ^ step) for i in range(count)])  14.2 us
    add x4, other arithmetic, smooth_step(): return centre + tau_step * spread + tau_step * fidelity * (source - centre)  12.4 us
    reduce_sum x4, other arithmetic, smooth_step(): energy_sum = jnp.sum(diff_col * diff_col + diff_row * diff_row, axis=0)  11 us
  transfers between devices with their start and end apart: 21, of which 17 were waited for; matrix products, arithmetic and copies ran while one was open for 7% of the time, Pallas kernels for 0%

profile of v1, /device:TPU:0, one launch (start us, length us, event | category | flops | bytes accessed | tf_op | source)
XLA Modules:
  0.0 218.1 jit_solution(5592540037595035185)
XLA Ops:
  4.4 5.6 %collective-permute-start = (f32[224,1,256]{2,0,1:T(8,128)S(1)}, f32[224,1,256]{2,0,1:T(8,128)S(1)}, u32[]{:S(2)}, u32[]{:S(2)}) collective-permute-start(f32[224,1,256]{2,0,1:T(8,128)S(1)} %copy.216), channel_id=1, source_target_pairs={{0,8},{8,16},{16,24},{1,9},{9,17},{17,25},{2,10},{10,18},{18,26},{... | collective-permute-start | bytes 688136 | tf_op jit(solution)/shard_map/ppermute | solution.py:22
  18.4 2.8 %collective-permute-done.2 = f32[224,10,1]{0,1,2:T(8,128)S(1)} collective-permute-done((f32[224,10,1]{0,1,2:T(8,128)S(1)}, f32[224,10,1]{0,1,2:T(8,128)S(1)}, u32[]{:S(2)}, u32[]{:S(2)}) %collective-permute-start.2) | collective-permute-done | bytes 8992 | tf_op jit(solution)/shard_map/ppermute | solution.py:24
  21.2 2.7 %add_reduce_fusion.3 = f32[9,257]{0,1:T(8,128)S(1)} fusion(f32[224,10,257]{0,1,2:T(8,128)S(1)} %maximum_maximum_fusion, f32[224,10,1]{0,1,2:T(8,128)S(1)} %collective-permute-done.2, f32[224,1,256]{0,1,2:T(1,128)S(1)} %copy.181, f32[224,8,256]{0,1,2:T(8,128)S(1)} %copy.184, f32[224,1,256]{0,1,2:T(1,128)S(1)} %copy.179), kind=kLoop, calls=%fused_computation.27 | loop fusion | flops 4660695 | bytes 6456868 | tf_op jit(solution)/shard_map/reduce_sum | solution.py:39
  24.2 6.5 %broadcast_multiply_fusion.7 = (f32[224,9,257]{0,1,2:T(8,128)S(1)}, f32[224,9,257]{0,1,2:T(8,128)S(1)}) fusion(f32[9,257]{0,1:T(8,128)S(1)} %copy.183, f32[224,10,257]{0,1,2:T(8,128)} %copy-done.1, f32[224,10,1]{0,1,2:T(8,128)S(1)} %collective-permute-done.2, f32[224,1,256]{0,1,2:T(1,128)S(1)} %copy.181, f32[224,8,256]{0,1,2:T(8,128)S(1)} %copy.184, ...), kind=kLoop, calls=%fused_computation.35 | loop fusion | flops 3626784 | bytes 10601764 | tf_op jit(solution)/shard_map/mul | solution.py:41
  35.0 5.0 %collective-permute-start.4 = (f32[224,1,256]{2,0,1:T(8,128)S(1)}, f32[224,1,256]{2,0,1:T(8,128)S(1)}, u32[]{:S(2)}, u32[]{:S(2)}) collective-permute-start(f32[224,1,256]{2,0,1:T(8,128)S(1)} %copy.187), channel_id=1, source_target_pairs={{0,8},{8,16},{16,24},{1,9},{9,17},{17,25},{2,10},{10,18},{18,26},{... | collective-permute-start | bytes 688136 | tf_op jit(solution)/shard_map/ppermute | solution.py:22
  40.0 2.5 %collective-permute-done.5 = f32[224,1,256]{2,0,1:T(8,128)S(1)} collective-permute-done((f32[224,1,256]{2,0,1:T(8,128)S(1)}, f32[224,1,256]{2,0,1:T(8,128)S(1)}, u32[]{:S(2)}, u32[]{:S(2)}) %collective-permute-start.5) | collective-permute-done | bytes 229408 | tf_op jit(solution)/shard_map/ppermute | solution.py:24
  45.5 3.6 %collective-permute-start.7 = (f32[224,10,1]{0,1,2:T(8,128)S(1)}, f32[224,10,1]{0,1,2:T(8,128)S(1)}, u32[]{:S(2)}, u32[]{:S(2)}) collective-permute-start(f32[224,10,1]{0,1,2:T(8,128)S(1)} %get-tuple-element.27), channel_id=1, source_target_pairs={{0,1},{1,2},{2,3},{3,4},{4,5},{5,6},{6,7},{8,9},{9,10},{10,11},{11... | collective-permute-start | bytes 26888 | tf_op jit(solution)/shard_map/ppermute | solution.py:22
  50.6 2.4 %maximum_maximum_fusion.1 = f32[224,10,257]{0,1,2:T(8,128)S(1)} fusion(f32[224,1,256]{0,1,2:T(1,128)S(1)} %copy.190, f32[224,8,256]{0,1,2:T(8,128)} %copy-done.11, f32[224,1,256]{0,1,2:T(1,128)S(1)} %copy.189, f32[224,10,1]{0,1,2:T(8,128)S(1)} %collective-permute-done.7), kind=kLoop, calls=%fused_computation.21 | loop fusion | flops 1727040 | bytes 4605440 | tf_op jit(solution)/shard_map/concatenate | solution.py:20
  55.3 2.8 %add_reduce_fusion.2 = f32[9,257]{0,1:T(8,128)S(1)} fusion(f32[224,10,257]{0,1,2:T(8,128)S(1)} %maximum_maximum_fusion.1, f32[224,10,1]{0,1,2:T(8,128)S(1)} %collective-permute-done.6, f32[224,1,256]{0,1,2:T(1,128)S(1)} %copy.190, f32[224,8,256]{0,1,2:T(8,128)S(1)} %copy-done.12, f32[224,1,256]{0,1,2:T(1,128)S(1)} %copy.189), kind=kLoop, calls=%fused_computation.26 | loop fusion | flops 4660695 | bytes 6456868 | tf_op jit(solution)/shard_map/reduce_sum | solution.py:39
  58.3 8.4 %broadcast_multiply_fusion.5 = (f32[224,9,257]{0,1,2:T(8,128)S(1)}, f32[224,9,257]{0,1,2:T(8,128)}) fusion(f32[9,257]{0,1:T(8,128)S(1)} %copy.192, f32[224,10,257]{0,1,2:T(8,128)} %copy-done.2, f32[224,10,1]{0,1,2:T(8,128)S(1)} %collective-permute-done.6, f32[224,1,256]{0,1,2:T(1,128)S(1)} %copy.190, f32[224,8,256]{0,1,2:T(8,128)} %copy-done.11, ...), kind=kLoop, calls=%fused_computation.33 | loop fusion | flops 3626784 | bytes 10601764 | tf_op jit(solution)/shard_map/mul | solution.py:41
  66.7 3.8 %fusion.12 = f32[224,8,256]{0,1,2:T(8,128)S(1)} fusion(f32[224,8,256]{0,1,2:T(8,128)S(1)} %copy-done.13, f32[224,9,257]{0,1,2:T(8,128)} %get-tuple-element.19, f32[224,9,257]{0,1,2:T(8,128)S(1)} %get-tuple-element.18, f32[224,8,256]{0,1,2:T(8,128)S(1)} %copy.184), kind=kLoop, calls=%fused_computation.51 | loop fusion | flops 3670016 | bytes 12845056 | tf_op jit(solution)/shard_map/add | solution.py:50
  73.8 5.0 %collective-permute-start.8 = (f32[224,1,256]{2,0,1:T(8,128)S(1)}, f32[224,1,256]{2,0,1:T(8,128)S(1)}, u32[]{:S(2)}, u32[]{:S(2)}) collective-permute-start(f32[224,1,256]{2,0,1:T(8,128)S(1)} %copy.194), channel_id=1, source_target_pairs={{0,8},{8,16},{16,24},{1,9},{9,17},{17,25},{2,10},{10,18},{18,26},{... | collective-permute-start | bytes 688136 | tf_op jit(solution)/shard_map/ppermute | solution.py:22
  83.4 5.0 %collective-permute-start.11 = (f32[224,10,1]{0,1,2:T(8,128)S(1)}, f32[224,10,1]{0,1,2:T(8,128)S(1)}, u32[]{:S(2)}, u32[]{:S(2)}) collective-permute-start(f32[224,10,1]{0,1,2:T(8,128)S(1)} %get-tuple-element.25), channel_id=1, source_target_pairs={{0,1},{1,2},{2,3},{3,4},{4,5},{5,6},{6,7},{8,9},{9,10},{10,11},{11... | collective-permute-start | bytes 26888 | tf_op jit(solution)/shard_map/ppermute | solution.py:22
  89.7 2.4 %maximum_maximum_fusion.2 = f32[224,10,257]{0,1,2:T(8,128)S(1)} fusion(f32[224,1,256]{0,1,2:T(1,128)S(1)} %copy.197, f32[224,8,256]{0,1,2:T(8,128)} %copy-done.8, f32[224,1,256]{0,1,2:T(1,128)S(1)} %copy.196, f32[224,10,1]{0,1,2:T(8,128)S(1)} %collective-permute-done.11), kind=kLoop, calls=%fused_computation.22 | loop fusion | flops 1727040 | bytes 4605440 | tf_op jit(solution)/shard_map/concatenate | solution.py:20
  94.3 2.8 %add_reduce_fusion.1 = f32[9,257]{0,1:T(8,128)S(1)} fusion(f32[224,10,257]{0,1,2:T(8,128)S(1)} %maximum_maximum_fusion.2, f32[224,10,1]{0,1,2:T(8,128)S(1)} %collective-permute-done.10, f32[224,1,256]{0,1,2:T(1,128)S(1)} %copy.197, f32[224,8,256]{0,1,2:T(8,128)S(1)} %copy-done.9, f32[224,1,256]{0,1,2:T(1,128)S(1)} %copy.196), kind=kLoop, calls=%fused_computation.25 | loop fusion | flops 4660695 | bytes 6456868 | tf_op jit(solution)/shard_map/reduce_sum | solution.py:39
  97.3 8.4 %broadcast_multiply_fusion.3 = (f32[224,9,257]{0,1,2:T(8,128)S(1)}, f32[224,9,257]{0,1,2:T(8,128)}) fusion(f32[9,257]{0,1:T(8,128)S(1)} %copy.199, f32[224,10,257]{0,1,2:T(8,128)} %copy-done.3, f32[224,10,1]{0,1,2:T(8,128)S(1)} %collective-permute-done.10, f32[224,1,256]{0,1,2:T(1,128)S(1)} %copy.197, f32[224,8,256]{0,1,2:T(8,128)} %copy-done.8, ...), kind=kLoop, calls=%fused_computation.31 | loop fusion | flops 3626784 | bytes 10601764 | tf_op jit(solution)/shard_map/mul | solution.py:41
  105.7 3.8 %fusion.9 = f32[224,8,256]{0,1,2:T(8,128)S(1)} fusion(f32[224,8,256]{0,1,2:T(8,128)S(1)} %copy-done.10, f32[224,9,257]{0,1,2:T(8,128)} %get-tuple-element.17, f32[224,9,257]{0,1,2:T(8,128)S(1)} %get-tuple-element.16, f32[224,8,256]{0,1,2:T(8,128)S(1)} %copy.184), kind=kLoop, calls=%fused_computation.45 | loop fusion | flops 3670016 | bytes 12845056 | tf_op jit(solution)/shard_map/add | solution.py:50
  112.8 5.2 %collective-permute-start.12 = (f32[224,1,256]{2,0,1:T(8,128)S(1)}, f32[224,1,256]{2,0,1:T(8,128)S(1)}, u32[]{:S(2)}, u32[]{:S(2)}) collective-permute-start(f32[224,1,256]{2,0,1:T(8,128)S(1)} %copy.201), channel_id=1, source_target_pairs={{0,8},{8,16},{16,24},{1,9},{9,17},{17,25},{2,10},{10,18},{18,26},{... | collective-permute-start | bytes 688136 | tf_op jit(solution)/shard_map/ppermute | solution.py:22
  122.4 4.8 %collective-permute-start.15 = (f32[224,10,1]{0,1,2:T(8,128)S(1)}, f32[224,10,1]{0,1,2:T(8,128)S(1)}, u32[]{:S(2)}, u32[]{:S(2)}) collective-permute-start(f32[224,10,1]{0,1,2:T(8,128)S(1)} %get-tuple-element.23), channel_id=1, source_target_pairs={{0,1},{1,2},{2,3},{3,4},{4,5},{5,6},{6,7},{8,9},{9,10},{10,11},{11... | collective-permute-start | bytes 26888 | tf_op jit(solution)/shard_map/ppermute | solution.py:22
  133.3 2.8 %add_reduce_fusion = f32[9,257]{0,1:T(8,128)S(1)} fusion(f32[224,10,257]{0,1,2:T(8,128)S(1)} %maximum_maximum_fusion.3, f32[224,10,1]{0,1,2:T(8,128)S(1)} %collective-permute-done.14, f32[224,1,256]{0,1,2:T(1,128)S(1)} %copy.204, f32[224,8,256]{0,1,2:T(8,128)S(1)} %copy-done.6, f32[224,1,256]{0,1,2:T(1,128)S(1)} %copy.203), kind=kLoop, calls=%fused_computation.24 | loop fusion | flops 4660695 | bytes 6456868 | tf_op jit(solution)/shard_map/reduce_sum | solution.py:39
  136.3 8.4 %broadcast_multiply_fusion.1 = (f32[224,9,257]{0,1,2:T(8,128)S(1)}, f32[224,9,257]{0,1,2:T(8,128)}) fusion(f32[9,257]{0,1:T(8,128)S(1)} %copy.206, f32[224,10,257]{0,1,2:T(8,128)} %copy-done.4, f32[224,10,1]{0,1,2:T(8,128)S(1)} %collective-permute-done.14, f32[224,1,256]{0,1,2:T(1,128)S(1)} %copy.204, f32[224,8,256]{0,1,2:T(8,128)} %copy-done.5, ...), kind=kLoop, calls=%fused_computation.29 | loop fusion | flops 3626784 | bytes 10601764 | tf_op jit(solution)/shard_map/mul | solution.py:41
  144.7 3.8 %fusion.6 = f32[224,8,256]{0,1,2:T(8,128)S(1)} fusion(f32[224,8,256]{0,1,2:T(8,128)S(1)} %copy-done.7, f32[224,9,257]{0,1,2:T(8,128)} %get-tuple-element.15, f32[224,9,257]{0,1,2:T(8,128)S(1)} %get-tuple-element.14, f32[224,8,256]{0,1,2:T(8,128)S(1)} %copy.184), kind=kLoop, calls=%fused_computation.39 | loop fusion | flops 3670016 | bytes 12845056 | tf_op jit(solution)/shard_map/add | solution.py:50
  149.8 4.3 %fusion.18 = f32[224,224]{1,0:T(8,128)S(1)} fusion(f32[224,8,256]{0,1,2:T(8,128)S(1)} %fusion.6), kind=kOutput, calls=%fused_computation.62 | convolution fusion | flops 1233125376 | bytes 2035712 | tf_op jit(solution)/shard_map/dot_general | solution.py:81
  154.2 3.8 %collective-permute-start.16 = (f32[224,224]{1,0:T(8,128)S(1)}, f32[224,224]{1,0:T(8,128)S(1)}, u32[]{:S(2)}, u32[]{:S(2)}) collective-permute-start(f32[224,224]{1,0:T(8,128)S(1)} %fusion.18), channel_id=1, source_target_pairs={{0,1},{1,0},{2,3},{3,2},{4,5},{5,4},{6,7},{7,6},{8,9},{9,8},{10,11... | collective-permute-start | bytes 602120 | tf_op jit(solution)/shard_map/ppermute | solution.py:61
  161.2 5.9 %collective-permute-done.17 = f32[224,224]{1,0:T(8,128)S(1)} collective-permute-done((f32[224,224]{1,0:T(8,128)S(1)}, f32[224,224]{1,0:T(8,128)S(1)}, u32[]{:S(2)}, u32[]{:S(2)}) %collective-permute-start.17) | collective-permute-done | bytes 200736 | tf_op jit(solution)/shard_map/ppermute | solution.py:61
  169.4 5.1 %collective-permute-done.18 = f32[224,224]{1,0:T(8,128)S(1)} collective-permute-done((f32[224,224]{1,0:T(8,128)S(1)}, f32[224,224]{1,0:T(8,128)S(1)}, u32[]{:S(2)}, u32[]{:S(2)}) %collective-permute-start.18) | collective-permute-done | bytes 200736 | tf_op jit(solution)/shard_map/ppermute | solution.py:61
  174.5 2.5 %collective-permute-start.19 = (f32[224,224]{1,0:T(8,128)S(1)}, f32[224,224]{1,0:T(8,128)S(1)}, u32[]{:S(2)}, u32[]{:S(2)}) collective-permute-start(f32[224,224]{1,0:T(8,128)S(1)} %add.121), channel_id=1, source_target_pairs={{0,8},{8,0},{16,24},{24,16},{1,9},{9,1},{17,25},{25,17},{2,10},{10... | collective-permute-start | bytes 602120 | tf_op jit(solution)/shard_map/ppermute | solution.py:61
  177.1 4.5 %collective-permute-done.19 = f32[224,224]{1,0:T(8,128)S(1)} collective-permute-done((f32[224,224]{1,0:T(8,128)S(1)}, f32[224,224]{1,0:T(8,128)S(1)}, u32[]{:S(2)}, u32[]{:S(2)}) %collective-permute-start.19) | collective-permute-done | bytes 200736 | tf_op jit(solution)/shard_map/ppermute | solution.py:61
  181.5 3.5 %collective-permute-start.20 = (f32[224,224]{1,0:T(8,128)S(1)}, f32[224,224]{1,0:T(8,128)S(1)}, u32[]{:S(2)}, u32[]{:S(2)}) collective-permute-start(f32[224,224]{1,0:T(8,128)S(1)} %add.122), channel_id=1, source_target_pairs={{0,16},{8,24},{16,0},{24,8},{1,17},{9,25},{17,1},{25,9},{2,18},{10... | collective-permute-start | bytes 602120 | tf_op jit(solution)/shard_map/ppermute | solution.py:61
  185.1 2.6 %copy.215 = f32[224,8,256]{2,1,0:T(8,128)S(1)} copy(f32[224,8,256]{0,1,2:T(8,128)} %copy-done.14) | data formatting | bytes 3670016
  189.6 4.2 %collective-permute-done.20 = f32[224,224]{1,0:T(8,128)S(1)} collective-permute-done((f32[224,224]{1,0:T(8,128)S(1)}, f32[224,224]{1,0:T(8,128)S(1)}, u32[]{:S(2)}, u32[]{:S(2)}) %collective-permute-start.20) | collective-permute-done | bytes 200736 | tf_op jit(solution)/shard_map/ppermute | solution.py:61
  212.0 2.5 %fusion.49 = f32[16,2048]{1,0:T(8,128)S(1)} fusion(f32[224,16]{0,1:T(8,128)S(1)} %convolution_bitcast_fusion, f32[224,2048]{1,0:T(8,128)} %bitcast.71), kind=kOutput, calls=%fused_computation.126 | convolution fusion | flops 88080384 | bytes 1980416 | tf_op jit(solution)/shard_map/dot_general | solution.py:92
  (144 shorter events, 79.3 us)
Async XLA Ops:
  0.6 193.2 %copy-start = (f32[224,16]{0,1:T(8,128)S(1)}, f32[224,16]{0,1:T(8,128)}, u32[]{:S(2)}) copy-start(f32[224,16]{0,1:T(8,128)} %param.6) | copy-start | bytes 43012
  3.0 10.5 %collective-permute-start.1 = (f32[224,1,256]{2,0,1:T(8,128)S(1)}, f32[224,1,256]{2,0,1:T(8,128)S(1)}, u32[]{:S(2)}, u32[]{:S(2)}) collective-permute-start(f32[224,1,256]{2,0,1:T(8,128)S(1)} %copy.217), channel_id=1, source_target_pairs={{8,0},{16,8},{24,16},{9,1},{17,9},{25,17},{10,2},{18,10},{26,18},{... | collective-permute-start | bytes 688136 | tf_op jit(solution)/shard_map/ppermute | solution.py:24
  4.4 10.4 %collective-permute-start = (f32[224,1,256]{2,0,1:T(8,128)S(1)}, f32[224,1,256]{2,0,1:T(8,128)S(1)}, u32[]{:S(2)}, u32[]{:S(2)}) collective-permute-start(f32[224,1,256]{2,0,1:T(8,128)S(1)} %copy.216), channel_id=1, source_target_pairs={{0,8},{8,16},{16,24},{1,9},{9,17},{17,25},{2,10},{10,18},{18,26},{... | collective-permute-start | bytes 688136 | tf_op jit(solution)/shard_map/ppermute | solution.py:22
  15.0 2.6 %collective-permute-start.3 = (f32[224,10,1]{0,1,2:T(8,128)S(1)}, f32[224,10,1]{0,1,2:T(8,128)S(1)}, u32[]{:S(2)}, u32[]{:S(2)}) collective-permute-start(f32[224,10,1]{0,1,2:T(8,128)S(1)} %get-tuple-element.29), channel_id=1, source_target_pairs={{0,1},{1,2},{2,3},{3,4},{4,5},{5,6},{6,7},{8,9},{9,10},{10,11},{11... | collective-permute-start | bytes 26888 | tf_op jit(solution)/shard_map/ppermute | solution.py:22
  16.3 5.0 %collective-permute-start.2 = (f32[224,10,1]{0,1,2:T(8,128)S(1)}, f32[224,10,1]{0,1,2:T(8,128)S(1)}, u32[]{:S(2)}, u32[]{:S(2)}) collective-permute-start(f32[224,10,1]{0,1,2:T(8,128)S(1)} %get-tuple-element.28), channel_id=1, source_target_pairs={{1,0},{2,1},{3,2},{4,3},{5,4},{6,5},{7,6},{9,8},{10,9},{11,10},{12... | collective-permute-start | bytes 26888 | tf_op jit(solution)/shard_map/ppermute | solution.py:24
  18.4 2.8 %copy-start.1 = (f32[224,10,257]{0,1,2:T(8,128)}, f32[224,10,257]{0,1,2:T(8,128)S(1)}, u32[]{:S(2)}) copy-start(f32[224,10,257]{0,1,2:T(8,128)S(1)} %maximum_maximum_fusion) | copy-start | bytes 6908164
  33.6 9.0 %collective-permute-start.5 = (f32[224,1,256]{2,0,1:T(8,128)S(1)}, f32[224,1,256]{2,0,1:T(8,128)S(1)}, u32[]{:S(2)}, u32[]{:S(2)}) collective-permute-start(f32[224,1,256]{2,0,1:T(8,128)S(1)} %copy.188), channel_id=1, source_target_pairs={{8,0},{16,8},{24,16},{9,1},{17,9},{25,17},{10,2},{18,10},{26,18},{... | collective-permute-start | bytes 688136 | tf_op jit(solution)/shard_map/ppermute | solution.py:24
  35.0 9.4 %collective-permute-start.4 = (f32[224,1,256]{2,0,1:T(8,128)S(1)}, f32[224,1,256]{2,0,1:T(8,128)S(1)}, u32[]{:S(2)}, u32[]{:S(2)}) collective-permute-start(f32[224,1,256]{2,0,1:T(8,128)S(1)} %copy.187), channel_id=1, source_target_pairs={{0,8},{8,16},{16,24},{1,9},{9,17},{17,25},{2,10},{10,18},{18,26},{... | collective-permute-start | bytes 688136 | tf_op jit(solution)/shard_map/ppermute | solution.py:22
  44.6 10.7 %copy-start.12 = (f32[224,8,256]{0,1,2:T(8,128)S(1)}, f32[224,8,256]{0,1,2:T(8,128)}, u32[]{:S(2)}) copy-start(f32[224,8,256]{0,1,2:T(8,128)} %copy-done.11) | copy-start | bytes 5505028
  45.5 5.1 %collective-permute-start.7 = (f32[224,10,1]{0,1,2:T(8,128)S(1)}, f32[224,10,1]{0,1,2:T(8,128)S(1)}, u32[]{:S(2)}, u32[]{:S(2)}) collective-permute-start(f32[224,10,1]{0,1,2:T(8,128)S(1)} %get-tuple-element.27), channel_id=1, source_target_pairs={{0,1},{1,2},{2,3},{3,4},{4,5},{5,6},{6,7},{8,9},{9,10},{10,11},{11... | collective-permute-start | bytes 26888 | tf_op jit(solution)/shard_map/ppermute | solution.py:22
  49.1 6.2 %collective-permute-start.6 = (f32[224,10,1]{0,1,2:T(8,128)S(1)}, f32[224,10,1]{0,1,2:T(8,128)S(1)}, u32[]{:S(2)}, u32[]{:S(2)}) collective-permute-start(f32[224,10,1]{0,1,2:T(8,128)S(1)} %get-tuple-element.26), channel_id=1, source_target_pairs={{1,0},{2,1},{3,2},{4,3},{5,4},{6,5},{7,6},{9,8},{10,9},{11,10},{12... | collective-permute-start | bytes 26888 | tf_op jit(solution)/shard_map/ppermute | solution.py:24
  53.0 2.3 %copy-start.2 = (f32[224,10,257]{0,1,2:T(8,128)}, f32[224,10,257]{0,1,2:T(8,128)S(1)}, u32[]{:S(2)}) copy-start(f32[224,10,257]{0,1,2:T(8,128)S(1)} %maximum_maximum_fusion.1) | copy-start | bytes 6908164
  58.3 8.4 %copy-start.13 = (f32[224,8,256]{0,1,2:T(8,128)S(1)}, f32[224,8,256]{0,1,2:T(8,128)}, u32[]{:S(2)}) copy-start(f32[224,8,256]{0,1,2:T(8,128)} %copy-done.11) | copy-start | bytes 5505028
  72.4 8.4 %collective-permute-start.9 = (f32[224,1,256]{2,0,1:T(8,128)S(1)}, f32[224,1,256]{2,0,1:T(8,128)S(1)}, u32[]{:S(2)}, u32[]{:S(2)}) collective-permute-start(f32[224,1,256]{2,0,1:T(8,128)S(1)} %copy.195), channel_id=1, source_target_pairs={{8,0},{16,8},{24,16},{9,1},{17,9},{25,17},{10,2},{18,10},{26,18},{... | collective-permute-start | bytes 688136 | tf_op jit(solution)/shard_map/ppermute | solution.py:24
  73.8 8.5 %collective-permute-start.8 = (f32[224,1,256]{2,0,1:T(8,128)S(1)}, f32[224,1,256]{2,0,1:T(8,128)S(1)}, u32[]{:S(2)}, u32[]{:S(2)}) collective-permute-start(f32[224,1,256]{2,0,1:T(8,128)S(1)} %copy.194), channel_id=1, source_target_pairs={{0,8},{8,16},{16,24},{1,9},{9,17},{17,25},{2,10},{10,18},{18,26},{... | collective-permute-start | bytes 688136 | tf_op jit(solution)/shard_map/ppermute | solution.py:22
  82.5 11.8 %copy-start.9 = (f32[224,8,256]{0,1,2:T(8,128)S(1)}, f32[224,8,256]{0,1,2:T(8,128)}, u32[]{:S(2)}) copy-start(f32[224,8,256]{0,1,2:T(8,128)} %copy-done.8) | copy-start | bytes 5505028
  83.4 6.3 %collective-permute-start.11 = (f32[224,10,1]{0,1,2:T(8,128)S(1)}, f32[224,10,1]{0,1,2:T(8,128)S(1)}, u32[]{:S(2)}, u32[]{:S(2)}) collective-permute-start(f32[224,10,1]{0,1,2:T(8,128)S(1)} %get-tuple-element.25), channel_id=1, source_target_pairs={{0,1},{1,2},{2,3},{3,4},{4,5},{5,6},{6,7},{8,9},{9,10},{10,11},{11... | collective-permute-start | bytes 26888 | tf_op jit(solution)/shard_map/ppermute | solution.py:22
  88.4 5.9 %collective-permute-start.10 = (f32[224,10,1]{0,1,2:T(8,128)S(1)}, f32[224,10,1]{0,1,2:T(8,128)S(1)}, u32[]{:S(2)}, u32[]{:S(2)}) collective-permute-start(f32[224,10,1]{0,1,2:T(8,128)S(1)} %get-tuple-element.24), channel_id=1, source_target_pairs={{1,0},{2,1},{3,2},{4,3},{5,4},{6,5},{7,6},{9,8},{10,9},{11,10},{12... | collective-permute-start | bytes 26888 | tf_op jit(solution)/shard_map/ppermute | solution.py:24
  97.3 8.4 %copy-start.10 = (f32[224,8,256]{0,1,2:T(8,128)S(1)}, f32[224,8,256]{0,1,2:T(8,128)}, u32[]{:S(2)}) copy-start(f32[224,8,256]{0,1,2:T(8,128)} %copy-done.8) | copy-start | bytes 5505028
  111.3 8.4 %collective-permute-start.13 = (f32[224,1,256]{2,0,1:T(8,128)S(1)}, f32[224,1,256]{2,0,1:T(8,128)S(1)}, u32[]{:S(2)}, u32[]{:S(2)}) collective-permute-start(f32[224,1,256]{2,0,1:T(8,128)S(1)} %copy.202), channel_id=1, source_target_pairs={{8,0},{16,8},{24,16},{9,1},{17,9},{25,17},{10,2},{18,10},{26,18},{... | collective-permute-start | bytes 688136 | tf_op jit(solution)/shard_map/ppermute | solution.py:24
  112.8 8.5 %collective-permute-start.12 = (f32[224,1,256]{2,0,1:T(8,128)S(1)}, f32[224,1,256]{2,0,1:T(8,128)S(1)}, u32[]{:S(2)}, u32[]{:S(2)}) collective-permute-start(f32[224,1,256]{2,0,1:T(8,128)S(1)} %copy.201), channel_id=1, source_target_pairs={{0,8},{8,16},{16,24},{1,9},{9,17},{17,25},{2,10},{10,18},{18,26},{... | collective-permute-start | bytes 688136 | tf_op jit(solution)/shard_map/ppermute | solution.py:22
  121.5 11.8 %copy-start.6 = (f32[224,8,256]{0,1,2:T(8,128)S(1)}, f32[224,8,256]{0,1,2:T(8,128)}, u32[]{:S(2)}) copy-start(f32[224,8,256]{0,1,2:T(8,128)} %copy-done.5) | copy-start | bytes 5505028
  122.4 6.1 %collective-permute-start.15 = (f32[224,10,1]{0,1,2:T(8,128)S(1)}, f32[224,10,1]{0,1,2:T(8,128)S(1)}, u32[]{:S(2)}, u32[]{:S(2)}) collective-permute-start(f32[224,10,1]{0,1,2:T(8,128)S(1)} %get-tuple-element.23), channel_id=1, source_target_pairs={{0,1},{1,2},{2,3},{3,4},{4,5},{5,6},{6,7},{8,9},{9,10},{10,11},{11... | collective-permute-start | bytes 26888 | tf_op jit(solution)/shard_map/ppermute | solution.py:22
  127.2 6.1 %collective-permute-start.14 = (f32[224,10,1]{0,1,2:T(8,128)S(1)}, f32[224,10,1]{0,1,2:T(8,128)S(1)}, u32[]{:S(2)}, u32[]{:S(2)}) collective-permute-start(f32[224,10,1]{0,1,2:T(8,128)S(1)} %get-tuple-element.22), channel_id=1, source_target_pairs={{1,0},{2,1},{3,2},{4,3},{5,4},{6,5},{7,6},{9,8},{10,9},{11,10},{12... | collective-permute-start | bytes 26888 | tf_op jit(solution)/shard_map/ppermute | solution.py:24
  130.9 2.3 %copy-start.4 = (f32[224,10,257]{0,1,2:T(8,128)}, f32[224,10,257]{0,1,2:T(8,128)S(1)}, u32[]{:S(2)}) copy-start(f32[224,10,257]{0,1,2:T(8,128)S(1)} %maximum_maximum_fusion.3) | copy-start | bytes 6908164
  136.3 8.4 %copy-start.7 = (f32[224,8,256]{0,1,2:T(8,128)S(1)}, f32[224,8,256]{0,1,2:T(8,128)}, u32[]{:S(2)}) copy-start(f32[224,8,256]{0,1,2:T(8,128)} %copy-done.5) | copy-start | bytes 5505028
  154.2 4.9 %collective-permute-start.16 = (f32[224,224]{1,0:T(8,128)S(1)}, f32[224,224]{1,0:T(8,128)S(1)}, u32[]{:S(2)}, u32[]{:S(2)}) collective-permute-start(f32[224,224]{1,0:T(8,128)S(1)} %fusion.18), channel_id=1, source_target_pairs={{0,1},{1,0},{2,3},{3,2},{4,5},{5,4},{6,7},{7,6},{8,9},{9,8},{10,11... | collective-permute-start | bytes 602120 | tf_op jit(solution)/shard_map/ppermute | solution.py:61
  159.1 8.0 %collective-permute-start.17 = (f32[224,224]{1,0:T(8,128)S(1)}, f32[224,224]{1,0:T(8,128)S(1)}, u32[]{:S(2)}, u32[]{:S(2)}) collective-permute-start(f32[224,224]{1,0:T(8,128)S(1)} %add.119), channel_id=1, source_target_pairs={{0,2},{1,3},{2,0},{3,1},{4,6},{5,7},{6,4},{7,5},{8,10},{9,11},{10,... | collective-permute-start | bytes 602120 | tf_op jit(solution)/shard_map/ppermute | solution.py:61
  167.1 7.3 %collective-permute-start.18 = (f32[224,224]{1,0:T(8,128)S(1)}, f32[224,224]{1,0:T(8,128)S(1)}, u32[]{:S(2)}, u32[]{:S(2)}) collective-permute-start(f32[224,224]{1,0:T(8,128)S(1)} %add.120), channel_id=1, source_target_pairs={{0,4},{1,5},{2,6},{3,7},{4,0},{5,1},{6,2},{7,3},{8,12},{9,13},{10,... | collective-permute-start | bytes 602120 | tf_op jit(solution)/shard_map/ppermute | solution.py:61
  174.5 7.0 %collective-permute-start.19 = (f32[224,224]{1,0:T(8,128)S(1)}, f32[224,224]{1,0:T(8,128)S(1)}, u32[]{:S(2)}, u32[]{:S(2)}) collective-permute-start(f32[224,224]{1,0:T(8,128)S(1)} %add.121), channel_id=1, source_target_pairs={{0,8},{8,0},{16,24},{24,16},{1,9},{9,1},{17,25},{25,17},{2,10},{10... | collective-permute-start | bytes 602120 | tf_op jit(solution)/shard_map/ppermute | solution.py:61
  181.5 12.3 %collective-permute-start.20 = (f32[224,224]{1,0:T(8,128)S(1)}, f32[224,224]{1,0:T(8,128)S(1)}, u32[]{:S(2)}, u32[]{:S(2)}) collective-permute-start(f32[224,224]{1,0:T(8,128)S(1)} %add.122), channel_id=1, source_target_pairs={{0,16},{8,24},{16,0},{24,8},{1,17},{9,25},{17,1},{25,9},{2,18},{10... | collective-permute-start | bytes 602120 | tf_op jit(solution)/shard_map/ppermute | solution.py:61
  187.7 28.5 %copy-start.15 = (f32[224,8,256]{2,1,0:T(8,128)}, f32[224,8,256]{2,1,0:T(8,128)S(1)}, u32[]{:S(2)}) copy-start(f32[224,8,256]{2,1,0:T(8,128)S(1)} %copy.215) | copy-start | bytes 5505028
  (5 other events, 7.6 us)

commit v2 on v1

v2 whole, which is shorter than its diff:
```python
import jax
import jax.numpy as jnp
from jax import lax
from jax.sharding import PartitionSpec as P

SWEEPS = 4
SUBIT = 2


tau_step = 0.22
fidelity = 0.1


def butterfly_sum(value, axes):
    for axis in axes:
        count = lax.axis_size(axis)
        if count & (count - 1):
            value = lax.psum(value, axis)
            continue
        step = 1
        while step < count:
            partner = lax.ppermute(value, axis, [(i, i ^ step) for i in range(count)])
            value = value + partner
            step *= 2
    return value


def with_halo(cells, axis, dim, width):
    count = lax.axis_size(axis)
    size = cells.shape[dim]
    head = lax.slice_in_dim(cells, 0, width, axis=dim)
    tail = lax.slice_in_dim(cells, size - width, size, axis=dim)
    before = lax.ppermute(tail, axis, [(i, i + 1) for i in range(count - 1)])
    after = lax.ppermute(head, axis, [(i + 1, i) for i in range(count - 1)])
    return jnp.concatenate([before, cells, after], axis=dim)


def inside_mask(axis, tile, width):
    count = lax.axis_size(axis)
    start = lax.axis_index(axis) * tile - width
    index = start + jnp.arange(tile + 2 * width, dtype=jnp.int32)
    return (index >= 0) & (index < count * tile)


def sweep(field, source, keep):
    diff_col = field[:-1, 1:] - field[:-1, :-1]
    diff_row = field[1:, :-1] - field[:-1, :-1]
    energy_sum = jnp.sum(diff_col * diff_col + diff_row * diff_row, axis=-1, keepdims=True)
    weight = 1.0 / jnp.sqrt(1.0 + energy_sum / field.shape[-1])
    flux_col = weight * diff_col
    flux_row = weight * diff_row
    spread = flux_col[1:, 1:] - flux_col[1:, :-1] + flux_row[1:, 1:] - flux_row[:-1, 1:]
    centre = field[1:-1, 1:-1]
    new = centre + tau_step * spread + tau_step * fidelity * (source - centre)
    return jnp.where(keep, new, 0.0)


def orthonormal(block):
    inner = jnp.dot(block.T, block, precision=lax.Precision.HIGHEST)
    lower = jnp.linalg.cholesky(inner)
    return lax.linalg.triangular_solve(lower, block, left_side=False, lower=True, transpose_a=True)


def shards(image, start_basis):
    band_count, tile_rows, tile_cols = image.shape
    width = SWEEPS
    cells = jnp.transpose(image, (1, 2, 0))
    ext = with_halo(cells, "row", 0, width)
    ext = with_halo(ext, "col", 1, width)
    row_in = inside_mask("row", tile_rows, width)
    col_in = inside_mask("col", tile_cols, width)
    field = ext
    for sweep_no in range(SWEEPS):
        left = width - sweep_no - 1
        lo = sweep_no + 1
        nr = tile_rows + 2 * left
        nc = tile_cols + 2 * left
        source = ext[lo:lo + nr, lo:lo + nc]
        keep = (row_in[lo:lo + nr, None] & col_in[None, lo:lo + nc])[:, :, None]
        field = sweep(field, source, keep)
    flat_cells = field.reshape(tile_rows * tile_cols, band_count)
    smoothed = jnp.transpose(field, (2, 0, 1))
    local_gram = lax.dot_general(
        flat_cells,
        flat_cells,
        (((0,), (0,)), ((), ())),
        precision=lax.Precision.HIGHEST,
        preferred_element_type=jnp.float32,
    )
    gram_full = butterfly_sum(local_gram, ("col", "row"))
    basis_now = start_basis
    for turn in range(SUBIT):
        product = jnp.dot(gram_full, basis_now, precision=lax.Precision.HIGHEST)
        basis_now = orthonormal(orthonormal(product))
    coeffs = jnp.dot(flat_cells, basis_now, precision=lax.Precision.HIGHEST)
    lowrank = lax.dot_general(
        basis_now,
        coeffs,
        (((1,), (1,)), ((), ())),
        precision=lax.Precision.HIGHEST,
    )
    return (smoothed, lowrank.reshape(band_count, tile_rows, tile_cols))


def solution(mesh):
    in_specs = (P(None, "row", "col"), P())
    out_specs = (P(None, "row", "col"), P(None, "row", "col"))
    return jax.shard_map(shards, mesh=mesh, in_specs=in_specs, out_specs=out_specs, check_vma=False)
```

time: 219 us -> 160 us (0.73)
  starting transfers between devices: 60.3 us -> 19.4 us
  other arithmetic: 81.9 us -> 64.1 us
  waiting for transfers between devices: 43.4 us -> 48.4 us
  matrix products: 10.4 us -> 6.33 us
    ppermute x16 -> x4, starting transfers between devices: 46.1 us -> 8.85 us  [the longest x2 6.27 us: with_halo(): before = lax.ppermute(tail, axis, [(i, i + 1) for i in range(count - 1)])]
    select_n x0 -> x4, other arithmetic: none -> 26.1 us  [sweep(): return jnp.where(keep, new, 0.0)]
    mul x4, other arithmetic: 31.7 us -> 10.3 us  [sweep(): flux_col = weight * diff_col]
    add x4 -> x0, other arithmetic: 12.4 us -> none  [smooth_step(): return centre + tau_step * spread + tau_step * fidelity * (source - centre)]
    unnamed x38 -> x7, local copies, waits for them, and re-layouts: 14.3 us -> 6.97 us
    reduce_sum x4, other arithmetic: 11 us -> 4.92 us  [sweep(): jnp.sum(diff_col * diff_col + diff_row * diff_row, axis=-1, keepdims=True)]
    slice x10 -> x12, local copies, waits for them, and re-layouts: 4.1 us -> 8.72 us  [the longest x3 6 us: with_halo(): tail = lax.slice_in_dim(cells, size - width, size, axis=dim)]
    ppermute x5, waiting for transfers between devices: 20.7 us -> 24.9 us  [butterfly_sum(): partner = lax.ppermute(value, axis, [(i, i ^ step) for i in range(count)])]
  transfers between devices with their start and end apart: 21 -> 9, of which waited for: 17 -> 8; matrix products, arithmetic and copies ran while one was open for 7% -> 5% of each run, Pallas kernels for 0% -> 0%
where the time goes in v2:
time: 160 us; the launch traced here: 159 us
  other arithmetic  64.1 us (40%)
  waiting for transfers between devices  48.4 us (30%)
  local copies, waits for them, and re-layouts  19.9 us (12%)
  starting transfers between devices  19.4 us (12%)
  matrix products  6.33 us (4%)
    select_n x4, other arithmetic, sweep(): return jnp.where(keep, new, 0.0)  26.1 us
    ppermute x5, waiting for transfers between devices, butterfly_sum(): partner = lax.ppermute(value, axis, [(i, i ^ step) for i in range(count)])  24.9 us
    ppermute x2, waiting for transfers between devices, with_halo(): before = lax.ppermute(tail, axis, [(i, i + 1) for i in range(count - 1)])  17.7 us
    ppermute x5, starting transfers between devices, butterfly_sum(): partner = lax.ppermute(value, axis, [(i, i ^ step) for i in range(count)])  10.6 us
    mul x4, other arithmetic, sweep(): flux_col = weight * diff_col  10.3 us
    another operation x12, other arithmetic, orthonormal(): lower = jnp.linalg.cholesky(inner)  8.57 us
    another operation x8, other arithmetic, orthonormal(): lax.linalg.triangular_solve(lower, block, left_side=False, lower=True, tr...  7.51 us
    unnamed x7, local copies, waits for them, and re-layouts  6.97 us
  transfers between devices with their start and end apart: 9, of which 8 were waited for; matrix products, arithmetic and copies ran while one was open for 5% of the time, Pallas kernels for 0%

profile of v2, /device:TPU:0, one launch (start us, length us, event | category | flops | bytes accessed | tf_op | source)
XLA Modules:
  0.0 159.1 jit_solution(5034119589637576076)
XLA Ops:
  0.6 2.1 %copy.43 = f32[224,8,256]{2,0,1:T(8,128)S(1)} copy(f32[224,8,256]{2,1,0:T(8,128)} %param.5) | data formatting | bytes 3670016 | tf_op args[0]
  4.2 5.0 %collective-permute-start = (f32[4,256,224]{1,2,0:T(8,128)}, f32[4,256,224]{1,2,0:T(8,128)S(1)}, u32[]{:S(2)}, u32[]{:S(2)}) collective-permute-start(f32[4,256,224]{1,2,0:T(8,128)} %get-tuple-element.20), channel_id=1, source_target_pairs={{0,8},{8,16},{16,24},{1,9},{9,17},{17,25},{2,10},{10,18},{18,26},{... | collective-permute-start | bytes 2752520 | tf_op jit(solution)/shard_map/ppermute | solution.py:33
  11.3 17.7 %collective-permute-done = f32[4,256,224]{1,2,0:T(8,128)S(1)} collective-permute-done((f32[4,256,224]{1,2,0:T(8,128)}, f32[4,256,224]{1,2,0:T(8,128)S(1)}, u32[]{:S(2)}, u32[]{:S(2)}) %collective-permute-start) | collective-permute-done | bytes 917536 | tf_op jit(solution)/shard_map/ppermute | solution.py:33
  29.0 4.2 %collective-permute-done.1 = f32[4,256,224]{1,2,0:T(8,128)} collective-permute-done((f32[4,256,224]{1,2,0:T(8,128)}, f32[4,256,224]{1,2,0:T(8,128)}, u32[]{:S(2)}, u32[]{:S(2)}) %collective-permute-start.1) | collective-permute-done | bytes 917536 | tf_op jit(solution)/shard_map/ppermute | solution.py:34
  34.6 2.4 %fusion.39 = (f32[16,4,224]{1,2,0:T(8,128)}, f32[16,4,224]{1,2,0:T(8,128)}) fusion(f32[16,256,224]{1,2,0:T(8,128)S(1)} %pad_maximum_fusion.1), kind=kLoop, calls=%fused_computation.106 | loop fusion | bytes 229376 | tf_op jit(solution)/shard_map/slice | solution.py:32
  37.0 2.1 %copy.28 = f32[16,4,224]{2,0,1:T(8,128)S(1)} copy(f32[16,4,224]{1,2,0:T(8,128)} %get-tuple-element.16) | data formatting | bytes 114688 | tf_op jit(solution)/shard_map/slice | solution.py:32
  40.5 2.1 %copy.29 = f32[16,4,224]{2,0,1:T(8,128)S(1)} copy(f32[16,4,224]{1,2,0:T(8,128)} %get-tuple-element.17) | data formatting | bytes 114688 | tf_op jit(solution)/shard_map/slice | solution.py:31
  44.0 1.8 %copy.30 = f32[16,4,224]{1,2,0:T(8,128)} copy(f32[16,4,224]{2,0,1:T(8,128)S(1)} %collective-permute-done.2) | data formatting | bytes 114688 | tf_op jit(solution)/shard_map/ppermute | solution.py:33
  45.8 1.7 %collective-permute-done.3 = f32[16,4,224]{2,0,1:T(8,128)S(1)} collective-permute-done((f32[16,4,224]{2,0,1:T(8,128)S(1)}, f32[16,4,224]{2,0,1:T(8,128)S(1)}, u32[]{:S(2)}, u32[]{:S(2)}) %collective-permute-start.3) | collective-permute-done | bytes 57376 | tf_op jit(solution)/shard_map/ppermute | solution.py:34
  47.5 1.8 %copy.31 = f32[16,4,224]{1,2,0:T(8,128)} copy(f32[16,4,224]{2,0,1:T(8,128)S(1)} %collective-permute-done.3) | data formatting | bytes 114688 | tf_op jit(solution)/shard_map/ppermute | solution.py:34
  49.3 4.9 %pad_maximum_fusion = f32[16,264,224]{1,2,0:T(8,128)S(1)} fusion(f32[16,4,224]{1,2,0:T(8,128)} %copy.31, f32[4,256,224]{1,2,0:T(8,128)} %collective-permute-done.1, f32[8,256,224]{1,2,0:T(8,128)S(1)} %bitcast.82, f32[4,256,224]{1,2,0:T(8,128)S(1)} %collective-permute-done, f32[16,4,224]{1,2,0:T(8,128)} %copy.30), kind=kLoop, calls=%fused_computation | loop fusion | flops 3784704 | bytes 7569408 | tf_op jit(solution)/shard_map/concatenate | solution.py:35
  54.2 1.7 %add_reduce_fusion = f32[15,263]{1,0:T(8,128)S(1)} fusion(f32[16,264,224]{1,2,0:T(8,128)S(1)} %pad_maximum_fusion), kind=kLoop, calls=%fused_computation.3 | loop fusion | flops 5298135 | bytes 10619940 | tf_op jit(solution)/shard_map/reduce_sum | solution.py:48
  55.9 2.0 %broadcast_multiply_fusion.1 = (f32[15,263,224]{1,2,0:T(8,128)S(1)}, f32[15,263,224]{1,2,0:T(8,128)S(1)}) fusion(f32[15,263]{1,0:T(8,128)S(1)} %add_rsqrt_fusion.3, f32[16,264,224]{1,2,0:T(8,128)S(1)} %pad_maximum_fusion), kind=kLoop, calls=%fused_computation.40 | loop fusion | flops 3534720 | bytes 17689380 | tf_op jit(solution)/shard_map/mul | solution.py:50
  57.9 5.4 %fusion.3 = f32[14,262,224]{1,2,0:T(8,128)S(1)} fusion(f32[15,263,224]{1,2,0:T(8,128)S(1)} %get-tuple-element.11, f32[15,263,224]{1,2,0:T(8,128)S(1)} %get-tuple-element.10, f32[16,264,224]{1,2,0:T(8,128)S(1)} %pad_maximum_fusion, pred[14,262]{1,0:T(8,128)(4,1)S(1)} %broadcast_and_fusion), kind=kLoop, calls=%fused_computation.8 | loop fusion | flops 7394688 | bytes 19722836 | tf_op jit(solution)/shard_map/jit(_where)/select_n | solution.py:55
  64.6 4.6 %broadcast_multiply_fusion.3 = (f32[13,261,224]{1,2,0:T(8,128)}, f32[13,261,224]{1,2,0:T(8,128)}) fusion(f32[13,261]{1,0:T(8,128)S(1)} %add_rsqrt_fusion.2, f32[14,262,224]{1,2,0:T(8,128)S(1)} %fusion.3), kind=kLoop, calls=%fused_computation.42 | loop fusion | flops 3040128 | bytes 15214212 | tf_op jit(solution)/shard_map/mul | solution.py:50
  69.1 11.7 %fusion.6 = f32[12,260,224]{1,2,0:T(8,128)S(1)} fusion(f32[16,264,224]{1,2,0:T(8,128)S(1)} %pad_maximum_fusion, f32[13,261,224]{1,2,0:T(8,128)} %get-tuple-element.13, f32[13,261,224]{1,2,0:T(8,128)} %get-tuple-element.12, f32[14,262,224]{1,2,0:T(8,128)S(1)} %fusion.3, pred[12,260]{1,0:T(8,128)(4,1)S(1)} %broadcast_and_fusion.1), kind=kLoop, calls=%fused_computation.17 | loop fusion | flops 6289920 | bytes 19571760 | tf_op jit(solution)/shard_map/jit(_where)/select_n | solution.py:55
  81.9 2.8 %broadcast_multiply_fusion.5 = (f32[11,259,224]{1,2,0:T(8,128)S(1)}, f32[11,259,224]{1,2,0:T(8,128)}) fusion(f32[11,259]{1,0:T(8,128)S(1)} %add_rsqrt_fusion.1, f32[12,260,224]{1,2,0:T(8,128)S(1)} %fusion.6), kind=kLoop, calls=%fused_computation.44 | loop fusion | flops 2552704 | bytes 12774916 | tf_op jit(solution)/shard_map/mul | solution.py:50
  84.7 6.8 %fusion.11 = f32[10,258,224]{1,2,0:T(8,128)S(1)} fusion(f32[16,264,224]{1,2,0:T(8,128)S(1)} %pad_maximum_fusion, f32[11,259,224]{1,2,0:T(8,128)} %get-tuple-element.15, f32[11,259,224]{1,2,0:T(8,128)S(1)} %get-tuple-element.14, f32[12,260,224]{1,2,0:T(8,128)S(1)} %fusion.6, pred[10,258]{1,0:T(8,128)(4,1)S(1)} %broadcast_and_fusion.2), kind=kLoop, calls=%fused_computation.30 | loop fusion | flops 5201280 | bytes 16184340 | tf_op jit(solution)/shard_map/jit(_where)/select_n | solution.py:55
  93.9 2.2 %fusion.17 = f32[8,256,224]{1,2,0:T(8,128)S(1)} fusion(f32[9,257,224]{1,2,0:T(8,128)S(1)} %get-tuple-element.19, f32[9,257,224]{1,2,0:T(8,128)S(1)} %get-tuple-element.18, f32[10,258,224]{1,2,0:T(8,128)S(1)} %fusion.11, pred[8,256]{1,0:T(8,128)(4,1)S(1)} %broadcast_and_fusion.3, f32[224,8,256]{2,1,0:T(8,128)S(1)} %copy-done.1), kind=kLoop, calls=%fused_computation.49 | loop fusion | flops 4128768 | bytes 12847104 | tf_op jit(solution)/shard_map/jit(_where)/select_n | solution.py:55
  96.2 1.6 %convolution_bitcast_fusion = f32[224,224]{1,0:T(8,128)S(1)} fusion(f32[8,256,224]{1,2,0:T(8,128)S(1)} %fusion.17), kind=kOutput, calls=%fused_computation.55 | convolution fusion | flops 1233125376 | bytes 2035712 | tf_op jit(solution)/shard_map/dot_general | solution.py:83
  97.8 3.0 %collective-permute-start.4 = (f32[224,224]{1,0:T(8,128)S(1)}, f32[224,224]{1,0:T(8,128)S(1)}, u32[]{:S(2)}, u32[]{:S(2)}) collective-permute-start(f32[224,224]{1,0:T(8,128)S(1)} %convolution_bitcast_fusion), channel_id=1, source_target_pairs={{0,1},{1,0},{2,3},{3,2},{4,5},{5,4},{6,7},{7,6},{8,9},{9,8},{10,11... | collective-permute-start | bytes 602120 | tf_op jit(solution)/shard_map/ppermute | solution.py:22
  102.0 2.5 %collective-permute-start.5 = (f32[224,224]{1,0:T(8,128)S(1)}, f32[224,224]{1,0:T(8,128)S(1)}, u32[]{:S(2)}, u32[]{:S(2)}) collective-permute-start(f32[224,224]{1,0:T(8,128)S(1)} %add.141), channel_id=1, source_target_pairs={{0,2},{1,3},{2,0},{3,1},{4,6},{5,7},{6,4},{7,5},{8,10},{9,11},{10,... | collective-permute-start | bytes 602120 | tf_op jit(solution)/shard_map/ppermute | solution.py:22
  104.4 6.1 %collective-permute-done.5 = f32[224,224]{1,0:T(8,128)S(1)} collective-permute-done((f32[224,224]{1,0:T(8,128)S(1)}, f32[224,224]{1,0:T(8,128)S(1)}, u32[]{:S(2)}, u32[]{:S(2)}) %collective-permute-start.5) | collective-permute-done | bytes 200736 | tf_op jit(solution)/shard_map/ppermute | solution.py:22
  111.5 6.4 %collective-permute-done.6 = f32[224,224]{1,0:T(8,128)S(1)} collective-permute-done((f32[224,224]{1,0:T(8,128)S(1)}, f32[224,224]{1,0:T(8,128)S(1)}, u32[]{:S(2)}, u32[]{:S(2)}) %collective-permute-start.6) | collective-permute-done | bytes 200736 | tf_op jit(solution)/shard_map/ppermute | solution.py:22
  118.0 1.6 collective-permute-start.7
  119.6 4.9 %collective-permute-done.7 = f32[224,224]{1,0:T(8,128)S(1)} collective-permute-done((f32[224,224]{1,0:T(8,128)S(1)}, f32[224,224]{1,0:T(8,128)S(1)}, u32[]{:S(2)}, u32[]{:S(2)}) %collective-permute-start.7) | collective-permute-done | bytes 200736 | tf_op jit(solution)/shard_map/ppermute | solution.py:22
  124.5 2.6 %collective-permute-start.8 = (f32[224,224]{1,0:T(8,128)S(1)}, f32[224,224]{1,0:T(8,128)S(1)}, u32[]{:S(2)}, u32[]{:S(2)}) collective-permute-start(f32[224,224]{1,0:T(8,128)S(1)} %add.144), channel_id=1, source_target_pairs={{0,16},{8,24},{16,0},{24,8},{1,17},{9,25},{17,1},{25,9},{2,18},{10... | collective-permute-start | bytes 602120 | tf_op jit(solution)/shard_map/ppermute | solution.py:22
  127.3 2.3 %copy.37 = f32[224,8,256]{2,1,0:T(8,128)} copy(f32[224,8,256]{2,0,1:T(8,128)S(1)} %bitcast.79) | data formatting | bytes 3670016
  129.6 6.3 %collective-permute-done.8 = f32[224,224]{1,0:T(8,128)S(1)} collective-permute-done((f32[224,224]{1,0:T(8,128)S(1)}, f32[224,224]{1,0:T(8,128)S(1)}, u32[]{:S(2)}, u32[]{:S(2)}) %collective-permute-start.8) | collective-permute-done | bytes 200736 | tf_op jit(solution)/shard_map/ppermute | solution.py:22
  150.2 1.5 cholesky.107
  155.5 1.6 %fusion.48 = f32[224,2048]{1,0:T(8,128)S(1)} fusion(f32[224,16]{0,1:T(8,128)S(1)} %convolution_bitcast_fusion.1, f32[2048,16]{0,1:T(8,128)S(1)} %fusion.47), kind=kOutput, calls=%fused_computation.115 | convolution fusion | flops 88080384 | bytes 1980416 | tf_op jit(solution)/shard_map/dot_general | solution.py:96
  157.2 2.0 %copy.39 = f32[28,8,8,256]{3,2,1,0:T(8,128)} copy(f32[28,8,8,256]{3,1,2,0:T(8,128)S(1)} %bitcast.84) | data formatting | bytes 3670016
  (78 shorter events, 32.8 us)
Async XLA Ops:
  0.6 135.3 %copy-start = (f32[224,16]{0,1:T(8,128)S(1)}, f32[224,16]{0,1:T(8,128)}, u32[]{:S(2)}) copy-start(f32[224,16]{0,1:T(8,128)} %param.6) | copy-start | bytes 43012
  4.2 24.8 %collective-permute-start = (f32[4,256,224]{1,2,0:T(8,128)}, f32[4,256,224]{1,2,0:T(8,128)S(1)}, u32[]{:S(2)}, u32[]{:S(2)}) collective-permute-start(f32[4,256,224]{1,2,0:T(8,128)} %get-tuple-element.20), channel_id=1, source_target_pairs={{0,8},{8,16},{16,24},{1,9},{9,17},{17,25},{2,10},{10,18},{18,26},{... | collective-permute-start | bytes 2752520 | tf_op jit(solution)/shard_map/ppermute | solution.py:33
  9.2 24.0 %collective-permute-start.1 = (f32[4,256,224]{1,2,0:T(8,128)}, f32[4,256,224]{1,2,0:T(8,128)}, u32[]{:S(2)}, u32[]{:S(2)}) collective-permute-start(f32[4,256,224]{1,2,0:T(8,128)} %get-tuple-element.21), channel_id=1, source_target_pairs={{8,0},{16,8},{24,16},{9,1},{17,9},{25,17},{10,2},{18,10},{26,18},{... | collective-permute-start | bytes 2752520 | tf_op jit(solution)/shard_map/ppermute | solution.py:34
  39.2 4.8 %collective-permute-start.2 = (f32[16,4,224]{2,0,1:T(8,128)S(1)}, f32[16,4,224]{2,0,1:T(8,128)S(1)}, u32[]{:S(2)}, u32[]{:S(2)}) collective-permute-start(f32[16,4,224]{2,0,1:T(8,128)S(1)} %copy.28), channel_id=1, source_target_pairs={{0,1},{1,2},{2,3},{3,4},{4,5},{5,6},{6,7},{8,9},{9,10},{10,11},{11... | collective-permute-start | bytes 172040 | tf_op jit(solution)/shard_map/ppermute | solution.py:33
  42.6 4.9 %collective-permute-start.3 = (f32[16,4,224]{2,0,1:T(8,128)S(1)}, f32[16,4,224]{2,0,1:T(8,128)S(1)}, u32[]{:S(2)}, u32[]{:S(2)}) collective-permute-start(f32[16,4,224]{2,0,1:T(8,128)S(1)} %copy.29), channel_id=1, source_target_pairs={{1,0},{2,1},{3,2},{4,3},{5,4},{6,5},{7,6},{9,8},{10,9},{11,10},{12... | collective-permute-start | bytes 172040 | tf_op jit(solution)/shard_map/ppermute | solution.py:34
  92.4 1.5 copy-start.1
  97.8 4.1 %collective-permute-start.4 = (f32[224,224]{1,0:T(8,128)S(1)}, f32[224,224]{1,0:T(8,128)S(1)}, u32[]{:S(2)}, u32[]{:S(2)}) collective-permute-start(f32[224,224]{1,0:T(8,128)S(1)} %convolution_bitcast_fusion), channel_id=1, source_target_pairs={{0,1},{1,0},{2,3},{3,2},{4,5},{5,4},{6,7},{7,6},{8,9},{9,8},{10,11... | collective-permute-start | bytes 602120 | tf_op jit(solution)/shard_map/ppermute | solution.py:22
  102.0 8.6 %collective-permute-start.5 = (f32[224,224]{1,0:T(8,128)S(1)}, f32[224,224]{1,0:T(8,128)S(1)}, u32[]{:S(2)}, u32[]{:S(2)}) collective-permute-start(f32[224,224]{1,0:T(8,128)S(1)} %add.141), channel_id=1, source_target_pairs={{0,2},{1,3},{2,0},{3,1},{4,6},{5,7},{6,4},{7,5},{8,10},{9,11},{10,... | collective-permute-start | bytes 602120 | tf_op jit(solution)/shard_map/ppermute | solution.py:22
  110.6 7.4 %collective-permute-start.6 = (f32[224,224]{1,0:T(8,128)S(1)}, f32[224,224]{1,0:T(8,128)S(1)}, u32[]{:S(2)}, u32[]{:S(2)}) collective-permute-start(f32[224,224]{1,0:T(8,128)S(1)} %add.142), channel_id=1, source_target_pairs={{0,4},{1,5},{2,6},{3,7},{4,0},{5,1},{6,2},{7,3},{8,12},{9,13},{10,... | collective-permute-start | bytes 602120 | tf_op jit(solution)/shard_map/ppermute | solution.py:22
  118.0 6.5 %collective-permute-start.7 = (f32[224,224]{1,0:T(8,128)S(1)}, f32[224,224]{1,0:T(8,128)S(1)}, u32[]{:S(2)}, u32[]{:S(2)}) collective-permute-start(f32[224,224]{1,0:T(8,128)S(1)} %add.143), channel_id=1, source_target_pairs={{0,8},{8,0},{16,24},{24,16},{1,9},{9,1},{17,25},{25,17},{2,10},{10... | collective-permute-start | bytes 602120 | tf_op jit(solution)/shard_map/ppermute | solution.py:22
  124.5 11.4 %collective-permute-start.8 = (f32[224,224]{1,0:T(8,128)S(1)}, f32[224,224]{1,0:T(8,128)S(1)}, u32[]{:S(2)}, u32[]{:S(2)}) collective-permute-start(f32[224,224]{1,0:T(8,128)S(1)} %add.144), channel_id=1, source_target_pairs={{0,16},{8,24},{16,0},{24,8},{1,17},{9,25},{17,1},{25,9},{2,18},{10... | collective-permute-start | bytes 602120 | tf_op jit(solution)/shard_map/ppermute | solution.py:22

commit v3 on v2

--- a/solution.py
+++ b/solution.py
@@ -55,6 +55,17 @@
     return jnp.where(keep, new, 0.0)
 
 
+def gram_times(flat_cells, basis):
+    along = jnp.dot(flat_cells, basis, precision=lax.Precision.HIGHEST)
+    return lax.dot_general(
+        flat_cells,
+        along,
+        (((0,), (0,)), ((), ())),
+        precision=lax.Precision.HIGHEST,
+        preferred_element_type=jnp.float32,
+    )
+
+
 def orthonormal(block):
     inner = jnp.dot(block.T, block, precision=lax.Precision.HIGHEST)
     lower = jnp.linalg.cholesky(inner)
@@ -80,17 +91,10 @@
         field = sweep(field, source, keep)
     flat_cells = field.reshape(tile_rows * tile_cols, band_count)
     smoothed = jnp.transpose(field, (2, 0, 1))
-    local_gram = lax.dot_general(
-        flat_cells,
-        flat_cells,
-        (((0,), (0,)), ((), ())),
-        precision=lax.Precision.HIGHEST,
-        preferred_element_type=jnp.float32,
-    )
-    gram_full = butterfly_sum(local_gram, ("col", "row"))
     basis_now = start_basis
     for turn in range(SUBIT):
-        product = jnp.dot(gram_full, basis_now, precision=lax.Precision.HIGHEST)
+        local_product = gram_times(flat_cells, basis_now)
+        product = butterfly_sum(local_product, ("col", "row"))
         basis_now = orthonormal(orthonormal(product))
     coeffs = jnp.dot(flat_cells, basis_now, precision=lax.Precision.HIGHEST)
     lowrank = lax.dot_general(

time: 160 us -> 162 us (1.012)
  waiting for transfers between devices: 48.4 us -> 40.7 us
  starting transfers between devices: 19.4 us -> 26.7 us
  matrix products: 6.33 us -> 9.51 us
    ppermute x5 -> x10, waiting for transfers between devices: 24.9 us -> 17.1 us  [butterfly_sum(): partner = lax.ppermute(value, axis, [(i, i ^ step) for i in range(count)])]
    ppermute x5 -> x10, starting transfers between devices: 10.6 us -> 17.9 us  [butterfly_sum(): partner = lax.ppermute(value, axis, [(i, i ^ step) for i in range(count)])]
    dot_general x3 -> x4, matrix products: 2.15 us -> 5.2 us  [the longest x2 3.06 us: gram_times(): lax.dot_general(flat_cells, along, (((0,), (0,)), ((), ())), precision=la...]
    unnamed x7 -> x11, local copies, waits for them, and re-layouts: 6.97 us -> 6.99 us
  transfers between devices with their start and end apart: 9 -> 14, of which waited for: 8 -> 12; matrix products, arithmetic and copies ran while one was open for 5% -> 4% of each run, Pallas kernels for 0% -> 0%
where the time goes in v3:
time: 162 us
  other arithmetic  63.9 us (39%)
  waiting for transfers between devices  40.7 us (25%)
  starting transfers between devices  26.7 us (16%)
  local copies, waits for them, and re-layouts  19.9 us (12%)
  matrix products  9.51 us (6%)
    select_n x4, other arithmetic, sweep(): return jnp.where(keep, new, 0.0)  26 us
    ppermute x10, starting transfers between devices, butterfly_sum(): partner = lax.ppermute(value, axis, [(i, i ^ step) for i in range(count)])  17.9 us
    ppermute x2, waiting for transfers between devices, with_halo(): before = lax.ppermute(tail, axis, [(i, i + 1) for i in range(count - 1)])  17.7 us
    ppermute x10, waiting for transfers between devices, butterfly_sum(): partner = lax.ppermute(value, axis, [(i, i ^ step) for i in range(count)])  17.1 us
    mul x4, other arithmetic, sweep(): flux_col = weight * diff_col  10.3 us
    another operation x12, other arithmetic, orthonormal(): lower = jnp.linalg.cholesky(inner)  8.57 us
    another operation x8, other arithmetic, orthonormal(): lax.linalg.triangular_solve(lower, block, left_side=False, lower=True, tr...  7.51 us
    unnamed x11, local copies, waits for them, and re-layouts  6.99 us
  transfers between devices with their start and end apart: 14, of which 12 were waited for; matrix products, arithmetic and copies ran while one was open for 4% of the time, Pallas kernels for 0%

profile of v3, /device:TPU:0, one launch (start us, length us, event | category | flops | bytes accessed | tf_op | source)
XLA Modules:
  0.0 161.7 jit_solution(17647002695469895818)
XLA Ops:
  0.6 2.1 %copy.37 = f32[224,8,256]{2,0,1:T(8,128)S(1)} copy(f32[224,8,256]{2,1,0:T(8,128)} %param.5) | data formatting | bytes 3670016 | tf_op args[0]
  4.2 5.0 %collective-permute-start = (f32[4,256,224]{1,2,0:T(8,128)}, f32[4,256,224]{1,2,0:T(8,128)S(1)}, u32[]{:S(2)}, u32[]{:S(2)}) collective-permute-start(f32[4,256,224]{1,2,0:T(8,128)} %get-tuple-element.20), channel_id=1, source_target_pairs={{0,8},{8,16},{16,24},{1,9},{9,17},{17,25},{2,10},{10,18},{18,26},{... | collective-permute-start | bytes 2752520 | tf_op jit(solution)/shard_map/ppermute | solution.py:33
  11.3 17.7 %collective-permute-done = f32[4,256,224]{1,2,0:T(8,128)S(1)} collective-permute-done((f32[4,256,224]{1,2,0:T(8,128)}, f32[4,256,224]{1,2,0:T(8,128)S(1)}, u32[]{:S(2)}, u32[]{:S(2)}) %collective-permute-start) | collective-permute-done | bytes 917536 | tf_op jit(solution)/shard_map/ppermute | solution.py:33
  29.0 4.2 %collective-permute-done.1 = f32[4,256,224]{1,2,0:T(8,128)} collective-permute-done((f32[4,256,224]{1,2,0:T(8,128)}, f32[4,256,224]{1,2,0:T(8,128)}, u32[]{:S(2)}, u32[]{:S(2)}) %collective-permute-start.1) | collective-permute-done | bytes 917536 | tf_op jit(solution)/shard_map/ppermute | solution.py:34
  34.6 2.4 %fusion.39 = (f32[16,4,224]{1,2,0:T(8,128)}, f32[16,4,224]{1,2,0:T(8,128)}) fusion(f32[16,256,224]{1,2,0:T(8,128)S(1)} %pad_maximum_fusion.1), kind=kLoop, calls=%fused_computation.105 | loop fusion | bytes 229376 | tf_op jit(solution)/shard_map/slice | solution.py:32
  37.0 2.1 %copy.22 = f32[16,4,224]{2,0,1:T(8,128)S(1)} copy(f32[16,4,224]{1,2,0:T(8,128)} %get-tuple-element.16) | data formatting | bytes 114688 | tf_op jit(solution)/shard_map/slice | solution.py:32
  40.5 2.1 %copy.23 = f32[16,4,224]{2,0,1:T(8,128)S(1)} copy(f32[16,4,224]{1,2,0:T(8,128)} %get-tuple-element.17) | data formatting | bytes 114688 | tf_op jit(solution)/shard_map/slice | solution.py:31
  44.0 1.8 %copy.24 = f32[16,4,224]{1,2,0:T(8,128)} copy(f32[16,4,224]{2,0,1:T(8,128)S(1)} %collective-permute-done.2) | data formatting | bytes 114688 | tf_op jit(solution)/shard_map/ppermute | solution.py:33
  47.5 1.8 %copy.25 = f32[16,4,224]{1,2,0:T(8,128)} copy(f32[16,4,224]{2,0,1:T(8,128)S(1)} %collective-permute-done.3) | data formatting | bytes 114688 | tf_op jit(solution)/shard_map/ppermute | solution.py:34
  49.3 4.9 %pad_maximum_fusion = f32[16,264,224]{1,2,0:T(8,128)S(1)} fusion(f32[16,4,224]{1,2,0:T(8,128)} %copy.25, f32[4,256,224]{1,2,0:T(8,128)} %collective-permute-done.1, f32[8,256,224]{1,2,0:T(8,128)S(1)} %bitcast.85, f32[4,256,224]{1,2,0:T(8,128)S(1)} %collective-permute-done, f32[16,4,224]{1,2,0:T(8,128)} %copy.24), kind=kLoop, calls=%fused_computation | loop fusion | flops 3784704 | bytes 7569408 | tf_op jit(solution)/shard_map/concatenate | solution.py:35
  54.2 1.7 %add_reduce_fusion = f32[15,263]{1,0:T(8,128)S(1)} fusion(f32[16,264,224]{1,2,0:T(8,128)S(1)} %pad_maximum_fusion), kind=kLoop, calls=%fused_computation.3 | loop fusion | flops 5298135 | bytes 10619940 | tf_op jit(solution)/shard_map/reduce_sum | solution.py:48
  55.9 2.0 %broadcast_multiply_fusion.1 = (f32[15,263,224]{1,2,0:T(8,128)S(1)}, f32[15,263,224]{1,2,0:T(8,128)S(1)}) fusion(f32[15,263]{1,0:T(8,128)S(1)} %add_rsqrt_fusion.3, f32[16,264,224]{1,2,0:T(8,128)S(1)} %pad_maximum_fusion), kind=kLoop, calls=%fused_computation.40 | loop fusion | flops 3534720 | bytes 17689380 | tf_op jit(solution)/shard_map/mul | solution.py:50
  57.9 5.4 %fusion.3 = f32[14,262,224]{1,2,0:T(8,128)S(1)} fusion(f32[15,263,224]{1,2,0:T(8,128)S(1)} %get-tuple-element.11, f32[15,263,224]{1,2,0:T(8,128)S(1)} %get-tuple-element.10, f32[16,264,224]{1,2,0:T(8,128)S(1)} %pad_maximum_fusion, pred[14,262]{1,0:T(8,128)(4,1)S(1)} %broadcast_and_fusion), kind=kLoop, calls=%fused_computation.8 | loop fusion | flops 7394688 | bytes 19722836 | tf_op jit(solution)/shard_map/jit(_where)/select_n | solution.py:55
  64.6 4.6 %broadcast_multiply_fusion.3 = (f32[13,261,224]{1,2,0:T(8,128)}, f32[13,261,224]{1,2,0:T(8,128)}) fusion(f32[13,261]{1,0:T(8,128)S(1)} %add_rsqrt_fusion.2, f32[14,262,224]{1,2,0:T(8,128)S(1)} %fusion.3), kind=kLoop, calls=%fused_computation.42 | loop fusion | flops 3040128 | bytes 15214212 | tf_op jit(solution)/shard_map/mul | solution.py:50
  69.1 11.7 %fusion.6 = f32[12,260,224]{1,2,0:T(8,128)S(1)} fusion(f32[16,264,224]{1,2,0:T(8,128)S(1)} %pad_maximum_fusion, f32[13,261,224]{1,2,0:T(8,128)} %get-tuple-element.13, f32[13,261,224]{1,2,0:T(8,128)} %get-tuple-element.12, f32[14,262,224]{1,2,0:T(8,128)S(1)} %fusion.3, pred[12,260]{1,0:T(8,128)(4,1)S(1)} %broadcast_and_fusion.1), kind=kLoop, calls=%fused_computation.17 | loop fusion | flops 6289920 | bytes 19571760 | tf_op jit(solution)/shard_map/jit(_where)/select_n | solution.py:55
  81.9 2.8 %broadcast_multiply_fusion.5 = (f32[11,259,224]{1,2,0:T(8,128)S(1)}, f32[11,259,224]{1,2,0:T(8,128)}) fusion(f32[11,259]{1,0:T(8,128)S(1)} %add_rsqrt_fusion.1, f32[12,260,224]{1,2,0:T(8,128)S(1)} %fusion.6), kind=kLoop, calls=%fused_computation.44 | loop fusion | flops 2552704 | bytes 12774916 | tf_op jit(solution)/shard_map/mul | solution.py:50
  84.7 6.8 %fusion.11 = f32[10,258,224]{1,2,0:T(8,128)S(1)} fusion(f32[16,264,224]{1,2,0:T(8,128)S(1)} %pad_maximum_fusion, f32[11,259,224]{1,2,0:T(8,128)} %get-tuple-element.15, f32[11,259,224]{1,2,0:T(8,128)S(1)} %get-tuple-element.14, f32[12,260,224]{1,2,0:T(8,128)S(1)} %fusion.6, pred[10,258]{1,0:T(8,128)(4,1)S(1)} %broadcast_and_fusion.2), kind=kLoop, calls=%fused_computation.30 | loop fusion | flops 5201280 | bytes 16184340 | tf_op jit(solution)/shard_map/jit(_where)/select_n | solution.py:55
  93.9 2.1 %fusion.17 = f32[8,256,224]{1,2,0:T(8,128)S(1)} fusion(f32[9,257,224]{1,2,0:T(8,128)S(1)} %get-tuple-element.19, f32[9,257,224]{1,2,0:T(8,128)S(1)} %get-tuple-element.18, f32[10,258,224]{1,2,0:T(8,128)S(1)} %fusion.11, pred[8,256]{1,0:T(8,128)(4,1)S(1)} %broadcast_and_fusion.3, f32[224,8,256]{2,1,0:T(8,128)S(1)} %copy-done.3), kind=kLoop, calls=%fused_computation.49 | loop fusion | flops 4128768 | bytes 12847104 | tf_op jit(solution)/shard_map/jit(_where)/select_n | solution.py:55
  98.9 3.0 %collective-permute-start.4 = (f32[224,16]{0,1:T(8,128)S(1)}, f32[224,16]{0,1:T(8,128)S(1)}, u32[]{:S(2)}, u32[]{:S(2)}) collective-permute-start(f32[224,16]{0,1:T(8,128)S(1)} %fusion.42), channel_id=1, source_target_pairs={{0,1},{1,0},{2,3},{3,2},{4,5},{5,4},{6,7},{7,6},{8,9},{9,8},{10,11... | collective-permute-start | bytes 43016 | tf_op jit(solution)/shard_map/ppermute | solution.py:22
  102.8 2.4 %collective-permute-start.5 = (f32[224,16]{0,1:T(8,128)S(1)}, f32[224,16]{0,1:T(8,128)S(1)}, u32[]{:S(2)}, u32[]{:S(2)}) collective-permute-start(f32[224,16]{0,1:T(8,128)S(1)} %add.156), channel_id=1, source_target_pairs={{0,2},{1,3},{2,0},{3,1},{4,6},{5,7},{6,4},{7,5},{8,10},{9,11},{10,... | collective-permute-start | bytes 43016 | tf_op jit(solution)/shard_map/ppermute | solution.py:22
  105.2 1.7 %collective-permute-done.5 = f32[224,16]{0,1:T(8,128)S(1)} collective-permute-done((f32[224,16]{0,1:T(8,128)S(1)}, f32[224,16]{0,1:T(8,128)S(1)}, u32[]{:S(2)}, u32[]{:S(2)}) %collective-permute-start.5) | collective-permute-done | bytes 14368 | tf_op jit(solution)/shard_map/ppermute | solution.py:22
  108.0 2.6 %collective-permute-done.6 = f32[224,16]{0,1:T(8,128)S(1)} collective-permute-done((f32[224,16]{0,1:T(8,128)S(1)}, f32[224,16]{0,1:T(8,128)S(1)}, u32[]{:S(2)}, u32[]{:S(2)}) %collective-permute-start.6) | collective-permute-done | bytes 14368 | tf_op jit(solution)/shard_map/ppermute | solution.py:22
  112.1 2.2 %collective-permute-done.7 = f32[224,16]{0,1:T(8,128)S(1)} collective-permute-done((f32[224,16]{0,1:T(8,128)S(1)}, f32[224,16]{0,1:T(8,128)S(1)}, u32[]{:S(2)}, u32[]{:S(2)}) %collective-permute-start.7) | collective-permute-done | bytes 14368 | tf_op jit(solution)/shard_map/ppermute | solution.py:22
  114.4 2.5 %collective-permute-start.8 = (f32[224,16]{0,1:T(8,128)S(1)}, f32[224,16]{0,1:T(8,128)S(1)}, u32[]{:S(2)}, u32[]{:S(2)}) collective-permute-start(f32[224,16]{0,1:T(8,128)S(1)} %add.159), channel_id=1, source_target_pairs={{0,16},{8,24},{16,0},{24,8},{1,17},{9,25},{17,1},{25,9},{2,18},{10... | collective-permute-start | bytes 43016 | tf_op jit(solution)/shard_map/ppermute | solution.py:22
  116.9 2.1 %collective-permute-done.8 = f32[224,16]{0,1:T(8,128)S(1)} collective-permute-done((f32[224,16]{0,1:T(8,128)S(1)}, f32[224,16]{0,1:T(8,128)S(1)}, u32[]{:S(2)}, u32[]{:S(2)}) %collective-permute-start.8) | collective-permute-done | bytes 14368 | tf_op jit(solution)/shard_map/ppermute | solution.py:22
  131.7 2.0 %collective-permute-start.10 = (f32[224,16]{0,1:T(8,128)S(1)}, f32[224,16]{0,1:T(8,128)S(1)}, u32[]{:S(2)}, u32[]{:S(2)}) collective-permute-start(f32[224,16]{0,1:T(8,128)S(1)} %add.161), channel_id=1, source_target_pairs={{0,2},{1,3},{2,0},{3,1},{4,6},{5,7},{6,4},{7,5},{8,10},{9,11},{10,... | collective-permute-start | bytes 43016 | tf_op jit(solution)/shard_map/ppermute | solution.py:22
  133.8 1.7 %collective-permute-done.10 = f32[224,16]{0,1:T(8,128)S(1)} collective-permute-done((f32[224,16]{0,1:T(8,128)S(1)}, f32[224,16]{0,1:T(8,128)S(1)}, u32[]{:S(2)}, u32[]{:S(2)}) %collective-permute-start.10) | collective-permute-done | bytes 14368 | tf_op jit(solution)/shard_map/ppermute | solution.py:22
  136.6 2.6 %collective-permute-done.11 = f32[224,16]{0,1:T(8,128)S(1)} collective-permute-done((f32[224,16]{0,1:T(8,128)S(1)}, f32[224,16]{0,1:T(8,128)S(1)}, u32[]{:S(2)}, u32[]{:S(2)}) %collective-permute-start.11) | collective-permute-done | bytes 14368 | tf_op jit(solution)/shard_map/ppermute | solution.py:22
  140.7 2.2 %collective-permute-done.12 = f32[224,16]{0,1:T(8,128)S(1)} collective-permute-done((f32[224,16]{0,1:T(8,128)S(1)}, f32[224,16]{0,1:T(8,128)S(1)}, u32[]{:S(2)}, u32[]{:S(2)}) %collective-permute-start.12) | collective-permute-done | bytes 14368 | tf_op jit(solution)/shard_map/ppermute | solution.py:22
  143.0 2.5 %collective-permute-start.13 = (f32[224,16]{0,1:T(8,128)S(1)}, f32[224,16]{0,1:T(8,128)S(1)}, u32[]{:S(2)}, u32[]{:S(2)}) collective-permute-start(f32[224,16]{0,1:T(8,128)S(1)} %add.164), channel_id=1, source_target_pairs={{0,16},{8,24},{16,0},{24,8},{1,17},{9,25},{17,1},{25,9},{2,18},{10... | collective-permute-start | bytes 43016 | tf_op jit(solution)/shard_map/ppermute | solution.py:22
  145.5 2.3 %copy.31 = f32[224,8,256]{2,1,0:T(8,128)} copy(f32[224,8,256]{2,0,1:T(8,128)S(1)} %bitcast.87) | data formatting | bytes 3670016
  159.7 2.0 %copy.33 = f32[28,8,8,256]{3,2,1,0:T(8,128)} copy(f32[28,8,8,256]{3,1,2,0:T(8,128)S(1)} %bitcast.88) | data formatting | bytes 3670016
  (98 shorter events, 47.7 us)
Async XLA Ops:
  0.6 95.7 %copy-start = (f32[224,16]{0,1:T(8,128)S(1)}, f32[224,16]{0,1:T(8,128)}, u32[]{:S(2)}) copy-start(f32[224,16]{0,1:T(8,128)} %param.6) | copy-start | bytes 43012
  4.2 24.8 %collective-permute-start = (f32[4,256,224]{1,2,0:T(8,128)}, f32[4,256,224]{1,2,0:T(8,128)S(1)}, u32[]{:S(2)}, u32[]{:S(2)}) collective-permute-start(f32[4,256,224]{1,2,0:T(8,128)} %get-tuple-element.20), channel_id=1, source_target_pairs={{0,8},{8,16},{16,24},{1,9},{9,17},{17,25},{2,10},{10,18},{18,26},{... | collective-permute-start | bytes 2752520 | tf_op jit(solution)/shard_map/ppermute | solution.py:33
  9.2 24.0 %collective-permute-start.1 = (f32[4,256,224]{1,2,0:T(8,128)}, f32[4,256,224]{1,2,0:T(8,128)}, u32[]{:S(2)}, u32[]{:S(2)}) collective-permute-start(f32[4,256,224]{1,2,0:T(8,128)} %get-tuple-element.21), channel_id=1, source_target_pairs={{8,0},{16,8},{24,16},{9,1},{17,9},{25,17},{10,2},{18,10},{26,18},{... | collective-permute-start | bytes 2752520 | tf_op jit(solution)/shard_map/ppermute | solution.py:34
  39.2 4.8 %collective-permute-start.2 = (f32[16,4,224]{2,0,1:T(8,128)S(1)}, f32[16,4,224]{2,0,1:T(8,128)S(1)}, u32[]{:S(2)}, u32[]{:S(2)}) collective-permute-start(f32[16,4,224]{2,0,1:T(8,128)S(1)} %copy.22), channel_id=1, source_target_pairs={{0,1},{1,2},{2,3},{3,4},{4,5},{5,6},{6,7},{8,9},{9,10},{10,11},{11... | collective-permute-start | bytes 172040 | tf_op jit(solution)/shard_map/ppermute | solution.py:33
  42.6 4.9 %collective-permute-start.3 = (f32[16,4,224]{2,0,1:T(8,128)S(1)}, f32[16,4,224]{2,0,1:T(8,128)S(1)}, u32[]{:S(2)}, u32[]{:S(2)}) collective-permute-start(f32[16,4,224]{2,0,1:T(8,128)S(1)} %copy.23), channel_id=1, source_target_pairs={{1,0},{2,1},{3,2},{4,3},{5,4},{6,5},{7,6},{9,8},{10,9},{11,10},{12... | collective-permute-start | bytes 172040 | tf_op jit(solution)/shard_map/ppermute | solution.py:34
  92.4 1.5 copy-start.3
  96.0 2.9 %copy-start.1 = (f32[8,256,224]{1,2,0:T(8,128)}, f32[8,256,224]{1,2,0:T(8,128)S(1)}, u32[]{:S(2)}) copy-start(f32[8,256,224]{1,2,0:T(8,128)S(1)} %fusion.17) | copy-start | bytes 5505028
  98.9 3.8 %collective-permute-start.4 = (f32[224,16]{0,1:T(8,128)S(1)}, f32[224,16]{0,1:T(8,128)S(1)}, u32[]{:S(2)}, u32[]{:S(2)}) collective-permute-start(f32[224,16]{0,1:T(8,128)S(1)} %fusion.42), channel_id=1, source_target_pairs={{0,1},{1,0},{2,3},{3,2},{4,5},{5,4},{6,7},{7,6},{8,9},{9,8},{10,11... | collective-permute-start | bytes 43016 | tf_op jit(solution)/shard_map/ppermute | solution.py:22
  102.8 4.1 %collective-permute-start.5 = (f32[224,16]{0,1:T(8,128)S(1)}, f32[224,16]{0,1:T(8,128)S(1)}, u32[]{:S(2)}, u32[]{:S(2)}) collective-permute-start(f32[224,16]{0,1:T(8,128)S(1)} %add.156), channel_id=1, source_target_pairs={{0,2},{1,3},{2,0},{3,1},{4,6},{5,7},{6,4},{7,5},{8,10},{9,11},{10,... | collective-permute-start | bytes 43016 | tf_op jit(solution)/shard_map/ppermute | solution.py:22
  106.9 3.7 %collective-permute-start.6 = (f32[224,16]{0,1:T(8,128)S(1)}, f32[224,16]{0,1:T(8,128)S(1)}, u32[]{:S(2)}, u32[]{:S(2)}) collective-permute-start(f32[224,16]{0,1:T(8,128)S(1)} %add.157), channel_id=1, source_target_pairs={{0,4},{1,5},{2,6},{3,7},{4,0},{5,1},{6,2},{7,3},{8,12},{9,13},{10,... | collective-permute-start | bytes 43016 | tf_op jit(solution)/shard_map/ppermute | solution.py:22
  110.6 3.7 %collective-permute-start.7 = (f32[224,16]{0,1:T(8,128)S(1)}, f32[224,16]{0,1:T(8,128)S(1)}, u32[]{:S(2)}, u32[]{:S(2)}) collective-permute-start(f32[224,16]{0,1:T(8,128)S(1)} %add.158), channel_id=1, source_target_pairs={{0,8},{8,0},{16,24},{24,16},{1,9},{9,1},{17,25},{25,17},{2,10},{10... | collective-permute-start | bytes 43016 | tf_op jit(solution)/shard_map/ppermute | solution.py:22
  114.4 4.6 %collective-permute-start.8 = (f32[224,16]{0,1:T(8,128)S(1)}, f32[224,16]{0,1:T(8,128)S(1)}, u32[]{:S(2)}, u32[]{:S(2)}) collective-permute-start(f32[224,16]{0,1:T(8,128)S(1)} %add.159), channel_id=1, source_target_pairs={{0,16},{8,24},{16,0},{24,8},{1,17},{9,25},{17,1},{25,9},{2,18},{10... | collective-permute-start | bytes 43016 | tf_op jit(solution)/shard_map/ppermute | solution.py:22
  127.7 17.8 %copy-start.2 = (f32[8,256,224]{1,2,0:T(8,128)S(1)}, f32[8,256,224]{1,2,0:T(8,128)}, u32[]{:S(2)}) copy-start(f32[8,256,224]{1,2,0:T(8,128)} %copy-done.1) | copy-start | bytes 5505028
  130.5 1.2 collective-permute-start.9
  131.7 3.7 %collective-permute-start.10 = (f32[224,16]{0,1:T(8,128)S(1)}, f32[224,16]{0,1:T(8,128)S(1)}, u32[]{:S(2)}, u32[]{:S(2)}) collective-permute-start(f32[224,16]{0,1:T(8,128)S(1)} %add.161), channel_id=1, source_target_pairs={{0,2},{1,3},{2,0},{3,1},{4,6},{5,7},{6,4},{7,5},{8,10},{9,11},{10,... | collective-permute-start | bytes 43016 | tf_op jit(solution)/shard_map/ppermute | solution.py:22
  135.5 3.7 %collective-permute-start.11 = (f32[224,16]{0,1:T(8,128)S(1)}, f32[224,16]{0,1:T(8,128)S(1)}, u32[]{:S(2)}, u32[]{:S(2)}) collective-permute-start(f32[224,16]{0,1:T(8,128)S(1)} %add.162), channel_id=1, source_target_pairs={{0,4},{1,5},{2,6},{3,7},{4,0},{5,1},{6,2},{7,3},{8,12},{9,13},{10,... | collective-permute-start | bytes 43016 | tf_op jit(solution)/shard_map/ppermute | solution.py:22
  139.2 3.7 %collective-permute-start.12 = (f32[224,16]{0,1:T(8,128)S(1)}, f32[224,16]{0,1:T(8,128)S(1)}, u32[]{:S(2)}, u32[]{:S(2)}) collective-permute-start(f32[224,16]{0,1:T(8,128)S(1)} %add.163), channel_id=1, source_target_pairs={{0,8},{8,0},{16,24},{24,16},{1,9},{9,1},{17,25},{25,17},{2,10},{10... | collective-permute-start | bytes 43016 | tf_op jit(solution)/shard_map/ppermute | solution.py:22
  143.0 4.8 %collective-permute-start.13 = (f32[224,16]{0,1:T(8,128)S(1)}, f32[224,16]{0,1:T(8,128)S(1)}, u32[]{:S(2)}, u32[]{:S(2)}) collective-permute-start(f32[224,16]{0,1:T(8,128)S(1)} %add.164), channel_id=1, source_target_pairs={{0,16},{8,24},{16,0},{24,8},{1,17},{9,25},{17,1},{25,9},{2,18},{10... | collective-permute-start | bytes 43016 | tf_op jit(solution)/shard_map/ppermute | solution.py:22

commit v4 on v2

--- a/solution.py
+++ b/solution.py
@@ -2,6 +2,8 @@
 import jax.numpy as jnp
 from jax import lax
 from jax.sharding import PartitionSpec as P
+from jax.experimental import pallas as pl
+from jax.experimental.pallas import tpu as pltpu
 
 SWEEPS = 4
 SUBIT = 2
@@ -55,6 +57,59 @@
     return jnp.where(keep, new, 0.0)
 
 
+def cholesky_qr(block):
+    size = block.shape[1]
+    inner = lax.dot_general(
+        block, block, (((0,), (0,)), ((), ())),
+        precision=lax.Precision.HIGHEST, preferred_element_type=jnp.float32,
+    )
+    sub = lax.broadcasted_iota(jnp.int32, (size, size), 0)
+    lane = lax.broadcasted_iota(jnp.int32, (size, size), 1)
+    lower = jnp.zeros((size, size), jnp.float32)
+    upper = jnp.zeros((size, size), jnp.float32)
+    rest = inner
+    for j in range(size):
+        col = jnp.sum(jnp.where(lane == j, rest, 0.0), axis=1, keepdims=True)
+        row = jnp.sum(jnp.where(sub == j, rest, 0.0), axis=0, keepdims=True)
+        pivot = jnp.sqrt(jnp.sum(jnp.where(lane[:1] == j, row, 0.0), axis=1, keepdims=True))
+        col = jnp.where(sub[:, :1] >= j, col / pivot, 0.0)
+        row = jnp.where(lane[:1] >= j, row / pivot, 0.0)
+        lower = lower + jnp.where(lane == j, col, 0.0)
+        upper = upper + jnp.where(sub == j, row, 0.0)
+        rest = rest - col * row
+    inverse = jnp.zeros((size, size), jnp.float32)
+    for i in range(size):
+        coef = jnp.sum(jnp.where(lane == i, upper, 0.0), axis=1, keepdims=True)
+        diag = jnp.sum(jnp.where(sub[:, :1] == i, coef, 0.0), axis=0, keepdims=True)
+        acc = jnp.sum(jnp.where(sub[:, :1] < i, coef, 0.0) * inverse, axis=0, keepdims=True)
+        unit = jnp.where(lane[:1] == i, 1.0, 0.0)
+        inverse = inverse + jnp.where(sub == i, (unit - acc) / diag, 0.0)
+    return lax.dot_general(
+        block, inverse, (((1,), (1,)), ((), ())),
+        precision=lax.Precision.HIGHEST, preferred_element_type=jnp.float32,
+    )
+
+
+def subspace_kernel(gram_ref, basis_ref, out_ref):
+    product = jnp.dot(
+        gram_ref[...], basis_ref[...],
+        precision=lax.Precision.HIGHEST, preferred_element_type=jnp.float32,
+    )
+    out_ref[...] = cholesky_qr(cholesky_qr(product))
+
+
+def subspace_step(gram_full, basis):
+    return pl.pallas_call(
+        subspace_kernel,
+        out_shape=jax.ShapeDtypeStruct(basis.shape, jnp.float32),
+        cost_estimate=pl.CostEstimate(
+            flops=2 * gram_full.shape[0] * gram_full.size + 8 * basis.size * basis.shape[1],
+            transcendentals=2 * basis.shape[1],
+            bytes_accessed=4 * (gram_full.size + 2 * basis.size),
+        ),
+    )(gram_full, basis)
+
+
 def orthonormal(block):
     inner = jnp.dot(block.T, block, precision=lax.Precision.HIGHEST)
     lower = jnp.linalg.cholesky(inner)
@@ -90,8 +145,7 @@
     gram_full = butterfly_sum(local_gram, ("col", "row"))
     basis_now = start_basis
     for turn in range(SUBIT):
-        product = jnp.dot(gram_full, basis_now, precision=lax.Precision.HIGHEST)
-        basis_now = orthonormal(orthonormal(product))
+        basis_now = subspace_step(gram_full, basis_now)
     coeffs = jnp.dot(flat_cells, basis_now, precision=lax.Precision.HIGHEST)
     lowrank = lax.dot_general(
         basis_now,

time: 160 us -> 158 us (0.988)
  other arithmetic: 64.1 us -> 48.6 us
  Pallas kernels: 0 us -> 14.1 us
  waiting for transfers between devices: 48.4 us -> 46.4 us
  local copies, waits for them, and re-layouts: 19.9 us -> 21.5 us
    another operation x20 -> x0, other arithmetic: 16.1 us -> none  [the longest x12 8.57 us: orthonormal(): lower = jnp.linalg.cholesky(inner)]
    pallas_call x0 -> x2, Pallas kernels: none -> 14.1 us  [subspace_step(): pl.pallas_call(subspace_kernel, out_shape=jax.ShapeDtypeStruct(basis.shap...]
    ppermute x5, waiting for transfers between devices: 24.9 us -> 22.9 us  [butterfly_sum(): partner = lax.ppermute(value, axis, [(i, i ^ step) for i in range(count)])]
    unnamed x7 -> x8, local copies, waits for them, and re-layouts: 6.97 us -> 7.68 us
  transfers between devices with their start and end apart: 9 -> 9, of which waited for: 8 -> 8; matrix products, arithmetic and copies ran while one was open for 5% -> 6% of each run, Pallas kernels for 0% -> 0%
where the time goes in v4:
time: 158 us
  other arithmetic  48.6 us (31%)
  waiting for transfers between devices  46.4 us (29%)
  local copies, waits for them, and re-layouts  21.5 us (14%)
  starting transfers between devices  19.4 us (12%)
  Pallas kernels  14.1 us (9%)
  matrix products  6.65 us (4%)
    select_n x4, other arithmetic, sweep(): return jnp.where(keep, new, 0.0)  25.9 us
    ppermute x5, waiting for transfers between devices, butterfly_sum(): partner = lax.ppermute(value, axis, [(i, i ^ step) for i in range(count)])  22.9 us
    ppermute x2, waiting for transfers between devices, with_halo(): before = lax.ppermute(tail, axis, [(i, i + 1) for i in range(count - 1)])  17.7 us
    pallas_call x2, Pallas kernels, subspace_step(): pl.pallas_call(subspace_kernel, out_shape=jax.ShapeDtypeStruct(basis.shap...  14.1 us
    ppermute x5, starting transfers between devices, butterfly_sum(): partner = lax.ppermute(value, axis, [(i, i ^ step) for i in range(count)])  10.6 us
    mul x4, other arithmetic, sweep(): flux_col = weight * diff_col  10.3 us
    unnamed x8, local copies, waits for them, and re-layouts  7.68 us
    concatenate x2, other arithmetic, with_halo(): return jnp.concatenate([before, cells, after], axis=dim)  6.27 us
  transfers between devices with their start and end apart: 9, of which 8 were waited for; matrix products, arithmetic and copies ran while one was open for 6% of the time, Pallas kernels for 0%

profile of v4, /device:TPU:0, one launch (start us, length us, event | category | flops | bytes accessed | tf_op | source)
XLA Modules:
  0.0 157.6 jit_solution(13054909709179858225)
XLA Ops:
  0.6 2.1 %copy.31 = f32[224,8,256]{2,0,1:T(8,128)S(1)} copy(f32[224,8,256]{2,1,0:T(8,128)} %param.2) | data formatting | bytes 3670016 | tf_op args[0]
  4.2 5.0 %collective-permute-start = (f32[4,256,224]{1,2,0:T(8,128)}, f32[4,256,224]{1,2,0:T(8,128)S(1)}, u32[]{:S(2)}, u32[]{:S(2)}) collective-permute-start(f32[4,256,224]{1,2,0:T(8,128)} %get-tuple-element.18), channel_id=1, source_target_pairs={{0,8},{8,16},{16,24},{1,9},{9,17},{17,25},{2,10},{10,18},{18,26},{... | collective-permute-start | bytes 2752520 | tf_op jit(solution)/shard_map/ppermute | solution.py:35
  11.3 17.7 %collective-permute-done = f32[4,256,224]{1,2,0:T(8,128)S(1)} collective-permute-done((f32[4,256,224]{1,2,0:T(8,128)}, f32[4,256,224]{1,2,0:T(8,128)S(1)}, u32[]{:S(2)}, u32[]{:S(2)}) %collective-permute-start) | collective-permute-done | bytes 917536 | tf_op jit(solution)/shard_map/ppermute | solution.py:35
  29.0 4.2 %collective-permute-done.1 = f32[4,256,224]{1,2,0:T(8,128)} collective-permute-done((f32[4,256,224]{1,2,0:T(8,128)}, f32[4,256,224]{1,2,0:T(8,128)}, u32[]{:S(2)}, u32[]{:S(2)}) %collective-permute-start.1) | collective-permute-done | bytes 917536 | tf_op jit(solution)/shard_map/ppermute | solution.py:36
  34.6 2.4 %fusion.21 = (f32[16,4,224]{1,2,0:T(8,128)}, f32[16,4,224]{1,2,0:T(8,128)}) fusion(f32[16,256,224]{1,2,0:T(8,128)S(1)} %pad_maximum_fusion.1), kind=kLoop, calls=%fused_computation.69 | loop fusion | bytes 229376 | tf_op jit(solution)/shard_map/slice | solution.py:34
  37.0 2.1 %copy.19 = f32[16,4,224]{2,0,1:T(8,128)S(1)} copy(f32[16,4,224]{1,2,0:T(8,128)} %get-tuple-element.14) | data formatting | bytes 114688 | tf_op jit(solution)/shard_map/slice | solution.py:34
  40.4 2.1 %copy.20 = f32[16,4,224]{2,0,1:T(8,128)S(1)} copy(f32[16,4,224]{1,2,0:T(8,128)} %get-tuple-element.15) | data formatting | bytes 114688 | tf_op jit(solution)/shard_map/slice | solution.py:33
  43.9 1.8 %copy.21 = f32[16,4,224]{1,2,0:T(8,128)} copy(f32[16,4,224]{2,0,1:T(8,128)S(1)} %collective-permute-done.2) | data formatting | bytes 114688 | tf_op jit(solution)/shard_map/ppermute | solution.py:35
  45.8 1.7 %collective-permute-done.3 = f32[16,4,224]{2,0,1:T(8,128)S(1)} collective-permute-done((f32[16,4,224]{2,0,1:T(8,128)S(1)}, f32[16,4,224]{2,0,1:T(8,128)S(1)}, u32[]{:S(2)}, u32[]{:S(2)}) %collective-permute-start.3) | collective-permute-done | bytes 57376 | tf_op jit(solution)/shard_map/ppermute | solution.py:36
  47.4 1.8 %copy.22 = f32[16,4,224]{1,2,0:T(8,128)} copy(f32[16,4,224]{2,0,1:T(8,128)S(1)} %collective-permute-done.3) | data formatting | bytes 114688 | tf_op jit(solution)/shard_map/ppermute | solution.py:36
  49.3 4.9 %pad_maximum_fusion = f32[16,264,224]{1,2,0:T(8,128)S(1)} fusion(f32[16,4,224]{1,2,0:T(8,128)} %copy.22, f32[4,256,224]{1,2,0:T(8,128)} %collective-permute-done.1, f32[8,256,224]{1,2,0:T(8,128)S(1)} %bitcast.22, f32[4,256,224]{1,2,0:T(8,128)S(1)} %collective-permute-done, f32[16,4,224]{1,2,0:T(8,128)} %copy.21), kind=kLoop, calls=%fused_computation | loop fusion | flops 3784704 | bytes 7569408 | tf_op jit(solution)/shard_map/concatenate | solution.py:37
  54.1 1.7 %add_reduce_fusion = f32[15,263]{1,0:T(8,128)S(1)} fusion(f32[16,264,224]{1,2,0:T(8,128)S(1)} %pad_maximum_fusion), kind=kLoop, calls=%fused_computation.3 | loop fusion | flops 5298135 | bytes 10619940 | tf_op jit(solution)/shard_map/reduce_sum | solution.py:50
  55.9 2.0 %broadcast_multiply_fusion.1 = (f32[15,263,224]{1,2,0:T(8,128)S(1)}, f32[15,263,224]{1,2,0:T(8,128)S(1)}) fusion(f32[15,263]{1,0:T(8,128)S(1)} %add_rsqrt_fusion.3, f32[16,264,224]{1,2,0:T(8,128)S(1)} %pad_maximum_fusion), kind=kLoop, calls=%fused_computation.40 | loop fusion | flops 3534720 | bytes 17689380 | tf_op jit(solution)/shard_map/mul | solution.py:52
  57.9 5.4 %fusion.3 = f32[14,262,224]{1,2,0:T(8,128)S(1)} fusion(f32[15,263,224]{1,2,0:T(8,128)S(1)} %get-tuple-element.9, f32[15,263,224]{1,2,0:T(8,128)S(1)} %get-tuple-element.8, f32[16,264,224]{1,2,0:T(8,128)S(1)} %pad_maximum_fusion, pred[14,262]{1,0:T(8,128)(4,1)S(1)} %broadcast_and_fusion), kind=kLoop, calls=%fused_computation.8 | loop fusion | flops 7394688 | bytes 19722836 | tf_op jit(solution)/shard_map/jit(_where)/select_n | solution.py:57
  64.6 4.6 %broadcast_multiply_fusion.3 = (f32[13,261,224]{1,2,0:T(8,128)}, f32[13,261,224]{1,2,0:T(8,128)}) fusion(f32[13,261]{1,0:T(8,128)S(1)} %add_rsqrt_fusion.2, f32[14,262,224]{1,2,0:T(8,128)S(1)} %fusion.3), kind=kLoop, calls=%fused_computation.42 | loop fusion | flops 3040128 | bytes 15214212 | tf_op jit(solution)/shard_map/mul | solution.py:52
  69.2 11.7 %fusion.6 = f32[12,260,224]{1,2,0:T(8,128)S(1)} fusion(f32[16,264,224]{1,2,0:T(8,128)S(1)} %pad_maximum_fusion, f32[13,261,224]{1,2,0:T(8,128)} %get-tuple-element.11, f32[13,261,224]{1,2,0:T(8,128)} %get-tuple-element.10, f32[14,262,224]{1,2,0:T(8,128)S(1)} %fusion.3, pred[12,260]{1,0:T(8,128)(4,1)S(1)} %broadcast_and_fusion.1), kind=kLoop, calls=%fused_computation.17 | loop fusion | flops 6289920 | bytes 19571760 | tf_op jit(solution)/shard_map/jit(_where)/select_n | solution.py:57
  82.0 2.8 %broadcast_multiply_fusion.5 = (f32[11,259,224]{1,2,0:T(8,128)S(1)}, f32[11,259,224]{1,2,0:T(8,128)}) fusion(f32[11,259]{1,0:T(8,128)S(1)} %add_rsqrt_fusion.1, f32[12,260,224]{1,2,0:T(8,128)S(1)} %fusion.6), kind=kLoop, calls=%fused_computation.44 | loop fusion | flops 2552704 | bytes 12774916 | tf_op jit(solution)/shard_map/mul | solution.py:52
  84.8 6.8 %fusion.11 = f32[10,258,224]{1,2,0:T(8,128)S(1)} fusion(f32[16,264,224]{1,2,0:T(8,128)S(1)} %pad_maximum_fusion, f32[11,259,224]{1,2,0:T(8,128)} %get-tuple-element.13, f32[11,259,224]{1,2,0:T(8,128)S(1)} %get-tuple-element.12, f32[12,260,224]{1,2,0:T(8,128)S(1)} %fusion.6, pred[10,258]{1,0:T(8,128)(4,1)S(1)} %broadcast_and_fusion.2), kind=kLoop, calls=%fused_computation.30 | loop fusion | flops 5201280 | bytes 16184340 | tf_op jit(solution)/shard_map/jit(_where)/select_n | solution.py:57
  94.0 2.0 %fusion.17 = f32[8,256,224]{1,2,0:T(8,128)S(1)} fusion(f32[9,257,224]{1,2,0:T(8,128)S(1)} %get-tuple-element.17, f32[9,257,224]{1,2,0:T(8,128)S(1)} %get-tuple-element.16, f32[10,258,224]{1,2,0:T(8,128)S(1)} %fusion.11, pred[8,256]{1,0:T(8,128)(4,1)S(1)} %broadcast_and_fusion.3, f32[224,8,256]{2,1,0:T(8,128)S(1)} %copy-done), kind=kLoop, calls=%fused_computation.49 | loop fusion | flops 4128768 | bytes 12847104 | tf_op jit(solution)/shard_map/jit(_where)/select_n | solution.py:57
  97.6 3.0 %collective-permute-start.4 = (f32[224,224]{1,0:T(8,128)S(1)}, f32[224,224]{1,0:T(8,128)S(1)}, u32[]{:S(2)}, u32[]{:S(2)}) collective-permute-start(f32[224,224]{1,0:T(8,128)S(1)} %convolution_bitcast_fusion), channel_id=1, source_target_pairs={{0,1},{1,0},{2,3},{3,2},{4,5},{5,4},{6,7},{7,6},{8,9},{9,8},{10,11... | collective-permute-start | bytes 602120 | tf_op jit(solution)/shard_map/ppermute | solution.py:24
  101.8 2.5 %collective-permute-start.5 = (f32[224,224]{1,0:T(8,128)S(1)}, f32[224,224]{1,0:T(8,128)S(1)}, u32[]{:S(2)}, u32[]{:S(2)}) collective-permute-start(f32[224,224]{1,0:T(8,128)S(1)} %add.133), channel_id=1, source_target_pairs={{0,2},{1,3},{2,0},{3,1},{4,6},{5,7},{6,4},{7,5},{8,10},{9,11},{10,... | collective-permute-start | bytes 602120 | tf_op jit(solution)/shard_map/ppermute | solution.py:24
  104.3 6.1 %collective-permute-done.5 = f32[224,224]{1,0:T(8,128)S(1)} collective-permute-done((f32[224,224]{1,0:T(8,128)S(1)}, f32[224,224]{1,0:T(8,128)S(1)}, u32[]{:S(2)}, u32[]{:S(2)}) %collective-permute-start.5) | collective-permute-done | bytes 200736 | tf_op jit(solution)/shard_map/ppermute | solution.py:24
  111.4 6.4 %collective-permute-done.6 = f32[224,224]{1,0:T(8,128)S(1)} collective-permute-done((f32[224,224]{1,0:T(8,128)S(1)}, f32[224,224]{1,0:T(8,128)S(1)}, u32[]{:S(2)}, u32[]{:S(2)}) %collective-permute-start.6) | collective-permute-done | bytes 200736 | tf_op jit(solution)/shard_map/ppermute | solution.py:24
  119.4 4.9 %collective-permute-done.7 = f32[224,224]{1,0:T(8,128)S(1)} collective-permute-done((f32[224,224]{1,0:T(8,128)S(1)}, f32[224,224]{1,0:T(8,128)S(1)}, u32[]{:S(2)}, u32[]{:S(2)}) %collective-permute-start.7) | collective-permute-done | bytes 200736 | tf_op jit(solution)/shard_map/ppermute | solution.py:24
  124.4 2.6 %collective-permute-start.8 = (f32[224,224]{1,0:T(8,128)S(1)}, f32[224,224]{1,0:T(8,128)S(1)}, u32[]{:S(2)}, u32[]{:S(2)}) collective-permute-start(f32[224,224]{1,0:T(8,128)S(1)} %add.136), channel_id=1, source_target_pairs={{0,16},{8,24},{16,0},{24,8},{1,17},{9,25},{17,1},{25,9},{2,18},{10... | collective-permute-start | bytes 602120 | tf_op jit(solution)/shard_map/ppermute | solution.py:24
  129.2 2.3 %copy.25 = f32[224,8,256]{2,1,0:T(8,128)} copy(f32[224,8,256]{2,0,1:T(8,128)S(1)} %bitcast.19) | data formatting | bytes 3670016
  131.4 4.3 %collective-permute-done.8 = f32[224,224]{1,0:T(8,128)S(1)} collective-permute-done((f32[224,224]{1,0:T(8,128)S(1)}, f32[224,224]{1,0:T(8,128)S(1)}, u32[]{:S(2)}, u32[]{:S(2)}) %collective-permute-start.8) | collective-permute-done | bytes 200736 | tf_op jit(solution)/shard_map/ppermute | solution.py:24
  136.4 7.1 %shard_map.41.basis_ref = f32[224,16]{1,0:T(8,128)} custom-call(f32[224,224]{1,0:T(8,128)} %add.137.gram_ref, f32[224,16]{1,0:T(8,128)} %copy.23.basis_ref), custom_call_target="tpu_custom_call" | custom-call | flops 22937600 | bytes 229376 | tf_op jit(solution)/shard_map/pallas_call | solution.py:102
  143.5 7.0 %shard_map.42 = f32[224,16]{1,0:T(8,128)} custom-call(f32[224,224]{1,0:T(8,128)} %add.137.gram_ref, f32[224,16]{1,0:T(8,128)} %shard_map.41.basis_ref), custom_call_target="tpu_custom_call" | custom-call | flops 22937600 | bytes 229376 | tf_op jit(solution)/shard_map/pallas_call | solution.py:102
  150.6 2.6 %fusion.23 = f32[2048,16]{0,1:T(8,128)S(1)} fusion(f32[2048,224]{0,1:T(8,128)} %bitcast.23, f32[224,16]{1,0:T(8,128)} %shard_map.42), kind=kOutput, calls=%fused_computation.71 | convolution fusion | flops 88080384 | bytes 1980416 | tf_op jit(solution)/shard_map/dot_general | solution.py:149
  153.1 2.5 %fusion.24 = f32[224,2048]{1,0:T(8,128)S(1)} fusion(f32[224,16]{1,0:T(8,128)} %shard_map.42, f32[2048,16]{0,1:T(8,128)S(1)} %fusion.23), kind=kOutput, calls=%fused_computation.72 | convolution fusion | flops 88080384 | bytes 1980416 | tf_op jit(solution)/shard_map/dot_general | solution.py:150
  155.6 2.0 %copy.27 = f32[28,8,8,256]{3,2,1,0:T(8,128)} copy(f32[28,8,8,256]{3,1,2,0:T(8,128)S(1)} %bitcast.24) | data formatting | bytes 3670016
  (43 shorter events, 20.7 us)
Async XLA Ops:
  4.2 24.8 %collective-permute-start = (f32[4,256,224]{1,2,0:T(8,128)}, f32[4,256,224]{1,2,0:T(8,128)S(1)}, u32[]{:S(2)}, u32[]{:S(2)}) collective-permute-start(f32[4,256,224]{1,2,0:T(8,128)} %get-tuple-element.18), channel_id=1, source_target_pairs={{0,8},{8,16},{16,24},{1,9},{9,17},{17,25},{2,10},{10,18},{18,26},{... | collective-permute-start | bytes 2752520 | tf_op jit(solution)/shard_map/ppermute | solution.py:35
  9.1 24.0 %collective-permute-start.1 = (f32[4,256,224]{1,2,0:T(8,128)}, f32[4,256,224]{1,2,0:T(8,128)}, u32[]{:S(2)}, u32[]{:S(2)}) collective-permute-start(f32[4,256,224]{1,2,0:T(8,128)} %get-tuple-element.19), channel_id=1, source_target_pairs={{8,0},{16,8},{24,16},{9,1},{17,9},{25,17},{10,2},{18,10},{26,18},{... | collective-permute-start | bytes 2752520 | tf_op jit(solution)/shard_map/ppermute | solution.py:36
  39.1 4.8 %collective-permute-start.2 = (f32[16,4,224]{2,0,1:T(8,128)S(1)}, f32[16,4,224]{2,0,1:T(8,128)S(1)}, u32[]{:S(2)}, u32[]{:S(2)}) collective-permute-start(f32[16,4,224]{2,0,1:T(8,128)S(1)} %copy.19), channel_id=1, source_target_pairs={{0,1},{1,2},{2,3},{3,4},{4,5},{5,6},{6,7},{8,9},{9,10},{10,11},{11... | collective-permute-start | bytes 172040 | tf_op jit(solution)/shard_map/ppermute | solution.py:35
  42.6 4.9 %collective-permute-start.3 = (f32[16,4,224]{2,0,1:T(8,128)S(1)}, f32[16,4,224]{2,0,1:T(8,128)S(1)}, u32[]{:S(2)}, u32[]{:S(2)}) collective-permute-start(f32[16,4,224]{2,0,1:T(8,128)S(1)} %copy.20), channel_id=1, source_target_pairs={{1,0},{2,1},{3,2},{4,3},{5,4},{6,5},{7,6},{9,8},{10,9},{11,10},{12... | collective-permute-start | bytes 172040 | tf_op jit(solution)/shard_map/ppermute | solution.py:36
  92.5 1.5 copy-start
  96.0 31.0 %copy-start.1 = (f32[224,16]{0,1:T(8,128)S(1)}, f32[224,16]{0,1:T(8,128)}, u32[]{:S(2)}) copy-start(f32[224,16]{0,1:T(8,128)} %param.3) | copy-start | bytes 43012
  97.6 4.1 %collective-permute-start.4 = (f32[224,224]{1,0:T(8,128)S(1)}, f32[224,224]{1,0:T(8,128)S(1)}, u32[]{:S(2)}, u32[]{:S(2)}) collective-permute-start(f32[224,224]{1,0:T(8,128)S(1)} %convolution_bitcast_fusion), channel_id=1, source_target_pairs={{0,1},{1,0},{2,3},{3,2},{4,5},{5,4},{6,7},{7,6},{8,9},{9,8},{10,11... | collective-permute-start | bytes 602120 | tf_op jit(solution)/shard_map/ppermute | solution.py:24
  101.8 8.6 %collective-permute-start.5 = (f32[224,224]{1,0:T(8,128)S(1)}, f32[224,224]{1,0:T(8,128)S(1)}, u32[]{:S(2)}, u32[]{:S(2)}) collective-permute-start(f32[224,224]{1,0:T(8,128)S(1)} %add.133), channel_id=1, source_target_pairs={{0,2},{1,3},{2,0},{3,1},{4,6},{5,7},{6,4},{7,5},{8,10},{9,11},{10,... | collective-permute-start | bytes 602120 | tf_op jit(solution)/shard_map/ppermute | solution.py:24
  110.4 7.4 %collective-permute-start.6 = (f32[224,224]{1,0:T(8,128)S(1)}, f32[224,224]{1,0:T(8,128)S(1)}, u32[]{:S(2)}, u32[]{:S(2)}) collective-permute-start(f32[224,224]{1,0:T(8,128)S(1)} %add.134), channel_id=1, source_target_pairs={{0,4},{1,5},{2,6},{3,7},{4,0},{5,1},{6,2},{7,3},{8,12},{9,13},{10,... | collective-permute-start | bytes 602120 | tf_op jit(solution)/shard_map/ppermute | solution.py:24
  117.8 6.5 %collective-permute-start.7 = (f32[224,224]{1,0:T(8,128)S(1)}, f32[224,224]{1,0:T(8,128)S(1)}, u32[]{:S(2)}, u32[]{:S(2)}) collective-permute-start(f32[224,224]{1,0:T(8,128)S(1)} %add.135), channel_id=1, source_target_pairs={{0,8},{8,0},{16,24},{24,16},{1,9},{9,1},{17,25},{25,17},{2,10},{10... | collective-permute-start | bytes 602120 | tf_op jit(solution)/shard_map/ppermute | solution.py:24
  124.4 11.4 %collective-permute-start.8 = (f32[224,224]{1,0:T(8,128)S(1)}, f32[224,224]{1,0:T(8,128)S(1)}, u32[]{:S(2)}, u32[]{:S(2)}) collective-permute-start(f32[224,224]{1,0:T(8,128)S(1)} %add.136), channel_id=1, source_target_pairs={{0,16},{8,24},{16,0},{24,8},{1,17},{9,25},{17,1},{25,9},{2,18},{10... | collective-permute-start | bytes 602120 | tf_op jit(solution)/shard_map/ppermute | solution.py:24

commit v5 on v4

--- a/solution.py
+++ b/solution.py
@@ -1,3 +1,5 @@
+import functools
+
 import jax
 import jax.numpy as jnp
 from jax import lax
@@ -13,18 +15,51 @@
 fidelity = 0.1
 
 
-def butterfly_sum(value, axes):
+def butterfly_sum(value, axes, start=1):
     for axis in axes:
         count = lax.axis_size(axis)
         if count & (count - 1):
             value = lax.psum(value, axis)
             continue
-        step = 1
+        step = start if axis == axes[0] else 1
         while step < count:
             partner = lax.ppermute(value, axis, [(i, i ^ step) for i in range(count)])
             value = value + partner
             step *= 2
     return value
+
+
+def paired_sum(value, axes):
+    first = axes[0]
+    count = lax.axis_size(first)
+    half = value.shape[0] // 2
+    if count < 2 or count & (count - 1) or value.shape[0] % 2:
+        return butterfly_sum(value, axes)
+    pairs = [(i, i ^ 1) for i in range(count)]
+    low = lax.axis_index(first) % 2 == 0
+    top, bottom = value[:half], value[half:]
+    keep = jnp.where(low, top, bottom)
+    give = jnp.where(low, bottom, top)
+    part = keep + lax.ppermute(give, first, pairs)
+    part = butterfly_sum(part, axes, start=2)
+    other = lax.ppermute(part, first, pairs)
+    return jnp.where(low, jnp.concatenate([part, other]), jnp.concatenate([other, part]))
+
+
+def core_first(mesh):
+    names = tuple(mesh.axis_names)
+    devices = mesh.devices
+    for pos, name in enumerate(names):
+        if devices.shape[pos] < 2:
+            continue
+        at = [0] * devices.ndim
+        one = devices[tuple(at)]
+        at[pos] = 1
+        two = devices[tuple(at)]
+        coords = getattr(one, "coords", None)
+        if coords is not None and tuple(coords) == tuple(getattr(two, "coords", ())):
+            return (name,) + tuple(n for n in names if n != name)
+    return names
 
 
 def with_halo(cells, axis, dim, width):
@@ -116,7 +151,7 @@
     return lax.linalg.triangular_solve(lower, block, left_side=False, lower=True, transpose_a=True)
 
 
-def shards(image, start_basis):
+def shards(order, image, start_basis):
     band_count, tile_rows, tile_cols = image.shape
     width = SWEEPS
     cells = jnp.transpose(image, (1, 2, 0))
@@ -142,7 +177,7 @@
         precision=lax.Precision.HIGHEST,
         preferred_element_type=jnp.float32,
     )
-    gram_full = butterfly_sum(local_gram, ("col", "row"))
+    gram_full = paired_sum(local_gram, order)
     basis_now = start_basis
     for turn in range(SUBIT):
         basis_now = subspace_step(gram_full, basis_now)
@@ -159,4 +194,5 @@
 def solution(mesh):
     in_specs = (P(None, "row", "col"), P())
     out_specs = (P(None, "row", "col"), P(None, "row", "col"))
-    return jax.shard_map(shards, mesh=mesh, in_specs=in_specs, out_specs=out_specs, check_vma=False)
+    body = functools.partial(shards, core_first(mesh))
+    return jax.shard_map(body, mesh=mesh, in_specs=in_specs, out_specs=out_specs, check_vma=False)

time: 158 us -> 151 us (0.956)
  waiting for transfers between devices: 46.4 us -> 39.8 us
    ppermute x5 -> x4, waiting for transfers between devices: 22.9 us -> 15.3 us  [butterfly_sum(): partner = lax.ppermute(value, axis, [(i, i ^ step) for i in range(count)])]
    ppermute x0 -> x2, starting transfers between devices: none -> 3.07 us  [the longest x1 3 us: paired_sum(): part = keep + lax.ppermute(give, first, pairs)]
    ppermute x5 -> x4, starting transfers between devices: 10.6 us -> 7.59 us  [butterfly_sum(): partner = lax.ppermute(value, axis, [(i, i ^ step) for i in range(count)])]
  transfers between devices with their start and end apart: 9 -> 10, of which waited for: 8 -> 8; matrix products, arithmetic and copies ran while one was open for 6% -> 6% of each run, Pallas kernels for 0% -> 0%
where the time goes in v5:
time: 151 us
  other arithmetic  48.5 us (32%)
  waiting for transfers between devices  39.8 us (26%)
  local copies, waits for them, and re-layouts  21.6 us (14%)
  starting transfers between devices  19.5 us (13%)
  Pallas kernels  14.1 us (9%)
  matrix products  6.65 us (4%)
    select_n x4, other arithmetic, sweep(): return jnp.where(keep, new, 0.0)  25.8 us
    ppermute x2, waiting for transfers between devices, with_halo(): before = lax.ppermute(tail, axis, [(i, i + 1) for i in range(count - 1)])  17.7 us
    ppermute x4, waiting for transfers between devices, butterfly_sum(): partner = lax.ppermute(value, axis, [(i, i ^ step) for i in range(count)])  15.3 us
    pallas_call x2, Pallas kernels, subspace_step(): pl.pallas_call(subspace_kernel, out_shape=jax.ShapeDtypeStruct(basis.shap...  14.1 us
    mul x4, other arithmetic, sweep(): flux_col = weight * diff_col  10.3 us
    unnamed x8, local copies, waits for them, and re-layouts  7.7 us
    ppermute x4, starting transfers between devices, butterfly_sum(): partner = lax.ppermute(value, axis, [(i, i ^ step) for i in range(count)])  7.59 us
    concatenate x2, other arithmetic, with_halo(): return jnp.concatenate([before, cells, after], axis=dim)  6.27 us
  transfers between devices with their start and end apart: 10, of which 8 were waited for; matrix products, arithmetic and copies ran while one was open for 6% of the time, Pallas kernels for 0%

profile of v5, /device:TPU:0, one launch (start us, length us, event | category | flops | bytes accessed | tf_op | source)
XLA Modules:
  0.0 151.0 jit_solution(1450395145406810477)
XLA Ops:
  0.6 2.1 %copy.31 = f32[224,8,256]{2,0,1:T(8,128)S(1)} copy(f32[224,8,256]{2,1,0:T(8,128)} %param.2) | data formatting | bytes 3670016 | tf_op args[0]
  4.2 5.0 %collective-permute-start = (f32[4,256,224]{1,2,0:T(8,128)}, f32[4,256,224]{1,2,0:T(8,128)S(1)}, u32[]{:S(2)}, u32[]{:S(2)}) collective-permute-start(f32[4,256,224]{1,2,0:T(8,128)} %get-tuple-element.18), channel_id=1, source_target_pairs={{0,8},{8,16},{16,24},{1,9},{9,17},{17,25},{2,10},{10,18},{18,26},{... | collective-permute-start | bytes 2752520 | tf_op jit(solution)/shard_map/ppermute | solution.py:70
  11.3 17.7 %collective-permute-done = f32[4,256,224]{1,2,0:T(8,128)S(1)} collective-permute-done((f32[4,256,224]{1,2,0:T(8,128)}, f32[4,256,224]{1,2,0:T(8,128)S(1)}, u32[]{:S(2)}, u32[]{:S(2)}) %collective-permute-start) | collective-permute-done | bytes 917536 | tf_op jit(solution)/shard_map/ppermute | solution.py:70
  29.0 4.2 %collective-permute-done.1 = f32[4,256,224]{1,2,0:T(8,128)} collective-permute-done((f32[4,256,224]{1,2,0:T(8,128)}, f32[4,256,224]{1,2,0:T(8,128)}, u32[]{:S(2)}, u32[]{:S(2)}) %collective-permute-start.1) | collective-permute-done | bytes 917536 | tf_op jit(solution)/shard_map/ppermute | solution.py:71
  34.6 2.4 %fusion.21 = (f32[16,4,224]{1,2,0:T(8,128)}, f32[16,4,224]{1,2,0:T(8,128)}) fusion(f32[16,256,224]{1,2,0:T(8,128)S(1)} %pad_maximum_fusion.1), kind=kLoop, calls=%fused_computation.72 | loop fusion | bytes 229376 | tf_op jit(solution)/shard_map/slice | solution.py:69
  37.0 2.1 %copy.19 = f32[16,4,224]{2,0,1:T(8,128)S(1)} copy(f32[16,4,224]{1,2,0:T(8,128)} %get-tuple-element.14) | data formatting | bytes 114688 | tf_op jit(solution)/shard_map/slice | solution.py:69
  40.4 2.1 %copy.20 = f32[16,4,224]{2,0,1:T(8,128)S(1)} copy(f32[16,4,224]{1,2,0:T(8,128)} %get-tuple-element.15) | data formatting | bytes 114688 | tf_op jit(solution)/shard_map/slice | solution.py:68
  43.9 1.8 %copy.21 = f32[16,4,224]{1,2,0:T(8,128)} copy(f32[16,4,224]{2,0,1:T(8,128)S(1)} %collective-permute-done.2) | data formatting | bytes 114688 | tf_op jit(solution)/shard_map/ppermute | solution.py:70
  45.8 1.7 %collective-permute-done.3 = f32[16,4,224]{2,0,1:T(8,128)S(1)} collective-permute-done((f32[16,4,224]{2,0,1:T(8,128)S(1)}, f32[16,4,224]{2,0,1:T(8,128)S(1)}, u32[]{:S(2)}, u32[]{:S(2)}) %collective-permute-start.3) | collective-permute-done | bytes 57376 | tf_op jit(solution)/shard_map/ppermute | solution.py:71
  47.4 1.8 %copy.22 = f32[16,4,224]{1,2,0:T(8,128)} copy(f32[16,4,224]{2,0,1:T(8,128)S(1)} %collective-permute-done.3) | data formatting | bytes 114688 | tf_op jit(solution)/shard_map/ppermute | solution.py:71
  49.3 4.9 %pad_maximum_fusion = f32[16,264,224]{1,2,0:T(8,128)S(1)} fusion(f32[16,4,224]{1,2,0:T(8,128)} %copy.22, f32[4,256,224]{1,2,0:T(8,128)} %collective-permute-done.1, f32[8,256,224]{1,2,0:T(8,128)S(1)} %bitcast.22, f32[4,256,224]{1,2,0:T(8,128)S(1)} %collective-permute-done, f32[16,4,224]{1,2,0:T(8,128)} %copy.21), kind=kLoop, calls=%fused_computation | loop fusion | flops 3784704 | bytes 7569408 | tf_op jit(solution)/shard_map/concatenate | solution.py:72
  54.1 1.7 %add_reduce_fusion = f32[15,263]{1,0:T(8,128)S(1)} fusion(f32[16,264,224]{1,2,0:T(8,128)S(1)} %pad_maximum_fusion), kind=kLoop, calls=%fused_computation.3 | loop fusion | flops 5298135 | bytes 10619940 | tf_op jit(solution)/shard_map/reduce_sum | solution.py:85
  55.9 2.0 %broadcast_multiply_fusion.1 = (f32[15,263,224]{1,2,0:T(8,128)S(1)}, f32[15,263,224]{1,2,0:T(8,128)S(1)}) fusion(f32[15,263]{1,0:T(8,128)S(1)} %add_rsqrt_fusion.3, f32[16,264,224]{1,2,0:T(8,128)S(1)} %pad_maximum_fusion), kind=kLoop, calls=%fused_computation.40 | loop fusion | flops 3534720 | bytes 17689380 | tf_op jit(solution)/shard_map/mul | solution.py:87
  57.9 5.4 %fusion.3 = f32[14,262,224]{1,2,0:T(8,128)S(1)} fusion(f32[15,263,224]{1,2,0:T(8,128)S(1)} %get-tuple-element.9, f32[15,263,224]{1,2,0:T(8,128)S(1)} %get-tuple-element.8, f32[16,264,224]{1,2,0:T(8,128)S(1)} %pad_maximum_fusion, pred[14,262]{1,0:T(8,128)(4,1)S(1)} %broadcast_and_fusion), kind=kLoop, calls=%fused_computation.8 | loop fusion | flops 7394688 | bytes 19722836 | tf_op jit(solution)/shard_map/jit(_where)/select_n | solution.py:92
  64.6 4.6 %broadcast_multiply_fusion.3 = (f32[13,261,224]{1,2,0:T(8,128)}, f32[13,261,224]{1,2,0:T(8,128)}) fusion(f32[13,261]{1,0:T(8,128)S(1)} %add_rsqrt_fusion.2, f32[14,262,224]{1,2,0:T(8,128)S(1)} %fusion.3), kind=kLoop, calls=%fused_computation.42 | loop fusion | flops 3040128 | bytes 15214212 | tf_op jit(solution)/shard_map/mul | solution.py:87
  69.1 11.7 %fusion.6 = f32[12,260,224]{1,2,0:T(8,128)S(1)} fusion(f32[16,264,224]{1,2,0:T(8,128)S(1)} %pad_maximum_fusion, f32[13,261,224]{1,2,0:T(8,128)} %get-tuple-element.11, f32[13,261,224]{1,2,0:T(8,128)} %get-tuple-element.10, f32[14,262,224]{1,2,0:T(8,128)S(1)} %fusion.3, pred[12,260]{1,0:T(8,128)(4,1)S(1)} %broadcast_and_fusion.1), kind=kLoop, calls=%fused_computation.17 | loop fusion | flops 6289920 | bytes 19571760 | tf_op jit(solution)/shard_map/jit(_where)/select_n | solution.py:92
  81.9 2.8 %broadcast_multiply_fusion.5 = (f32[11,259,224]{1,2,0:T(8,128)S(1)}, f32[11,259,224]{1,2,0:T(8,128)}) fusion(f32[11,259]{1,0:T(8,128)S(1)} %add_rsqrt_fusion.1, f32[12,260,224]{1,2,0:T(8,128)S(1)} %fusion.6), kind=kLoop, calls=%fused_computation.44 | loop fusion | flops 2552704 | bytes 12774916 | tf_op jit(solution)/shard_map/mul | solution.py:87
  84.8 6.8 %fusion.11 = f32[10,258,224]{1,2,0:T(8,128)S(1)} fusion(f32[16,264,224]{1,2,0:T(8,128)S(1)} %pad_maximum_fusion, f32[11,259,224]{1,2,0:T(8,128)} %get-tuple-element.13, f32[11,259,224]{1,2,0:T(8,128)S(1)} %get-tuple-element.12, f32[12,260,224]{1,2,0:T(8,128)S(1)} %fusion.6, pred[10,258]{1,0:T(8,128)(4,1)S(1)} %broadcast_and_fusion.2), kind=kLoop, calls=%fused_computation.30 | loop fusion | flops 5201280 | bytes 16184340 | tf_op jit(solution)/shard_map/jit(_where)/select_n | solution.py:92
  94.0 2.0 %fusion.17 = f32[8,256,224]{1,2,0:T(8,128)S(1)} fusion(f32[9,257,224]{1,2,0:T(8,128)S(1)} %get-tuple-element.17, f32[9,257,224]{1,2,0:T(8,128)S(1)} %get-tuple-element.16, f32[10,258,224]{1,2,0:T(8,128)S(1)} %fusion.11, pred[8,256]{1,0:T(8,128)(4,1)S(1)} %broadcast_and_fusion.3, f32[224,8,256]{2,1,0:T(8,128)S(1)} %copy-done), kind=kLoop, calls=%fused_computation.49 | loop fusion | flops 4128768 | bytes 12847104 | tf_op jit(solution)/shard_map/jit(_where)/select_n | solution.py:92
  97.6 3.0 %collective-permute-start.4 = (f32[112,224]{1,0:T(8,128)S(1)}, f32[112,224]{1,0:T(8,128)S(1)}, u32[]{:S(2)}, u32[]{:S(2)}) collective-permute-start(f32[112,224]{1,0:T(8,128)S(1)} %slice_select_fusion), channel_id=1, source_target_pairs={{0,1},{1,0},{2,3},{3,2},{4,5},{5,4},{6,7},{7,6},{8,9},{9,8},{10,11... | collective-permute-start | bytes 301064 | tf_op jit(solution)/shard_map/ppermute | solution.py:43
  101.6 2.5 %collective-permute-start.5 = (f32[112,224]{1,0:T(8,128)S(1)}, f32[112,224]{1,0:T(8,128)S(1)}, u32[]{:S(2)}, u32[]{:S(2)}) collective-permute-start(f32[112,224]{1,0:T(8,128)S(1)} %select_add_fusion), channel_id=1, source_target_pairs={{0,2},{1,3},{2,0},{3,1},{4,6},{5,7},{6,4},{7,5},{8,10},{9,11},{10,... | collective-permute-start | bytes 301064 | tf_op jit(solution)/shard_map/ppermute | solution.py:26
  104.1 3.7 %collective-permute-done.5 = f32[112,224]{1,0:T(8,128)S(1)} collective-permute-done((f32[112,224]{1,0:T(8,128)S(1)}, f32[112,224]{1,0:T(8,128)S(1)}, u32[]{:S(2)}, u32[]{:S(2)}) %collective-permute-start.5) | collective-permute-done | bytes 100384 | tf_op jit(solution)/shard_map/ppermute | solution.py:26
  108.7 4.0 %collective-permute-done.6 = f32[112,224]{1,0:T(8,128)S(1)} collective-permute-done((f32[112,224]{1,0:T(8,128)S(1)}, f32[112,224]{1,0:T(8,128)S(1)}, u32[]{:S(2)}, u32[]{:S(2)}) %collective-permute-start.6) | collective-permute-done | bytes 100384 | tf_op jit(solution)/shard_map/ppermute | solution.py:26
  114.3 3.3 %collective-permute-done.7 = f32[112,224]{1,0:T(8,128)S(1)} collective-permute-done((f32[112,224]{1,0:T(8,128)S(1)}, f32[112,224]{1,0:T(8,128)S(1)}, u32[]{:S(2)}, u32[]{:S(2)}) %collective-permute-start.7) | collective-permute-done | bytes 100384 | tf_op jit(solution)/shard_map/ppermute | solution.py:26
  117.6 2.6 %collective-permute-start.8 = (f32[112,224]{1,0:T(8,128)S(1)}, f32[112,224]{1,0:T(8,128)S(1)}, u32[]{:S(2)}, u32[]{:S(2)}) collective-permute-start(f32[112,224]{1,0:T(8,128)S(1)} %add.141), channel_id=1, source_target_pairs={{0,16},{8,24},{16,0},{24,8},{1,17},{9,25},{17,1},{25,9},{2,18},{10... | collective-permute-start | bytes 301064 | tf_op jit(solution)/shard_map/ppermute | solution.py:26
  120.2 4.4 %collective-permute-done.8 = f32[112,224]{1,0:T(8,128)S(1)} collective-permute-done((f32[112,224]{1,0:T(8,128)S(1)}, f32[112,224]{1,0:T(8,128)S(1)}, u32[]{:S(2)}, u32[]{:S(2)}) %collective-permute-start.8) | collective-permute-done | bytes 100384 | tf_op jit(solution)/shard_map/ppermute | solution.py:26
  126.9 2.3 %copy.25 = f32[224,8,256]{2,1,0:T(8,128)} copy(f32[224,8,256]{2,0,1:T(8,128)S(1)} %bitcast.19) | data formatting | bytes 3670016
  129.9 7.1 %shard_map.41.basis_ref = f32[224,16]{1,0:T(8,128)} custom-call(f32[224,224]{1,0:T(8,128)} %maximum_select_fusion.gram_ref, f32[224,16]{1,0:T(8,128)} %copy.23.basis_ref), custom_call_target="tpu_custom_call" | custom-call | flops 22937600 | bytes 229376 | tf_op jit(solution)/shard_map/pallas_call | solution.py:137
  136.9 7.1 %shard_map.42 = f32[224,16]{1,0:T(8,128)} custom-call(f32[224,224]{1,0:T(8,128)} %maximum_select_fusion.gram_ref, f32[224,16]{1,0:T(8,128)} %shard_map.41.basis_ref), custom_call_target="tpu_custom_call" | custom-call | flops 22937600 | bytes 229376 | tf_op jit(solution)/shard_map/pallas_call | solution.py:137
  144.0 2.6 %fusion.23 = f32[2048,16]{0,1:T(8,128)S(1)} fusion(f32[2048,224]{0,1:T(8,128)} %bitcast.23, f32[224,16]{1,0:T(8,128)} %shard_map.42), kind=kOutput, calls=%fused_computation.74 | convolution fusion | flops 88080384 | bytes 1980416 | tf_op jit(solution)/shard_map/dot_general | solution.py:184
  146.5 2.5 %fusion.24 = f32[224,2048]{1,0:T(8,128)S(1)} fusion(f32[224,16]{1,0:T(8,128)} %shard_map.42, f32[2048,16]{0,1:T(8,128)S(1)} %fusion.23), kind=kOutput, calls=%fused_computation.75 | convolution fusion | flops 88080384 | bytes 1980416 | tf_op jit(solution)/shard_map/dot_general | solution.py:185
  149.0 2.0 %copy.27 = f32[28,8,8,256]{3,2,1,0:T(8,128)} copy(f32[28,8,8,256]{3,1,2,0:T(8,128)S(1)} %bitcast.24) | data formatting | bytes 3670016
  (47 shorter events, 20.6 us)
Async XLA Ops:
  4.2 24.8 %collective-permute-start = (f32[4,256,224]{1,2,0:T(8,128)}, f32[4,256,224]{1,2,0:T(8,128)S(1)}, u32[]{:S(2)}, u32[]{:S(2)}) collective-permute-start(f32[4,256,224]{1,2,0:T(8,128)} %get-tuple-element.18), channel_id=1, source_target_pairs={{0,8},{8,16},{16,24},{1,9},{9,17},{17,25},{2,10},{10,18},{18,26},{... | collective-permute-start | bytes 2752520 | tf_op jit(solution)/shard_map/ppermute | solution.py:70
  9.1 24.0 %collective-permute-start.1 = (f32[4,256,224]{1,2,0:T(8,128)}, f32[4,256,224]{1,2,0:T(8,128)}, u32[]{:S(2)}, u32[]{:S(2)}) collective-permute-start(f32[4,256,224]{1,2,0:T(8,128)} %get-tuple-element.19), channel_id=1, source_target_pairs={{8,0},{16,8},{24,16},{9,1},{17,9},{25,17},{10,2},{18,10},{26,18},{... | collective-permute-start | bytes 2752520 | tf_op jit(solution)/shard_map/ppermute | solution.py:71
  39.1 4.8 %collective-permute-start.2 = (f32[16,4,224]{2,0,1:T(8,128)S(1)}, f32[16,4,224]{2,0,1:T(8,128)S(1)}, u32[]{:S(2)}, u32[]{:S(2)}) collective-permute-start(f32[16,4,224]{2,0,1:T(8,128)S(1)} %copy.19), channel_id=1, source_target_pairs={{0,1},{1,2},{2,3},{3,4},{4,5},{5,6},{6,7},{8,9},{9,10},{10,11},{11... | collective-permute-start | bytes 172040 | tf_op jit(solution)/shard_map/ppermute | solution.py:70
  42.6 4.9 %collective-permute-start.3 = (f32[16,4,224]{2,0,1:T(8,128)S(1)}, f32[16,4,224]{2,0,1:T(8,128)S(1)}, u32[]{:S(2)}, u32[]{:S(2)}) collective-permute-start(f32[16,4,224]{2,0,1:T(8,128)S(1)} %copy.20), channel_id=1, source_target_pairs={{1,0},{2,1},{3,2},{4,3},{5,4},{6,5},{7,6},{9,8},{10,9},{11,10},{12... | collective-permute-start | bytes 172040 | tf_op jit(solution)/shard_map/ppermute | solution.py:71
  92.5 1.5 copy-start
  96.0 28.7 %copy-start.1 = (f32[224,16]{0,1:T(8,128)S(1)}, f32[224,16]{0,1:T(8,128)}, u32[]{:S(2)}) copy-start(f32[224,16]{0,1:T(8,128)} %param.3) | copy-start | bytes 43012
  97.6 4.0 %collective-permute-start.4 = (f32[112,224]{1,0:T(8,128)S(1)}, f32[112,224]{1,0:T(8,128)S(1)}, u32[]{:S(2)}, u32[]{:S(2)}) collective-permute-start(f32[112,224]{1,0:T(8,128)S(1)} %slice_select_fusion), channel_id=1, source_target_pairs={{0,1},{1,0},{2,3},{3,2},{4,5},{5,4},{6,7},{7,6},{8,9},{9,8},{10,11... | collective-permute-start | bytes 301064 | tf_op jit(solution)/shard_map/ppermute | solution.py:43
  101.6 6.1 %collective-permute-start.5 = (f32[112,224]{1,0:T(8,128)S(1)}, f32[112,224]{1,0:T(8,128)S(1)}, u32[]{:S(2)}, u32[]{:S(2)}) collective-permute-start(f32[112,224]{1,0:T(8,128)S(1)} %select_add_fusion), channel_id=1, source_target_pairs={{0,2},{1,3},{2,0},{3,1},{4,6},{5,7},{6,4},{7,5},{8,10},{9,11},{10,... | collective-permute-start | bytes 301064 | tf_op jit(solution)/shard_map/ppermute | solution.py:26
  107.8 4.9 %collective-permute-start.6 = (f32[112,224]{1,0:T(8,128)S(1)}, f32[112,224]{1,0:T(8,128)S(1)}, u32[]{:S(2)}, u32[]{:S(2)}) collective-permute-start(f32[112,224]{1,0:T(8,128)S(1)} %add.139), channel_id=1, source_target_pairs={{0,4},{1,5},{2,6},{3,7},{4,0},{5,1},{6,2},{7,3},{8,12},{9,13},{10,... | collective-permute-start | bytes 301064 | tf_op jit(solution)/shard_map/ppermute | solution.py:26
  112.7 4.9 %collective-permute-start.7 = (f32[112,224]{1,0:T(8,128)S(1)}, f32[112,224]{1,0:T(8,128)S(1)}, u32[]{:S(2)}, u32[]{:S(2)}) collective-permute-start(f32[112,224]{1,0:T(8,128)S(1)} %add.140), channel_id=1, source_target_pairs={{0,8},{8,0},{16,24},{24,16},{1,9},{9,1},{17,25},{25,17},{2,10},{10... | collective-permute-start | bytes 301064 | tf_op jit(solution)/shard_map/ppermute | solution.py:26
  117.6 7.0 %collective-permute-start.8 = (f32[112,224]{1,0:T(8,128)S(1)}, f32[112,224]{1,0:T(8,128)S(1)}, u32[]{:S(2)}, u32[]{:S(2)}) collective-permute-start(f32[112,224]{1,0:T(8,128)S(1)} %add.141), channel_id=1, source_target_pairs={{0,16},{8,24},{16,0},{24,8},{1,17},{9,25},{17,1},{25,9},{2,18},{10... | collective-permute-start | bytes 301064 | tf_op jit(solution)/shard_map/ppermute | solution.py:26
  124.6 4.6 %collective-permute-start.9 = (f32[112,224]{1,0:T(8,128)S(1)}, f32[112,224]{1,0:T(8,128)S(1)}, u32[]{:S(2)}, u32[]{:S(2)}) collective-permute-start(f32[112,224]{1,0:T(8,128)S(1)} %add.142), channel_id=1, source_target_pairs={{0,1},{1,0},{2,3},{3,2},{4,5},{5,4},{6,7},{7,6},{8,9},{9,8},{10,11... | collective-permute-start | bytes 301064 | tf_op jit(solution)/shard_map/ppermute | solution.py:45

commit v6 on v5

--- a/solution.py
+++ b/solution.py
@@ -70,6 +70,40 @@
     before = lax.ppermute(tail, axis, [(i, i + 1) for i in range(count - 1)])
     after = lax.ppermute(head, axis, [(i + 1, i) for i in range(count - 1)])
     return jnp.concatenate([before, cells, after], axis=dim)
+
+
+def with_ring(cells, width):
+    rows_n = lax.axis_size("row")
+    cols_n = lax.axis_size("col")
+    tile_rows, tile_cols = cells.shape[0], cells.shape[1]
+
+    def shift(block, down, across):
+        pairs = [
+            (r * cols_n + c, (r + down) * cols_n + c + across)
+            for r in range(rows_n)
+            for c in range(cols_n)
+            if 0 <= r + down < rows_n and 0 <= c + across < cols_n
+        ]
+        return lax.ppermute(block, ("row", "col"), pairs)
+
+    low_r, high_r = slice(0, width), slice(tile_rows - width, tile_rows)
+    low_c, high_c = slice(0, width), slice(tile_cols - width, tile_cols)
+    top = shift(cells[high_r], 1, 0)
+    bottom = shift(cells[low_r], -1, 0)
+    left = shift(cells[:, high_c], 0, 1)
+    right = shift(cells[:, low_c], 0, -1)
+    top_left = shift(cells[high_r, high_c], 1, 1)
+    top_right = shift(cells[high_r, low_c], 1, -1)
+    bottom_left = shift(cells[low_r, high_c], -1, 1)
+    bottom_right = shift(cells[low_r, low_c], -1, -1)
+    return jnp.concatenate(
+        [
+            jnp.concatenate([top_left, top, top_right], axis=1),
+            jnp.concatenate([left, cells, right], axis=1),
+            jnp.concatenate([bottom_left, bottom, bottom_right], axis=1),
+        ],
+        axis=0,
+    )
 
 
 def inside_mask(axis, tile, width):
@@ -155,8 +189,7 @@
     band_count, tile_rows, tile_cols = image.shape
     width = SWEEPS
     cells = jnp.transpose(image, (1, 2, 0))
-    ext = with_halo(cells, "row", 0, width)
-    ext = with_halo(ext, "col", 1, width)
+    ext = with_ring(cells, width)
     row_in = inside_mask("row", tile_rows, width)
     col_in = inside_mask("col", tile_cols, width)
     field = ext

time: 151 us -> 167 us (1.11)
  waiting for transfers between devices: 39.8 us -> 52.4 us
  starting transfers between devices: 19.5 us -> 27.6 us
  local copies, waits for them, and re-layouts: 21.6 us -> 17.3 us
    ppermute x4 -> x8, starting transfers between devices: 8.85 us -> 19.1 us  [shift(): return lax.ppermute(block, ('row', 'col'), pairs)]
    ppermute x4 -> x8, waiting for transfers between devices: 23.5 us -> 32 us  [shift(): return lax.ppermute(block, ('row', 'col'), pairs)]
    ppermute x4, starting transfers between devices: 7.59 us -> 2.71 us  [butterfly_sum(): partner = lax.ppermute(value, axis, [(i, i ^ step) for i in range(count)])]
    ppermute x4, waiting for transfers between devices: 15.3 us -> 19.5 us  [butterfly_sum(): partner = lax.ppermute(value, axis, [(i, i ^ step) for i in range(count)])]
    ppermute x1, starting transfers between devices: 3 us -> 5.73 us  [paired_sum(): part = keep + lax.ppermute(give, first, pairs)]
    slice x4 -> x5, local copies, waits for them, and re-layouts: 8.12 us -> 5.88 us  [the longest x2 2.74 us: with_ring(): left = shift(cells[:, high_c], 0, 1)]
    ppermute x2, local copies, waits for them, and re-layouts: 3.67 us -> 1.63 us  [shift(): return lax.ppermute(block, ('row', 'col'), pairs)]
    concatenate x2 -> x1, other arithmetic: 6.27 us -> 5.77 us  [with_ring(): jnp.concatenate([jnp.concatenate([top_left, top, top_right], axis=1), jnp...]
  transfers between devices with their start and end apart: 10 -> 14, of which waited for: 8 -> 6; matrix products, arithmetic and copies ran while one was open for 6% -> 7% of each run, Pallas kernels for 0% -> 0%
where the time goes in v6:
time: 167 us
  waiting for transfers between devices  52.4 us (31%)
  other arithmetic  48 us (29%)
  starting transfers between devices  27.6 us (17%)
  local copies, waits for them, and re-layouts  17.3 us (10%)
  Pallas kernels  14.1 us (8%)
  matrix products  6.67 us (4%)
    ppermute x8, waiting for transfers between devices, shift(): return lax.ppermute(block, ('row', 'col'), pairs)  32 us
    select_n x4, other arithmetic, sweep(): return jnp.where(keep, new, 0.0)  25.9 us
    ppermute x4, waiting for transfers between devices, butterfly_sum(): partner = lax.ppermute(value, axis, [(i, i ^ step) for i in range(count)])  19.5 us
    ppermute x8, starting transfers between devices, shift(): return lax.ppermute(block, ('row', 'col'), pairs)  19.1 us
    pallas_call x2, Pallas kernels, subspace_step(): pl.pallas_call(subspace_kernel, out_shape=jax.ShapeDtypeStruct(basis.shap...  14.1 us
    mul x4, other arithmetic, sweep(): flux_col = weight * diff_col  10.3 us
    unnamed x8, local copies, waits for them, and re-layouts  7.7 us
    concatenate x1, other arithmetic, with_ring(): jnp.concatenate([jnp.concatenate([top_left, top, top_right], axis=1), jnp...  5.77 us
  transfers between devices with their start and end apart: 14, of which 6 were waited for; matrix products, arithmetic and copies ran while one was open for 7% of the time, Pallas kernels for 0%

profile of v6, /device:TPU:0, one launch (start us, length us, event | category | flops | bytes accessed | tf_op | source)
XLA Modules:
  0.0 167.0 jit_solution(7947043782798340417)
XLA Ops:
  0.6 2.1 %copy.31 = f32[224,8,256]{2,0,1:T(8,128)S(1)} copy(f32[224,8,256]{2,1,0:T(8,128)} %param.2) | data formatting | bytes 3670016 | tf_op args[0]
  4.1 5.1 %collective-permute-start = (f32[4,4,224]{1,2,0:T(8,128)}, f32[4,4,224]{1,2,0:T(8,128)}, u32[]{:S(2)}, u32[]{:S(2)}) collective-permute-start(f32[4,4,224]{1,2,0:T(8,128)} %get-tuple-element.16), channel_id=1, source_target_pairs={{0,9},{1,10},{2,11},{3,12},{4,13},{5,14},{6,15},{8,17},{9,18},{10,... | collective-permute-start | bytes 43016 | tf_op jit(solution)/shard_map/ppermute | solution.py:87
  10.5 1.5 copy.19
  12.0 3.5 %collective-permute-start.3 = (f32[8,4,224]{2,0,1:T(8,128)S(1)}, f32[8,4,224]{2,0,1:T(8,128)S(1)}, u32[]{:S(2)}, u32[]{:S(2)}) collective-permute-start(f32[8,4,224]{2,0,1:T(8,128)S(1)} %copy.19), channel_id=1, source_target_pairs={{0,1},{1,2},{2,3},{3,4},{4,5},{5,6},{6,7},{8,9},{9,10},{10,11},{11... | collective-permute-start | bytes 86024 | tf_op jit(solution)/shard_map/ppermute | solution.py:87
  17.1 1.4 fusion.22
  18.6 3.7 %collective-permute-start.1 = (f32[4,256,224]{1,2,0:T(8,128)}, f32[4,256,224]{1,2,0:T(8,128)}, u32[]{:S(2)}, u32[]{:S(2)}) collective-permute-start(f32[4,256,224]{1,2,0:T(8,128)} %get-tuple-element.20), channel_id=1, source_target_pairs={{0,8},{1,9},{2,10},{3,11},{4,12},{5,13},{6,14},{7,15},{8,16},{9,17... | collective-permute-start | bytes 2752520 | tf_op jit(solution)/shard_map/ppermute | solution.py:87
  24.4 1.4 collective-permute-start.2
  25.9 1.5 collective-permute-start.5
  30.3 32.0 %collective-permute-done.7 = f32[4,4,224]{1,2,0:T(8,128)} collective-permute-done((f32[4,4,224]{1,2,0:T(8,128)S(1)}, f32[4,4,224]{1,2,0:T(8,128)}, u32[]{:S(2)}, u32[]{:S(2)}) %collective-permute-start.7) | collective-permute-done | bytes 14368 | tf_op jit(solution)/shard_map/ppermute | solution.py:87
  62.3 5.8 %maximum_maximum_fusion = f32[16,264,224]{1,2,0:T(8,128)S(1)} fusion(f32[4,4,224]{1,2,0:T(8,128)} %collective-permute-done.7, f32[4,256,224]{1,2,0:T(8,128)} %collective-permute-done.6, f32[4,4,224]{1,2,0:T(8,128)} %collective-permute-done.5, f32[8,4,224]{1,2,0:T(8,128)} %copy.22, f32[8,256,224]{1,2,0:T(8,128)S(1)} %bitcast.21, f32[8,4,224]{1,2,0:T(8,128)S(1)} %copy.21, ...), kind=kLoop, calls=%fused_computation | loop fusion | flops 7569408 | bytes 7569408 | tf_op jit(solution)/shard_map/concatenate | solution.py:99
  68.1 1.7 %add_reduce_fusion = f32[15,263]{1,0:T(8,128)S(1)} fusion(f32[16,264,224]{1,2,0:T(8,128)S(1)} %maximum_maximum_fusion), kind=kLoop, calls=%fused_computation.3 | loop fusion | flops 5298135 | bytes 10619940 | tf_op jit(solution)/shard_map/reduce_sum | solution.py:119
  69.8 2.0 %broadcast_multiply_fusion.1 = (f32[15,263,224]{1,2,0:T(8,128)S(1)}, f32[15,263,224]{1,2,0:T(8,128)S(1)}) fusion(f32[15,263]{1,0:T(8,128)S(1)} %add_rsqrt_fusion.3, f32[16,264,224]{1,2,0:T(8,128)S(1)} %maximum_maximum_fusion), kind=kLoop, calls=%fused_computation.39 | loop fusion | flops 3534720 | bytes 17689380 | tf_op jit(solution)/shard_map/mul | solution.py:121
  71.8 5.4 %fusion.3 = f32[14,262,224]{1,2,0:T(8,128)S(1)} fusion(f32[15,263,224]{1,2,0:T(8,128)S(1)} %get-tuple-element.9, f32[15,263,224]{1,2,0:T(8,128)S(1)} %get-tuple-element.8, f32[16,264,224]{1,2,0:T(8,128)S(1)} %maximum_maximum_fusion, pred[14,262]{1,0:T(8,128)(4,1)S(1)} %broadcast_and_fusion), kind=kLoop, calls=%fused_computation.8 | loop fusion | flops 7394688 | bytes 19722836 | tf_op jit(solution)/shard_map/jit(_where)/select_n | solution.py:126
  78.5 4.6 %broadcast_multiply_fusion.3 = (f32[13,261,224]{1,2,0:T(8,128)}, f32[13,261,224]{1,2,0:T(8,128)}) fusion(f32[13,261]{1,0:T(8,128)S(1)} %add_rsqrt_fusion.2, f32[14,262,224]{1,2,0:T(8,128)S(1)} %fusion.3), kind=kLoop, calls=%fused_computation.41 | loop fusion | flops 3040128 | bytes 15214212 | tf_op jit(solution)/shard_map/mul | solution.py:121
  83.1 11.7 %fusion.6 = f32[12,260,224]{1,2,0:T(8,128)S(1)} fusion(f32[16,264,224]{1,2,0:T(8,128)S(1)} %maximum_maximum_fusion, f32[13,261,224]{1,2,0:T(8,128)} %get-tuple-element.11, f32[13,261,224]{1,2,0:T(8,128)} %get-tuple-element.10, f32[14,262,224]{1,2,0:T(8,128)S(1)} %fusion.3, pred[12,260]{1,0:T(8,128)(4,1)S(1)} %broadcast_and_fusion.1), kind=kLoop, calls=%fused_computation.17 | loop fusion | flops 6289920 | bytes 19571760 | tf_op jit(solution)/shard_map/jit(_where)/select_n | solution.py:126
  95.9 2.8 %broadcast_multiply_fusion.5 = (f32[11,259,224]{1,2,0:T(8,128)S(1)}, f32[11,259,224]{1,2,0:T(8,128)}) fusion(f32[11,259]{1,0:T(8,128)S(1)} %add_rsqrt_fusion.1, f32[12,260,224]{1,2,0:T(8,128)S(1)} %fusion.6), kind=kLoop, calls=%fused_computation.43 | loop fusion | flops 2552704 | bytes 12774916 | tf_op jit(solution)/shard_map/mul | solution.py:121
  98.7 6.8 %fusion.11 = f32[10,258,224]{1,2,0:T(8,128)S(1)} fusion(f32[16,264,224]{1,2,0:T(8,128)S(1)} %maximum_maximum_fusion, f32[11,259,224]{1,2,0:T(8,128)} %get-tuple-element.13, f32[11,259,224]{1,2,0:T(8,128)S(1)} %get-tuple-element.12, f32[12,260,224]{1,2,0:T(8,128)S(1)} %fusion.6, pred[10,258]{1,0:T(8,128)(4,1)S(1)} %broadcast_and_fusion.2), kind=kLoop, calls=%fused_computation.29 | loop fusion | flops 5201280 | bytes 16184340 | tf_op jit(solution)/shard_map/jit(_where)/select_n | solution.py:126
  107.9 2.0 %fusion.17 = f32[8,256,224]{1,2,0:T(8,128)S(1)} fusion(f32[9,257,224]{1,2,0:T(8,128)S(1)} %get-tuple-element.15, f32[9,257,224]{1,2,0:T(8,128)S(1)} %get-tuple-element.14, f32[10,258,224]{1,2,0:T(8,128)S(1)} %fusion.11, pred[8,256]{1,0:T(8,128)(4,1)S(1)} %broadcast_and_fusion.3, f32[224,8,256]{2,1,0:T(8,128)S(1)} %copy-done), kind=kLoop, calls=%fused_computation.48 | loop fusion | flops 4128768 | bytes 12847104 | tf_op jit(solution)/shard_map/jit(_where)/select_n | solution.py:126
  109.9 1.6 convolution_bitcast_fusion
  111.6 5.7 %collective-permute-start.8 = (f32[112,224]{1,0:T(8,128)S(1)}, f32[112,224]{1,0:T(8,128)S(1)}, u32[]{:S(2)}, u32[]{:S(2)}) collective-permute-start(f32[112,224]{1,0:T(8,128)S(1)} %slice_select_fusion), channel_id=1, source_target_pairs={{0,1},{1,0},{2,3},{3,2},{4,5},{5,4},{6,7},{7,6},{8,9},{9,8},{10,11... | collective-permute-start | bytes 301064 | tf_op jit(solution)/shard_map/ppermute | solution.py:43
  118.3 1.6 collective-permute-start.9
  119.9 3.9 %collective-permute-done.9 = f32[112,224]{1,0:T(8,128)S(1)} collective-permute-done((f32[112,224]{1,0:T(8,128)S(1)}, f32[112,224]{1,0:T(8,128)S(1)}, u32[]{:S(2)}, u32[]{:S(2)}) %collective-permute-start.9) | collective-permute-done | bytes 100384 | tf_op jit(solution)/shard_map/ppermute | solution.py:26
  123.9 4.8 %collective-permute-done.10 = f32[112,224]{1,0:T(8,128)S(1)} collective-permute-done((f32[112,224]{1,0:T(8,128)S(1)}, f32[112,224]{1,0:T(8,128)S(1)}, u32[]{:S(2)}, u32[]{:S(2)}) %collective-permute-start.10) | collective-permute-done | bytes 100384 | tf_op jit(solution)/shard_map/ppermute | solution.py:26
  129.4 4.2 %collective-permute-done.11 = f32[112,224]{1,0:T(8,128)S(1)} collective-permute-done((f32[112,224]{1,0:T(8,128)S(1)}, f32[112,224]{1,0:T(8,128)S(1)}, u32[]{:S(2)}, u32[]{:S(2)}) %collective-permute-start.11) | collective-permute-done | bytes 100384 | tf_op jit(solution)/shard_map/ppermute | solution.py:26
  134.0 6.6 %collective-permute-done.12 = f32[112,224]{1,0:T(8,128)S(1)} collective-permute-done((f32[112,224]{1,0:T(8,128)S(1)}, f32[112,224]{1,0:T(8,128)S(1)}, u32[]{:S(2)}, u32[]{:S(2)}) %collective-permute-start.12) | collective-permute-done | bytes 100384 | tf_op jit(solution)/shard_map/ppermute | solution.py:26
  141.4 1.5 copy.26
  142.9 2.3 %copy.25 = f32[224,8,256]{2,1,0:T(8,128)} copy(f32[224,8,256]{2,0,1:T(8,128)S(1)} %bitcast.23) | data formatting | bytes 3670016
  145.9 7.0 %shard_map.41.basis_ref = f32[224,16]{1,0:T(8,128)} custom-call(f32[224,224]{1,0:T(8,128)} %maximum_select_fusion.gram_ref, f32[224,16]{1,0:T(8,128)} %copy.23.basis_ref), custom_call_target="tpu_custom_call" | custom-call | flops 22937600 | bytes 229376 | tf_op jit(solution)/shard_map/pallas_call | solution.py:171
  152.9 7.1 %shard_map.42 = f32[224,16]{1,0:T(8,128)} custom-call(f32[224,224]{1,0:T(8,128)} %maximum_select_fusion.gram_ref, f32[224,16]{1,0:T(8,128)} %shard_map.41.basis_ref), custom_call_target="tpu_custom_call" | custom-call | flops 22937600 | bytes 229376 | tf_op jit(solution)/shard_map/pallas_call | solution.py:171
  160.0 2.6 %fusion.24 = f32[2048,16]{0,1:T(8,128)S(1)} fusion(f32[2048,224]{0,1:T(8,128)} %bitcast.24, f32[224,16]{1,0:T(8,128)} %shard_map.42), kind=kOutput, calls=%fused_computation.74 | convolution fusion | flops 88080384 | bytes 1980416 | tf_op jit(solution)/shard_map/dot_general | solution.py:217
  162.5 2.5 %fusion.25 = f32[224,2048]{1,0:T(8,128)S(1)} fusion(f32[224,16]{1,0:T(8,128)} %shard_map.42, f32[2048,16]{0,1:T(8,128)S(1)} %fusion.24), kind=kOutput, calls=%fused_computation.75 | convolution fusion | flops 88080384 | bytes 1980416 | tf_op jit(solution)/shard_map/dot_general | solution.py:218
  165.0 2.0 %copy.27 = f32[28,8,8,256]{3,2,1,0:T(8,128)} copy(f32[28,8,8,256]{3,1,2,0:T(8,128)S(1)} %bitcast.25) | data formatting | bytes 3670016
  (55 shorter events, 17.9 us)
Async XLA Ops:
  4.1 20.3 %collective-permute-start = (f32[4,4,224]{1,2,0:T(8,128)}, f32[4,4,224]{1,2,0:T(8,128)}, u32[]{:S(2)}, u32[]{:S(2)}) collective-permute-start(f32[4,4,224]{1,2,0:T(8,128)} %get-tuple-element.16), channel_id=1, source_target_pairs={{0,9},{1,10},{2,11},{3,12},{4,13},{5,14},{6,15},{8,17},{9,18},{10,... | collective-permute-start | bytes 43016 | tf_op jit(solution)/shard_map/ppermute | solution.py:87
  12.0 13.9 %collective-permute-start.3 = (f32[8,4,224]{2,0,1:T(8,128)S(1)}, f32[8,4,224]{2,0,1:T(8,128)S(1)}, u32[]{:S(2)}, u32[]{:S(2)}) collective-permute-start(f32[8,4,224]{2,0,1:T(8,128)S(1)} %copy.19), channel_id=1, source_target_pairs={{0,1},{1,2},{2,3},{3,4},{4,5},{5,6},{6,7},{8,9},{9,10},{10,11},{11... | collective-permute-start | bytes 86024 | tf_op jit(solution)/shard_map/ppermute | solution.py:87
  15.8 11.5 %collective-permute-start.4 = (f32[8,4,224]{2,0,1:T(8,128)S(1)}, f32[8,4,224]{2,0,1:T(8,128)S(1)}, u32[]{:S(2)}, u32[]{:S(2)}) collective-permute-start(f32[8,4,224]{2,0,1:T(8,128)S(1)} %copy.20), channel_id=1, source_target_pairs={{1,0},{2,1},{3,2},{4,3},{5,4},{6,5},{7,6},{9,8},{10,9},{11,10},{12... | collective-permute-start | bytes 86024 | tf_op jit(solution)/shard_map/ppermute | solution.py:87
  18.6 43.7 %collective-permute-start.1 = (f32[4,256,224]{1,2,0:T(8,128)}, f32[4,256,224]{1,2,0:T(8,128)}, u32[]{:S(2)}, u32[]{:S(2)}) collective-permute-start(f32[4,256,224]{1,2,0:T(8,128)} %get-tuple-element.20), channel_id=1, source_target_pairs={{0,8},{1,9},{2,10},{3,11},{4,12},{5,13},{6,14},{7,15},{8,16},{9,17... | collective-permute-start | bytes 2752520 | tf_op jit(solution)/shard_map/ppermute | solution.py:87
  22.3 40.1 %collective-permute-start.6 = (f32[4,256,224]{1,2,0:T(8,128)}, f32[4,256,224]{1,2,0:T(8,128)}, u32[]{:S(2)}, u32[]{:S(2)}) collective-permute-start(f32[4,256,224]{1,2,0:T(8,128)} %get-tuple-element.21), channel_id=1, source_target_pairs={{8,0},{9,1},{10,2},{11,3},{12,4},{13,5},{14,6},{15,7},{16,8},{17,9... | collective-permute-start | bytes 2752520 | tf_op jit(solution)/shard_map/ppermute | solution.py:87
  24.4 5.9 %collective-permute-start.2 = (f32[4,4,224]{1,2,0:T(8,128)}, f32[4,4,224]{1,2,0:T(8,128)}, u32[]{:S(2)}, u32[]{:S(2)}) collective-permute-start(f32[4,4,224]{1,2,0:T(8,128)} %get-tuple-element.19), channel_id=1, source_target_pairs={{1,8},{2,9},{3,10},{4,11},{5,12},{6,13},{7,14},{9,16},{10,17},{11,... | collective-permute-start | bytes 43016 | tf_op jit(solution)/shard_map/ppermute | solution.py:87
  25.9 4.5 %collective-permute-start.5 = (f32[4,4,224]{1,2,0:T(8,128)}, f32[4,4,224]{1,2,0:T(8,128)}, u32[]{:S(2)}, u32[]{:S(2)}) collective-permute-start(f32[4,4,224]{1,2,0:T(8,128)} %get-tuple-element.18), channel_id=1, source_target_pairs={{8,1},{9,2},{10,3},{11,4},{12,5},{13,6},{14,7},{16,9},{17,10},{18,... | collective-permute-start | bytes 43016 | tf_op jit(solution)/shard_map/ppermute | solution.py:87
  27.3 35.0 %collective-permute-start.7 = (f32[4,4,224]{1,2,0:T(8,128)S(1)}, f32[4,4,224]{1,2,0:T(8,128)}, u32[]{:S(2)}, u32[]{:S(2)}) collective-permute-start(f32[4,4,224]{1,2,0:T(8,128)S(1)} %get-tuple-element.17), channel_id=1, source_target_pairs={{9,0},{10,1},{11,2},{12,3},{13,4},{14,5},{15,6},{17,8},{18,9},{19,... | collective-permute-start | bytes 43016 | tf_op jit(solution)/shard_map/ppermute | solution.py:87
  106.4 1.5 copy-start
  109.9 30.7 %copy-start.1 = (f32[224,16]{0,1:T(8,128)S(1)}, f32[224,16]{0,1:T(8,128)}, u32[]{:S(2)}) copy-start(f32[224,16]{0,1:T(8,128)} %param.3) | copy-start | bytes 43012
  111.6 6.7 %collective-permute-start.8 = (f32[112,224]{1,0:T(8,128)S(1)}, f32[112,224]{1,0:T(8,128)S(1)}, u32[]{:S(2)}, u32[]{:S(2)}) collective-permute-start(f32[112,224]{1,0:T(8,128)S(1)} %slice_select_fusion), channel_id=1, source_target_pairs={{0,1},{1,0},{2,3},{3,2},{4,5},{5,4},{6,7},{7,6},{8,9},{9,8},{10,11... | collective-permute-start | bytes 301064 | tf_op jit(solution)/shard_map/ppermute | solution.py:43
  118.3 5.5 %collective-permute-start.9 = (f32[112,224]{1,0:T(8,128)S(1)}, f32[112,224]{1,0:T(8,128)S(1)}, u32[]{:S(2)}, u32[]{:S(2)}) collective-permute-start(f32[112,224]{1,0:T(8,128)S(1)} %select_add_fusion), channel_id=1, source_target_pairs={{0,2},{1,3},{2,0},{3,1},{4,6},{5,7},{6,4},{7,5},{8,10},{9,11},{10,... | collective-permute-start | bytes 301064 | tf_op jit(solution)/shard_map/ppermute | solution.py:26
  123.8 4.9 %collective-permute-start.10 = (f32[112,224]{1,0:T(8,128)S(1)}, f32[112,224]{1,0:T(8,128)S(1)}, u32[]{:S(2)}, u32[]{:S(2)}) collective-permute-start(f32[112,224]{1,0:T(8,128)S(1)} %add.139), channel_id=1, source_target_pairs={{0,4},{1,5},{2,6},{3,7},{4,0},{5,1},{6,2},{7,3},{8,12},{9,13},{10,... | collective-permute-start | bytes 301064 | tf_op jit(solution)/shard_map/ppermute | solution.py:26
  128.7 4.9 %collective-permute-start.11 = (f32[112,224]{1,0:T(8,128)S(1)}, f32[112,224]{1,0:T(8,128)S(1)}, u32[]{:S(2)}, u32[]{:S(2)}) collective-permute-start(f32[112,224]{1,0:T(8,128)S(1)} %add.140), channel_id=1, source_target_pairs={{0,8},{8,0},{16,24},{24,16},{1,9},{9,1},{17,25},{25,17},{2,10},{10... | collective-permute-start | bytes 301064 | tf_op jit(solution)/shard_map/ppermute | solution.py:26
  133.6 7.0 %collective-permute-start.12 = (f32[112,224]{1,0:T(8,128)S(1)}, f32[112,224]{1,0:T(8,128)S(1)}, u32[]{:S(2)}, u32[]{:S(2)}) collective-permute-start(f32[112,224]{1,0:T(8,128)S(1)} %add.141), channel_id=1, source_target_pairs={{0,16},{8,24},{16,0},{24,8},{1,17},{9,25},{17,1},{25,9},{2,18},{10... | collective-permute-start | bytes 301064 | tf_op jit(solution)/shard_map/ppermute | solution.py:26
  140.6 4.6 %collective-permute-start.13 = (f32[112,224]{1,0:T(8,128)S(1)}, f32[112,224]{1,0:T(8,128)S(1)}, u32[]{:S(2)}, u32[]{:S(2)}) collective-permute-start(f32[112,224]{1,0:T(8,128)S(1)} %add.142), channel_id=1, source_target_pairs={{0,1},{1,0},{2,3},{3,2},{4,5},{5,4},{6,7},{7,6},{8,9},{9,8},{10,11... | collective-permute-start | bytes 301064 | tf_op jit(solution)/shard_map/ppermute | solution.py:45

commit v7 on v5

--- a/solution.py
+++ b/solution.py
@@ -70,6 +70,31 @@
     before = lax.ppermute(tail, axis, [(i, i + 1) for i in range(count - 1)])
     after = lax.ppermute(head, axis, [(i + 1, i) for i in range(count - 1)])
     return jnp.concatenate([before, cells, after], axis=dim)
+
+
+def with_ring(cells, width):
+    rows_n = lax.axis_size("row")
+    cols_n = lax.axis_size("col")
+    tile_rows, tile_cols = cells.shape[0], cells.shape[1]
+    down = [(i, i + 1) for i in range(rows_n - 1)]
+    up = [(i + 1, i) for i in range(rows_n - 1)]
+    right = [(i, i + 1) for i in range(cols_n - 1)]
+    left = [(i + 1, i) for i in range(cols_n - 1)]
+    top = lax.ppermute(cells[tile_rows - width:], "row", down)
+    bottom = lax.ppermute(cells[:width], "row", up)
+    west = lax.ppermute(cells[:, tile_cols - width:], "col", right)
+    east = lax.ppermute(cells[:, :width], "col", left)
+    rims = jnp.concatenate([top, bottom], axis=0)
+    rim_west = lax.ppermute(rims[:, tile_cols - width:], "col", right)
+    rim_east = lax.ppermute(rims[:, :width], "col", left)
+    return jnp.concatenate(
+        [
+            jnp.concatenate([rim_west[:width], top, rim_east[:width]], axis=1),
+            jnp.concatenate([west, cells, east], axis=1),
+            jnp.concatenate([rim_west[width:], bottom, rim_east[width:]], axis=1),
+        ],
+        axis=0,
+    )
 
 
 def inside_mask(axis, tile, width):
@@ -155,8 +180,7 @@
     band_count, tile_rows, tile_cols = image.shape
     width = SWEEPS
     cells = jnp.transpose(image, (1, 2, 0))
-    ext = with_halo(cells, "row", 0, width)
-    ext = with_halo(ext, "col", 1, width)
+    ext = with_ring(cells, width)
     row_in = inside_mask("row", tile_rows, width)
     col_in = inside_mask("col", tile_cols, width)
     field = ext

time: 151 us -> 153 us (1.013)
  local copies, waits for them, and re-layouts: 21.6 us -> 27.4 us
  waiting for transfers between devices: 39.8 us -> 34 us
  starting transfers between devices: 19.5 us -> 22 us
    ppermute x4 -> x6, waiting for transfers between devices: 23.5 us -> 17.8 us  [the longest x1 10.3 us: with_ring(): top = lax.ppermute(cells[tile_rows - width:], 'row', down)]
    slice x4 -> x13, local copies, waits for them, and re-layouts: 8.12 us -> 13.7 us  [the longest x2 3.06 us: with_ring(): west = lax.ppermute(cells[:, tile_cols - width:], 'col', right)]
    ppermute x4 -> x6, starting transfers between devices: 8.85 us -> 11.6 us  [the longest x1 4.97 us: with_ring(): top = lax.ppermute(cells[tile_rows - width:], 'row', down)]
    concatenate x2 -> x1, other arithmetic: 6.27 us -> 5.54 us  [with_ring(): jnp.concatenate([jnp.concatenate([rim_west[:width], top, rim_east[:width]...]
    unnamed x8 -> x9, local copies, waits for them, and re-layouts: 7.7 us -> 7.76 us
  transfers between devices with their start and end apart: 10 -> 12, of which waited for: 8 -> 8; matrix products, arithmetic and copies ran while one was open for 6% -> 12% of each run, Pallas kernels for 0% -> 0%
where the time goes in v7:
time: 153 us
  other arithmetic  47.8 us (31%)
  waiting for transfers between devices  34 us (22%)
  local copies, waits for them, and re-layouts  27.4 us (18%)
  starting transfers between devices  22 us (14%)
  Pallas kernels  14.1 us (9%)
  matrix products  6.65 us (4%)
    select_n x4, other arithmetic, sweep(): return jnp.where(keep, new, 0.0)  25.9 us
    ppermute x4, waiting for transfers between devices, butterfly_sum(): partner = lax.ppermute(value, axis, [(i, i ^ step) for i in range(count)])  15.3 us
    pallas_call x2, Pallas kernels, subspace_step(): pl.pallas_call(subspace_kernel, out_shape=jax.ShapeDtypeStruct(basis.shap...  14.1 us
    ppermute x1, waiting for transfers between devices, with_ring(): top = lax.ppermute(cells[tile_rows - width:], 'row', down)  10.3 us
    mul x4, other arithmetic, sweep(): flux_col = weight * diff_col  10.3 us
    unnamed x9, local copies, waits for them, and re-layouts  7.76 us
    ppermute x4, starting transfers between devices, butterfly_sum(): partner = lax.ppermute(value, axis, [(i, i ^ step) for i in range(count)])  7.57 us
    concatenate x1, other arithmetic, with_ring(): jnp.concatenate([jnp.concatenate([rim_west[:width], top, rim_east[:width]...  5.54 us
  transfers between devices with their start and end apart: 12, of which 8 were waited for; matrix products, arithmetic and copies ran while one was open for 12% of the time, Pallas kernels for 0%

profile of v7, /device:TPU:0, one launch (start us, length us, event | category | flops | bytes accessed | tf_op | source)
XLA Modules:
  0.0 152.8 jit_solution(8205131128466247277)
XLA Ops:
  0.6 2.1 %copy.37 = f32[224,8,256]{2,0,1:T(8,128)S(1)} copy(f32[224,8,256]{2,1,0:T(8,128)} %param.2) | data formatting | bytes 3670016 | tf_op args[0]
  4.2 5.0 %collective-permute-start = (f32[4,256,224]{1,2,0:T(8,128)}, f32[4,256,224]{1,2,0:T(8,128)S(1)}, u32[]{:S(2)}, u32[]{:S(2)}) collective-permute-start(f32[4,256,224]{1,2,0:T(8,128)} %get-tuple-element.21), channel_id=1, source_target_pairs={{0,8},{8,16},{16,24},{1,9},{9,17},{17,25},{2,10},{10,18},{18,26},{... | collective-permute-start | bytes 2752520 | tf_op jit(solution)/shard_map/ppermute | solution.py:83
  10.4 1.6 %fusion.21 = (f32[8,4,224]{1,2,0:T(8,128)}, f32[8,4,224]{1,2,0:T(8,128)}) fusion(f32[8,256,224]{1,2,0:T(8,128)S(1)} %bitcast.21), kind=kLoop, calls=%fused_computation.73 | loop fusion | bytes 114688 | tf_op jit(solution)/shard_map/slice | solution.py:85
  15.0 1.5 copy.24
  18.6 10.3 %collective-permute-done = f32[4,256,224]{1,2,0:T(8,128)S(1)} collective-permute-done((f32[4,256,224]{1,2,0:T(8,128)}, f32[4,256,224]{1,2,0:T(8,128)S(1)}, u32[]{:S(2)}, u32[]{:S(2)}) %collective-permute-start) | collective-permute-done | bytes 917536 | tf_op jit(solution)/shard_map/ppermute | solution.py:83
  29.0 4.1 %collective-permute-done.1 = f32[4,256,224]{1,2,0:T(8,128)} collective-permute-done((f32[4,256,224]{1,2,0:T(8,128)}, f32[4,256,224]{1,2,0:T(8,128)}, u32[]{:S(2)}, u32[]{:S(2)}) %collective-permute-start.1) | collective-permute-done | bytes 917536 | tf_op jit(solution)/shard_map/ppermute | solution.py:84
  34.4 1.5 fusion.22
  44.4 3.3 %collective-permute-done.3 = f32[8,4,224]{2,0,1:T(8,128)S(1)} collective-permute-done((f32[8,4,224]{2,0,1:T(8,128)S(1)}, f32[8,4,224]{2,0,1:T(8,128)S(1)}, u32[]{:S(2)}, u32[]{:S(2)}) %collective-permute-start.3) | collective-permute-done | bytes 28704 | tf_op jit(solution)/shard_map/ppermute | solution.py:89
  50.7 5.5 %maximum_maximum_fusion = f32[16,264,224]{1,2,0:T(8,128)S(1)} fusion(f32[4,4,224]{1,2,0:T(8,128)} %copy.28, f32[4,256,224]{1,2,0:T(8,128)} %collective-permute-done.1, f32[4,4,224]{1,2,0:T(8,128)} %copy.27, f32[8,4,224]{1,2,0:T(8,128)} %copy.26, f32[8,256,224]{1,2,0:T(8,128)S(1)} %bitcast.22, f32[8,4,224]{1,2,0:T(8,128)} %copy.25, f32[4,4,224]{1,2,0:T(8,128)} %copy.22, ...), kind=kLoop, calls=%fused_computation | loop fusion | flops 7569408 | bytes 7569408 | tf_op jit(solution)/shard_map/concatenate | solution.py:90
  56.2 1.7 %add_reduce_fusion = f32[15,263]{1,0:T(8,128)S(1)} fusion(f32[16,264,224]{1,2,0:T(8,128)S(1)} %maximum_maximum_fusion), kind=kLoop, calls=%fused_computation.3 | loop fusion | flops 5298135 | bytes 10619940 | tf_op jit(solution)/shard_map/reduce_sum | solution.py:110
  58.0 2.0 %broadcast_multiply_fusion.1 = (f32[15,263,224]{1,2,0:T(8,128)S(1)}, f32[15,263,224]{1,2,0:T(8,128)S(1)}) fusion(f32[15,263]{1,0:T(8,128)S(1)} %add_rsqrt_fusion.3, f32[16,264,224]{1,2,0:T(8,128)S(1)} %maximum_maximum_fusion), kind=kLoop, calls=%fused_computation.39 | loop fusion | flops 3534720 | bytes 17689380 | tf_op jit(solution)/shard_map/mul | solution.py:112
  60.0 5.4 %fusion.3 = f32[14,262,224]{1,2,0:T(8,128)S(1)} fusion(f32[15,263,224]{1,2,0:T(8,128)S(1)} %get-tuple-element.9, f32[15,263,224]{1,2,0:T(8,128)S(1)} %get-tuple-element.8, f32[16,264,224]{1,2,0:T(8,128)S(1)} %maximum_maximum_fusion, pred[14,262]{1,0:T(8,128)(4,1)S(1)} %broadcast_and_fusion), kind=kLoop, calls=%fused_computation.8 | loop fusion | flops 7394688 | bytes 19722836 | tf_op jit(solution)/shard_map/jit(_where)/select_n | solution.py:117
  66.7 4.6 %broadcast_multiply_fusion.3 = (f32[13,261,224]{1,2,0:T(8,128)}, f32[13,261,224]{1,2,0:T(8,128)}) fusion(f32[13,261]{1,0:T(8,128)S(1)} %add_rsqrt_fusion.2, f32[14,262,224]{1,2,0:T(8,128)S(1)} %fusion.3), kind=kLoop, calls=%fused_computation.41 | loop fusion | flops 3040128 | bytes 15214212 | tf_op jit(solution)/shard_map/mul | solution.py:112
  71.2 11.7 %fusion.6 = f32[12,260,224]{1,2,0:T(8,128)S(1)} fusion(f32[16,264,224]{1,2,0:T(8,128)S(1)} %maximum_maximum_fusion, f32[13,261,224]{1,2,0:T(8,128)} %get-tuple-element.11, f32[13,261,224]{1,2,0:T(8,128)} %get-tuple-element.10, f32[14,262,224]{1,2,0:T(8,128)S(1)} %fusion.3, pred[12,260]{1,0:T(8,128)(4,1)S(1)} %broadcast_and_fusion.1), kind=kLoop, calls=%fused_computation.17 | loop fusion | flops 6289920 | bytes 19571760 | tf_op jit(solution)/shard_map/jit(_where)/select_n | solution.py:117
  84.1 2.8 %broadcast_multiply_fusion.5 = (f32[11,259,224]{1,2,0:T(8,128)S(1)}, f32[11,259,224]{1,2,0:T(8,128)}) fusion(f32[11,259]{1,0:T(8,128)S(1)} %add_rsqrt_fusion.1, f32[12,260,224]{1,2,0:T(8,128)S(1)} %fusion.6), kind=kLoop, calls=%fused_computation.43 | loop fusion | flops 2552704 | bytes 12774916 | tf_op jit(solution)/shard_map/mul | solution.py:112
  86.9 6.8 %fusion.11 = f32[10,258,224]{1,2,0:T(8,128)S(1)} fusion(f32[16,264,224]{1,2,0:T(8,128)S(1)} %maximum_maximum_fusion, f32[11,259,224]{1,2,0:T(8,128)} %get-tuple-element.13, f32[11,259,224]{1,2,0:T(8,128)S(1)} %get-tuple-element.12, f32[12,260,224]{1,2,0:T(8,128)S(1)} %fusion.6, pred[10,258]{1,0:T(8,128)(4,1)S(1)} %broadcast_and_fusion.2), kind=kLoop, calls=%fused_computation.29 | loop fusion | flops 5201280 | bytes 16184340 | tf_op jit(solution)/shard_map/jit(_where)/select_n | solution.py:117
  96.1 2.0 %fusion.17 = f32[8,256,224]{1,2,0:T(8,128)S(1)} fusion(f32[9,257,224]{1,2,0:T(8,128)S(1)} %get-tuple-element.15, f32[9,257,224]{1,2,0:T(8,128)S(1)} %get-tuple-element.14, f32[10,258,224]{1,2,0:T(8,128)S(1)} %fusion.11, pred[8,256]{1,0:T(8,128)(4,1)S(1)} %broadcast_and_fusion.3, f32[224,8,256]{2,1,0:T(8,128)S(1)} %copy-done), kind=kLoop, calls=%fused_computation.48 | loop fusion | flops 4128768 | bytes 12847104 | tf_op jit(solution)/shard_map/jit(_where)/select_n | solution.py:117
  98.1 1.6 %convolution_bitcast_fusion = f32[224,224]{1,0:T(8,128)S(1)} fusion(f32[8,256,224]{1,2,0:T(8,128)S(1)} %fusion.17), kind=kOutput, calls=%fused_computation.54 | convolution fusion | flops 1233125376 | bytes 2035712 | tf_op jit(solution)/shard_map/dot_general | solution.py:197
  99.7 2.7 %collective-permute-start.6 = (f32[112,224]{1,0:T(8,128)S(1)}, f32[112,224]{1,0:T(8,128)S(1)}, u32[]{:S(2)}, u32[]{:S(2)}) collective-permute-start(f32[112,224]{1,0:T(8,128)S(1)} %slice_select_fusion), channel_id=1, source_target_pairs={{0,1},{1,0},{2,3},{3,2},{4,5},{5,4},{6,7},{7,6},{8,9},{9,8},{10,11... | collective-permute-start | bytes 301064 | tf_op jit(solution)/shard_map/ppermute | solution.py:43
  103.4 2.5 %collective-permute-start.7 = (f32[112,224]{1,0:T(8,128)S(1)}, f32[112,224]{1,0:T(8,128)S(1)}, u32[]{:S(2)}, u32[]{:S(2)}) collective-permute-start(f32[112,224]{1,0:T(8,128)S(1)} %select_add_fusion), channel_id=1, source_target_pairs={{0,2},{1,3},{2,0},{3,1},{4,6},{5,7},{6,4},{7,5},{8,10},{9,11},{10,... | collective-permute-start | bytes 301064 | tf_op jit(solution)/shard_map/ppermute | solution.py:26
  105.9 3.7 %collective-permute-done.7 = f32[112,224]{1,0:T(8,128)S(1)} collective-permute-done((f32[112,224]{1,0:T(8,128)S(1)}, f32[112,224]{1,0:T(8,128)S(1)}, u32[]{:S(2)}, u32[]{:S(2)}) %collective-permute-start.7) | collective-permute-done | bytes 100384 | tf_op jit(solution)/shard_map/ppermute | solution.py:26
  110.5 4.0 %collective-permute-done.8 = f32[112,224]{1,0:T(8,128)S(1)} collective-permute-done((f32[112,224]{1,0:T(8,128)S(1)}, f32[112,224]{1,0:T(8,128)S(1)}, u32[]{:S(2)}, u32[]{:S(2)}) %collective-permute-start.8) | collective-permute-done | bytes 100384 | tf_op jit(solution)/shard_map/ppermute | solution.py:26
  114.5 1.6 %collective-permute-start.9 = (f32[112,224]{1,0:T(8,128)S(1)}, f32[112,224]{1,0:T(8,128)S(1)}, u32[]{:S(2)}, u32[]{:S(2)}) collective-permute-start(f32[112,224]{1,0:T(8,128)S(1)} %add.140), channel_id=1, source_target_pairs={{0,8},{8,0},{16,24},{24,16},{1,9},{9,1},{17,25},{25,17},{2,10},{10... | collective-permute-start | bytes 301064 | tf_op jit(solution)/shard_map/ppermute | solution.py:26
  116.1 3.3 %collective-permute-done.9 = f32[112,224]{1,0:T(8,128)S(1)} collective-permute-done((f32[112,224]{1,0:T(8,128)S(1)}, f32[112,224]{1,0:T(8,128)S(1)}, u32[]{:S(2)}, u32[]{:S(2)}) %collective-permute-start.9) | collective-permute-done | bytes 100384 | tf_op jit(solution)/shard_map/ppermute | solution.py:26
  119.4 2.6 %collective-permute-start.10 = (f32[112,224]{1,0:T(8,128)S(1)}, f32[112,224]{1,0:T(8,128)S(1)}, u32[]{:S(2)}, u32[]{:S(2)}) collective-permute-start(f32[112,224]{1,0:T(8,128)S(1)} %add.141), channel_id=1, source_target_pairs={{0,16},{8,24},{16,0},{24,8},{1,17},{9,25},{17,1},{25,9},{2,18},{10... | collective-permute-start | bytes 301064 | tf_op jit(solution)/shard_map/ppermute | solution.py:26
  122.0 4.4 %collective-permute-done.10 = f32[112,224]{1,0:T(8,128)S(1)} collective-permute-done((f32[112,224]{1,0:T(8,128)S(1)}, f32[112,224]{1,0:T(8,128)S(1)}, u32[]{:S(2)}, u32[]{:S(2)}) %collective-permute-start.10) | collective-permute-done | bytes 100384 | tf_op jit(solution)/shard_map/ppermute | solution.py:26
  128.7 2.3 %copy.31 = f32[224,8,256]{2,1,0:T(8,128)} copy(f32[224,8,256]{2,0,1:T(8,128)S(1)} %bitcast.19) | data formatting | bytes 3670016
  131.7 7.0 %shard_map.41.basis_ref = f32[224,16]{1,0:T(8,128)} custom-call(f32[224,224]{1,0:T(8,128)} %maximum_select_fusion.gram_ref, f32[224,16]{1,0:T(8,128)} %copy.29.basis_ref), custom_call_target="tpu_custom_call" | custom-call | flops 22937600 | bytes 229376 | tf_op jit(solution)/shard_map/pallas_call | solution.py:162
  138.7 7.1 %shard_map.42 = f32[224,16]{1,0:T(8,128)} custom-call(f32[224,224]{1,0:T(8,128)} %maximum_select_fusion.gram_ref, f32[224,16]{1,0:T(8,128)} %shard_map.41.basis_ref), custom_call_target="tpu_custom_call" | custom-call | flops 22937600 | bytes 229376 | tf_op jit(solution)/shard_map/pallas_call | solution.py:162
  145.8 2.6 %fusion.26 = f32[2048,16]{0,1:T(8,128)S(1)} fusion(f32[2048,224]{0,1:T(8,128)} %bitcast.23, f32[224,16]{1,0:T(8,128)} %shard_map.42), kind=kOutput, calls=%fused_computation.78 | convolution fusion | flops 88080384 | bytes 1980416 | tf_op jit(solution)/shard_map/dot_general | solution.py:208
  148.3 2.5 %fusion.27 = f32[224,2048]{1,0:T(8,128)S(1)} fusion(f32[224,16]{1,0:T(8,128)} %shard_map.42, f32[2048,16]{0,1:T(8,128)S(1)} %fusion.26), kind=kOutput, calls=%fused_computation.79 | convolution fusion | flops 88080384 | bytes 1980416 | tf_op jit(solution)/shard_map/dot_general | solution.py:209
  150.8 2.0 %copy.33 = f32[28,8,8,256]{3,2,1,0:T(8,128)} copy(f32[28,8,8,256]{3,1,2,0:T(8,128)S(1)} %bitcast.24) | data formatting | bytes 3670016
  (61 shorter events, 30.3 us)
Async XLA Ops:
  4.2 24.8 %collective-permute-start = (f32[4,256,224]{1,2,0:T(8,128)}, f32[4,256,224]{1,2,0:T(8,128)S(1)}, u32[]{:S(2)}, u32[]{:S(2)}) collective-permute-start(f32[4,256,224]{1,2,0:T(8,128)} %get-tuple-element.21), channel_id=1, source_target_pairs={{0,8},{8,16},{16,24},{1,9},{9,17},{17,25},{2,10},{10,18},{18,26},{... | collective-permute-start | bytes 2752520 | tf_op jit(solution)/shard_map/ppermute | solution.py:83
  9.1 24.0 %collective-permute-start.1 = (f32[4,256,224]{1,2,0:T(8,128)}, f32[4,256,224]{1,2,0:T(8,128)}, u32[]{:S(2)}, u32[]{:S(2)}) collective-permute-start(f32[4,256,224]{1,2,0:T(8,128)} %get-tuple-element.20), channel_id=1, source_target_pairs={{8,0},{16,8},{24,16},{9,1},{17,9},{25,17},{10,2},{18,10},{26,18},{... | collective-permute-start | bytes 2752520 | tf_op jit(solution)/shard_map/ppermute | solution.py:84
  13.5 25.3 %collective-permute-start.4 = (f32[8,4,224]{2,0,1:T(8,128)S(1)}, f32[8,4,224]{2,0,1:T(8,128)S(1)}, u32[]{:S(2)}, u32[]{:S(2)}) collective-permute-start(f32[8,4,224]{2,0,1:T(8,128)S(1)} %copy.23), channel_id=1, source_target_pairs={{0,1},{1,2},{2,3},{3,4},{4,5},{5,6},{6,7},{8,9},{9,10},{10,11},{11... | collective-permute-start | bytes 86024 | tf_op jit(solution)/shard_map/ppermute | solution.py:85
  16.5 23.6 %collective-permute-start.5 = (f32[8,4,224]{2,0,1:T(8,128)S(1)}, f32[8,4,224]{2,0,1:T(8,128)S(1)}, u32[]{:S(2)}, u32[]{:S(2)}) collective-permute-start(f32[8,4,224]{2,0,1:T(8,128)S(1)} %copy.24), channel_id=1, source_target_pairs={{1,0},{2,1},{3,2},{4,3},{5,4},{6,5},{7,6},{9,8},{10,9},{11,10},{12... | collective-permute-start | bytes 86024 | tf_op jit(solution)/shard_map/ppermute | solution.py:86
  37.4 6.8 %collective-permute-start.2 = (f32[8,4,224]{2,0,1:T(8,128)S(1)}, f32[8,4,224]{2,0,1:T(8,128)S(1)}, u32[]{:S(2)}, u32[]{:S(2)}) collective-permute-start(f32[8,4,224]{2,0,1:T(8,128)S(1)} %copy.19), channel_id=1, source_target_pairs={{0,1},{1,2},{2,3},{3,4},{4,5},{5,6},{6,7},{8,9},{9,10},{10,11},{11... | collective-permute-start | bytes 86024 | tf_op jit(solution)/shard_map/ppermute | solution.py:88
  42.9 4.8 %collective-permute-start.3 = (f32[8,4,224]{2,0,1:T(8,128)S(1)}, f32[8,4,224]{2,0,1:T(8,128)S(1)}, u32[]{:S(2)}, u32[]{:S(2)}) collective-permute-start(f32[8,4,224]{2,0,1:T(8,128)S(1)} %copy.20), channel_id=1, source_target_pairs={{1,0},{2,1},{3,2},{4,3},{5,4},{6,5},{7,6},{9,8},{10,9},{11,10},{12... | collective-permute-start | bytes 86024 | tf_op jit(solution)/shard_map/ppermute | solution.py:89
  94.6 1.5 copy-start
  98.1 28.4 %copy-start.1 = (f32[224,16]{0,1:T(8,128)S(1)}, f32[224,16]{0,1:T(8,128)}, u32[]{:S(2)}) copy-start(f32[224,16]{0,1:T(8,128)} %param.3) | copy-start | bytes 43012
  99.7 3.7 %collective-permute-start.6 = (f32[112,224]{1,0:T(8,128)S(1)}, f32[112,224]{1,0:T(8,128)S(1)}, u32[]{:S(2)}, u32[]{:S(2)}) collective-permute-start(f32[112,224]{1,0:T(8,128)S(1)} %slice_select_fusion), channel_id=1, source_target_pairs={{0,1},{1,0},{2,3},{3,2},{4,5},{5,4},{6,7},{7,6},{8,9},{9,8},{10,11... | collective-permute-start | bytes 301064 | tf_op jit(solution)/shard_map/ppermute | solution.py:43
  103.4 6.1 %collective-permute-start.7 = (f32[112,224]{1,0:T(8,128)S(1)}, f32[112,224]{1,0:T(8,128)S(1)}, u32[]{:S(2)}, u32[]{:S(2)}) collective-permute-start(f32[112,224]{1,0:T(8,128)S(1)} %select_add_fusion), channel_id=1, source_target_pairs={{0,2},{1,3},{2,0},{3,1},{4,6},{5,7},{6,4},{7,5},{8,10},{9,11},{10,... | collective-permute-start | bytes 301064 | tf_op jit(solution)/shard_map/ppermute | solution.py:26
  109.6 4.9 %collective-permute-start.8 = (f32[112,224]{1,0:T(8,128)S(1)}, f32[112,224]{1,0:T(8,128)S(1)}, u32[]{:S(2)}, u32[]{:S(2)}) collective-permute-start(f32[112,224]{1,0:T(8,128)S(1)} %add.139), channel_id=1, source_target_pairs={{0,4},{1,5},{2,6},{3,7},{4,0},{5,1},{6,2},{7,3},{8,12},{9,13},{10,... | collective-permute-start | bytes 301064 | tf_op jit(solution)/shard_map/ppermute | solution.py:26
  114.5 4.9 %collective-permute-start.9 = (f32[112,224]{1,0:T(8,128)S(1)}, f32[112,224]{1,0:T(8,128)S(1)}, u32[]{:S(2)}, u32[]{:S(2)}) collective-permute-start(f32[112,224]{1,0:T(8,128)S(1)} %add.140), channel_id=1, source_target_pairs={{0,8},{8,0},{16,24},{24,16},{1,9},{9,1},{17,25},{25,17},{2,10},{10... | collective-permute-start | bytes 301064 | tf_op jit(solution)/shard_map/ppermute | solution.py:26
  119.4 7.0 %collective-permute-start.10 = (f32[112,224]{1,0:T(8,128)S(1)}, f32[112,224]{1,0:T(8,128)S(1)}, u32[]{:S(2)}, u32[]{:S(2)}) collective-permute-start(f32[112,224]{1,0:T(8,128)S(1)} %add.141), channel_id=1, source_target_pairs={{0,16},{8,24},{16,0},{24,8},{1,17},{9,25},{17,1},{25,9},{2,18},{10... | collective-permute-start | bytes 301064 | tf_op jit(solution)/shard_map/ppermute | solution.py:26
  126.4 4.6 %collective-permute-start.11 = (f32[112,224]{1,0:T(8,128)S(1)}, f32[112,224]{1,0:T(8,128)S(1)}, u32[]{:S(2)}, u32[]{:S(2)}) collective-permute-start(f32[112,224]{1,0:T(8,128)S(1)} %add.142), channel_id=1, source_target_pairs={{0,1},{1,0},{2,3},{3,2},{4,5},{5,4},{6,7},{7,6},{8,9},{9,8},{10,11... | collective-permute-start | bytes 301064 | tf_op jit(solution)/shard_map/ppermute | solution.py:45

commit v8 on v5

--- a/solution.py
+++ b/solution.py
@@ -5,6 +5,7 @@
 from jax import lax
 from jax.sharding import PartitionSpec as P
 from jax.experimental import pallas as pl
+from jax.experimental.layout import Layout, with_layout_constraint
 from jax.experimental.pallas import tpu as pltpu
 
 SWEEPS = 4
@@ -70,6 +71,10 @@
     before = lax.ppermute(tail, axis, [(i, i + 1) for i in range(count - 1)])
     after = lax.ppermute(head, axis, [(i + 1, i) for i in range(count - 1)])
     return jnp.concatenate([before, cells, after], axis=dim)
+
+
+def pinned(cells):
+    return with_layout_constraint(cells, Layout(major_to_minor=tuple(range(cells.ndim))))
 
 
 def inside_mask(axis, tile, width):
@@ -154,7 +159,7 @@
 def shards(order, image, start_basis):
     band_count, tile_rows, tile_cols = image.shape
     width = SWEEPS
-    cells = jnp.transpose(image, (1, 2, 0))
+    cells = pinned(jnp.transpose(image, (1, 2, 0)))
     ext = with_halo(cells, "row", 0, width)
     ext = with_halo(ext, "col", 1, width)
     row_in = inside_mask("row", tile_rows, width)
@@ -167,7 +172,7 @@
         nc = tile_cols + 2 * left
         source = ext[lo:lo + nr, lo:lo + nc]
         keep = (row_in[lo:lo + nr, None] & col_in[None, lo:lo + nc])[:, :, None]
-        field = sweep(field, source, keep)
+        field = pinned(sweep(field, source, keep))
     flat_cells = field.reshape(tile_rows * tile_cols, band_count)
     smoothed = jnp.transpose(field, (2, 0, 1))
     local_gram = lax.dot_general(

time: 151 us -> 122 us (0.81)
  other arithmetic: 48.5 us -> 20.9 us
  local copies, waits for them, and re-layouts: 21.6 us -> 16.9 us
  waiting for transfers between devices: 39.8 us -> 41.9 us
    select_n x4, other arithmetic: 25.8 us -> 8.82 us  [sweep(): return jnp.where(keep, new, 0.0)]
    mul x4, other arithmetic: 10.3 us -> 4.35 us  [sweep(): flux_col = weight * diff_col]
    concatenate x2 -> x1, other arithmetic: 6.27 us -> 1.69 us  [with_halo(): return jnp.concatenate([before, cells, after], axis=dim)]
    ppermute x2, waiting for transfers between devices: 5.83 us -> 8.29 us  [with_halo(): after = lax.ppermute(head, axis, [(i + 1, i) for i in range(count - 1)])]
    slice x3 -> x2, local copies, waits for them, and re-layouts: 6 us -> 3.64 us  [with_halo(): tail = lax.slice_in_dim(cells, size - width, size, axis=dim)]
    ppermute x2, waiting for transfers between devices: 17.7 us -> 15.6 us  [with_halo(): before = lax.ppermute(tail, axis, [(i, i + 1) for i in range(count - 1)])]
    dot_general x1, matrix products: 1.63 us -> 3.64 us  [shards(): lax.dot_general(flat_cells, flat_cells, (((0,), (0,)), ((), ())), precisi...]
    ppermute x4, waiting for transfers between devices: 15.3 us -> 17.1 us  [butterfly_sum(): partner = lax.ppermute(value, axis, [(i, i ^ step) for i in range(count)])]
where the time goes in v8:
time: 122 us; the launch traced here: 121 us
  waiting for transfers between devices  41.9 us (34%)
  other arithmetic  20.9 us (17%)
  starting transfers between devices  18.6 us (15%)
  local copies, waits for them, and re-layouts  16.9 us (14%)
  Pallas kernels  14.1 us (12%)
  matrix products  8.03 us (7%)
    ppermute x4, waiting for transfers between devices, butterfly_sum(): partner = lax.ppermute(value, axis, [(i, i ^ step) for i in range(count)])  17.1 us
    ppermute x2, waiting for transfers between devices, with_halo(): before = lax.ppermute(tail, axis, [(i, i + 1) for i in range(count - 1)])  15.6 us
    pallas_call x2, Pallas kernels, subspace_step(): pl.pallas_call(subspace_kernel, out_shape=jax.ShapeDtypeStruct(basis.shap...  14.1 us
    select_n x4, other arithmetic, sweep(): return jnp.where(keep, new, 0.0)  8.82 us
    ppermute x2, waiting for transfers between devices, with_halo(): after = lax.ppermute(head, axis, [(i + 1, i) for i in range(count - 1)])  8.29 us
    unnamed x12, local copies, waits for them, and re-layouts  7.46 us
    ppermute x2, starting transfers between devices, with_halo(): before = lax.ppermute(tail, axis, [(i, i + 1) for i in range(count - 1)])  7.18 us
    ppermute x4, starting transfers between devices, butterfly_sum(): partner = lax.ppermute(value, axis, [(i, i ^ step) for i in range(count)])  5.8 us
  transfers between devices with their start and end apart: 10, of which 8 were waited for; matrix products, arithmetic and copies ran while one was open for 6% of the time, Pallas kernels for 0%

profile of v8, /device:TPU:0, one launch (start us, length us, event | category | flops | bytes accessed | tf_op | source)
XLA Modules:
  0.0 121.4 jit_solution(16751234878855807367)
XLA Ops:
  0.6 1.9 %copy.7 = f32[224,8,256]{0,2,1:T(8,128)S(1)} copy(f32[224,8,256]{2,1,0:T(8,128)} %param.2) | data formatting | bytes 3670016 | tf_op args[0]
  3.7 2.5 %copy.8 = f32[4,256,224]{1,2,0:T(8,128)} copy(f32[4,256,224]{2,1,0:T(8,128)} %get-tuple-element.16) | data formatting | bytes 1835008 | tf_op jit(solution)/shard_map/slice | solution.py:70
  6.2 5.9 %collective-permute-start = (f32[4,256,224]{1,2,0:T(8,128)}, f32[4,256,224]{1,2,0:T(8,128)}, u32[]{:S(2)}, u32[]{:S(2)}) collective-permute-start(f32[4,256,224]{1,2,0:T(8,128)} %copy.8), channel_id=1, source_target_pairs={{0,8},{8,16},{16,24},{1,9},{9,17},{17,25},{2,10},{10,18},{18,26},{... | collective-permute-start | bytes 2752520 | tf_op jit(solution)/shard_map/ppermute | solution.py:71
  13.3 1.3 %collective-permute-start.1 = (f32[4,256,224]{1,2,0:T(8,128)}, f32[4,256,224]{1,2,0:T(8,128)}, u32[]{:S(2)}, u32[]{:S(2)}) collective-permute-start(f32[4,256,224]{1,2,0:T(8,128)} %copy.9), channel_id=1, source_target_pairs={{8,0},{16,8},{24,16},{9,1},{17,9},{25,17},{10,2},{18,10},{26,18},{... | collective-permute-start | bytes 2752520 | tf_op jit(solution)/shard_map/ppermute | solution.py:72
  15.5 15.6 %collective-permute-done = f32[4,256,224]{1,2,0:T(8,128)} collective-permute-done((f32[4,256,224]{1,2,0:T(8,128)}, f32[4,256,224]{1,2,0:T(8,128)}, u32[]{:S(2)}, u32[]{:S(2)}) %collective-permute-start) | collective-permute-done | bytes 917536 | tf_op jit(solution)/shard_map/ppermute | solution.py:71
  31.0 1.5 %copy.10 = f32[4,256,224]{2,1,0:T(8,128)S(1)} copy(f32[4,256,224]{1,2,0:T(8,128)} %collective-permute-done) | data formatting | bytes 1835008 | tf_op jit(solution)/shard_map/ppermute | solution.py:71
  32.5 4.8 %collective-permute-done.1 = f32[4,256,224]{1,2,0:T(8,128)} collective-permute-done((f32[4,256,224]{1,2,0:T(8,128)}, f32[4,256,224]{1,2,0:T(8,128)}, u32[]{:S(2)}, u32[]{:S(2)}) %collective-permute-start.1) | collective-permute-done | bytes 917536 | tf_op jit(solution)/shard_map/ppermute | solution.py:72
  37.3 2.5 %copy.11 = f32[4,256,224]{2,1,0:T(8,128)} copy(f32[4,256,224]{1,2,0:T(8,128)} %collective-permute-done.1) | data formatting | bytes 1835008 | tf_op jit(solution)/shard_map/ppermute | solution.py:72
  40.6 1.3 %collective-permute-start.2 = (f32[16,4,224]{2,1,0:T(4,128)S(1)}, f32[16,4,224]{2,1,0:T(4,128)S(1)}, u32[]{:S(2)}, u32[]{:S(2)}) collective-permute-start(f32[16,4,224]{2,1,0:T(4,128)S(1)} %get-tuple-element.8), channel_id=1, source_target_pairs={{0,1},{1,2},{2,3},{3,4},{4,5},{5,6},{6,7},{8,9},{9,10},{10,11},{11... | collective-permute-start | bytes 172040 | tf_op jit(solution)/shard_map/ppermute | solution.py:71
  41.9 1.3 %collective-permute-start.3 = (f32[16,4,224]{2,1,0:T(4,128)S(1)}, f32[16,4,224]{2,1,0:T(4,128)S(1)}, u32[]{:S(2)}, u32[]{:S(2)}) collective-permute-start(f32[16,4,224]{2,1,0:T(4,128)S(1)} %get-tuple-element.9), channel_id=1, source_target_pairs={{1,0},{2,1},{3,2},{4,3},{5,4},{6,5},{7,6},{9,8},{10,9},{11,10},{12... | collective-permute-start | bytes 172040 | tf_op jit(solution)/shard_map/ppermute | solution.py:72
  43.3 3.5 %collective-permute-done.3 = f32[16,4,224]{2,1,0:T(4,128)S(1)} collective-permute-done((f32[16,4,224]{2,1,0:T(4,128)S(1)}, f32[16,4,224]{2,1,0:T(4,128)S(1)}, u32[]{:S(2)}, u32[]{:S(2)}) %collective-permute-start.3) | collective-permute-done | bytes 57376 | tf_op jit(solution)/shard_map/ppermute | solution.py:72
  46.8 1.7 %pad_maximum_fusion = f32[16,264,224]{2,1,0:T(8,128)S(1)} fusion(f32[16,4,224]{2,1,0:T(4,128)S(1)} %collective-permute-done.3, f32[4,256,224]{2,1,0:T(8,128)} %copy.11, f32[8,256,224]{2,1,0:T(8,128)S(1)} %bitcast.16, f32[4,256,224]{2,1,0:T(8,128)S(1)} %copy.10, f32[16,4,224]{2,1,0:T(4,128)S(1)} %collective-permute-done.2), kind=kLoop, calls=%fused_computation | loop fusion | flops 3784704 | bytes 7569408 | tf_op jit(solution)/shard_map/concatenate | solution.py:73
  48.5 1.3 %add_reduce_fusion = f32[15,263]{1,0:T(8,128)S(1)} fusion(f32[16,264,224]{2,1,0:T(8,128)S(1)} %pad_maximum_fusion), kind=kLoop, calls=%fused_computation.3 | loop fusion | flops 5298135 | bytes 10619940 | tf_op jit(solution)/shard_map/reduce_sum | solution.py:90
  49.7 1.6 %broadcast_multiply_fusion.1 = (f32[15,263,224]{2,1,0:T(8,128)S(1)}, f32[15,263,224]{2,1,0:T(8,128)S(1)}) fusion(f32[15,263]{1,0:T(8,128)S(1)} %add_rsqrt_fusion.3, f32[16,264,224]{2,1,0:T(8,128)S(1)} %pad_maximum_fusion), kind=kLoop, calls=%fused_computation.46 | loop fusion | flops 3534720 | bytes 17689380 | tf_op jit(solution)/shard_map/mul | solution.py:92
  51.3 2.6 %fusion.3 = f32[14,262,224]{2,1,0:T(8,128)S(1)} fusion(f32[15,263,224]{2,1,0:T(8,128)S(1)} %get-tuple-element.7, f32[15,263,224]{2,1,0:T(8,128)S(1)} %get-tuple-element.6, f32[16,264,224]{2,1,0:T(8,128)S(1)} %pad_maximum_fusion, pred[14,262]{1,0:T(8,128)(4,1)S(1)} %broadcast_and_fusion), kind=kLoop, calls=%fused_computation.8 | loop fusion | flops 7394688 | bytes 19722836 | tf_op jit(solution)/shard_map/jit(_where)/select_n | solution.py:97
  56.3 2.4 %fusion.6 = f32[12,260,224]{2,1,0:T(8,128)S(1)} fusion(f32[16,264,224]{2,1,0:T(8,128)S(1)} %pad_maximum_fusion, f32[13,261,224]{2,1,0:T(8,128)S(1)} %get-tuple-element.11, f32[13,261,224]{2,1,0:T(8,128)S(1)} %get-tuple-element.10, f32[14,262,224]{2,1,0:T(8,128)S(1)} %fusion.3, pred[12,260]{1,0:T(8,128)(4,1)S(1)} %broadcast_and_fusion.1), kind=kLoop, calls=%fused_computation.17 | loop fusion | flops 6289920 | bytes 19571760 | tf_op jit(solution)/shard_map/jit(_where)/select_n | solution.py:97
  60.6 2.4 %fusion.11 = f32[10,258,224]{2,1,0:T(8,128)S(1)} fusion(f32[16,264,224]{2,1,0:T(8,128)S(1)} %pad_maximum_fusion, f32[11,259,224]{2,1,0:T(8,128)S(1)} %get-tuple-element.13, f32[11,259,224]{2,1,0:T(8,128)S(1)} %get-tuple-element.12, f32[12,260,224]{2,1,0:T(8,128)S(1)} %fusion.6, pred[10,258]{1,0:T(8,128)(4,1)S(1)} %broadcast_and_fusion.2), kind=kLoop, calls=%fused_computation.29 | loop fusion | flops 5201280 | bytes 16184340 | tf_op jit(solution)/shard_map/jit(_where)/select_n | solution.py:97
  64.5 1.4 %fusion.17 = f32[8,256,224]{2,1,0:T(8,128)S(1)} fusion(f32[9,257,224]{2,1,0:T(8,128)S(1)} %get-tuple-element.15, f32[9,257,224]{2,1,0:T(8,128)S(1)} %get-tuple-element.14, f32[10,258,224]{2,1,0:T(8,128)S(1)} %fusion.11, pred[8,256]{1,0:T(8,128)(4,1)S(1)} %broadcast_and_fusion.3, f32[224,8,256]{0,2,1:T(8,128)S(1)} %copy.7), kind=kLoop, calls=%fused_computation.42 | loop fusion | flops 4128768 | bytes 12847104 | tf_op jit(solution)/shard_map/jit(_where)/select_n | solution.py:97
  65.9 3.6 %convolution_bitcast_fusion = f32[224,224]{1,0:T(8,128)S(1)} fusion(f32[8,256,224]{2,1,0:T(8,128)S(1)} %fusion.17), kind=kOutput, calls=%fused_computation.53 | convolution fusion | flops 1233125376 | bytes 2035712 | tf_op jit(solution)/shard_map/dot_general | solution.py:178
  69.5 3.0 %collective-permute-start.4 = (f32[112,224]{1,0:T(8,128)S(1)}, f32[112,224]{1,0:T(8,128)S(1)}, u32[]{:S(2)}, u32[]{:S(2)}) collective-permute-start(f32[112,224]{1,0:T(8,128)S(1)} %slice_select_fusion), channel_id=1, source_target_pairs={{0,1},{1,0},{2,3},{3,2},{4,5},{5,4},{6,7},{7,6},{8,9},{9,8},{10,11... | collective-permute-start | bytes 301064 | tf_op jit(solution)/shard_map/ppermute | solution.py:44
  73.5 2.5 %collective-permute-start.5 = (f32[112,224]{1,0:T(8,128)S(1)}, f32[112,224]{1,0:T(8,128)S(1)}, u32[]{:S(2)}, u32[]{:S(2)}) collective-permute-start(f32[112,224]{1,0:T(8,128)S(1)} %select_add_fusion), channel_id=1, source_target_pairs={{0,2},{1,3},{2,0},{3,1},{4,6},{5,7},{6,4},{7,5},{8,10},{9,11},{10,... | collective-permute-start | bytes 301064 | tf_op jit(solution)/shard_map/ppermute | solution.py:27
  76.0 3.7 %collective-permute-done.5 = f32[112,224]{1,0:T(8,128)S(1)} collective-permute-done((f32[112,224]{1,0:T(8,128)S(1)}, f32[112,224]{1,0:T(8,128)S(1)}, u32[]{:S(2)}, u32[]{:S(2)}) %collective-permute-start.5) | collective-permute-done | bytes 100384 | tf_op jit(solution)/shard_map/ppermute | solution.py:27
  80.6 4.0 %collective-permute-done.6 = f32[112,224]{1,0:T(8,128)S(1)} collective-permute-done((f32[112,224]{1,0:T(8,128)S(1)}, f32[112,224]{1,0:T(8,128)S(1)}, u32[]{:S(2)}, u32[]{:S(2)}) %collective-permute-start.6) | collective-permute-done | bytes 100384 | tf_op jit(solution)/shard_map/ppermute | solution.py:27
  85.3 4.2 %collective-permute-done.7 = f32[112,224]{1,0:T(8,128)S(1)} collective-permute-done((f32[112,224]{1,0:T(8,128)S(1)}, f32[112,224]{1,0:T(8,128)S(1)}, u32[]{:S(2)}, u32[]{:S(2)}) %collective-permute-start.7) | collective-permute-done | bytes 100384 | tf_op jit(solution)/shard_map/ppermute | solution.py:27
  89.5 1.7 %collective-permute-start.8 = (f32[112,224]{1,0:T(8,128)S(1)}, f32[112,224]{1,0:T(8,128)S(1)}, u32[]{:S(2)}, u32[]{:S(2)}) collective-permute-start(f32[112,224]{1,0:T(8,128)S(1)} %add.141), channel_id=1, source_target_pairs={{0,16},{8,24},{16,0},{24,8},{1,17},{9,25},{17,1},{25,9},{2,18},{10... | collective-permute-start | bytes 301064 | tf_op jit(solution)/shard_map/ppermute | solution.py:27
  91.2 5.3 %collective-permute-done.8 = f32[112,224]{1,0:T(8,128)S(1)} collective-permute-done((f32[112,224]{1,0:T(8,128)S(1)}, f32[112,224]{1,0:T(8,128)S(1)}, u32[]{:S(2)}, u32[]{:S(2)}) %collective-permute-start.8) | collective-permute-done | bytes 100384 | tf_op jit(solution)/shard_map/ppermute | solution.py:27
  97.3 2.8 %copy.13 = f32[224,8,256]{2,1,0:T(8,128)} copy(f32[224,8,256]{0,2,1:T(8,128)} %bitcast.17) | data formatting | bytes 3670016
  100.9 7.1 %shard_map.41.basis_ref = f32[224,16]{1,0:T(8,128)} custom-call(f32[224,224]{1,0:T(8,128)} %maximum_select_fusion.gram_ref, f32[224,16]{1,0:T(8,128)} %copy.12.basis_ref), custom_call_target="tpu_custom_call" | custom-call | flops 22937600 | bytes 229376 | tf_op jit(solution)/shard_map/pallas_call | solution.py:142
  107.9 7.0 %shard_map.42 = f32[224,16]{1,0:T(8,128)} custom-call(f32[224,224]{1,0:T(8,128)} %maximum_select_fusion.gram_ref, f32[224,16]{1,0:T(8,128)} %shard_map.41.basis_ref), custom_call_target="tpu_custom_call" | custom-call | flops 22937600 | bytes 229376 | tf_op jit(solution)/shard_map/pallas_call | solution.py:142
  115.0 2.8 %fusion.22 = f32[2048,16]{1,0:T(8,128)S(1)} fusion(f32[2048,224]{1,0:T(8,128)S(1)} %bitcast.18, f32[224,16]{1,0:T(8,128)} %shard_map.42), kind=kOutput, calls=%fused_computation.74 | convolution fusion | flops 88080384 | bytes 1980416 | tf_op jit(solution)/shard_map/dot_general | solution.py:189
  117.8 1.6 %fusion.23 = f32[224,2048]{1,0:T(8,128)S(1)} fusion(f32[224,16]{1,0:T(8,128)S(1)} %copy-done.2, f32[2048,16]{1,0:T(8,128)S(1)} %fusion.22), kind=kOutput, calls=%fused_computation.75 | convolution fusion | flops 88080384 | bytes 1980416 | tf_op jit(solution)/shard_map/dot_general | solution.py:190
  119.4 2.0 %copy.14 = f32[28,8,8,256]{3,2,1,0:T(8,128)} copy(f32[28,8,8,256]{3,1,2,0:T(8,128)S(1)} %bitcast.19) | data formatting | bytes 3670016
  (49 shorter events, 14.0 us)
Async XLA Ops:
  6.2 24.8 %collective-permute-start = (f32[4,256,224]{1,2,0:T(8,128)}, f32[4,256,224]{1,2,0:T(8,128)}, u32[]{:S(2)}, u32[]{:S(2)}) collective-permute-start(f32[4,256,224]{1,2,0:T(8,128)} %copy.8), channel_id=1, source_target_pairs={{0,8},{8,16},{16,24},{1,9},{9,17},{17,25},{2,10},{10,18},{18,26},{... | collective-permute-start | bytes 2752520 | tf_op jit(solution)/shard_map/ppermute | solution.py:71
  13.3 24.0 %collective-permute-start.1 = (f32[4,256,224]{1,2,0:T(8,128)}, f32[4,256,224]{1,2,0:T(8,128)}, u32[]{:S(2)}, u32[]{:S(2)}) collective-permute-start(f32[4,256,224]{1,2,0:T(8,128)} %copy.9), channel_id=1, source_target_pairs={{8,0},{16,8},{24,16},{9,1},{17,9},{25,17},{10,2},{18,10},{26,18},{... | collective-permute-start | bytes 2752520 | tf_op jit(solution)/shard_map/ppermute | solution.py:72
  40.6 2.7 %collective-permute-start.2 = (f32[16,4,224]{2,1,0:T(4,128)S(1)}, f32[16,4,224]{2,1,0:T(4,128)S(1)}, u32[]{:S(2)}, u32[]{:S(2)}) collective-permute-start(f32[16,4,224]{2,1,0:T(4,128)S(1)} %get-tuple-element.8), channel_id=1, source_target_pairs={{0,1},{1,2},{2,3},{3,4},{4,5},{5,6},{6,7},{8,9},{9,10},{10,11},{11... | collective-permute-start | bytes 172040 | tf_op jit(solution)/shard_map/ppermute | solution.py:71
  41.9 4.9 %collective-permute-start.3 = (f32[16,4,224]{2,1,0:T(4,128)S(1)}, f32[16,4,224]{2,1,0:T(4,128)S(1)}, u32[]{:S(2)}, u32[]{:S(2)}) collective-permute-start(f32[16,4,224]{2,1,0:T(4,128)S(1)} %get-tuple-element.9), channel_id=1, source_target_pairs={{1,0},{2,1},{3,2},{4,3},{5,4},{6,5},{7,6},{9,8},{10,9},{11,10},{12... | collective-permute-start | bytes 172040 | tf_op jit(solution)/shard_map/ppermute | solution.py:72
  65.9 30.6 %copy-start = (f32[8,256,224]{2,1,0:T(8,128)}, f32[8,256,224]{2,1,0:T(8,128)S(1)}, u32[]{:S(2)}) copy-start(f32[8,256,224]{2,1,0:T(8,128)S(1)} %fusion.17) | copy-start | bytes 5505028
  65.9 30.7 %copy-start.3 = (f32[224,16]{0,1:T(8,128)S(1)}, f32[224,16]{0,1:T(8,128)}, u32[]{:S(2)}) copy-start(f32[224,16]{0,1:T(8,128)} %param.3) | copy-start | bytes 43012
  69.5 4.0 %collective-permute-start.4 = (f32[112,224]{1,0:T(8,128)S(1)}, f32[112,224]{1,0:T(8,128)S(1)}, u32[]{:S(2)}, u32[]{:S(2)}) collective-permute-start(f32[112,224]{1,0:T(8,128)S(1)} %slice_select_fusion), channel_id=1, source_target_pairs={{0,1},{1,0},{2,3},{3,2},{4,5},{5,4},{6,7},{7,6},{8,9},{9,8},{10,11... | collective-permute-start | bytes 301064 | tf_op jit(solution)/shard_map/ppermute | solution.py:44
  73.5 6.1 %collective-permute-start.5 = (f32[112,224]{1,0:T(8,128)S(1)}, f32[112,224]{1,0:T(8,128)S(1)}, u32[]{:S(2)}, u32[]{:S(2)}) collective-permute-start(f32[112,224]{1,0:T(8,128)S(1)} %select_add_fusion), channel_id=1, source_target_pairs={{0,2},{1,3},{2,0},{3,1},{4,6},{5,7},{6,4},{7,5},{8,10},{9,11},{10,... | collective-permute-start | bytes 301064 | tf_op jit(solution)/shard_map/ppermute | solution.py:27
  79.7 4.9 %collective-permute-start.6 = (f32[112,224]{1,0:T(8,128)S(1)}, f32[112,224]{1,0:T(8,128)S(1)}, u32[]{:S(2)}, u32[]{:S(2)}) collective-permute-start(f32[112,224]{1,0:T(8,128)S(1)} %add.139), channel_id=1, source_target_pairs={{0,4},{1,5},{2,6},{3,7},{4,0},{5,1},{6,2},{7,3},{8,12},{9,13},{10,... | collective-permute-start | bytes 301064 | tf_op jit(solution)/shard_map/ppermute | solution.py:27
  84.6 4.9 %collective-permute-start.7 = (f32[112,224]{1,0:T(8,128)S(1)}, f32[112,224]{1,0:T(8,128)S(1)}, u32[]{:S(2)}, u32[]{:S(2)}) collective-permute-start(f32[112,224]{1,0:T(8,128)S(1)} %add.140), channel_id=1, source_target_pairs={{0,8},{8,0},{16,24},{24,16},{1,9},{9,1},{17,25},{25,17},{2,10},{10... | collective-permute-start | bytes 301064 | tf_op jit(solution)/shard_map/ppermute | solution.py:27
  89.5 7.0 %collective-permute-start.8 = (f32[112,224]{1,0:T(8,128)S(1)}, f32[112,224]{1,0:T(8,128)S(1)}, u32[]{:S(2)}, u32[]{:S(2)}) collective-permute-start(f32[112,224]{1,0:T(8,128)S(1)} %add.141), channel_id=1, source_target_pairs={{0,16},{8,24},{16,0},{24,8},{1,17},{9,25},{17,1},{25,9},{2,18},{10... | collective-permute-start | bytes 301064 | tf_op jit(solution)/shard_map/ppermute | solution.py:27
  96.5 3.7 %collective-permute-start.9 = (f32[112,224]{1,0:T(8,128)S(1)}, f32[112,224]{1,0:T(8,128)S(1)}, u32[]{:S(2)}, u32[]{:S(2)}) collective-permute-start(f32[112,224]{1,0:T(8,128)S(1)} %add.142), channel_id=1, source_target_pairs={{0,1},{1,0},{2,3},{3,2},{4,5},{5,4},{6,7},{7,6},{8,9},{9,8},{10,11... | collective-permute-start | bytes 301064 | tf_op jit(solution)/shard_map/ppermute | solution.py:46
  96.6 18.4 %copy-start.1 = (f32[8,256,224]{2,1,0:T(8,128)S(1)}, f32[8,256,224]{2,1,0:T(8,128)}, u32[]{:S(2)}) copy-start(f32[8,256,224]{2,1,0:T(8,128)} %copy-done) | copy-start | bytes 5505028
  115.0 2.8 %copy-start.2 = (f32[224,16]{1,0:T(8,128)S(1)}, f32[224,16]{1,0:T(8,128)}, u32[]{:S(2)}) copy-start(f32[224,16]{1,0:T(8,128)} %shard_map.42) | copy-start | bytes 43012

commit v9 on v8

--- a/solution.py
+++ b/solution.py
@@ -63,13 +63,21 @@
     return names
 
 
+def flat_permute(block, axis, pairs):
+    pixels = block.size // block.shape[-1]
+    if pixels % 64 or pixels <= block.shape[-1]:
+        return lax.ppermute(block, axis, pairs)
+    flat = block.reshape(pixels // 64, 64, block.shape[-1])
+    return lax.ppermute(flat, axis, pairs).reshape(block.shape)
+
+
 def with_halo(cells, axis, dim, width):
     count = lax.axis_size(axis)
     size = cells.shape[dim]
     head = lax.slice_in_dim(cells, 0, width, axis=dim)
     tail = lax.slice_in_dim(cells, size - width, size, axis=dim)
-    before = lax.ppermute(tail, axis, [(i, i + 1) for i in range(count - 1)])
-    after = lax.ppermute(head, axis, [(i + 1, i) for i in range(count - 1)])
+    before = flat_permute(tail, axis, [(i, i + 1) for i in range(count - 1)])
+    after = flat_permute(head, axis, [(i + 1, i) for i in range(count - 1)])
     return jnp.concatenate([before, cells, after], axis=dim)
 
 

time: 122 us -> 118 us (0.967)
  local copies, waits for them, and re-layouts: 16.9 us -> 9.53 us
  waiting for transfers between devices: 41.9 us -> 44.4 us
    ppermute x4, waiting for transfers between devices: 23.8 us -> 28.2 us  [the longest x2 24.7 us: flat_permute(): return lax.ppermute(flat, axis, pairs).reshape(block.shape)]
    ppermute x2 -> x0, local copies, waits for them, and re-layouts: 3.99 us -> none  [the longest x1 2.48 us: with_halo(): after = lax.ppermute(head, axis, [(i + 1, i) for i in range(count - 1)])]
    slice x2 -> x1, local copies, waits for them, and re-layouts: 3.64 us -> 1.46 us  [with_halo(): tail = lax.slice_in_dim(cells, size - width, size, axis=dim)]
    ppermute x4, starting transfers between devices: 5.8 us -> 7.57 us  [butterfly_sum(): partner = lax.ppermute(value, axis, [(i, i ^ step) for i in range(count)])]
    ppermute x4, waiting for transfers between devices: 17.1 us -> 15.3 us  [butterfly_sum(): partner = lax.ppermute(value, axis, [(i, i ^ step) for i in range(count)])]
    slice x1 -> x0, local copies, waits for them, and re-layouts: 1.25 us -> none  [with_halo(): head = lax.slice_in_dim(cells, 0, width, axis=dim)]
  transfers between devices with their start and end apart: 10 -> 10, of which waited for: 8 -> 8; matrix products, arithmetic and copies ran while one was open for 6% -> 4% of each run, Pallas kernels for 0% -> 0%
where the time goes in v9:
time: 118 us; the launch traced here: 117 us
  waiting for transfers between devices  44.4 us (38%)
  other arithmetic  20.9 us (18%)
  starting transfers between devices  19.5 us (17%)
  Pallas kernels  14.1 us (12%)
  local copies, waits for them, and re-layouts  9.53 us (8%)
  matrix products  8.02 us (7%)
    ppermute x2, waiting for transfers between devices, flat_permute(): return lax.ppermute(flat, axis, pairs).reshape(block.shape)  24.7 us
    ppermute x4, waiting for transfers between devices, butterfly_sum(): partner = lax.ppermute(value, axis, [(i, i ^ step) for i in range(count)])  15.3 us
    pallas_call x2, Pallas kernels, subspace_step(): pl.pallas_call(subspace_kernel, out_shape=jax.ShapeDtypeStruct(basis.shap...  14.1 us
    select_n x4, other arithmetic, sweep(): return jnp.where(keep, new, 0.0)  8.82 us
    ppermute x4, starting transfers between devices, butterfly_sum(): partner = lax.ppermute(value, axis, [(i, i ^ step) for i in range(count)])  7.57 us
    unnamed x12, local copies, waits for them, and re-layouts  7.46 us
    ppermute x2, starting transfers between devices, flat_permute(): return lax.ppermute(flat, axis, pairs).reshape(block.shape)  6.27 us
    mul x4, other arithmetic, sweep(): flux_col = weight * diff_col  4.35 us
  transfers between devices with their start and end apart: 10, of which 8 were waited for; matrix products, arithmetic and copies ran while one was open for 4% of the time, Pallas kernels for 0%

profile of v9, /device:TPU:0, one launch (start us, length us, event | category | flops | bytes accessed | tf_op | source)
XLA Modules:
  0.0 117.4 jit_solution(17679262728729463236)
XLA Ops:
  0.6 1.9 %copy.4 = f32[224,8,256]{0,2,1:T(8,128)S(1)} copy(f32[224,8,256]{2,1,0:T(8,128)} %param.2) | data formatting | bytes 3670016 | tf_op args[0]
  2.5 1.5 %fusion.21 = (f32[4,256,224]{2,1,0:T(8,128)}, f32[4,256,224]{2,1,0:T(8,128)}) fusion(f32[8,256,224]{2,1,0:T(8,128)S(1)} %bitcast.18), kind=kLoop, calls=%fused_computation.73 | loop fusion | bytes 3670016 | tf_op jit(solution)/shard_map/slice | solution.py:78
  4.0 5.0 %collective-permute-start = (f32[16,64,224]{2,1,0:T(8,128)}, f32[16,64,224]{2,1,0:T(8,128)S(1)}, u32[]{:S(2)}, u32[]{:S(2)}) collective-permute-start(f32[16,64,224]{2,1,0:T(8,128)} %bitcast.1), channel_id=1, source_target_pairs={{0,8},{8,16},{16,24},{1,9},{9,17},{17,25},{2,10},{10,18},{18,26},{... | collective-permute-start | bytes 2752520 | tf_op jit(solution)/shard_map/ppermute | solution.py:71
  9.0 1.3 %collective-permute-start.1 = (f32[16,64,224]{2,1,0:T(8,128)}, f32[16,64,224]{2,1,0:T(8,128)}, u32[]{:S(2)}, u32[]{:S(2)}) collective-permute-start(f32[16,64,224]{2,1,0:T(8,128)} %bitcast.3), channel_id=1, source_target_pairs={{8,0},{16,8},{24,16},{9,1},{17,9},{25,17},{10,2},{18,10},{26,18},{... | collective-permute-start | bytes 2752520 | tf_op jit(solution)/shard_map/ppermute | solution.py:71
  11.1 20.5 %collective-permute-done = f32[16,64,224]{2,1,0:T(8,128)S(1)} collective-permute-done((f32[16,64,224]{2,1,0:T(8,128)}, f32[16,64,224]{2,1,0:T(8,128)S(1)}, u32[]{:S(2)}, u32[]{:S(2)}) %collective-permute-start) | collective-permute-done | bytes 917536 | tf_op jit(solution)/shard_map/ppermute | solution.py:71
  31.6 4.2 %collective-permute-done.1 = f32[16,64,224]{2,1,0:T(8,128)} collective-permute-done((f32[16,64,224]{2,1,0:T(8,128)}, f32[16,64,224]{2,1,0:T(8,128)}, u32[]{:S(2)}, u32[]{:S(2)}) %collective-permute-start.1) | collective-permute-done | bytes 917536 | tf_op jit(solution)/shard_map/ppermute | solution.py:71
  36.6 1.3 %collective-permute-start.2 = (f32[16,4,224]{2,1,0:T(4,128)S(1)}, f32[16,4,224]{2,1,0:T(4,128)S(1)}, u32[]{:S(2)}, u32[]{:S(2)}) collective-permute-start(f32[16,4,224]{2,1,0:T(4,128)S(1)} %get-tuple-element.6), channel_id=1, source_target_pairs={{0,1},{1,2},{2,3},{3,4},{4,5},{5,6},{6,7},{8,9},{9,10},{10,11},{11... | collective-permute-start | bytes 172040 | tf_op jit(solution)/shard_map/ppermute | solution.py:69
  37.9 1.3 %collective-permute-start.3 = (f32[16,4,224]{2,1,0:T(4,128)S(1)}, f32[16,4,224]{2,1,0:T(4,128)S(1)}, u32[]{:S(2)}, u32[]{:S(2)}) collective-permute-start(f32[16,4,224]{2,1,0:T(4,128)S(1)} %get-tuple-element.7), channel_id=1, source_target_pairs={{1,0},{2,1},{3,2},{4,3},{5,4},{6,5},{7,6},{9,8},{10,9},{11,10},{12... | collective-permute-start | bytes 172040 | tf_op jit(solution)/shard_map/ppermute | solution.py:69
  39.3 3.5 %collective-permute-done.3 = f32[16,4,224]{2,1,0:T(4,128)S(1)} collective-permute-done((f32[16,4,224]{2,1,0:T(4,128)S(1)}, f32[16,4,224]{2,1,0:T(4,128)S(1)}, u32[]{:S(2)}, u32[]{:S(2)}) %collective-permute-start.3) | collective-permute-done | bytes 57376 | tf_op jit(solution)/shard_map/ppermute | solution.py:69
  42.8 1.7 %pad_maximum_fusion = f32[16,264,224]{2,1,0:T(8,128)S(1)} fusion(f32[16,4,224]{2,1,0:T(4,128)S(1)} %collective-permute-done.3, f32[4,256,224]{2,1,0:T(8,128)} %bitcast.4, f32[8,256,224]{2,1,0:T(8,128)S(1)} %bitcast.20, f32[4,256,224]{2,1,0:T(8,128)S(1)} %bitcast.25, f32[16,4,224]{2,1,0:T(4,128)S(1)} %collective-permute-done.2), kind=kLoop, calls=%fused_computation | loop fusion | flops 3784704 | bytes 7569408 | tf_op jit(solution)/shard_map/concatenate | solution.py:81
  44.5 1.3 %add_reduce_fusion = f32[15,263]{1,0:T(8,128)S(1)} fusion(f32[16,264,224]{2,1,0:T(8,128)S(1)} %pad_maximum_fusion), kind=kLoop, calls=%fused_computation.3 | loop fusion | flops 5298135 | bytes 10619940 | tf_op jit(solution)/shard_map/reduce_sum | solution.py:98
  45.8 1.6 %broadcast_multiply_fusion.1 = (f32[15,263,224]{2,1,0:T(8,128)S(1)}, f32[15,263,224]{2,1,0:T(8,128)S(1)}) fusion(f32[15,263]{1,0:T(8,128)S(1)} %add_rsqrt_fusion.3, f32[16,264,224]{2,1,0:T(8,128)S(1)} %pad_maximum_fusion), kind=kLoop, calls=%fused_computation.46 | loop fusion | flops 3534720 | bytes 17689380 | tf_op jit(solution)/shard_map/mul | solution.py:100
  47.3 2.6 %fusion.3 = f32[14,262,224]{2,1,0:T(8,128)S(1)} fusion(f32[15,263,224]{2,1,0:T(8,128)S(1)} %get-tuple-element.5, f32[15,263,224]{2,1,0:T(8,128)S(1)} %get-tuple-element.4, f32[16,264,224]{2,1,0:T(8,128)S(1)} %pad_maximum_fusion, pred[14,262]{1,0:T(8,128)(4,1)S(1)} %broadcast_and_fusion), kind=kLoop, calls=%fused_computation.8 | loop fusion | flops 7394688 | bytes 19722836 | tf_op jit(solution)/shard_map/jit(_where)/select_n | solution.py:105
  51.1 1.2 %broadcast_multiply_fusion.3 = (f32[13,261,224]{2,1,0:T(8,128)S(1)}, f32[13,261,224]{2,1,0:T(8,128)S(1)}) fusion(f32[13,261]{1,0:T(8,128)S(1)} %add_rsqrt_fusion.2, f32[14,262,224]{2,1,0:T(8,128)S(1)} %fusion.3), kind=kLoop, calls=%fused_computation.48 | loop fusion | flops 3040128 | bytes 15214212 | tf_op jit(solution)/shard_map/mul | solution.py:100
  52.3 2.4 %fusion.6 = f32[12,260,224]{2,1,0:T(8,128)S(1)} fusion(f32[16,264,224]{2,1,0:T(8,128)S(1)} %pad_maximum_fusion, f32[13,261,224]{2,1,0:T(8,128)S(1)} %get-tuple-element.9, f32[13,261,224]{2,1,0:T(8,128)S(1)} %get-tuple-element.8, f32[14,262,224]{2,1,0:T(8,128)S(1)} %fusion.3, pred[12,260]{1,0:T(8,128)(4,1)S(1)} %broadcast_and_fusion.1), kind=kLoop, calls=%fused_computation.17 | loop fusion | flops 6289920 | bytes 19571760 | tf_op jit(solution)/shard_map/jit(_where)/select_n | solution.py:105
  56.6 2.4 %fusion.11 = f32[10,258,224]{2,1,0:T(8,128)S(1)} fusion(f32[16,264,224]{2,1,0:T(8,128)S(1)} %pad_maximum_fusion, f32[11,259,224]{2,1,0:T(8,128)S(1)} %get-tuple-element.11, f32[11,259,224]{2,1,0:T(8,128)S(1)} %get-tuple-element.10, f32[12,260,224]{2,1,0:T(8,128)S(1)} %fusion.6, pred[10,258]{1,0:T(8,128)(4,1)S(1)} %broadcast_and_fusion.2), kind=kLoop, calls=%fused_computation.29 | loop fusion | flops 5201280 | bytes 16184340 | tf_op jit(solution)/shard_map/jit(_where)/select_n | solution.py:105
  60.5 1.4 %fusion.17 = f32[8,256,224]{2,1,0:T(8,128)S(1)} fusion(f32[9,257,224]{2,1,0:T(8,128)S(1)} %get-tuple-element.13, f32[9,257,224]{2,1,0:T(8,128)S(1)} %get-tuple-element.12, f32[10,258,224]{2,1,0:T(8,128)S(1)} %fusion.11, pred[8,256]{1,0:T(8,128)(4,1)S(1)} %broadcast_and_fusion.3, f32[224,8,256]{0,2,1:T(8,128)S(1)} %copy.4), kind=kLoop, calls=%fused_computation.42 | loop fusion | flops 4128768 | bytes 12847104 | tf_op jit(solution)/shard_map/jit(_where)/select_n | solution.py:105
  61.9 3.6 %convolution_bitcast_fusion = f32[224,224]{1,0:T(8,128)S(1)} fusion(f32[8,256,224]{2,1,0:T(8,128)S(1)} %fusion.17), kind=kOutput, calls=%fused_computation.53 | convolution fusion | flops 1233125376 | bytes 2035712 | tf_op jit(solution)/shard_map/dot_general | solution.py:186
  65.6 3.0 %collective-permute-start.4 = (f32[112,224]{1,0:T(8,128)S(1)}, f32[112,224]{1,0:T(8,128)S(1)}, u32[]{:S(2)}, u32[]{:S(2)}) collective-permute-start(f32[112,224]{1,0:T(8,128)S(1)} %slice_select_fusion), channel_id=1, source_target_pairs={{0,1},{1,0},{2,3},{3,2},{4,5},{5,4},{6,7},{7,6},{8,9},{9,8},{10,11... | collective-permute-start | bytes 301064 | tf_op jit(solution)/shard_map/ppermute | solution.py:44
  69.5 2.5 %collective-permute-start.5 = (f32[112,224]{1,0:T(8,128)S(1)}, f32[112,224]{1,0:T(8,128)S(1)}, u32[]{:S(2)}, u32[]{:S(2)}) collective-permute-start(f32[112,224]{1,0:T(8,128)S(1)} %select_add_fusion), channel_id=1, source_target_pairs={{0,2},{1,3},{2,0},{3,1},{4,6},{5,7},{6,4},{7,5},{8,10},{9,11},{10,... | collective-permute-start | bytes 301064 | tf_op jit(solution)/shard_map/ppermute | solution.py:27
  72.0 3.7 %collective-permute-done.5 = f32[112,224]{1,0:T(8,128)S(1)} collective-permute-done((f32[112,224]{1,0:T(8,128)S(1)}, f32[112,224]{1,0:T(8,128)S(1)}, u32[]{:S(2)}, u32[]{:S(2)}) %collective-permute-start.5) | collective-permute-done | bytes 100384 | tf_op jit(solution)/shard_map/ppermute | solution.py:27
  76.6 4.0 %collective-permute-done.6 = f32[112,224]{1,0:T(8,128)S(1)} collective-permute-done((f32[112,224]{1,0:T(8,128)S(1)}, f32[112,224]{1,0:T(8,128)S(1)}, u32[]{:S(2)}, u32[]{:S(2)}) %collective-permute-start.6) | collective-permute-done | bytes 100384 | tf_op jit(solution)/shard_map/ppermute | solution.py:27
  80.6 1.6 %collective-permute-start.7 = (f32[112,224]{1,0:T(8,128)S(1)}, f32[112,224]{1,0:T(8,128)S(1)}, u32[]{:S(2)}, u32[]{:S(2)}) collective-permute-start(f32[112,224]{1,0:T(8,128)S(1)} %add.140), channel_id=1, source_target_pairs={{0,8},{8,0},{16,24},{24,16},{1,9},{9,1},{17,25},{25,17},{2,10},{10... | collective-permute-start | bytes 301064 | tf_op jit(solution)/shard_map/ppermute | solution.py:27
  82.2 3.3 %collective-permute-done.7 = f32[112,224]{1,0:T(8,128)S(1)} collective-permute-done((f32[112,224]{1,0:T(8,128)S(1)}, f32[112,224]{1,0:T(8,128)S(1)}, u32[]{:S(2)}, u32[]{:S(2)}) %collective-permute-start.7) | collective-permute-done | bytes 100384 | tf_op jit(solution)/shard_map/ppermute | solution.py:27
  85.5 2.6 %collective-permute-start.8 = (f32[112,224]{1,0:T(8,128)S(1)}, f32[112,224]{1,0:T(8,128)S(1)}, u32[]{:S(2)}, u32[]{:S(2)}) collective-permute-start(f32[112,224]{1,0:T(8,128)S(1)} %add.141), channel_id=1, source_target_pairs={{0,16},{8,24},{16,0},{24,8},{1,17},{9,25},{17,1},{25,9},{2,18},{10... | collective-permute-start | bytes 301064 | tf_op jit(solution)/shard_map/ppermute | solution.py:27
  88.1 4.4 %collective-permute-done.8 = f32[112,224]{1,0:T(8,128)S(1)} collective-permute-done((f32[112,224]{1,0:T(8,128)S(1)}, f32[112,224]{1,0:T(8,128)S(1)}, u32[]{:S(2)}, u32[]{:S(2)}) %collective-permute-start.8) | collective-permute-done | bytes 100384 | tf_op jit(solution)/shard_map/ppermute | solution.py:27
  93.3 2.8 %copy.6 = f32[224,8,256]{2,1,0:T(8,128)} copy(f32[224,8,256]{0,2,1:T(8,128)} %bitcast.21) | data formatting | bytes 3670016
  96.9 7.1 %shard_map.41.basis_ref = f32[224,16]{1,0:T(8,128)} custom-call(f32[224,224]{1,0:T(8,128)} %maximum_select_fusion.gram_ref, f32[224,16]{1,0:T(8,128)} %copy.5.basis_ref), custom_call_target="tpu_custom_call" | custom-call | flops 22937600 | bytes 229376 | tf_op jit(solution)/shard_map/pallas_call | solution.py:150
  103.9 7.0 %shard_map.42 = f32[224,16]{1,0:T(8,128)} custom-call(f32[224,224]{1,0:T(8,128)} %maximum_select_fusion.gram_ref, f32[224,16]{1,0:T(8,128)} %shard_map.41.basis_ref), custom_call_target="tpu_custom_call" | custom-call | flops 22937600 | bytes 229376 | tf_op jit(solution)/shard_map/pallas_call | solution.py:150
  111.0 2.8 %fusion.22 = f32[2048,16]{1,0:T(8,128)S(1)} fusion(f32[2048,224]{1,0:T(8,128)S(1)} %bitcast.22, f32[224,16]{1,0:T(8,128)} %shard_map.42), kind=kOutput, calls=%fused_computation.74 | convolution fusion | flops 88080384 | bytes 1980416 | tf_op jit(solution)/shard_map/dot_general | solution.py:197
  113.8 1.6 %fusion.23 = f32[224,2048]{1,0:T(8,128)S(1)} fusion(f32[224,16]{1,0:T(8,128)S(1)} %copy-done.2, f32[2048,16]{1,0:T(8,128)S(1)} %fusion.22), kind=kOutput, calls=%fused_computation.75 | convolution fusion | flops 88080384 | bytes 1980416 | tf_op jit(solution)/shard_map/dot_general | solution.py:198
  115.4 2.0 %copy.7 = f32[28,8,8,256]{3,2,1,0:T(8,128)} copy(f32[28,8,8,256]{3,1,2,0:T(8,128)S(1)} %bitcast.23) | data formatting | bytes 3670016
  (45 shorter events, 9.7 us)
Async XLA Ops:
  4.0 27.6 %collective-permute-start = (f32[16,64,224]{2,1,0:T(8,128)}, f32[16,64,224]{2,1,0:T(8,128)S(1)}, u32[]{:S(2)}, u32[]{:S(2)}) collective-permute-start(f32[16,64,224]{2,1,0:T(8,128)} %bitcast.1), channel_id=1, source_target_pairs={{0,8},{8,16},{16,24},{1,9},{9,17},{17,25},{2,10},{10,18},{18,26},{... | collective-permute-start | bytes 2752520 | tf_op jit(solution)/shard_map/ppermute | solution.py:71
  9.0 26.8 %collective-permute-start.1 = (f32[16,64,224]{2,1,0:T(8,128)}, f32[16,64,224]{2,1,0:T(8,128)}, u32[]{:S(2)}, u32[]{:S(2)}) collective-permute-start(f32[16,64,224]{2,1,0:T(8,128)} %bitcast.3), channel_id=1, source_target_pairs={{8,0},{16,8},{24,16},{9,1},{17,9},{25,17},{10,2},{18,10},{26,18},{... | collective-permute-start | bytes 2752520 | tf_op jit(solution)/shard_map/ppermute | solution.py:71
  36.6 2.7 %collective-permute-start.2 = (f32[16,4,224]{2,1,0:T(4,128)S(1)}, f32[16,4,224]{2,1,0:T(4,128)S(1)}, u32[]{:S(2)}, u32[]{:S(2)}) collective-permute-start(f32[16,4,224]{2,1,0:T(4,128)S(1)} %get-tuple-element.6), channel_id=1, source_target_pairs={{0,1},{1,2},{2,3},{3,4},{4,5},{5,6},{6,7},{8,9},{9,10},{10,11},{11... | collective-permute-start | bytes 172040 | tf_op jit(solution)/shard_map/ppermute | solution.py:69
  37.9 4.9 %collective-permute-start.3 = (f32[16,4,224]{2,1,0:T(4,128)S(1)}, f32[16,4,224]{2,1,0:T(4,128)S(1)}, u32[]{:S(2)}, u32[]{:S(2)}) collective-permute-start(f32[16,4,224]{2,1,0:T(4,128)S(1)} %get-tuple-element.7), channel_id=1, source_target_pairs={{1,0},{2,1},{3,2},{4,3},{5,4},{6,5},{7,6},{9,8},{10,9},{11,10},{12... | collective-permute-start | bytes 172040 | tf_op jit(solution)/shard_map/ppermute | solution.py:69
  61.9 30.6 %copy-start = (f32[8,256,224]{2,1,0:T(8,128)}, f32[8,256,224]{2,1,0:T(8,128)S(1)}, u32[]{:S(2)}) copy-start(f32[8,256,224]{2,1,0:T(8,128)S(1)} %fusion.17) | copy-start | bytes 5505028
  61.9 30.7 %copy-start.3 = (f32[224,16]{0,1:T(8,128)S(1)}, f32[224,16]{0,1:T(8,128)}, u32[]{:S(2)}) copy-start(f32[224,16]{0,1:T(8,128)} %param.3) | copy-start | bytes 43012
  65.6 4.0 %collective-permute-start.4 = (f32[112,224]{1,0:T(8,128)S(1)}, f32[112,224]{1,0:T(8,128)S(1)}, u32[]{:S(2)}, u32[]{:S(2)}) collective-permute-start(f32[112,224]{1,0:T(8,128)S(1)} %slice_select_fusion), channel_id=1, source_target_pairs={{0,1},{1,0},{2,3},{3,2},{4,5},{5,4},{6,7},{7,6},{8,9},{9,8},{10,11... | collective-permute-start | bytes 301064 | tf_op jit(solution)/shard_map/ppermute | solution.py:44
  69.5 6.1 %collective-permute-start.5 = (f32[112,224]{1,0:T(8,128)S(1)}, f32[112,224]{1,0:T(8,128)S(1)}, u32[]{:S(2)}, u32[]{:S(2)}) collective-permute-start(f32[112,224]{1,0:T(8,128)S(1)} %select_add_fusion), channel_id=1, source_target_pairs={{0,2},{1,3},{2,0},{3,1},{4,6},{5,7},{6,4},{7,5},{8,10},{9,11},{10,... | collective-permute-start | bytes 301064 | tf_op jit(solution)/shard_map/ppermute | solution.py:27
  75.7 4.9 %collective-permute-start.6 = (f32[112,224]{1,0:T(8,128)S(1)}, f32[112,224]{1,0:T(8,128)S(1)}, u32[]{:S(2)}, u32[]{:S(2)}) collective-permute-start(f32[112,224]{1,0:T(8,128)S(1)} %add.139), channel_id=1, source_target_pairs={{0,4},{1,5},{2,6},{3,7},{4,0},{5,1},{6,2},{7,3},{8,12},{9,13},{10,... | collective-permute-start | bytes 301064 | tf_op jit(solution)/shard_map/ppermute | solution.py:27
  80.6 4.9 %collective-permute-start.7 = (f32[112,224]{1,0:T(8,128)S(1)}, f32[112,224]{1,0:T(8,128)S(1)}, u32[]{:S(2)}, u32[]{:S(2)}) collective-permute-start(f32[112,224]{1,0:T(8,128)S(1)} %add.140), channel_id=1, source_target_pairs={{0,8},{8,0},{16,24},{24,16},{1,9},{9,1},{17,25},{25,17},{2,10},{10... | collective-permute-start | bytes 301064 | tf_op jit(solution)/shard_map/ppermute | solution.py:27
  85.5 7.0 %collective-permute-start.8 = (f32[112,224]{1,0:T(8,128)S(1)}, f32[112,224]{1,0:T(8,128)S(1)}, u32[]{:S(2)}, u32[]{:S(2)}) collective-permute-start(f32[112,224]{1,0:T(8,128)S(1)} %add.141), channel_id=1, source_target_pairs={{0,16},{8,24},{16,0},{24,8},{1,17},{9,25},{17,1},{25,9},{2,18},{10... | collective-permute-start | bytes 301064 | tf_op jit(solution)/shard_map/ppermute | solution.py:27
  92.5 3.7 %collective-permute-start.9 = (f32[112,224]{1,0:T(8,128)S(1)}, f32[112,224]{1,0:T(8,128)S(1)}, u32[]{:S(2)}, u32[]{:S(2)}) collective-permute-start(f32[112,224]{1,0:T(8,128)S(1)} %add.142), channel_id=1, source_target_pairs={{0,1},{1,0},{2,3},{3,2},{4,5},{5,4},{6,7},{7,6},{8,9},{9,8},{10,11... | collective-permute-start | bytes 301064 | tf_op jit(solution)/shard_map/ppermute | solution.py:46
  92.6 18.4 %copy-start.1 = (f32[8,256,224]{2,1,0:T(8,128)S(1)}, f32[8,256,224]{2,1,0:T(8,128)}, u32[]{:S(2)}) copy-start(f32[8,256,224]{2,1,0:T(8,128)} %copy-done) | copy-start | bytes 5505028
  111.0 2.8 %copy-start.2 = (f32[224,16]{1,0:T(8,128)S(1)}, f32[224,16]{1,0:T(8,128)}, u32[]{:S(2)}) copy-start(f32[224,16]{1,0:T(8,128)} %shard_map.42) | copy-start | bytes 43012

commit v10 on v9

--- a/solution.py
+++ b/solution.py
@@ -113,8 +113,8 @@
     )
     sub = lax.broadcasted_iota(jnp.int32, (size, size), 0)
     lane = lax.broadcasted_iota(jnp.int32, (size, size), 1)
-    lower = jnp.zeros((size, size), jnp.float32)
     upper = jnp.zeros((size, size), jnp.float32)
+    inverse = jnp.zeros((size, size), jnp.float32)
     rest = inner
     for j in range(size):
         col = jnp.sum(jnp.where(lane == j, rest, 0.0), axis=1, keepdims=True)
@@ -122,16 +122,13 @@
         pivot = jnp.sqrt(jnp.sum(jnp.where(lane[:1] == j, row, 0.0), axis=1, keepdims=True))
         col = jnp.where(sub[:, :1] >= j, col / pivot, 0.0)
         row = jnp.where(lane[:1] >= j, row / pivot, 0.0)
-        lower = lower + jnp.where(lane == j, col, 0.0)
         upper = upper + jnp.where(sub == j, row, 0.0)
         rest = rest - col * row
-    inverse = jnp.zeros((size, size), jnp.float32)
-    for i in range(size):
-        coef = jnp.sum(jnp.where(lane == i, upper, 0.0), axis=1, keepdims=True)
-        diag = jnp.sum(jnp.where(sub[:, :1] == i, coef, 0.0), axis=0, keepdims=True)
-        acc = jnp.sum(jnp.where(sub[:, :1] < i, coef, 0.0) * inverse, axis=0, keepdims=True)
-        unit = jnp.where(lane[:1] == i, 1.0, 0.0)
-        inverse = inverse + jnp.where(sub == i, (unit - acc) / diag, 0.0)
+        coef = jnp.sum(jnp.where(lane == j, upper, 0.0), axis=1, keepdims=True)
+        diag = jnp.sum(jnp.where(sub[:, :1] == j, coef, 0.0), axis=0, keepdims=True)
+        acc = jnp.sum(jnp.where(sub[:, :1] < j, coef, 0.0) * inverse, axis=0, keepdims=True)
+        unit = jnp.where(lane[:1] == j, 1.0, 0.0)
+        inverse = inverse + jnp.where(sub == j, (unit - acc) / diag, 0.0)
     return lax.dot_general(
         block, inverse, (((1,), (1,)), ((), ())),
         precision=lax.Precision.HIGHEST, preferred_element_type=jnp.float32,

time: 118 us -> 117 us (level)
  no operation moved by 1% of the time
where the time goes in v10:
time: 117 us
  waiting for transfers between devices  44.4 us (38%)
  other arithmetic  20.9 us (18%)
  starting transfers between devices  19.5 us (17%)
  Pallas kernels  13.7 us (12%)
  local copies, waits for them, and re-layouts  9.53 us (8%)
  matrix products  8.03 us (7%)
    ppermute x2, waiting for transfers between devices, flat_permute(): return lax.ppermute(flat, axis, pairs).reshape(block.shape)  24.7 us
    ppermute x4, waiting for transfers between devices, butterfly_sum(): partner = lax.ppermute(value, axis, [(i, i ^ step) for i in range(count)])  15.3 us
    pallas_call x2, Pallas kernels, subspace_step(): pl.pallas_call(subspace_kernel, out_shape=jax.ShapeDtypeStruct(basis.shap...  13.7 us
    select_n x4, other arithmetic, sweep(): return jnp.where(keep, new, 0.0)  8.82 us
    ppermute x4, starting transfers between devices, butterfly_sum(): partner = lax.ppermute(value, axis, [(i, i ^ step) for i in range(count)])  7.57 us
    unnamed x12, local copies, waits for them, and re-layouts  7.46 us
    ppermute x2, starting transfers between devices, flat_permute(): return lax.ppermute(flat, axis, pairs).reshape(block.shape)  6.27 us
    mul x4, other arithmetic, sweep(): flux_col = weight * diff_col  4.35 us
  transfers between devices with their start and end apart: 10, of which 8 were waited for; matrix products, arithmetic and copies ran while one was open for 4% of the time, Pallas kernels for 0%

profile of v10, /device:TPU:0, one launch (start us, length us, event | category | flops | bytes accessed | tf_op | source)
XLA Modules:
  0.0 117.0 jit_solution(8147855056444920475)
XLA Ops:
  0.6 1.9 %copy.4 = f32[224,8,256]{0,2,1:T(8,128)S(1)} copy(f32[224,8,256]{2,1,0:T(8,128)} %param.2) | data formatting | bytes 3670016 | tf_op args[0]
  2.5 1.5 %fusion.21 = (f32[4,256,224]{2,1,0:T(8,128)}, f32[4,256,224]{2,1,0:T(8,128)}) fusion(f32[8,256,224]{2,1,0:T(8,128)S(1)} %bitcast.18), kind=kLoop, calls=%fused_computation.73 | loop fusion | bytes 3670016 | tf_op jit(solution)/shard_map/slice | solution.py:78
  4.0 5.0 %collective-permute-start = (f32[16,64,224]{2,1,0:T(8,128)}, f32[16,64,224]{2,1,0:T(8,128)S(1)}, u32[]{:S(2)}, u32[]{:S(2)}) collective-permute-start(f32[16,64,224]{2,1,0:T(8,128)} %bitcast.1), channel_id=1, source_target_pairs={{0,8},{8,16},{16,24},{1,9},{9,17},{17,25},{2,10},{10,18},{18,26},{... | collective-permute-start | bytes 2752520 | tf_op jit(solution)/shard_map/ppermute | solution.py:71
  9.0 1.3 %collective-permute-start.1 = (f32[16,64,224]{2,1,0:T(8,128)}, f32[16,64,224]{2,1,0:T(8,128)}, u32[]{:S(2)}, u32[]{:S(2)}) collective-permute-start(f32[16,64,224]{2,1,0:T(8,128)} %bitcast.3), channel_id=1, source_target_pairs={{8,0},{16,8},{24,16},{9,1},{17,9},{25,17},{10,2},{18,10},{26,18},{... | collective-permute-start | bytes 2752520 | tf_op jit(solution)/shard_map/ppermute | solution.py:71
  11.1 20.5 %collective-permute-done = f32[16,64,224]{2,1,0:T(8,128)S(1)} collective-permute-done((f32[16,64,224]{2,1,0:T(8,128)}, f32[16,64,224]{2,1,0:T(8,128)S(1)}, u32[]{:S(2)}, u32[]{:S(2)}) %collective-permute-start) | collective-permute-done | bytes 917536 | tf_op jit(solution)/shard_map/ppermute | solution.py:71
  31.6 4.2 %collective-permute-done.1 = f32[16,64,224]{2,1,0:T(8,128)} collective-permute-done((f32[16,64,224]{2,1,0:T(8,128)}, f32[16,64,224]{2,1,0:T(8,128)}, u32[]{:S(2)}, u32[]{:S(2)}) %collective-permute-start.1) | collective-permute-done | bytes 917536 | tf_op jit(solution)/shard_map/ppermute | solution.py:71
  36.6 1.3 %collective-permute-start.2 = (f32[16,4,224]{2,1,0:T(4,128)S(1)}, f32[16,4,224]{2,1,0:T(4,128)S(1)}, u32[]{:S(2)}, u32[]{:S(2)}) collective-permute-start(f32[16,4,224]{2,1,0:T(4,128)S(1)} %get-tuple-element.6), channel_id=1, source_target_pairs={{0,1},{1,2},{2,3},{3,4},{4,5},{5,6},{6,7},{8,9},{9,10},{10,11},{11... | collective-permute-start | bytes 172040 | tf_op jit(solution)/shard_map/ppermute | solution.py:69
  37.9 1.3 %collective-permute-start.3 = (f32[16,4,224]{2,1,0:T(4,128)S(1)}, f32[16,4,224]{2,1,0:T(4,128)S(1)}, u32[]{:S(2)}, u32[]{:S(2)}) collective-permute-start(f32[16,4,224]{2,1,0:T(4,128)S(1)} %get-tuple-element.7), channel_id=1, source_target_pairs={{1,0},{2,1},{3,2},{4,3},{5,4},{6,5},{7,6},{9,8},{10,9},{11,10},{12... | collective-permute-start | bytes 172040 | tf_op jit(solution)/shard_map/ppermute | solution.py:69
  39.3 3.5 %collective-permute-done.3 = f32[16,4,224]{2,1,0:T(4,128)S(1)} collective-permute-done((f32[16,4,224]{2,1,0:T(4,128)S(1)}, f32[16,4,224]{2,1,0:T(4,128)S(1)}, u32[]{:S(2)}, u32[]{:S(2)}) %collective-permute-start.3) | collective-permute-done | bytes 57376 | tf_op jit(solution)/shard_map/ppermute | solution.py:69
  42.8 1.7 %pad_maximum_fusion = f32[16,264,224]{2,1,0:T(8,128)S(1)} fusion(f32[16,4,224]{2,1,0:T(4,128)S(1)} %collective-permute-done.3, f32[4,256,224]{2,1,0:T(8,128)} %bitcast.4, f32[8,256,224]{2,1,0:T(8,128)S(1)} %bitcast.20, f32[4,256,224]{2,1,0:T(8,128)S(1)} %bitcast.25, f32[16,4,224]{2,1,0:T(4,128)S(1)} %collective-permute-done.2), kind=kLoop, calls=%fused_computation | loop fusion | flops 3784704 | bytes 7569408 | tf_op jit(solution)/shard_map/concatenate | solution.py:81
  44.5 1.3 %add_reduce_fusion = f32[15,263]{1,0:T(8,128)S(1)} fusion(f32[16,264,224]{2,1,0:T(8,128)S(1)} %pad_maximum_fusion), kind=kLoop, calls=%fused_computation.3 | loop fusion | flops 5298135 | bytes 10619940 | tf_op jit(solution)/shard_map/reduce_sum | solution.py:98
  45.8 1.6 %broadcast_multiply_fusion.1 = (f32[15,263,224]{2,1,0:T(8,128)S(1)}, f32[15,263,224]{2,1,0:T(8,128)S(1)}) fusion(f32[15,263]{1,0:T(8,128)S(1)} %add_rsqrt_fusion.3, f32[16,264,224]{2,1,0:T(8,128)S(1)} %pad_maximum_fusion), kind=kLoop, calls=%fused_computation.46 | loop fusion | flops 3534720 | bytes 17689380 | tf_op jit(solution)/shard_map/mul | solution.py:100
  47.3 2.6 %fusion.3 = f32[14,262,224]{2,1,0:T(8,128)S(1)} fusion(f32[15,263,224]{2,1,0:T(8,128)S(1)} %get-tuple-element.5, f32[15,263,224]{2,1,0:T(8,128)S(1)} %get-tuple-element.4, f32[16,264,224]{2,1,0:T(8,128)S(1)} %pad_maximum_fusion, pred[14,262]{1,0:T(8,128)(4,1)S(1)} %broadcast_and_fusion), kind=kLoop, calls=%fused_computation.8 | loop fusion | flops 7394688 | bytes 19722836 | tf_op jit(solution)/shard_map/jit(_where)/select_n | solution.py:105
  51.1 1.2 %broadcast_multiply_fusion.3 = (f32[13,261,224]{2,1,0:T(8,128)S(1)}, f32[13,261,224]{2,1,0:T(8,128)S(1)}) fusion(f32[13,261]{1,0:T(8,128)S(1)} %add_rsqrt_fusion.2, f32[14,262,224]{2,1,0:T(8,128)S(1)} %fusion.3), kind=kLoop, calls=%fused_computation.48 | loop fusion | flops 3040128 | bytes 15214212 | tf_op jit(solution)/shard_map/mul | solution.py:100
  52.3 2.4 %fusion.6 = f32[12,260,224]{2,1,0:T(8,128)S(1)} fusion(f32[16,264,224]{2,1,0:T(8,128)S(1)} %pad_maximum_fusion, f32[13,261,224]{2,1,0:T(8,128)S(1)} %get-tuple-element.9, f32[13,261,224]{2,1,0:T(8,128)S(1)} %get-tuple-element.8, f32[14,262,224]{2,1,0:T(8,128)S(1)} %fusion.3, pred[12,260]{1,0:T(8,128)(4,1)S(1)} %broadcast_and_fusion.1), kind=kLoop, calls=%fused_computation.17 | loop fusion | flops 6289920 | bytes 19571760 | tf_op jit(solution)/shard_map/jit(_where)/select_n | solution.py:105
  56.6 2.4 %fusion.11 = f32[10,258,224]{2,1,0:T(8,128)S(1)} fusion(f32[16,264,224]{2,1,0:T(8,128)S(1)} %pad_maximum_fusion, f32[11,259,224]{2,1,0:T(8,128)S(1)} %get-tuple-element.11, f32[11,259,224]{2,1,0:T(8,128)S(1)} %get-tuple-element.10, f32[12,260,224]{2,1,0:T(8,128)S(1)} %fusion.6, pred[10,258]{1,0:T(8,128)(4,1)S(1)} %broadcast_and_fusion.2), kind=kLoop, calls=%fused_computation.29 | loop fusion | flops 5201280 | bytes 16184340 | tf_op jit(solution)/shard_map/jit(_where)/select_n | solution.py:105
  60.5 1.4 %fusion.17 = f32[8,256,224]{2,1,0:T(8,128)S(1)} fusion(f32[9,257,224]{2,1,0:T(8,128)S(1)} %get-tuple-element.13, f32[9,257,224]{2,1,0:T(8,128)S(1)} %get-tuple-element.12, f32[10,258,224]{2,1,0:T(8,128)S(1)} %fusion.11, pred[8,256]{1,0:T(8,128)(4,1)S(1)} %broadcast_and_fusion.3, f32[224,8,256]{0,2,1:T(8,128)S(1)} %copy.4), kind=kLoop, calls=%fused_computation.42 | loop fusion | flops 4128768 | bytes 12847104 | tf_op jit(solution)/shard_map/jit(_where)/select_n | solution.py:105
  61.9 3.6 %convolution_bitcast_fusion = f32[224,224]{1,0:T(8,128)S(1)} fusion(f32[8,256,224]{2,1,0:T(8,128)S(1)} %fusion.17), kind=kOutput, calls=%fused_computation.53 | convolution fusion | flops 1233125376 | bytes 2035712 | tf_op jit(solution)/shard_map/dot_general | solution.py:183
  65.6 3.0 %collective-permute-start.4 = (f32[112,224]{1,0:T(8,128)S(1)}, f32[112,224]{1,0:T(8,128)S(1)}, u32[]{:S(2)}, u32[]{:S(2)}) collective-permute-start(f32[112,224]{1,0:T(8,128)S(1)} %slice_select_fusion), channel_id=1, source_target_pairs={{0,1},{1,0},{2,3},{3,2},{4,5},{5,4},{6,7},{7,6},{8,9},{9,8},{10,11... | collective-permute-start | bytes 301064 | tf_op jit(solution)/shard_map/ppermute | solution.py:44
  69.5 2.5 %collective-permute-start.5 = (f32[112,224]{1,0:T(8,128)S(1)}, f32[112,224]{1,0:T(8,128)S(1)}, u32[]{:S(2)}, u32[]{:S(2)}) collective-permute-start(f32[112,224]{1,0:T(8,128)S(1)} %select_add_fusion), channel_id=1, source_target_pairs={{0,2},{1,3},{2,0},{3,1},{4,6},{5,7},{6,4},{7,5},{8,10},{9,11},{10,... | collective-permute-start | bytes 301064 | tf_op jit(solution)/shard_map/ppermute | solution.py:27
  72.0 3.7 %collective-permute-done.5 = f32[112,224]{1,0:T(8,128)S(1)} collective-permute-done((f32[112,224]{1,0:T(8,128)S(1)}, f32[112,224]{1,0:T(8,128)S(1)}, u32[]{:S(2)}, u32[]{:S(2)}) %collective-permute-start.5) | collective-permute-done | bytes 100384 | tf_op jit(solution)/shard_map/ppermute | solution.py:27
  76.6 4.0 %collective-permute-done.6 = f32[112,224]{1,0:T(8,128)S(1)} collective-permute-done((f32[112,224]{1,0:T(8,128)S(1)}, f32[112,224]{1,0:T(8,128)S(1)}, u32[]{:S(2)}, u32[]{:S(2)}) %collective-permute-start.6) | collective-permute-done | bytes 100384 | tf_op jit(solution)/shard_map/ppermute | solution.py:27
  80.6 1.6 %collective-permute-start.7 = (f32[112,224]{1,0:T(8,128)S(1)}, f32[112,224]{1,0:T(8,128)S(1)}, u32[]{:S(2)}, u32[]{:S(2)}) collective-permute-start(f32[112,224]{1,0:T(8,128)S(1)} %add.140), channel_id=1, source_target_pairs={{0,8},{8,0},{16,24},{24,16},{1,9},{9,1},{17,25},{25,17},{2,10},{10... | collective-permute-start | bytes 301064 | tf_op jit(solution)/shard_map/ppermute | solution.py:27
  82.2 3.3 %collective-permute-done.7 = f32[112,224]{1,0:T(8,128)S(1)} collective-permute-done((f32[112,224]{1,0:T(8,128)S(1)}, f32[112,224]{1,0:T(8,128)S(1)}, u32[]{:S(2)}, u32[]{:S(2)}) %collective-permute-start.7) | collective-permute-done | bytes 100384 | tf_op jit(solution)/shard_map/ppermute | solution.py:27
  85.5 2.6 %collective-permute-start.8 = (f32[112,224]{1,0:T(8,128)S(1)}, f32[112,224]{1,0:T(8,128)S(1)}, u32[]{:S(2)}, u32[]{:S(2)}) collective-permute-start(f32[112,224]{1,0:T(8,128)S(1)} %add.141), channel_id=1, source_target_pairs={{0,16},{8,24},{16,0},{24,8},{1,17},{9,25},{17,1},{25,9},{2,18},{10... | collective-permute-start | bytes 301064 | tf_op jit(solution)/shard_map/ppermute | solution.py:27
  88.1 4.4 %collective-permute-done.8 = f32[112,224]{1,0:T(8,128)S(1)} collective-permute-done((f32[112,224]{1,0:T(8,128)S(1)}, f32[112,224]{1,0:T(8,128)S(1)}, u32[]{:S(2)}, u32[]{:S(2)}) %collective-permute-start.8) | collective-permute-done | bytes 100384 | tf_op jit(solution)/shard_map/ppermute | solution.py:27
  93.3 2.8 %copy.6 = f32[224,8,256]{2,1,0:T(8,128)} copy(f32[224,8,256]{0,2,1:T(8,128)} %bitcast.21) | data formatting | bytes 3670016
  96.9 6.9 %shard_map.41.basis_ref = f32[224,16]{1,0:T(8,128)} custom-call(f32[224,224]{1,0:T(8,128)} %maximum_select_fusion.gram_ref, f32[224,16]{1,0:T(8,128)} %copy.5.basis_ref), custom_call_target="tpu_custom_call" | custom-call | flops 22937600 | bytes 229376 | tf_op jit(solution)/shard_map/pallas_call | solution.py:147
  103.8 6.9 %shard_map.42 = f32[224,16]{1,0:T(8,128)} custom-call(f32[224,224]{1,0:T(8,128)} %maximum_select_fusion.gram_ref, f32[224,16]{1,0:T(8,128)} %shard_map.41.basis_ref), custom_call_target="tpu_custom_call" | custom-call | flops 22937600 | bytes 229376 | tf_op jit(solution)/shard_map/pallas_call | solution.py:147
  110.6 2.8 %fusion.22 = f32[2048,16]{1,0:T(8,128)S(1)} fusion(f32[2048,224]{1,0:T(8,128)S(1)} %bitcast.22, f32[224,16]{1,0:T(8,128)} %shard_map.42), kind=kOutput, calls=%fused_computation.74 | convolution fusion | flops 88080384 | bytes 1980416 | tf_op jit(solution)/shard_map/dot_general | solution.py:194
  113.4 1.6 %fusion.23 = f32[224,2048]{1,0:T(8,128)S(1)} fusion(f32[224,16]{1,0:T(8,128)S(1)} %copy-done.2, f32[2048,16]{1,0:T(8,128)S(1)} %fusion.22), kind=kOutput, calls=%fused_computation.75 | convolution fusion | flops 88080384 | bytes 1980416 | tf_op jit(solution)/shard_map/dot_general | solution.py:195
  115.1 2.0 %copy.7 = f32[28,8,8,256]{3,2,1,0:T(8,128)} copy(f32[28,8,8,256]{3,1,2,0:T(8,128)S(1)} %bitcast.23) | data formatting | bytes 3670016
  (45 shorter events, 9.7 us)
Async XLA Ops:
  4.0 27.6 %collective-permute-start = (f32[16,64,224]{2,1,0:T(8,128)}, f32[16,64,224]{2,1,0:T(8,128)S(1)}, u32[]{:S(2)}, u32[]{:S(2)}) collective-permute-start(f32[16,64,224]{2,1,0:T(8,128)} %bitcast.1), channel_id=1, source_target_pairs={{0,8},{8,16},{16,24},{1,9},{9,17},{17,25},{2,10},{10,18},{18,26},{... | collective-permute-start | bytes 2752520 | tf_op jit(solution)/shard_map/ppermute | solution.py:71
  9.0 26.8 %collective-permute-start.1 = (f32[16,64,224]{2,1,0:T(8,128)}, f32[16,64,224]{2,1,0:T(8,128)}, u32[]{:S(2)}, u32[]{:S(2)}) collective-permute-start(f32[16,64,224]{2,1,0:T(8,128)} %bitcast.3), channel_id=1, source_target_pairs={{8,0},{16,8},{24,16},{9,1},{17,9},{25,17},{10,2},{18,10},{26,18},{... | collective-permute-start | bytes 2752520 | tf_op jit(solution)/shard_map/ppermute | solution.py:71
  36.6 2.7 %collective-permute-start.2 = (f32[16,4,224]{2,1,0:T(4,128)S(1)}, f32[16,4,224]{2,1,0:T(4,128)S(1)}, u32[]{:S(2)}, u32[]{:S(2)}) collective-permute-start(f32[16,4,224]{2,1,0:T(4,128)S(1)} %get-tuple-element.6), channel_id=1, source_target_pairs={{0,1},{1,2},{2,3},{3,4},{4,5},{5,6},{6,7},{8,9},{9,10},{10,11},{11... | collective-permute-start | bytes 172040 | tf_op jit(solution)/shard_map/ppermute | solution.py:69
  37.9 4.9 %collective-permute-start.3 = (f32[16,4,224]{2,1,0:T(4,128)S(1)}, f32[16,4,224]{2,1,0:T(4,128)S(1)}, u32[]{:S(2)}, u32[]{:S(2)}) collective-permute-start(f32[16,4,224]{2,1,0:T(4,128)S(1)} %get-tuple-element.7), channel_id=1, source_target_pairs={{1,0},{2,1},{3,2},{4,3},{5,4},{6,5},{7,6},{9,8},{10,9},{11,10},{12... | collective-permute-start | bytes 172040 | tf_op jit(solution)/shard_map/ppermute | solution.py:69
  61.9 30.6 %copy-start = (f32[8,256,224]{2,1,0:T(8,128)}, f32[8,256,224]{2,1,0:T(8,128)S(1)}, u32[]{:S(2)}) copy-start(f32[8,256,224]{2,1,0:T(8,128)S(1)} %fusion.17) | copy-start | bytes 5505028
  61.9 30.7 %copy-start.3 = (f32[224,16]{0,1:T(8,128)S(1)}, f32[224,16]{0,1:T(8,128)}, u32[]{:S(2)}) copy-start(f32[224,16]{0,1:T(8,128)} %param.3) | copy-start | bytes 43012
  65.6 4.0 %collective-permute-start.4 = (f32[112,224]{1,0:T(8,128)S(1)}, f32[112,224]{1,0:T(8,128)S(1)}, u32[]{:S(2)}, u32[]{:S(2)}) collective-permute-start(f32[112,224]{1,0:T(8,128)S(1)} %slice_select_fusion), channel_id=1, source_target_pairs={{0,1},{1,0},{2,3},{3,2},{4,5},{5,4},{6,7},{7,6},{8,9},{9,8},{10,11... | collective-permute-start | bytes 301064 | tf_op jit(solution)/shard_map/ppermute | solution.py:44
  69.5 6.1 %collective-permute-start.5 = (f32[112,224]{1,0:T(8,128)S(1)}, f32[112,224]{1,0:T(8,128)S(1)}, u32[]{:S(2)}, u32[]{:S(2)}) collective-permute-start(f32[112,224]{1,0:T(8,128)S(1)} %select_add_fusion), channel_id=1, source_target_pairs={{0,2},{1,3},{2,0},{3,1},{4,6},{5,7},{6,4},{7,5},{8,10},{9,11},{10,... | collective-permute-start | bytes 301064 | tf_op jit(solution)/shard_map/ppermute | solution.py:27
  75.7 4.9 %collective-permute-start.6 = (f32[112,224]{1,0:T(8,128)S(1)}, f32[112,224]{1,0:T(8,128)S(1)}, u32[]{:S(2)}, u32[]{:S(2)}) collective-permute-start(f32[112,224]{1,0:T(8,128)S(1)} %add.139), channel_id=1, source_target_pairs={{0,4},{1,5},{2,6},{3,7},{4,0},{5,1},{6,2},{7,3},{8,12},{9,13},{10,... | collective-permute-start | bytes 301064 | tf_op jit(solution)/shard_map/ppermute | solution.py:27
  80.6 4.9 %collective-permute-start.7 = (f32[112,224]{1,0:T(8,128)S(1)}, f32[112,224]{1,0:T(8,128)S(1)}, u32[]{:S(2)}, u32[]{:S(2)}) collective-permute-start(f32[112,224]{1,0:T(8,128)S(1)} %add.140), channel_id=1, source_target_pairs={{0,8},{8,0},{16,24},{24,16},{1,9},{9,1},{17,25},{25,17},{2,10},{10... | collective-permute-start | bytes 301064 | tf_op jit(solution)/shard_map/ppermute | solution.py:27
  85.5 7.0 %collective-permute-start.8 = (f32[112,224]{1,0:T(8,128)S(1)}, f32[112,224]{1,0:T(8,128)S(1)}, u32[]{:S(2)}, u32[]{:S(2)}) collective-permute-start(f32[112,224]{1,0:T(8,128)S(1)} %add.141), channel_id=1, source_target_pairs={{0,16},{8,24},{16,0},{24,8},{1,17},{9,25},{17,1},{25,9},{2,18},{10... | collective-permute-start | bytes 301064 | tf_op jit(solution)/shard_map/ppermute | solution.py:27
  92.5 3.7 %collective-permute-start.9 = (f32[112,224]{1,0:T(8,128)S(1)}, f32[112,224]{1,0:T(8,128)S(1)}, u32[]{:S(2)}, u32[]{:S(2)}) collective-permute-start(f32[112,224]{1,0:T(8,128)S(1)} %add.142), channel_id=1, source_target_pairs={{0,1},{1,0},{2,3},{3,2},{4,5},{5,4},{6,7},{7,6},{8,9},{9,8},{10,11... | collective-permute-start | bytes 301064 | tf_op jit(solution)/shard_map/ppermute | solution.py:46
  92.6 18.1 %copy-start.1 = (f32[8,256,224]{2,1,0:T(8,128)S(1)}, f32[8,256,224]{2,1,0:T(8,128)}, u32[]{:S(2)}) copy-start(f32[8,256,224]{2,1,0:T(8,128)} %copy-done) | copy-start | bytes 5505028
  110.6 2.8 %copy-start.2 = (f32[224,16]{1,0:T(8,128)S(1)}, f32[224,16]{1,0:T(8,128)}, u32[]{:S(2)}) copy-start(f32[224,16]{1,0:T(8,128)} %shard_map.42) | copy-start | bytes 43012

commit v11 on v10

--- a/solution.py
+++ b/solution.py
@@ -83,6 +83,31 @@
 
 def pinned(cells):
     return with_layout_constraint(cells, Layout(major_to_minor=tuple(range(cells.ndim))))
+
+
+def with_ring(cells, width):
+    rows_n = lax.axis_size("row")
+    cols_n = lax.axis_size("col")
+    tile_rows, tile_cols = cells.shape[0], cells.shape[1]
+    down = [(i, i + 1) for i in range(rows_n - 1)]
+    up = [(i + 1, i) for i in range(rows_n - 1)]
+    right = [(i, i + 1) for i in range(cols_n - 1)]
+    left = [(i + 1, i) for i in range(cols_n - 1)]
+    top = flat_permute(cells[tile_rows - width:], "row", down)
+    bottom = flat_permute(cells[:width], "row", up)
+    west = lax.ppermute(cells[:, tile_cols - width:], "col", right)
+    east = lax.ppermute(cells[:, :width], "col", left)
+    rims = jnp.concatenate([top, bottom], axis=0)
+    rim_west = lax.ppermute(rims[:, tile_cols - width:], "col", right)
+    rim_east = lax.ppermute(rims[:, :width], "col", left)
+    return jnp.concatenate(
+        [
+            jnp.concatenate([rim_west[:width], top, rim_east[:width]], axis=1),
+            jnp.concatenate([west, cells, east], axis=1),
+            jnp.concatenate([rim_west[width:], bottom, rim_east[width:]], axis=1),
+        ],
+        axis=0,
+    )
 
 
 def inside_mask(axis, tile, width):
@@ -165,8 +190,7 @@
     band_count, tile_rows, tile_cols = image.shape
     width = SWEEPS
     cells = pinned(jnp.transpose(image, (1, 2, 0)))
-    ext = with_halo(cells, "row", 0, width)
-    ext = with_halo(ext, "col", 1, width)
+    ext = with_ring(cells, width)
     row_in = inside_mask("row", tile_rows, width)
     col_in = inside_mask("col", tile_cols, width)
     field = ext

time: 117 us -> 117 us (level)
  waiting for transfers between devices: 44.4 us -> 41.6 us
  starting transfers between devices: 19.5 us -> 21.9 us
    ppermute x2, waiting for transfers between devices: 24.7 us -> 21.9 us  [flat_permute(): return lax.ppermute(flat, axis, pairs).reshape(block.shape)]
    ppermute x2 -> x4, starting transfers between devices: 2.59 us -> 5.32 us  [the longest x1 1.46 us: with_ring(): west = lax.ppermute(cells[:, tile_cols - width:], 'col', right)]
    ppermute x2 -> x4, waiting for transfers between devices: 3.5 us -> 3.51 us  [the longest x1 3.5 us: with_ring(): rim_east = lax.ppermute(rims[:, :width], 'col', left)]
  transfers between devices with their start and end apart: 10 -> 12, of which waited for: 8 -> 8; matrix products, arithmetic and copies ran while one was open for 4% -> 4% of each run, Pallas kernels for 0% -> 0%
where the time goes in v11:
time: 117 us
  waiting for transfers between devices  41.6 us (36%)
  starting transfers between devices  21.9 us (19%)
  other arithmetic  21 us (18%)
  Pallas kernels  13.8 us (12%)
  local copies, waits for them, and re-layouts  9.59 us (8%)
  matrix products  7.86 us (7%)
    ppermute x2, waiting for transfers between devices, flat_permute(): return lax.ppermute(flat, axis, pairs).reshape(block.shape)  21.9 us
    ppermute x4, waiting for transfers between devices, butterfly_sum(): partner = lax.ppermute(value, axis, [(i, i ^ step) for i in range(count)])  15.3 us
    pallas_call x2, Pallas kernels, subspace_step(): pl.pallas_call(subspace_kernel, out_shape=jax.ShapeDtypeStruct(basis.shap...  13.8 us
    select_n x4, other arithmetic, sweep(): return jnp.where(keep, new, 0.0)  8.95 us
    ppermute x4, starting transfers between devices, butterfly_sum(): partner = lax.ppermute(value, axis, [(i, i ^ step) for i in range(count)])  7.57 us
    unnamed x12, local copies, waits for them, and re-layouts  7.35 us
    ppermute x2, starting transfers between devices, flat_permute(): return lax.ppermute(flat, axis, pairs).reshape(block.shape)  6.27 us
    mul x4, other arithmetic, sweep(): flux_col = weight * diff_col  4.16 us
  transfers between devices with their start and end apart: 12, of which 8 were waited for; matrix products, arithmetic and copies ran while one was open for 4% of the time, Pallas kernels for 0%

profile of v11, /device:TPU:0, one launch (start us, length us, event | category | flops | bytes accessed | tf_op | source)
XLA Modules:
  0.0 116.7 jit_solution(18282578326550973693)
XLA Ops:
  0.6 1.9 %copy.4 = f32[224,8,256]{0,2,1:T(8,128)S(1)} copy(f32[224,8,256]{2,1,0:T(8,128)} %param.2) | data formatting | bytes 3670016 | tf_op args[0]
  2.5 1.6 %fusion.22 = (f32[4,256,224]{2,1,0:T(8,128)}, f32[4,256,224]{2,1,0:T(8,128)}) fusion(f32[8,256,224]{2,1,0:T(8,128)S(1)} %bitcast.20), kind=kLoop, calls=%fused_computation.73 | loop fusion | bytes 3670016 | tf_op jit(solution)/shard_map/slice | solution.py:96
  4.1 5.0 %collective-permute-start = (f32[16,64,224]{2,1,0:T(8,128)}, f32[16,64,224]{2,1,0:T(8,128)S(1)}, u32[]{:S(2)}, u32[]{:S(2)}) collective-permute-start(f32[16,64,224]{2,1,0:T(8,128)} %bitcast.1), channel_id=1, source_target_pairs={{0,8},{8,16},{16,24},{1,9},{9,17},{17,25},{2,10},{10,18},{18,26},{... | collective-permute-start | bytes 2752520 | tf_op jit(solution)/shard_map/ppermute | solution.py:71
  9.1 1.3 %collective-permute-start.1 = (f32[16,64,224]{2,1,0:T(8,128)}, f32[16,64,224]{2,1,0:T(8,128)}, u32[]{:S(2)}, u32[]{:S(2)}) collective-permute-start(f32[16,64,224]{2,1,0:T(8,128)} %bitcast.3), channel_id=1, source_target_pairs={{8,0},{16,8},{24,16},{9,1},{17,9},{25,17},{10,2},{18,10},{26,18},{... | collective-permute-start | bytes 2752520 | tf_op jit(solution)/shard_map/ppermute | solution.py:71
  10.5 1.5 %collective-permute-start.4 = (f32[8,4,224]{2,1,0:T(4,128)S(1)}, f32[8,4,224]{2,1,0:T(4,128)S(1)}, u32[]{:S(2)}, u32[]{:S(2)}) collective-permute-start(f32[8,4,224]{2,1,0:T(4,128)S(1)} %get-tuple-element.12), channel_id=1, source_target_pairs={{0,1},{1,2},{2,3},{3,4},{4,5},{5,6},{6,7},{8,9},{9,10},{10,11},{11... | collective-permute-start | bytes 86024 | tf_op jit(solution)/shard_map/ppermute | solution.py:98
  11.9 1.3 %collective-permute-start.5 = (f32[8,4,224]{2,1,0:T(4,128)S(1)}, f32[8,4,224]{2,1,0:T(4,128)S(1)}, u32[]{:S(2)}, u32[]{:S(2)}) collective-permute-start(f32[8,4,224]{2,1,0:T(4,128)S(1)} %get-tuple-element.13), channel_id=1, source_target_pairs={{1,0},{2,1},{3,2},{4,3},{5,4},{6,5},{7,6},{9,8},{10,9},{11,10},{12... | collective-permute-start | bytes 86024 | tf_op jit(solution)/shard_map/ppermute | solution.py:99
  14.1 17.7 %collective-permute-done = f32[16,64,224]{2,1,0:T(8,128)S(1)} collective-permute-done((f32[16,64,224]{2,1,0:T(8,128)}, f32[16,64,224]{2,1,0:T(8,128)S(1)}, u32[]{:S(2)}, u32[]{:S(2)}) %collective-permute-start) | collective-permute-done | bytes 917536 | tf_op jit(solution)/shard_map/ppermute | solution.py:71
  31.8 4.2 %collective-permute-done.1 = f32[16,64,224]{2,1,0:T(8,128)} collective-permute-done((f32[16,64,224]{2,1,0:T(8,128)}, f32[16,64,224]{2,1,0:T(8,128)}, u32[]{:S(2)}, u32[]{:S(2)}) %collective-permute-start.1) | collective-permute-done | bytes 917536 | tf_op jit(solution)/shard_map/ppermute | solution.py:71
  36.8 1.3 %collective-permute-start.2 = (f32[8,4,224]{2,1,0:T(4,128)S(1)}, f32[8,4,224]{2,1,0:T(4,128)S(1)}, u32[]{:S(2)}, u32[]{:S(2)}) collective-permute-start(f32[8,4,224]{2,1,0:T(4,128)S(1)} %get-tuple-element.14), channel_id=1, source_target_pairs={{0,1},{1,2},{2,3},{3,4},{4,5},{5,6},{6,7},{8,9},{9,10},{10,11},{11... | collective-permute-start | bytes 86024 | tf_op jit(solution)/shard_map/ppermute | solution.py:101
  38.1 1.3 %collective-permute-start.3 = (f32[8,4,224]{2,1,0:T(4,128)S(1)}, f32[8,4,224]{2,1,0:T(4,128)S(1)}, u32[]{:S(2)}, u32[]{:S(2)}) collective-permute-start(f32[8,4,224]{2,1,0:T(4,128)S(1)} %get-tuple-element.15), channel_id=1, source_target_pairs={{1,0},{2,1},{3,2},{4,3},{5,4},{6,5},{7,6},{9,8},{10,9},{11,10},{12... | collective-permute-start | bytes 86024 | tf_op jit(solution)/shard_map/ppermute | solution.py:102
  39.4 3.5 %collective-permute-done.3 = f32[8,4,224]{2,1,0:T(4,128)S(1)} collective-permute-done((f32[8,4,224]{2,1,0:T(4,128)S(1)}, f32[8,4,224]{2,1,0:T(4,128)S(1)}, u32[]{:S(2)}, u32[]{:S(2)}) %collective-permute-start.3) | collective-permute-done | bytes 28704 | tf_op jit(solution)/shard_map/ppermute | solution.py:102
  43.0 1.8 %maximum_maximum_fusion = f32[16,264,224]{2,1,0:T(8,128)S(1)} fusion(f32[4,4,224]{2,1,0:T(4,128)S(1)} %get-tuple-element.21, f32[4,256,224]{2,1,0:T(8,128)} %bitcast.4, f32[4,4,224]{2,1,0:T(4,128)S(1)} %get-tuple-element.19, f32[8,4,224]{2,1,0:T(4,128)S(1)} %collective-permute-done.5, f32[8,256,224]{2,1,0:T(8,128)S(1)} %bitcast.22, ...), kind=kLoop, calls=%fused_computation | loop fusion | flops 7569408 | bytes 7569408 | tf_op jit(solution)/shard_map/concatenate | solution.py:103
  46.1 1.4 %broadcast_multiply_fusion.1 = (f32[15,263,224]{2,1,0:T(8,128)S(1)}, f32[15,263,224]{2,1,0:T(8,128)S(1)}) fusion(f32[15,263]{1,0:T(8,128)S(1)} %add_rsqrt_fusion.3, f32[16,264,224]{2,1,0:T(8,128)S(1)} %maximum_maximum_fusion), kind=kLoop, calls=%fused_computation.46 | loop fusion | flops 3534720 | bytes 17689380 | tf_op jit(solution)/shard_map/mul | solution.py:125
  47.5 2.6 %fusion.3 = f32[14,262,224]{2,1,0:T(8,128)S(1)} fusion(f32[15,263,224]{2,1,0:T(8,128)S(1)} %get-tuple-element.5, f32[15,263,224]{2,1,0:T(8,128)S(1)} %get-tuple-element.4, f32[16,264,224]{2,1,0:T(8,128)S(1)} %maximum_maximum_fusion, pred[14,262]{1,0:T(8,128)(4,1)S(1)} %broadcast_and_fusion), kind=kLoop, calls=%fused_computation.8 | loop fusion | flops 7394688 | bytes 19722836 | tf_op jit(solution)/shard_map/jit(_where)/select_n | solution.py:130
  52.5 2.4 %fusion.6 = f32[12,260,224]{2,1,0:T(8,128)S(1)} fusion(f32[16,264,224]{2,1,0:T(8,128)S(1)} %maximum_maximum_fusion, f32[13,261,224]{2,1,0:T(8,128)S(1)} %get-tuple-element.7, f32[13,261,224]{2,1,0:T(8,128)S(1)} %get-tuple-element.6, f32[14,262,224]{2,1,0:T(8,128)S(1)} %fusion.3, pred[12,260]{1,0:T(8,128)(4,1)S(1)} %broadcast_and_fusion.1), kind=kLoop, calls=%fused_computation.17 | loop fusion | flops 6289920 | bytes 19571760 | tf_op jit(solution)/shard_map/jit(_where)/select_n | solution.py:130
  56.8 2.4 %fusion.11 = f32[10,258,224]{2,1,0:T(8,128)S(1)} fusion(f32[16,264,224]{2,1,0:T(8,128)S(1)} %maximum_maximum_fusion, f32[11,259,224]{2,1,0:T(8,128)S(1)} %get-tuple-element.9, f32[11,259,224]{2,1,0:T(8,128)S(1)} %get-tuple-element.8, f32[12,260,224]{2,1,0:T(8,128)S(1)} %fusion.6, pred[10,258]{1,0:T(8,128)(4,1)S(1)} %broadcast_and_fusion.2), kind=kLoop, calls=%fused_computation.29 | loop fusion | flops 5201280 | bytes 16184340 | tf_op jit(solution)/shard_map/jit(_where)/select_n | solution.py:130
  61.6 1.5 %fusion.17 = f32[8,256,224]{2,1,0:T(8,128)S(1)} fusion(f32[9,257,224]{2,1,0:T(8,128)S(1)} %get-tuple-element.11, f32[9,257,224]{2,1,0:T(8,128)S(1)} %get-tuple-element.10, f32[10,258,224]{2,1,0:T(8,128)S(1)} %fusion.11, pred[8,256]{1,0:T(8,128)(4,1)S(1)} %broadcast_and_fusion.3, f32[224,8,256]{0,2,1:T(8,128)S(1)} %copy-done.1), kind=kLoop, calls=%fused_computation.42 | loop fusion | flops 4128768 | bytes 12847104 | tf_op jit(solution)/shard_map/jit(_where)/select_n | solution.py:130
  63.1 3.5 %convolution_bitcast_fusion = f32[224,224]{1,0:T(8,128)S(1)} fusion(f32[8,256,224]{2,1,0:T(8,128)S(1)} %fusion.17), kind=kOutput, calls=%fused_computation.53 | convolution fusion | flops 1233125376 | bytes 2035712 | tf_op jit(solution)/shard_map/dot_general | solution.py:207
  66.6 2.7 %collective-permute-start.6 = (f32[112,224]{1,0:T(8,128)S(1)}, f32[112,224]{1,0:T(8,128)S(1)}, u32[]{:S(2)}, u32[]{:S(2)}) collective-permute-start(f32[112,224]{1,0:T(8,128)S(1)} %slice_select_fusion), channel_id=1, source_target_pairs={{0,1},{1,0},{2,3},{3,2},{4,5},{5,4},{6,7},{7,6},{8,9},{9,8},{10,11... | collective-permute-start | bytes 301064 | tf_op jit(solution)/shard_map/ppermute | solution.py:44
  70.3 2.5 %collective-permute-start.7 = (f32[112,224]{1,0:T(8,128)S(1)}, f32[112,224]{1,0:T(8,128)S(1)}, u32[]{:S(2)}, u32[]{:S(2)}) collective-permute-start(f32[112,224]{1,0:T(8,128)S(1)} %select_add_fusion), channel_id=1, source_target_pairs={{0,2},{1,3},{2,0},{3,1},{4,6},{5,7},{6,4},{7,5},{8,10},{9,11},{10,... | collective-permute-start | bytes 301064 | tf_op jit(solution)/shard_map/ppermute | solution.py:27
  72.8 3.7 %collective-permute-done.7 = f32[112,224]{1,0:T(8,128)S(1)} collective-permute-done((f32[112,224]{1,0:T(8,128)S(1)}, f32[112,224]{1,0:T(8,128)S(1)}, u32[]{:S(2)}, u32[]{:S(2)}) %collective-permute-start.7) | collective-permute-done | bytes 100384 | tf_op jit(solution)/shard_map/ppermute | solution.py:27
  77.4 4.0 %collective-permute-done.8 = f32[112,224]{1,0:T(8,128)S(1)} collective-permute-done((f32[112,224]{1,0:T(8,128)S(1)}, f32[112,224]{1,0:T(8,128)S(1)}, u32[]{:S(2)}, u32[]{:S(2)}) %collective-permute-start.8) | collective-permute-done | bytes 100384 | tf_op jit(solution)/shard_map/ppermute | solution.py:27
  81.4 1.6 %collective-permute-start.9 = (f32[112,224]{1,0:T(8,128)S(1)}, f32[112,224]{1,0:T(8,128)S(1)}, u32[]{:S(2)}, u32[]{:S(2)}) collective-permute-start(f32[112,224]{1,0:T(8,128)S(1)} %add.140), channel_id=1, source_target_pairs={{0,8},{8,0},{16,24},{24,16},{1,9},{9,1},{17,25},{25,17},{2,10},{10... | collective-permute-start | bytes 301064 | tf_op jit(solution)/shard_map/ppermute | solution.py:27
  83.0 3.3 %collective-permute-done.9 = f32[112,224]{1,0:T(8,128)S(1)} collective-permute-done((f32[112,224]{1,0:T(8,128)S(1)}, f32[112,224]{1,0:T(8,128)S(1)}, u32[]{:S(2)}, u32[]{:S(2)}) %collective-permute-start.9) | collective-permute-done | bytes 100384 | tf_op jit(solution)/shard_map/ppermute | solution.py:27
  86.3 2.6 %collective-permute-start.10 = (f32[112,224]{1,0:T(8,128)S(1)}, f32[112,224]{1,0:T(8,128)S(1)}, u32[]{:S(2)}, u32[]{:S(2)}) collective-permute-start(f32[112,224]{1,0:T(8,128)S(1)} %add.141), channel_id=1, source_target_pairs={{0,16},{8,24},{16,0},{24,8},{1,17},{9,25},{17,1},{25,9},{2,18},{10... | collective-permute-start | bytes 301064 | tf_op jit(solution)/shard_map/ppermute | solution.py:27
  88.9 4.4 %collective-permute-done.10 = f32[112,224]{1,0:T(8,128)S(1)} collective-permute-done((f32[112,224]{1,0:T(8,128)S(1)}, f32[112,224]{1,0:T(8,128)S(1)}, u32[]{:S(2)}, u32[]{:S(2)}) %collective-permute-start.10) | collective-permute-done | bytes 100384 | tf_op jit(solution)/shard_map/ppermute | solution.py:27
  94.1 1.8 %copy.6 = f32[224,8,256]{2,1,0:T(8,128)} copy(f32[224,8,256]{0,2,1:T(8,128)S(1)} %bitcast.18) | data formatting | bytes 3670016
  96.6 6.9 %shard_map.41.basis_ref = f32[224,16]{1,0:T(8,128)} custom-call(f32[224,224]{1,0:T(8,128)} %maximum_select_fusion.gram_ref, f32[224,16]{1,0:T(8,128)} %copy.5.basis_ref), custom_call_target="tpu_custom_call" | custom-call | flops 22937600 | bytes 229376 | tf_op jit(solution)/shard_map/pallas_call | solution.py:172
  103.5 6.9 %shard_map.42 = f32[224,16]{1,0:T(8,128)} custom-call(f32[224,224]{1,0:T(8,128)} %maximum_select_fusion.gram_ref, f32[224,16]{1,0:T(8,128)} %shard_map.41.basis_ref), custom_call_target="tpu_custom_call" | custom-call | flops 22937600 | bytes 229376 | tf_op jit(solution)/shard_map/pallas_call | solution.py:172
  110.3 2.8 %fusion.25 = f32[2048,16]{1,0:T(8,128)S(1)} fusion(f32[2048,224]{1,0:T(8,128)S(1)} %bitcast.19, f32[224,16]{1,0:T(8,128)} %shard_map.42), kind=kOutput, calls=%fused_computation.76 | convolution fusion | flops 88080384 | bytes 1980416 | tf_op jit(solution)/shard_map/dot_general | solution.py:218
  113.1 1.6 %fusion.26 = f32[224,2048]{1,0:T(8,128)S(1)} fusion(f32[224,16]{1,0:T(8,128)S(1)} %copy-done.2, f32[2048,16]{1,0:T(8,128)S(1)} %fusion.25), kind=kOutput, calls=%fused_computation.77 | convolution fusion | flops 88080384 | bytes 1980416 | tf_op jit(solution)/shard_map/dot_general | solution.py:219
  114.8 2.0 %copy.7 = f32[28,8,8,256]{3,2,1,0:T(8,128)} copy(f32[28,8,8,256]{3,1,2,0:T(8,128)S(1)} %bitcast.23) | data formatting | bytes 3670016
  (52 shorter events, 13.2 us)
Async XLA Ops:
  2.5 40.4 %copy-start = (f32[224,8,256]{0,2,1:T(8,128)}, f32[224,8,256]{0,2,1:T(8,128)S(1)}, u32[]{:S(2)}) copy-start(f32[224,8,256]{0,2,1:T(8,128)S(1)} %copy.4) | copy-start | bytes 5505028
  4.1 27.6 %collective-permute-start = (f32[16,64,224]{2,1,0:T(8,128)}, f32[16,64,224]{2,1,0:T(8,128)S(1)}, u32[]{:S(2)}, u32[]{:S(2)}) collective-permute-start(f32[16,64,224]{2,1,0:T(8,128)} %bitcast.1), channel_id=1, source_target_pairs={{0,8},{8,16},{16,24},{1,9},{9,17},{17,25},{2,10},{10,18},{18,26},{... | collective-permute-start | bytes 2752520 | tf_op jit(solution)/shard_map/ppermute | solution.py:71
  9.1 26.8 %collective-permute-start.1 = (f32[16,64,224]{2,1,0:T(8,128)}, f32[16,64,224]{2,1,0:T(8,128)}, u32[]{:S(2)}, u32[]{:S(2)}) collective-permute-start(f32[16,64,224]{2,1,0:T(8,128)} %bitcast.3), channel_id=1, source_target_pairs={{8,0},{16,8},{24,16},{9,1},{17,9},{25,17},{10,2},{18,10},{26,18},{... | collective-permute-start | bytes 2752520 | tf_op jit(solution)/shard_map/ppermute | solution.py:71
  10.5 32.5 %collective-permute-start.4 = (f32[8,4,224]{2,1,0:T(4,128)S(1)}, f32[8,4,224]{2,1,0:T(4,128)S(1)}, u32[]{:S(2)}, u32[]{:S(2)}) collective-permute-start(f32[8,4,224]{2,1,0:T(4,128)S(1)} %get-tuple-element.12), channel_id=1, source_target_pairs={{0,1},{1,2},{2,3},{3,4},{4,5},{5,6},{6,7},{8,9},{9,10},{10,11},{11... | collective-permute-start | bytes 86024 | tf_op jit(solution)/shard_map/ppermute | solution.py:98
  11.9 31.0 %collective-permute-start.5 = (f32[8,4,224]{2,1,0:T(4,128)S(1)}, f32[8,4,224]{2,1,0:T(4,128)S(1)}, u32[]{:S(2)}, u32[]{:S(2)}) collective-permute-start(f32[8,4,224]{2,1,0:T(4,128)S(1)} %get-tuple-element.13), channel_id=1, source_target_pairs={{1,0},{2,1},{3,2},{4,3},{5,4},{6,5},{7,6},{9,8},{10,9},{11,10},{12... | collective-permute-start | bytes 86024 | tf_op jit(solution)/shard_map/ppermute | solution.py:99
  36.8 2.7 %collective-permute-start.2 = (f32[8,4,224]{2,1,0:T(4,128)S(1)}, f32[8,4,224]{2,1,0:T(4,128)S(1)}, u32[]{:S(2)}, u32[]{:S(2)}) collective-permute-start(f32[8,4,224]{2,1,0:T(4,128)S(1)} %get-tuple-element.14), channel_id=1, source_target_pairs={{0,1},{1,2},{2,3},{3,4},{4,5},{5,6},{6,7},{8,9},{9,10},{10,11},{11... | collective-permute-start | bytes 86024 | tf_op jit(solution)/shard_map/ppermute | solution.py:101
  38.1 4.8 %collective-permute-start.3 = (f32[8,4,224]{2,1,0:T(4,128)S(1)}, f32[8,4,224]{2,1,0:T(4,128)S(1)}, u32[]{:S(2)}, u32[]{:S(2)}) collective-permute-start(f32[8,4,224]{2,1,0:T(4,128)S(1)} %get-tuple-element.15), channel_id=1, source_target_pairs={{1,0},{2,1},{3,2},{4,3},{5,4},{6,5},{7,6},{9,8},{10,9},{11,10},{12... | collective-permute-start | bytes 86024 | tf_op jit(solution)/shard_map/ppermute | solution.py:102
  60.0 1.6 %copy-start.1 = (f32[224,8,256]{0,2,1:T(8,128)S(1)}, f32[224,8,256]{0,2,1:T(8,128)}, u32[]{:S(2)}) copy-start(f32[224,8,256]{0,2,1:T(8,128)} %copy-done) | copy-start | bytes 5505028
  63.1 30.2 %copy-start.3 = (f32[224,16]{0,1:T(8,128)S(1)}, f32[224,16]{0,1:T(8,128)}, u32[]{:S(2)}) copy-start(f32[224,16]{0,1:T(8,128)} %param.3) | copy-start | bytes 43012
  66.6 3.7 %collective-permute-start.6 = (f32[112,224]{1,0:T(8,128)S(1)}, f32[112,224]{1,0:T(8,128)S(1)}, u32[]{:S(2)}, u32[]{:S(2)}) collective-permute-start(f32[112,224]{1,0:T(8,128)S(1)} %slice_select_fusion), channel_id=1, source_target_pairs={{0,1},{1,0},{2,3},{3,2},{4,5},{5,4},{6,7},{7,6},{8,9},{9,8},{10,11... | collective-permute-start | bytes 301064 | tf_op jit(solution)/shard_map/ppermute | solution.py:44
  70.3 6.1 %collective-permute-start.7 = (f32[112,224]{1,0:T(8,128)S(1)}, f32[112,224]{1,0:T(8,128)S(1)}, u32[]{:S(2)}, u32[]{:S(2)}) collective-permute-start(f32[112,224]{1,0:T(8,128)S(1)} %select_add_fusion), channel_id=1, source_target_pairs={{0,2},{1,3},{2,0},{3,1},{4,6},{5,7},{6,4},{7,5},{8,10},{9,11},{10,... | collective-permute-start | bytes 301064 | tf_op jit(solution)/shard_map/ppermute | solution.py:27
  76.5 4.9 %collective-permute-start.8 = (f32[112,224]{1,0:T(8,128)S(1)}, f32[112,224]{1,0:T(8,128)S(1)}, u32[]{:S(2)}, u32[]{:S(2)}) collective-permute-start(f32[112,224]{1,0:T(8,128)S(1)} %add.139), channel_id=1, source_target_pairs={{0,4},{1,5},{2,6},{3,7},{4,0},{5,1},{6,2},{7,3},{8,12},{9,13},{10,... | collective-permute-start | bytes 301064 | tf_op jit(solution)/shard_map/ppermute | solution.py:27
  81.4 4.9 %collective-permute-start.9 = (f32[112,224]{1,0:T(8,128)S(1)}, f32[112,224]{1,0:T(8,128)S(1)}, u32[]{:S(2)}, u32[]{:S(2)}) collective-permute-start(f32[112,224]{1,0:T(8,128)S(1)} %add.140), channel_id=1, source_target_pairs={{0,8},{8,0},{16,24},{24,16},{1,9},{9,1},{17,25},{25,17},{2,10},{10... | collective-permute-start | bytes 301064 | tf_op jit(solution)/shard_map/ppermute | solution.py:27
  86.3 7.0 %collective-permute-start.10 = (f32[112,224]{1,0:T(8,128)S(1)}, f32[112,224]{1,0:T(8,128)S(1)}, u32[]{:S(2)}, u32[]{:S(2)}) collective-permute-start(f32[112,224]{1,0:T(8,128)S(1)} %add.141), channel_id=1, source_target_pairs={{0,16},{8,24},{16,0},{24,8},{1,17},{9,25},{17,1},{25,9},{2,18},{10... | collective-permute-start | bytes 301064 | tf_op jit(solution)/shard_map/ppermute | solution.py:27
  93.3 2.6 %collective-permute-start.11 = (f32[112,224]{1,0:T(8,128)S(1)}, f32[112,224]{1,0:T(8,128)S(1)}, u32[]{:S(2)}, u32[]{:S(2)}) collective-permute-start(f32[112,224]{1,0:T(8,128)S(1)} %add.142), channel_id=1, source_target_pairs={{0,1},{1,0},{2,3},{3,2},{4,5},{5,4},{6,7},{7,6},{8,9},{9,8},{10,11... | collective-permute-start | bytes 301064 | tf_op jit(solution)/shard_map/ppermute | solution.py:46
  110.3 2.8 %copy-start.2 = (f32[224,16]{1,0:T(8,128)S(1)}, f32[224,16]{1,0:T(8,128)}, u32[]{:S(2)}) copy-start(f32[224,16]{1,0:T(8,128)} %shard_map.42) | copy-start | bytes 43012

commit v12 on v11

--- a/solution.py
+++ b/solution.py
@@ -142,15 +142,15 @@
     inverse = jnp.zeros((size, size), jnp.float32)
     rest = inner
     for j in range(size):
-        col = jnp.sum(jnp.where(lane == j, rest, 0.0), axis=1, keepdims=True)
-        row = jnp.sum(jnp.where(sub == j, rest, 0.0), axis=0, keepdims=True)
-        pivot = jnp.sqrt(jnp.sum(jnp.where(lane[:1] == j, row, 0.0), axis=1, keepdims=True))
+        col = rest[:, j:j + 1]
+        row = rest[j:j + 1, :]
+        pivot = jnp.sqrt(rest[j:j + 1, j:j + 1])
         col = jnp.where(sub[:, :1] >= j, col / pivot, 0.0)
         row = jnp.where(lane[:1] >= j, row / pivot, 0.0)
         upper = upper + jnp.where(sub == j, row, 0.0)
         rest = rest - col * row
-        coef = jnp.sum(jnp.where(lane == j, upper, 0.0), axis=1, keepdims=True)
-        diag = jnp.sum(jnp.where(sub[:, :1] == j, coef, 0.0), axis=0, keepdims=True)
+        coef = upper[:, j:j + 1]
+        diag = upper[j:j + 1, j:j + 1]
         acc = jnp.sum(jnp.where(sub[:, :1] < j, coef, 0.0) * inverse, axis=0, keepdims=True)
         unit = jnp.where(lane[:1] == j, 1.0, 0.0)
         inverse = inverse + jnp.where(sub == j, (unit - acc) / diag, 0.0)

time: 117 us -> 116 us (level)
  no operation moved by 1% of the time
where the time goes in v12:
time: 116 us
  waiting for transfers between devices  41.6 us (36%)
  starting transfers between devices  21.9 us (19%)
  other arithmetic  21 us (18%)
  Pallas kernels  12.8 us (11%)
  local copies, waits for them, and re-layouts  9.59 us (8%)
  matrix products  7.86 us (7%)
    ppermute x2, waiting for transfers between devices, flat_permute(): return lax.ppermute(flat, axis, pairs).reshape(block.shape)  21.9 us
    ppermute x4, waiting for transfers between devices, butterfly_sum(): partner = lax.ppermute(value, axis, [(i, i ^ step) for i in range(count)])  15.3 us
    pallas_call x2, Pallas kernels, subspace_step(): pl.pallas_call(subspace_kernel, out_shape=jax.ShapeDtypeStruct(basis.shap...  12.8 us
    select_n x4, other arithmetic, sweep(): return jnp.where(keep, new, 0.0)  8.95 us
    ppermute x4, starting transfers between devices, butterfly_sum(): partner = lax.ppermute(value, axis, [(i, i ^ step) for i in range(count)])  7.57 us
    unnamed x12, local copies, waits for them, and re-layouts  7.35 us
    ppermute x2, starting transfers between devices, flat_permute(): return lax.ppermute(flat, axis, pairs).reshape(block.shape)  6.27 us
    mul x4, other arithmetic, sweep(): flux_col = weight * diff_col  4.16 us
  transfers between devices with their start and end apart: 12, of which 8 were waited for; matrix products, arithmetic and copies ran while one was open for 4% of the time, Pallas kernels for 0%

profile of v12, /device:TPU:0, one launch (start us, length us, event | category | flops | bytes accessed | tf_op | source)
XLA Modules:
  0.0 115.8 jit_solution(1919069421582193276)
XLA Ops:
  0.6 1.9 %copy.4 = f32[224,8,256]{0,2,1:T(8,128)S(1)} copy(f32[224,8,256]{2,1,0:T(8,128)} %param.2) | data formatting | bytes 3670016 | tf_op args[0]
  2.5 1.6 %fusion.22 = (f32[4,256,224]{2,1,0:T(8,128)}, f32[4,256,224]{2,1,0:T(8,128)}) fusion(f32[8,256,224]{2,1,0:T(8,128)S(1)} %bitcast.20), kind=kLoop, calls=%fused_computation.73 | loop fusion | bytes 3670016 | tf_op jit(solution)/shard_map/slice | solution.py:96
  4.1 5.0 %collective-permute-start = (f32[16,64,224]{2,1,0:T(8,128)}, f32[16,64,224]{2,1,0:T(8,128)S(1)}, u32[]{:S(2)}, u32[]{:S(2)}) collective-permute-start(f32[16,64,224]{2,1,0:T(8,128)} %bitcast.1), channel_id=1, source_target_pairs={{0,8},{8,16},{16,24},{1,9},{9,17},{17,25},{2,10},{10,18},{18,26},{... | collective-permute-start | bytes 2752520 | tf_op jit(solution)/shard_map/ppermute | solution.py:71
  9.1 1.3 %collective-permute-start.1 = (f32[16,64,224]{2,1,0:T(8,128)}, f32[16,64,224]{2,1,0:T(8,128)}, u32[]{:S(2)}, u32[]{:S(2)}) collective-permute-start(f32[16,64,224]{2,1,0:T(8,128)} %bitcast.3), channel_id=1, source_target_pairs={{8,0},{16,8},{24,16},{9,1},{17,9},{25,17},{10,2},{18,10},{26,18},{... | collective-permute-start | bytes 2752520 | tf_op jit(solution)/shard_map/ppermute | solution.py:71
  10.5 1.5 %collective-permute-start.4 = (f32[8,4,224]{2,1,0:T(4,128)S(1)}, f32[8,4,224]{2,1,0:T(4,128)S(1)}, u32[]{:S(2)}, u32[]{:S(2)}) collective-permute-start(f32[8,4,224]{2,1,0:T(4,128)S(1)} %get-tuple-element.12), channel_id=1, source_target_pairs={{0,1},{1,2},{2,3},{3,4},{4,5},{5,6},{6,7},{8,9},{9,10},{10,11},{11... | collective-permute-start | bytes 86024 | tf_op jit(solution)/shard_map/ppermute | solution.py:98
  11.9 1.3 %collective-permute-start.5 = (f32[8,4,224]{2,1,0:T(4,128)S(1)}, f32[8,4,224]{2,1,0:T(4,128)S(1)}, u32[]{:S(2)}, u32[]{:S(2)}) collective-permute-start(f32[8,4,224]{2,1,0:T(4,128)S(1)} %get-tuple-element.13), channel_id=1, source_target_pairs={{1,0},{2,1},{3,2},{4,3},{5,4},{6,5},{7,6},{9,8},{10,9},{11,10},{12... | collective-permute-start | bytes 86024 | tf_op jit(solution)/shard_map/ppermute | solution.py:99
  14.1 17.7 %collective-permute-done = f32[16,64,224]{2,1,0:T(8,128)S(1)} collective-permute-done((f32[16,64,224]{2,1,0:T(8,128)}, f32[16,64,224]{2,1,0:T(8,128)S(1)}, u32[]{:S(2)}, u32[]{:S(2)}) %collective-permute-start) | collective-permute-done | bytes 917536 | tf_op jit(solution)/shard_map/ppermute | solution.py:71
  31.8 4.2 %collective-permute-done.1 = f32[16,64,224]{2,1,0:T(8,128)} collective-permute-done((f32[16,64,224]{2,1,0:T(8,128)}, f32[16,64,224]{2,1,0:T(8,128)}, u32[]{:S(2)}, u32[]{:S(2)}) %collective-permute-start.1) | collective-permute-done | bytes 917536 | tf_op jit(solution)/shard_map/ppermute | solution.py:71
  36.8 1.3 %collective-permute-start.2 = (f32[8,4,224]{2,1,0:T(4,128)S(1)}, f32[8,4,224]{2,1,0:T(4,128)S(1)}, u32[]{:S(2)}, u32[]{:S(2)}) collective-permute-start(f32[8,4,224]{2,1,0:T(4,128)S(1)} %get-tuple-element.14), channel_id=1, source_target_pairs={{0,1},{1,2},{2,3},{3,4},{4,5},{5,6},{6,7},{8,9},{9,10},{10,11},{11... | collective-permute-start | bytes 86024 | tf_op jit(solution)/shard_map/ppermute | solution.py:101
  38.1 1.3 %collective-permute-start.3 = (f32[8,4,224]{2,1,0:T(4,128)S(1)}, f32[8,4,224]{2,1,0:T(4,128)S(1)}, u32[]{:S(2)}, u32[]{:S(2)}) collective-permute-start(f32[8,4,224]{2,1,0:T(4,128)S(1)} %get-tuple-element.15), channel_id=1, source_target_pairs={{1,0},{2,1},{3,2},{4,3},{5,4},{6,5},{7,6},{9,8},{10,9},{11,10},{12... | collective-permute-start | bytes 86024 | tf_op jit(solution)/shard_map/ppermute | solution.py:102
  39.4 3.5 %collective-permute-done.3 = f32[8,4,224]{2,1,0:T(4,128)S(1)} collective-permute-done((f32[8,4,224]{2,1,0:T(4,128)S(1)}, f32[8,4,224]{2,1,0:T(4,128)S(1)}, u32[]{:S(2)}, u32[]{:S(2)}) %collective-permute-start.3) | collective-permute-done | bytes 28704 | tf_op jit(solution)/shard_map/ppermute | solution.py:102
  43.0 1.8 %maximum_maximum_fusion = f32[16,264,224]{2,1,0:T(8,128)S(1)} fusion(f32[4,4,224]{2,1,0:T(4,128)S(1)} %get-tuple-element.21, f32[4,256,224]{2,1,0:T(8,128)} %bitcast.4, f32[4,4,224]{2,1,0:T(4,128)S(1)} %get-tuple-element.19, f32[8,4,224]{2,1,0:T(4,128)S(1)} %collective-permute-done.5, f32[8,256,224]{2,1,0:T(8,128)S(1)} %bitcast.22, ...), kind=kLoop, calls=%fused_computation | loop fusion | flops 7569408 | bytes 7569408 | tf_op jit(solution)/shard_map/concatenate | solution.py:103
  46.1 1.4 %broadcast_multiply_fusion.1 = (f32[15,263,224]{2,1,0:T(8,128)S(1)}, f32[15,263,224]{2,1,0:T(8,128)S(1)}) fusion(f32[15,263]{1,0:T(8,128)S(1)} %add_rsqrt_fusion.3, f32[16,264,224]{2,1,0:T(8,128)S(1)} %maximum_maximum_fusion), kind=kLoop, calls=%fused_computation.46 | loop fusion | flops 3534720 | bytes 17689380 | tf_op jit(solution)/shard_map/mul | solution.py:125
  47.5 2.6 %fusion.3 = f32[14,262,224]{2,1,0:T(8,128)S(1)} fusion(f32[15,263,224]{2,1,0:T(8,128)S(1)} %get-tuple-element.5, f32[15,263,224]{2,1,0:T(8,128)S(1)} %get-tuple-element.4, f32[16,264,224]{2,1,0:T(8,128)S(1)} %maximum_maximum_fusion, pred[14,262]{1,0:T(8,128)(4,1)S(1)} %broadcast_and_fusion), kind=kLoop, calls=%fused_computation.8 | loop fusion | flops 7394688 | bytes 19722836 | tf_op jit(solution)/shard_map/jit(_where)/select_n | solution.py:130
  52.5 2.4 %fusion.6 = f32[12,260,224]{2,1,0:T(8,128)S(1)} fusion(f32[16,264,224]{2,1,0:T(8,128)S(1)} %maximum_maximum_fusion, f32[13,261,224]{2,1,0:T(8,128)S(1)} %get-tuple-element.7, f32[13,261,224]{2,1,0:T(8,128)S(1)} %get-tuple-element.6, f32[14,262,224]{2,1,0:T(8,128)S(1)} %fusion.3, pred[12,260]{1,0:T(8,128)(4,1)S(1)} %broadcast_and_fusion.1), kind=kLoop, calls=%fused_computation.17 | loop fusion | flops 6289920 | bytes 19571760 | tf_op jit(solution)/shard_map/jit(_where)/select_n | solution.py:130
  56.8 2.4 %fusion.11 = f32[10,258,224]{2,1,0:T(8,128)S(1)} fusion(f32[16,264,224]{2,1,0:T(8,128)S(1)} %maximum_maximum_fusion, f32[11,259,224]{2,1,0:T(8,128)S(1)} %get-tuple-element.9, f32[11,259,224]{2,1,0:T(8,128)S(1)} %get-tuple-element.8, f32[12,260,224]{2,1,0:T(8,128)S(1)} %fusion.6, pred[10,258]{1,0:T(8,128)(4,1)S(1)} %broadcast_and_fusion.2), kind=kLoop, calls=%fused_computation.29 | loop fusion | flops 5201280 | bytes 16184340 | tf_op jit(solution)/shard_map/jit(_where)/select_n | solution.py:130
  61.6 1.5 %fusion.17 = f32[8,256,224]{2,1,0:T(8,128)S(1)} fusion(f32[9,257,224]{2,1,0:T(8,128)S(1)} %get-tuple-element.11, f32[9,257,224]{2,1,0:T(8,128)S(1)} %get-tuple-element.10, f32[10,258,224]{2,1,0:T(8,128)S(1)} %fusion.11, pred[8,256]{1,0:T(8,128)(4,1)S(1)} %broadcast_and_fusion.3, f32[224,8,256]{0,2,1:T(8,128)S(1)} %copy-done.1), kind=kLoop, calls=%fused_computation.42 | loop fusion | flops 4128768 | bytes 12847104 | tf_op jit(solution)/shard_map/jit(_where)/select_n | solution.py:130
  63.1 3.5 %convolution_bitcast_fusion = f32[224,224]{1,0:T(8,128)S(1)} fusion(f32[8,256,224]{2,1,0:T(8,128)S(1)} %fusion.17), kind=kOutput, calls=%fused_computation.53 | convolution fusion | flops 1233125376 | bytes 2035712 | tf_op jit(solution)/shard_map/dot_general | solution.py:207
  66.6 2.7 %collective-permute-start.6 = (f32[112,224]{1,0:T(8,128)S(1)}, f32[112,224]{1,0:T(8,128)S(1)}, u32[]{:S(2)}, u32[]{:S(2)}) collective-permute-start(f32[112,224]{1,0:T(8,128)S(1)} %slice_select_fusion), channel_id=1, source_target_pairs={{0,1},{1,0},{2,3},{3,2},{4,5},{5,4},{6,7},{7,6},{8,9},{9,8},{10,11... | collective-permute-start | bytes 301064 | tf_op jit(solution)/shard_map/ppermute | solution.py:44
  70.3 2.5 %collective-permute-start.7 = (f32[112,224]{1,0:T(8,128)S(1)}, f32[112,224]{1,0:T(8,128)S(1)}, u32[]{:S(2)}, u32[]{:S(2)}) collective-permute-start(f32[112,224]{1,0:T(8,128)S(1)} %select_add_fusion), channel_id=1, source_target_pairs={{0,2},{1,3},{2,0},{3,1},{4,6},{5,7},{6,4},{7,5},{8,10},{9,11},{10,... | collective-permute-start | bytes 301064 | tf_op jit(solution)/shard_map/ppermute | solution.py:27
  72.8 3.7 %collective-permute-done.7 = f32[112,224]{1,0:T(8,128)S(1)} collective-permute-done((f32[112,224]{1,0:T(8,128)S(1)}, f32[112,224]{1,0:T(8,128)S(1)}, u32[]{:S(2)}, u32[]{:S(2)}) %collective-permute-start.7) | collective-permute-done | bytes 100384 | tf_op jit(solution)/shard_map/ppermute | solution.py:27
  77.4 4.0 %collective-permute-done.8 = f32[112,224]{1,0:T(8,128)S(1)} collective-permute-done((f32[112,224]{1,0:T(8,128)S(1)}, f32[112,224]{1,0:T(8,128)S(1)}, u32[]{:S(2)}, u32[]{:S(2)}) %collective-permute-start.8) | collective-permute-done | bytes 100384 | tf_op jit(solution)/shard_map/ppermute | solution.py:27
  81.4 1.6 %collective-permute-start.9 = (f32[112,224]{1,0:T(8,128)S(1)}, f32[112,224]{1,0:T(8,128)S(1)}, u32[]{:S(2)}, u32[]{:S(2)}) collective-permute-start(f32[112,224]{1,0:T(8,128)S(1)} %add.140), channel_id=1, source_target_pairs={{0,8},{8,0},{16,24},{24,16},{1,9},{9,1},{17,25},{25,17},{2,10},{10... | collective-permute-start | bytes 301064 | tf_op jit(solution)/shard_map/ppermute | solution.py:27
  83.0 3.3 %collective-permute-done.9 = f32[112,224]{1,0:T(8,128)S(1)} collective-permute-done((f32[112,224]{1,0:T(8,128)S(1)}, f32[112,224]{1,0:T(8,128)S(1)}, u32[]{:S(2)}, u32[]{:S(2)}) %collective-permute-start.9) | collective-permute-done | bytes 100384 | tf_op jit(solution)/shard_map/ppermute | solution.py:27
  86.3 2.6 %collective-permute-start.10 = (f32[112,224]{1,0:T(8,128)S(1)}, f32[112,224]{1,0:T(8,128)S(1)}, u32[]{:S(2)}, u32[]{:S(2)}) collective-permute-start(f32[112,224]{1,0:T(8,128)S(1)} %add.141), channel_id=1, source_target_pairs={{0,16},{8,24},{16,0},{24,8},{1,17},{9,25},{17,1},{25,9},{2,18},{10... | collective-permute-start | bytes 301064 | tf_op jit(solution)/shard_map/ppermute | solution.py:27
  88.9 4.4 %collective-permute-done.10 = f32[112,224]{1,0:T(8,128)S(1)} collective-permute-done((f32[112,224]{1,0:T(8,128)S(1)}, f32[112,224]{1,0:T(8,128)S(1)}, u32[]{:S(2)}, u32[]{:S(2)}) %collective-permute-start.10) | collective-permute-done | bytes 100384 | tf_op jit(solution)/shard_map/ppermute | solution.py:27
  94.1 1.8 %copy.6 = f32[224,8,256]{2,1,0:T(8,128)} copy(f32[224,8,256]{0,2,1:T(8,128)S(1)} %bitcast.18) | data formatting | bytes 3670016
  96.6 6.4 %shard_map.41.basis_ref = f32[224,16]{1,0:T(8,128)} custom-call(f32[224,224]{1,0:T(8,128)} %maximum_select_fusion.gram_ref, f32[224,16]{1,0:T(8,128)} %copy.5.basis_ref), custom_call_target="tpu_custom_call" | custom-call | flops 22937600 | bytes 229376 | tf_op jit(solution)/shard_map/pallas_call | solution.py:172
  103.0 6.4 %shard_map.42 = f32[224,16]{1,0:T(8,128)} custom-call(f32[224,224]{1,0:T(8,128)} %maximum_select_fusion.gram_ref, f32[224,16]{1,0:T(8,128)} %shard_map.41.basis_ref), custom_call_target="tpu_custom_call" | custom-call | flops 22937600 | bytes 229376 | tf_op jit(solution)/shard_map/pallas_call | solution.py:172
  109.4 2.8 %fusion.25 = f32[2048,16]{1,0:T(8,128)S(1)} fusion(f32[2048,224]{1,0:T(8,128)S(1)} %bitcast.19, f32[224,16]{1,0:T(8,128)} %shard_map.42), kind=kOutput, calls=%fused_computation.76 | convolution fusion | flops 88080384 | bytes 1980416 | tf_op jit(solution)/shard_map/dot_general | solution.py:218
  112.2 1.6 %fusion.26 = f32[224,2048]{1,0:T(8,128)S(1)} fusion(f32[224,16]{1,0:T(8,128)S(1)} %copy-done.2, f32[2048,16]{1,0:T(8,128)S(1)} %fusion.25), kind=kOutput, calls=%fused_computation.77 | convolution fusion | flops 88080384 | bytes 1980416 | tf_op jit(solution)/shard_map/dot_general | solution.py:219
  113.8 2.0 %copy.7 = f32[28,8,8,256]{3,2,1,0:T(8,128)} copy(f32[28,8,8,256]{3,1,2,0:T(8,128)S(1)} %bitcast.23) | data formatting | bytes 3670016
  (52 shorter events, 13.2 us)
Async XLA Ops:
  2.5 40.4 %copy-start = (f32[224,8,256]{0,2,1:T(8,128)}, f32[224,8,256]{0,2,1:T(8,128)S(1)}, u32[]{:S(2)}) copy-start(f32[224,8,256]{0,2,1:T(8,128)S(1)} %copy.4) | copy-start | bytes 5505028
  4.1 27.6 %collective-permute-start = (f32[16,64,224]{2,1,0:T(8,128)}, f32[16,64,224]{2,1,0:T(8,128)S(1)}, u32[]{:S(2)}, u32[]{:S(2)}) collective-permute-start(f32[16,64,224]{2,1,0:T(8,128)} %bitcast.1), channel_id=1, source_target_pairs={{0,8},{8,16},{16,24},{1,9},{9,17},{17,25},{2,10},{10,18},{18,26},{... | collective-permute-start | bytes 2752520 | tf_op jit(solution)/shard_map/ppermute | solution.py:71
  9.1 26.8 %collective-permute-start.1 = (f32[16,64,224]{2,1,0:T(8,128)}, f32[16,64,224]{2,1,0:T(8,128)}, u32[]{:S(2)}, u32[]{:S(2)}) collective-permute-start(f32[16,64,224]{2,1,0:T(8,128)} %bitcast.3), channel_id=1, source_target_pairs={{8,0},{16,8},{24,16},{9,1},{17,9},{25,17},{10,2},{18,10},{26,18},{... | collective-permute-start | bytes 2752520 | tf_op jit(solution)/shard_map/ppermute | solution.py:71
  10.5 32.5 %collective-permute-start.4 = (f32[8,4,224]{2,1,0:T(4,128)S(1)}, f32[8,4,224]{2,1,0:T(4,128)S(1)}, u32[]{:S(2)}, u32[]{:S(2)}) collective-permute-start(f32[8,4,224]{2,1,0:T(4,128)S(1)} %get-tuple-element.12), channel_id=1, source_target_pairs={{0,1},{1,2},{2,3},{3,4},{4,5},{5,6},{6,7},{8,9},{9,10},{10,11},{11... | collective-permute-start | bytes 86024 | tf_op jit(solution)/shard_map/ppermute | solution.py:98
  11.9 31.0 %collective-permute-start.5 = (f32[8,4,224]{2,1,0:T(4,128)S(1)}, f32[8,4,224]{2,1,0:T(4,128)S(1)}, u32[]{:S(2)}, u32[]{:S(2)}) collective-permute-start(f32[8,4,224]{2,1,0:T(4,128)S(1)} %get-tuple-element.13), channel_id=1, source_target_pairs={{1,0},{2,1},{3,2},{4,3},{5,4},{6,5},{7,6},{9,8},{10,9},{11,10},{12... | collective-permute-start | bytes 86024 | tf_op jit(solution)/shard_map/ppermute | solution.py:99
  36.8 2.7 %collective-permute-start.2 = (f32[8,4,224]{2,1,0:T(4,128)S(1)}, f32[8,4,224]{2,1,0:T(4,128)S(1)}, u32[]{:S(2)}, u32[]{:S(2)}) collective-permute-start(f32[8,4,224]{2,1,0:T(4,128)S(1)} %get-tuple-element.14), channel_id=1, source_target_pairs={{0,1},{1,2},{2,3},{3,4},{4,5},{5,6},{6,7},{8,9},{9,10},{10,11},{11... | collective-permute-start | bytes 86024 | tf_op jit(solution)/shard_map/ppermute | solution.py:101
  38.1 4.8 %collective-permute-start.3 = (f32[8,4,224]{2,1,0:T(4,128)S(1)}, f32[8,4,224]{2,1,0:T(4,128)S(1)}, u32[]{:S(2)}, u32[]{:S(2)}) collective-permute-start(f32[8,4,224]{2,1,0:T(4,128)S(1)} %get-tuple-element.15), channel_id=1, source_target_pairs={{1,0},{2,1},{3,2},{4,3},{5,4},{6,5},{7,6},{9,8},{10,9},{11,10},{12... | collective-permute-start | bytes 86024 | tf_op jit(solution)/shard_map/ppermute | solution.py:102
  60.0 1.6 %copy-start.1 = (f32[224,8,256]{0,2,1:T(8,128)S(1)}, f32[224,8,256]{0,2,1:T(8,128)}, u32[]{:S(2)}) copy-start(f32[224,8,256]{0,2,1:T(8,128)} %copy-done) | copy-start | bytes 5505028
  63.1 30.2 %copy-start.3 = (f32[224,16]{0,1:T(8,128)S(1)}, f32[224,16]{0,1:T(8,128)}, u32[]{:S(2)}) copy-start(f32[224,16]{0,1:T(8,128)} %param.3) | copy-start | bytes 43012
  66.6 3.7 %collective-permute-start.6 = (f32[112,224]{1,0:T(8,128)S(1)}, f32[112,224]{1,0:T(8,128)S(1)}, u32[]{:S(2)}, u32[]{:S(2)}) collective-permute-start(f32[112,224]{1,0:T(8,128)S(1)} %slice_select_fusion), channel_id=1, source_target_pairs={{0,1},{1,0},{2,3},{3,2},{4,5},{5,4},{6,7},{7,6},{8,9},{9,8},{10,11... | collective-permute-start | bytes 301064 | tf_op jit(solution)/shard_map/ppermute | solution.py:44
  70.3 6.1 %collective-permute-start.7 = (f32[112,224]{1,0:T(8,128)S(1)}, f32[112,224]{1,0:T(8,128)S(1)}, u32[]{:S(2)}, u32[]{:S(2)}) collective-permute-start(f32[112,224]{1,0:T(8,128)S(1)} %select_add_fusion), channel_id=1, source_target_pairs={{0,2},{1,3},{2,0},{3,1},{4,6},{5,7},{6,4},{7,5},{8,10},{9,11},{10,... | collective-permute-start | bytes 301064 | tf_op jit(solution)/shard_map/ppermute | solution.py:27
  76.5 4.9 %collective-permute-start.8 = (f32[112,224]{1,0:T(8,128)S(1)}, f32[112,224]{1,0:T(8,128)S(1)}, u32[]{:S(2)}, u32[]{:S(2)}) collective-permute-start(f32[112,224]{1,0:T(8,128)S(1)} %add.139), channel_id=1, source_target_pairs={{0,4},{1,5},{2,6},{3,7},{4,0},{5,1},{6,2},{7,3},{8,12},{9,13},{10,... | collective-permute-start | bytes 301064 | tf_op jit(solution)/shard_map/ppermute | solution.py:27
  81.4 4.9 %collective-permute-start.9 = (f32[112,224]{1,0:T(8,128)S(1)}, f32[112,224]{1,0:T(8,128)S(1)}, u32[]{:S(2)}, u32[]{:S(2)}) collective-permute-start(f32[112,224]{1,0:T(8,128)S(1)} %add.140), channel_id=1, source_target_pairs={{0,8},{8,0},{16,24},{24,16},{1,9},{9,1},{17,25},{25,17},{2,10},{10... | collective-permute-start | bytes 301064 | tf_op jit(solution)/shard_map/ppermute | solution.py:27
  86.3 7.0 %collective-permute-start.10 = (f32[112,224]{1,0:T(8,128)S(1)}, f32[112,224]{1,0:T(8,128)S(1)}, u32[]{:S(2)}, u32[]{:S(2)}) collective-permute-start(f32[112,224]{1,0:T(8,128)S(1)} %add.141), channel_id=1, source_target_pairs={{0,16},{8,24},{16,0},{24,8},{1,17},{9,25},{17,1},{25,9},{2,18},{10... | collective-permute-start | bytes 301064 | tf_op jit(solution)/shard_map/ppermute | solution.py:27
  93.3 2.6 %collective-permute-start.11 = (f32[112,224]{1,0:T(8,128)S(1)}, f32[112,224]{1,0:T(8,128)S(1)}, u32[]{:S(2)}, u32[]{:S(2)}) collective-permute-start(f32[112,224]{1,0:T(8,128)S(1)} %add.142), channel_id=1, source_target_pairs={{0,1},{1,0},{2,3},{3,2},{4,5},{5,4},{6,7},{7,6},{8,9},{9,8},{10,11... | collective-permute-start | bytes 301064 | tf_op jit(solution)/shard_map/ppermute | solution.py:46
  109.4 2.8 %copy-start.2 = (f32[224,16]{1,0:T(8,128)S(1)}, f32[224,16]{1,0:T(8,128)}, u32[]{:S(2)}) copy-start(f32[224,16]{1,0:T(8,128)} %shard_map.42) | copy-start | bytes 43012

commit v13 on v12

--- a/solution.py
+++ b/solution.py
@@ -161,11 +161,14 @@
 
 
 def subspace_kernel(gram_ref, basis_ref, out_ref):
-    product = jnp.dot(
-        gram_ref[...], basis_ref[...],
-        precision=lax.Precision.HIGHEST, preferred_element_type=jnp.float32,
-    )
-    out_ref[...] = cholesky_qr(cholesky_qr(product))
+    basis = basis_ref[...]
+    for turn in range(SUBIT):
+        product = jnp.dot(
+            gram_ref[...], basis,
+            precision=lax.Precision.HIGHEST, preferred_element_type=jnp.float32,
+        )
+        basis = cholesky_qr(cholesky_qr(product))
+    out_ref[...] = basis
 
 
 def subspace_step(gram_full, basis):
@@ -173,8 +176,8 @@
         subspace_kernel,
         out_shape=jax.ShapeDtypeStruct(basis.shape, jnp.float32),
         cost_estimate=pl.CostEstimate(
-            flops=2 * gram_full.shape[0] * gram_full.size + 8 * basis.size * basis.shape[1],
-            transcendentals=2 * basis.shape[1],
+            flops=SUBIT * (2 * gram_full.shape[0] * gram_full.size + 8 * basis.size * basis.shape[1]),
+            transcendentals=SUBIT * 2 * basis.shape[1],
             bytes_accessed=4 * (gram_full.size + 2 * basis.size),
         ),
     )(gram_full, basis)
@@ -213,8 +216,7 @@
     )
     gram_full = paired_sum(local_gram, order)
     basis_now = start_basis
-    for turn in range(SUBIT):
-        basis_now = subspace_step(gram_full, basis_now)
+    basis_now = subspace_step(gram_full, basis_now)
     coeffs = jnp.dot(flat_cells, basis_now, precision=lax.Precision.HIGHEST)
     lowrank = lax.dot_general(
         basis_now,

time: 116 us -> 115 us (level)
  Pallas kernels: 12.8 us -> 11.1 us
    pallas_call x2 -> x1, Pallas kernels: 12.8 us -> 11.1 us  [subspace_step(): pl.pallas_call(subspace_kernel, out_shape=jax.ShapeDtypeStruct(basis.shap...]
where the time goes in v13:
time: 115 us; the launch traced here: 114 us
  waiting for transfers between devices  41.6 us (36%)
  starting transfers between devices  21.9 us (19%)
  other arithmetic  21 us (18%)
  Pallas kernels  11.1 us (10%)
  local copies, waits for them, and re-layouts  9.73 us (8%)
  matrix products  7.86 us (7%)
    ppermute x2, waiting for transfers between devices, flat_permute(): return lax.ppermute(flat, axis, pairs).reshape(block.shape)  21.9 us
    ppermute x4, waiting for transfers between devices, butterfly_sum(): partner = lax.ppermute(value, axis, [(i, i ^ step) for i in range(count)])  15.3 us
    pallas_call x1, Pallas kernels, subspace_step(): pl.pallas_call(subspace_kernel, out_shape=jax.ShapeDtypeStruct(basis.shap...  11.1 us
    select_n x4, other arithmetic, sweep(): return jnp.where(keep, new, 0.0)  8.95 us
    ppermute x4, starting transfers between devices, butterfly_sum(): partner = lax.ppermute(value, axis, [(i, i ^ step) for i in range(count)])  7.58 us
    unnamed x12, local copies, waits for them, and re-layouts  7.35 us
    ppermute x2, starting transfers between devices, flat_permute(): return lax.ppermute(flat, axis, pairs).reshape(block.shape)  6.27 us
    mul x4, other arithmetic, sweep(): flux_col = weight * diff_col  4.17 us
  transfers between devices with their start and end apart: 12, of which 8 were waited for; matrix products, arithmetic and copies ran while one was open for 4% of the time, Pallas kernels for 0%

profile of v13, /device:TPU:0, one launch (start us, length us, event | category | flops | bytes accessed | tf_op | source)
XLA Modules:
  0.0 114.2 jit_solution(8776292342045322004)
XLA Ops:
  0.6 1.9 %copy.4 = f32[224,8,256]{0,2,1:T(8,128)S(1)} copy(f32[224,8,256]{2,1,0:T(8,128)} %param.2) | data formatting | bytes 3670016 | tf_op args[0]
  2.5 1.8 %fusion.22 = (f32[4,256,224]{2,1,0:T(8,128)}, f32[4,256,224]{2,1,0:T(8,128)}) fusion(f32[8,256,224]{2,1,0:T(8,128)S(1)} %bitcast.20), kind=kLoop, calls=%fused_computation.73 | loop fusion | bytes 3670016 | tf_op jit(solution)/shard_map/slice | solution.py:96
  4.3 5.0 %collective-permute-start = (f32[16,64,224]{2,1,0:T(8,128)}, f32[16,64,224]{2,1,0:T(8,128)S(1)}, u32[]{:S(2)}, u32[]{:S(2)}) collective-permute-start(f32[16,64,224]{2,1,0:T(8,128)} %bitcast.1), channel_id=1, source_target_pairs={{0,8},{8,16},{16,24},{1,9},{9,17},{17,25},{2,10},{10,18},{18,26},{... | collective-permute-start | bytes 2752520 | tf_op jit(solution)/shard_map/ppermute | solution.py:71
  9.3 1.3 %collective-permute-start.1 = (f32[16,64,224]{2,1,0:T(8,128)}, f32[16,64,224]{2,1,0:T(8,128)}, u32[]{:S(2)}, u32[]{:S(2)}) collective-permute-start(f32[16,64,224]{2,1,0:T(8,128)} %bitcast.3), channel_id=1, source_target_pairs={{8,0},{16,8},{24,16},{9,1},{17,9},{25,17},{10,2},{18,10},{26,18},{... | collective-permute-start | bytes 2752520 | tf_op jit(solution)/shard_map/ppermute | solution.py:71
  10.6 1.5 %collective-permute-start.4 = (f32[8,4,224]{2,1,0:T(4,128)S(1)}, f32[8,4,224]{2,1,0:T(4,128)S(1)}, u32[]{:S(2)}, u32[]{:S(2)}) collective-permute-start(f32[8,4,224]{2,1,0:T(4,128)S(1)} %get-tuple-element.12), channel_id=1, source_target_pairs={{0,1},{1,2},{2,3},{3,4},{4,5},{5,6},{6,7},{8,9},{9,10},{10,11},{11... | collective-permute-start | bytes 86024 | tf_op jit(solution)/shard_map/ppermute | solution.py:98
  12.1 1.3 %collective-permute-start.5 = (f32[8,4,224]{2,1,0:T(4,128)S(1)}, f32[8,4,224]{2,1,0:T(4,128)S(1)}, u32[]{:S(2)}, u32[]{:S(2)}) collective-permute-start(f32[8,4,224]{2,1,0:T(4,128)S(1)} %get-tuple-element.13), channel_id=1, source_target_pairs={{1,0},{2,1},{3,2},{4,3},{5,4},{6,5},{7,6},{9,8},{10,9},{11,10},{12... | collective-permute-start | bytes 86024 | tf_op jit(solution)/shard_map/ppermute | solution.py:99
  14.2 17.7 %collective-permute-done = f32[16,64,224]{2,1,0:T(8,128)S(1)} collective-permute-done((f32[16,64,224]{2,1,0:T(8,128)}, f32[16,64,224]{2,1,0:T(8,128)S(1)}, u32[]{:S(2)}, u32[]{:S(2)}) %collective-permute-start) | collective-permute-done | bytes 917536 | tf_op jit(solution)/shard_map/ppermute | solution.py:71
  31.9 4.2 %collective-permute-done.1 = f32[16,64,224]{2,1,0:T(8,128)} collective-permute-done((f32[16,64,224]{2,1,0:T(8,128)}, f32[16,64,224]{2,1,0:T(8,128)}, u32[]{:S(2)}, u32[]{:S(2)}) %collective-permute-start.1) | collective-permute-done | bytes 917536 | tf_op jit(solution)/shard_map/ppermute | solution.py:71
  36.9 1.3 %collective-permute-start.2 = (f32[8,4,224]{2,1,0:T(4,128)S(1)}, f32[8,4,224]{2,1,0:T(4,128)S(1)}, u32[]{:S(2)}, u32[]{:S(2)}) collective-permute-start(f32[8,4,224]{2,1,0:T(4,128)S(1)} %get-tuple-element.14), channel_id=1, source_target_pairs={{0,1},{1,2},{2,3},{3,4},{4,5},{5,6},{6,7},{8,9},{9,10},{10,11},{11... | collective-permute-start | bytes 86024 | tf_op jit(solution)/shard_map/ppermute | solution.py:101
  38.3 1.3 %collective-permute-start.3 = (f32[8,4,224]{2,1,0:T(4,128)S(1)}, f32[8,4,224]{2,1,0:T(4,128)S(1)}, u32[]{:S(2)}, u32[]{:S(2)}) collective-permute-start(f32[8,4,224]{2,1,0:T(4,128)S(1)} %get-tuple-element.15), channel_id=1, source_target_pairs={{1,0},{2,1},{3,2},{4,3},{5,4},{6,5},{7,6},{9,8},{10,9},{11,10},{12... | collective-permute-start | bytes 86024 | tf_op jit(solution)/shard_map/ppermute | solution.py:102
  39.6 3.5 %collective-permute-done.3 = f32[8,4,224]{2,1,0:T(4,128)S(1)} collective-permute-done((f32[8,4,224]{2,1,0:T(4,128)S(1)}, f32[8,4,224]{2,1,0:T(4,128)S(1)}, u32[]{:S(2)}, u32[]{:S(2)}) %collective-permute-start.3) | collective-permute-done | bytes 28704 | tf_op jit(solution)/shard_map/ppermute | solution.py:102
  43.1 1.8 %maximum_maximum_fusion = f32[16,264,224]{2,1,0:T(8,128)S(1)} fusion(f32[4,4,224]{2,1,0:T(4,128)S(1)} %get-tuple-element.21, f32[4,256,224]{2,1,0:T(8,128)} %bitcast.4, f32[4,4,224]{2,1,0:T(4,128)S(1)} %get-tuple-element.19, f32[8,4,224]{2,1,0:T(4,128)S(1)} %collective-permute-done.5, f32[8,256,224]{2,1,0:T(8,128)S(1)} %bitcast.22, ...), kind=kLoop, calls=%fused_computation | loop fusion | flops 7569408 | bytes 7569408 | tf_op jit(solution)/shard_map/concatenate | solution.py:103
  45.0 1.3 %add_reduce_fusion = f32[15,263]{1,0:T(8,128)S(1)} fusion(f32[16,264,224]{2,1,0:T(8,128)S(1)} %maximum_maximum_fusion), kind=kLoop, calls=%fused_computation.3 | loop fusion | flops 5298135 | bytes 10619940 | tf_op jit(solution)/shard_map/reduce_sum | solution.py:123
  46.2 1.4 %broadcast_multiply_fusion.1 = (f32[15,263,224]{2,1,0:T(8,128)S(1)}, f32[15,263,224]{2,1,0:T(8,128)S(1)}) fusion(f32[15,263]{1,0:T(8,128)S(1)} %add_rsqrt_fusion.3, f32[16,264,224]{2,1,0:T(8,128)S(1)} %maximum_maximum_fusion), kind=kLoop, calls=%fused_computation.46 | loop fusion | flops 3534720 | bytes 17689380 | tf_op jit(solution)/shard_map/mul | solution.py:125
  47.6 2.6 %fusion.3 = f32[14,262,224]{2,1,0:T(8,128)S(1)} fusion(f32[15,263,224]{2,1,0:T(8,128)S(1)} %get-tuple-element.5, f32[15,263,224]{2,1,0:T(8,128)S(1)} %get-tuple-element.4, f32[16,264,224]{2,1,0:T(8,128)S(1)} %maximum_maximum_fusion, pred[14,262]{1,0:T(8,128)(4,1)S(1)} %broadcast_and_fusion), kind=kLoop, calls=%fused_computation.8 | loop fusion | flops 7394688 | bytes 19722836 | tf_op jit(solution)/shard_map/jit(_where)/select_n | solution.py:130
  52.6 2.4 %fusion.6 = f32[12,260,224]{2,1,0:T(8,128)S(1)} fusion(f32[16,264,224]{2,1,0:T(8,128)S(1)} %maximum_maximum_fusion, f32[13,261,224]{2,1,0:T(8,128)S(1)} %get-tuple-element.7, f32[13,261,224]{2,1,0:T(8,128)S(1)} %get-tuple-element.6, f32[14,262,224]{2,1,0:T(8,128)S(1)} %fusion.3, pred[12,260]{1,0:T(8,128)(4,1)S(1)} %broadcast_and_fusion.1), kind=kLoop, calls=%fused_computation.17 | loop fusion | flops 6289920 | bytes 19571760 | tf_op jit(solution)/shard_map/jit(_where)/select_n | solution.py:130
  56.9 2.4 %fusion.11 = f32[10,258,224]{2,1,0:T(8,128)S(1)} fusion(f32[16,264,224]{2,1,0:T(8,128)S(1)} %maximum_maximum_fusion, f32[11,259,224]{2,1,0:T(8,128)S(1)} %get-tuple-element.9, f32[11,259,224]{2,1,0:T(8,128)S(1)} %get-tuple-element.8, f32[12,260,224]{2,1,0:T(8,128)S(1)} %fusion.6, pred[10,258]{1,0:T(8,128)(4,1)S(1)} %broadcast_and_fusion.2), kind=kLoop, calls=%fused_computation.29 | loop fusion | flops 5201280 | bytes 16184340 | tf_op jit(solution)/shard_map/jit(_where)/select_n | solution.py:130
  61.8 1.5 %fusion.17 = f32[8,256,224]{2,1,0:T(8,128)S(1)} fusion(f32[9,257,224]{2,1,0:T(8,128)S(1)} %get-tuple-element.11, f32[9,257,224]{2,1,0:T(8,128)S(1)} %get-tuple-element.10, f32[10,258,224]{2,1,0:T(8,128)S(1)} %fusion.11, pred[8,256]{1,0:T(8,128)(4,1)S(1)} %broadcast_and_fusion.3, f32[224,8,256]{0,2,1:T(8,128)S(1)} %copy-done.1), kind=kLoop, calls=%fused_computation.42 | loop fusion | flops 4128768 | bytes 12847104 | tf_op jit(solution)/shard_map/jit(_where)/select_n | solution.py:130
  63.3 3.5 %convolution_bitcast_fusion = f32[224,224]{1,0:T(8,128)S(1)} fusion(f32[8,256,224]{2,1,0:T(8,128)S(1)} %fusion.17), kind=kOutput, calls=%fused_computation.53 | convolution fusion | flops 1233125376 | bytes 2035712 | tf_op jit(solution)/shard_map/dot_general | solution.py:210
  66.8 2.7 %collective-permute-start.6 = (f32[112,224]{1,0:T(8,128)S(1)}, f32[112,224]{1,0:T(8,128)S(1)}, u32[]{:S(2)}, u32[]{:S(2)}) collective-permute-start(f32[112,224]{1,0:T(8,128)S(1)} %slice_select_fusion), channel_id=1, source_target_pairs={{0,1},{1,0},{2,3},{3,2},{4,5},{5,4},{6,7},{7,6},{8,9},{9,8},{10,11... | collective-permute-start | bytes 301064 | tf_op jit(solution)/shard_map/ppermute | solution.py:44
  70.5 2.5 %collective-permute-start.7 = (f32[112,224]{1,0:T(8,128)S(1)}, f32[112,224]{1,0:T(8,128)S(1)}, u32[]{:S(2)}, u32[]{:S(2)}) collective-permute-start(f32[112,224]{1,0:T(8,128)S(1)} %select_add_fusion), channel_id=1, source_target_pairs={{0,2},{1,3},{2,0},{3,1},{4,6},{5,7},{6,4},{7,5},{8,10},{9,11},{10,... | collective-permute-start | bytes 301064 | tf_op jit(solution)/shard_map/ppermute | solution.py:27
  73.0 3.7 %collective-permute-done.7 = f32[112,224]{1,0:T(8,128)S(1)} collective-permute-done((f32[112,224]{1,0:T(8,128)S(1)}, f32[112,224]{1,0:T(8,128)S(1)}, u32[]{:S(2)}, u32[]{:S(2)}) %collective-permute-start.7) | collective-permute-done | bytes 100384 | tf_op jit(solution)/shard_map/ppermute | solution.py:27
  77.6 4.0 %collective-permute-done.8 = f32[112,224]{1,0:T(8,128)S(1)} collective-permute-done((f32[112,224]{1,0:T(8,128)S(1)}, f32[112,224]{1,0:T(8,128)S(1)}, u32[]{:S(2)}, u32[]{:S(2)}) %collective-permute-start.8) | collective-permute-done | bytes 100384 | tf_op jit(solution)/shard_map/ppermute | solution.py:27
  81.5 1.6 %collective-permute-start.9 = (f32[112,224]{1,0:T(8,128)S(1)}, f32[112,224]{1,0:T(8,128)S(1)}, u32[]{:S(2)}, u32[]{:S(2)}) collective-permute-start(f32[112,224]{1,0:T(8,128)S(1)} %add.140), channel_id=1, source_target_pairs={{0,8},{8,0},{16,24},{24,16},{1,9},{9,1},{17,25},{25,17},{2,10},{10... | collective-permute-start | bytes 301064 | tf_op jit(solution)/shard_map/ppermute | solution.py:27
  83.1 3.3 %collective-permute-done.9 = f32[112,224]{1,0:T(8,128)S(1)} collective-permute-done((f32[112,224]{1,0:T(8,128)S(1)}, f32[112,224]{1,0:T(8,128)S(1)}, u32[]{:S(2)}, u32[]{:S(2)}) %collective-permute-start.9) | collective-permute-done | bytes 100384 | tf_op jit(solution)/shard_map/ppermute | solution.py:27
  86.4 2.6 %collective-permute-start.10 = (f32[112,224]{1,0:T(8,128)S(1)}, f32[112,224]{1,0:T(8,128)S(1)}, u32[]{:S(2)}, u32[]{:S(2)}) collective-permute-start(f32[112,224]{1,0:T(8,128)S(1)} %add.141), channel_id=1, source_target_pairs={{0,16},{8,24},{16,0},{24,8},{1,17},{9,25},{17,1},{25,9},{2,18},{10... | collective-permute-start | bytes 301064 | tf_op jit(solution)/shard_map/ppermute | solution.py:27
  89.0 4.4 %collective-permute-done.10 = f32[112,224]{1,0:T(8,128)S(1)} collective-permute-done((f32[112,224]{1,0:T(8,128)S(1)}, f32[112,224]{1,0:T(8,128)S(1)}, u32[]{:S(2)}, u32[]{:S(2)}) %collective-permute-start.10) | collective-permute-done | bytes 100384 | tf_op jit(solution)/shard_map/ppermute | solution.py:27
  94.3 1.8 %copy.6 = f32[224,8,256]{2,1,0:T(8,128)} copy(f32[224,8,256]{0,2,1:T(8,128)S(1)} %bitcast.18) | data formatting | bytes 3670016
  96.7 11.1 %shard_map.41 = f32[224,16]{1,0:T(8,128)} custom-call(f32[224,224]{1,0:T(8,128)} %maximum_select_fusion.gram_ref, f32[224,16]{1,0:T(8,128)} %copy.5.basis_ref), custom_call_target="tpu_custom_call" | custom-call | flops 45875200 | bytes 229376 | tf_op jit(solution)/shard_map/pallas_call | solution.py:175
  107.8 2.8 %fusion.25 = f32[2048,16]{1,0:T(8,128)S(1)} fusion(f32[2048,224]{1,0:T(8,128)S(1)} %bitcast.19, f32[224,16]{1,0:T(8,128)} %shard_map.41), kind=kOutput, calls=%fused_computation.76 | convolution fusion | flops 88080384 | bytes 1980416 | tf_op jit(solution)/shard_map/dot_general | solution.py:220
  110.6 1.6 %fusion.26 = f32[224,2048]{1,0:T(8,128)S(1)} fusion(f32[224,16]{1,0:T(8,128)S(1)} %copy-done.2, f32[2048,16]{1,0:T(8,128)S(1)} %fusion.25), kind=kOutput, calls=%fused_computation.77 | convolution fusion | flops 88080384 | bytes 1980416 | tf_op jit(solution)/shard_map/dot_general | solution.py:221
  112.2 2.0 %copy.7 = f32[28,8,8,256]{3,2,1,0:T(8,128)} copy(f32[28,8,8,256]{3,1,2,0:T(8,128)S(1)} %bitcast.23) | data formatting | bytes 3670016
  (51 shorter events, 11.9 us)
Async XLA Ops:
  2.5 40.6 %copy-start = (f32[224,8,256]{0,2,1:T(8,128)}, f32[224,8,256]{0,2,1:T(8,128)S(1)}, u32[]{:S(2)}) copy-start(f32[224,8,256]{0,2,1:T(8,128)S(1)} %copy.4) | copy-start | bytes 5505028
  4.3 27.6 %collective-permute-start = (f32[16,64,224]{2,1,0:T(8,128)}, f32[16,64,224]{2,1,0:T(8,128)S(1)}, u32[]{:S(2)}, u32[]{:S(2)}) collective-permute-start(f32[16,64,224]{2,1,0:T(8,128)} %bitcast.1), channel_id=1, source_target_pairs={{0,8},{8,16},{16,24},{1,9},{9,17},{17,25},{2,10},{10,18},{18,26},{... | collective-permute-start | bytes 2752520 | tf_op jit(solution)/shard_map/ppermute | solution.py:71
  9.3 26.8 %collective-permute-start.1 = (f32[16,64,224]{2,1,0:T(8,128)}, f32[16,64,224]{2,1,0:T(8,128)}, u32[]{:S(2)}, u32[]{:S(2)}) collective-permute-start(f32[16,64,224]{2,1,0:T(8,128)} %bitcast.3), channel_id=1, source_target_pairs={{8,0},{16,8},{24,16},{9,1},{17,9},{25,17},{10,2},{18,10},{26,18},{... | collective-permute-start | bytes 2752520 | tf_op jit(solution)/shard_map/ppermute | solution.py:71
  10.6 32.5 %collective-permute-start.4 = (f32[8,4,224]{2,1,0:T(4,128)S(1)}, f32[8,4,224]{2,1,0:T(4,128)S(1)}, u32[]{:S(2)}, u32[]{:S(2)}) collective-permute-start(f32[8,4,224]{2,1,0:T(4,128)S(1)} %get-tuple-element.12), channel_id=1, source_target_pairs={{0,1},{1,2},{2,3},{3,4},{4,5},{5,6},{6,7},{8,9},{9,10},{10,11},{11... | collective-permute-start | bytes 86024 | tf_op jit(solution)/shard_map/ppermute | solution.py:98
  12.1 31.0 %collective-permute-start.5 = (f32[8,4,224]{2,1,0:T(4,128)S(1)}, f32[8,4,224]{2,1,0:T(4,128)S(1)}, u32[]{:S(2)}, u32[]{:S(2)}) collective-permute-start(f32[8,4,224]{2,1,0:T(4,128)S(1)} %get-tuple-element.13), channel_id=1, source_target_pairs={{1,0},{2,1},{3,2},{4,3},{5,4},{6,5},{7,6},{9,8},{10,9},{11,10},{12... | collective-permute-start | bytes 86024 | tf_op jit(solution)/shard_map/ppermute | solution.py:99
  36.9 2.7 %collective-permute-start.2 = (f32[8,4,224]{2,1,0:T(4,128)S(1)}, f32[8,4,224]{2,1,0:T(4,128)S(1)}, u32[]{:S(2)}, u32[]{:S(2)}) collective-permute-start(f32[8,4,224]{2,1,0:T(4,128)S(1)} %get-tuple-element.14), channel_id=1, source_target_pairs={{0,1},{1,2},{2,3},{3,4},{4,5},{5,6},{6,7},{8,9},{9,10},{10,11},{11... | collective-permute-start | bytes 86024 | tf_op jit(solution)/shard_map/ppermute | solution.py:101
  38.3 4.8 %collective-permute-start.3 = (f32[8,4,224]{2,1,0:T(4,128)S(1)}, f32[8,4,224]{2,1,0:T(4,128)S(1)}, u32[]{:S(2)}, u32[]{:S(2)}) collective-permute-start(f32[8,4,224]{2,1,0:T(4,128)S(1)} %get-tuple-element.15), channel_id=1, source_target_pairs={{1,0},{2,1},{3,2},{4,3},{5,4},{6,5},{7,6},{9,8},{10,9},{11,10},{12... | collective-permute-start | bytes 86024 | tf_op jit(solution)/shard_map/ppermute | solution.py:102
  60.2 1.6 %copy-start.1 = (f32[224,8,256]{0,2,1:T(8,128)S(1)}, f32[224,8,256]{0,2,1:T(8,128)}, u32[]{:S(2)}) copy-start(f32[224,8,256]{0,2,1:T(8,128)} %copy-done) | copy-start | bytes 5505028
  63.3 30.2 %copy-start.3 = (f32[224,16]{0,1:T(8,128)S(1)}, f32[224,16]{0,1:T(8,128)}, u32[]{:S(2)}) copy-start(f32[224,16]{0,1:T(8,128)} %param.3) | copy-start | bytes 43012
  66.8 3.7 %collective-permute-start.6 = (f32[112,224]{1,0:T(8,128)S(1)}, f32[112,224]{1,0:T(8,128)S(1)}, u32[]{:S(2)}, u32[]{:S(2)}) collective-permute-start(f32[112,224]{1,0:T(8,128)S(1)} %slice_select_fusion), channel_id=1, source_target_pairs={{0,1},{1,0},{2,3},{3,2},{4,5},{5,4},{6,7},{7,6},{8,9},{9,8},{10,11... | collective-permute-start | bytes 301064 | tf_op jit(solution)/shard_map/ppermute | solution.py:44
  70.5 6.1 %collective-permute-start.7 = (f32[112,224]{1,0:T(8,128)S(1)}, f32[112,224]{1,0:T(8,128)S(1)}, u32[]{:S(2)}, u32[]{:S(2)}) collective-permute-start(f32[112,224]{1,0:T(8,128)S(1)} %select_add_fusion), channel_id=1, source_target_pairs={{0,2},{1,3},{2,0},{3,1},{4,6},{5,7},{6,4},{7,5},{8,10},{9,11},{10,... | collective-permute-start | bytes 301064 | tf_op jit(solution)/shard_map/ppermute | solution.py:27
  76.6 4.9 %collective-permute-start.8 = (f32[112,224]{1,0:T(8,128)S(1)}, f32[112,224]{1,0:T(8,128)S(1)}, u32[]{:S(2)}, u32[]{:S(2)}) collective-permute-start(f32[112,224]{1,0:T(8,128)S(1)} %add.139), channel_id=1, source_target_pairs={{0,4},{1,5},{2,6},{3,7},{4,0},{5,1},{6,2},{7,3},{8,12},{9,13},{10,... | collective-permute-start | bytes 301064 | tf_op jit(solution)/shard_map/ppermute | solution.py:27
  81.5 4.9 %collective-permute-start.9 = (f32[112,224]{1,0:T(8,128)S(1)}, f32[112,224]{1,0:T(8,128)S(1)}, u32[]{:S(2)}, u32[]{:S(2)}) collective-permute-start(f32[112,224]{1,0:T(8,128)S(1)} %add.140), channel_id=1, source_target_pairs={{0,8},{8,0},{16,24},{24,16},{1,9},{9,1},{17,25},{25,17},{2,10},{10... | collective-permute-start | bytes 301064 | tf_op jit(solution)/shard_map/ppermute | solution.py:27
  86.4 7.0 %collective-permute-start.10 = (f32[112,224]{1,0:T(8,128)S(1)}, f32[112,224]{1,0:T(8,128)S(1)}, u32[]{:S(2)}, u32[]{:S(2)}) collective-permute-start(f32[112,224]{1,0:T(8,128)S(1)} %add.141), channel_id=1, source_target_pairs={{0,16},{8,24},{16,0},{24,8},{1,17},{9,25},{17,1},{25,9},{2,18},{10... | collective-permute-start | bytes 301064 | tf_op jit(solution)/shard_map/ppermute | solution.py:27
  93.4 2.6 %collective-permute-start.11 = (f32[112,224]{1,0:T(8,128)S(1)}, f32[112,224]{1,0:T(8,128)S(1)}, u32[]{:S(2)}, u32[]{:S(2)}) collective-permute-start(f32[112,224]{1,0:T(8,128)S(1)} %add.142), channel_id=1, source_target_pairs={{0,1},{1,0},{2,3},{3,2},{4,5},{5,4},{6,7},{7,6},{8,9},{9,8},{10,11... | collective-permute-start | bytes 301064 | tf_op jit(solution)/shard_map/ppermute | solution.py:46
  107.8 2.8 %copy-start.2 = (f32[224,16]{1,0:T(8,128)S(1)}, f32[224,16]{1,0:T(8,128)}, u32[]{:S(2)}) copy-start(f32[224,16]{1,0:T(8,128)} %shard_map.41) | copy-start | bytes 43012

commit v14 on v13

--- a/solution.py
+++ b/solution.py
@@ -71,6 +71,15 @@
     return lax.ppermute(flat, axis, pairs).reshape(block.shape)
 
 
+def grouped_permute(block, axis, pairs):
+    bands, rows, cols = block.shape
+    group = 1
+    while bands % (group * 2) == 0 and bands // (group * 2) >= group * 2 * rows:
+        group *= 2
+    flat = block.reshape(bands // group, group * rows, cols)
+    return lax.ppermute(flat, axis, pairs).reshape(block.shape)
+
+
 def with_halo(cells, axis, dim, width):
     count = lax.axis_size(axis)
     size = cells.shape[dim]
@@ -85,7 +94,7 @@
     return with_layout_constraint(cells, Layout(major_to_minor=tuple(range(cells.ndim))))
 
 
-def with_ring(cells, width):
+def with_ring(cells, width, top, bottom):
     rows_n = lax.axis_size("row")
     cols_n = lax.axis_size("col")
     tile_rows, tile_cols = cells.shape[0], cells.shape[1]
@@ -93,8 +102,6 @@
     up = [(i + 1, i) for i in range(rows_n - 1)]
     right = [(i, i + 1) for i in range(cols_n - 1)]
     left = [(i + 1, i) for i in range(cols_n - 1)]
-    top = flat_permute(cells[tile_rows - width:], "row", down)
-    bottom = flat_permute(cells[:width], "row", up)
     west = lax.ppermute(cells[:, tile_cols - width:], "col", right)
     east = lax.ppermute(cells[:, :width], "col", left)
     rims = jnp.concatenate([top, bottom], axis=0)
@@ -192,8 +199,16 @@
 def shards(order, image, start_basis):
     band_count, tile_rows, tile_cols = image.shape
     width = SWEEPS
+    down = [(i, i + 1) for i in range(lax.axis_size("row") - 1)]
+    up = [(i + 1, i) for i in range(lax.axis_size("row") - 1)]
+    top = grouped_permute(image[:, tile_rows - width:], "row", down)
+    bottom = grouped_permute(image[:, :width], "row", up)
     cells = pinned(jnp.transpose(image, (1, 2, 0)))
-    ext = with_ring(cells, width)
+    ext = with_ring(
+        cells, width,
+        pinned(jnp.transpose(top, (1, 2, 0))),
+        pinned(jnp.transpose(bottom, (1, 2, 0))),
+    )
     row_in = inside_mask("row", tile_rows, width)
     col_in = inside_mask("col", tile_cols, width)
     field = ext

time: 115 us -> 118 us (1.026)
  local copies, waits for them, and re-layouts: 9.73 us -> 20.6 us
  waiting for transfers between devices: 41.6 us -> 34.6 us
    reshape x0 -> x6, local copies, waits for them, and re-layouts: none -> 10.3 us  [the longest x4 8.73 us: grouped_permute(): return lax.ppermute(flat, axis, pairs).reshape(block.shape)]
    ppermute x2, waiting for transfers between devices: 21.9 us -> 13.3 us  [grouped_permute(): return lax.ppermute(flat, axis, pairs).reshape(block.shape)]
    ppermute x4, starting transfers between devices: 7.58 us -> 5.83 us  [butterfly_sum(): partner = lax.ppermute(value, axis, [(i, i ^ step) for i in range(count)])]
    ppermute x4, waiting for transfers between devices: 15.3 us -> 17 us  [butterfly_sum(): partner = lax.ppermute(value, axis, [(i, i ^ step) for i in range(count)])]
  transfers between devices with their start and end apart: 12 -> 12, of which waited for: 8 -> 8; matrix products, arithmetic and copies ran while one was open for 4% -> 14% of each run, Pallas kernels for 0% -> 0%
where the time goes in v14:
time: 118 us; the launch traced here: 117 us
  waiting for transfers between devices  34.6 us (29%)
  starting transfers between devices  21.3 us (18%)
  other arithmetic  21.1 us (18%)
  local copies, waits for them, and re-layouts  20.6 us (17%)
  Pallas kernels  11.1 us (9%)
  matrix products  7.87 us (7%)
    ppermute x4, waiting for transfers between devices, butterfly_sum(): partner = lax.ppermute(value, axis, [(i, i ^ step) for i in range(count)])  17 us
    ppermute x2, waiting for transfers between devices, grouped_permute(): return lax.ppermute(flat, axis, pairs).reshape(block.shape)  13.3 us
    pallas_call x1, Pallas kernels, subspace_step(): pl.pallas_call(subspace_kernel, out_shape=jax.ShapeDtypeStruct(basis.shap...  11.1 us
    select_n x4, other arithmetic, sweep(): return jnp.where(keep, new, 0.0)  8.99 us
    reshape x4, local copies, waits for them, and re-layouts, grouped_permute(): return lax.ppermute(flat, axis, pairs).reshape(block.shape)  8.73 us
    unnamed x12, local copies, waits for them, and re-layouts  7.35 us
    ppermute x2, starting transfers between devices, grouped_permute(): return lax.ppermute(flat, axis, pairs).reshape(block.shape)  7.16 us
    ppermute x4, starting transfers between devices, butterfly_sum(): partner = lax.ppermute(value, axis, [(i, i ^ step) for i in range(count)])  5.83 us
  transfers between devices with their start and end apart: 12, of which 8 were waited for; matrix products, arithmetic and copies ran while one was open for 14% of the time, Pallas kernels for 0%

profile of v14, /device:TPU:0, one launch (start us, length us, event | category | flops | bytes accessed | tf_op | source)
XLA Modules:
  0.0 117.4 jit_solution(13981165187167254276)
XLA Ops:
  0.6 2.4 %fusion.22 = (f32[224,4,256]{2,1,0:T(4,128)S(1)}, f32[224,4,256]{2,1,0:T(4,128)S(1)}) fusion(f32[224,8,256]{2,1,0:T(8,128)} %param.2), kind=kLoop, calls=%fused_computation.73 | loop fusion | bytes 3670016 | tf_op jit(solution)/shard_map/slice | solution.py:204
  3.3 5.9 %collective-permute-start = (f32[56,16,256]{2,1,0:T(8,128)S(1)}, f32[56,16,256]{2,1,0:T(8,128)}, u32[]{:S(2)}, u32[]{:S(2)}) collective-permute-start(f32[56,16,256]{2,1,0:T(8,128)S(1)} %reshape.166), channel_id=1, source_target_pairs={{0,8},{8,16},{16,24},{1,9},{9,17},{17,25},{2,10},{10,18},{18,26},{... | collective-permute-start | bytes 2752520 | tf_op jit(solution)/shard_map/ppermute | solution.py:80
  11.7 1.9 %copy.9 = f32[224,8,256]{0,2,1:T(8,128)S(1)} copy(f32[224,8,256]{2,1,0:T(8,128)} %param.2) | data formatting | bytes 3670016 | tf_op args[0]
  13.7 1.5 %collective-permute-start.4 = (f32[8,4,224]{2,1,0:T(4,128)S(1)}, f32[8,4,224]{2,1,0:T(4,128)S(1)}, u32[]{:S(2)}, u32[]{:S(2)}) collective-permute-start(f32[8,4,224]{2,1,0:T(4,128)S(1)} %get-tuple-element.14), channel_id=1, source_target_pairs={{0,1},{1,2},{2,3},{3,4},{4,5},{5,6},{6,7},{8,9},{9,10},{10,11},{11... | collective-permute-start | bytes 86024 | tf_op jit(solution)/shard_map/ppermute | solution.py:105
  15.1 1.3 %collective-permute-start.5 = (f32[8,4,224]{2,1,0:T(4,128)S(1)}, f32[8,4,224]{2,1,0:T(4,128)S(1)}, u32[]{:S(2)}, u32[]{:S(2)}) collective-permute-start(f32[8,4,224]{2,1,0:T(4,128)S(1)} %get-tuple-element.15), channel_id=1, source_target_pairs={{1,0},{2,1},{3,2},{4,3},{5,4},{6,5},{7,6},{9,8},{10,9},{11,10},{12... | collective-permute-start | bytes 86024 | tf_op jit(solution)/shard_map/ppermute | solution.py:106
  17.3 10.6 %collective-permute-done = f32[56,16,256]{2,1,0:T(8,128)} collective-permute-done((f32[56,16,256]{2,1,0:T(8,128)S(1)}, f32[56,16,256]{2,1,0:T(8,128)}, u32[]{:S(2)}, u32[]{:S(2)}) %collective-permute-start) | collective-permute-done | bytes 917536 | tf_op jit(solution)/shard_map/ppermute | solution.py:80
  27.9 2.4 %reshape.167 = f32[224,4,256]{2,1,0:T(4,128)} reshape(f32[56,16,256]{2,1,0:T(8,128)} %collective-permute-done) | data formatting | bytes 1835008 | tf_op jit(solution)/shard_map/reshape | solution.py:80
  30.2 1.5 %copy.7 = f32[224,4,256]{0,2,1:T(8,128)S(1)} copy(f32[224,4,256]{2,1,0:T(4,128)} %reshape.167) | data formatting | bytes 1835008 | tf_op jit(solution)/shard_map/reshape | solution.py:80
  31.7 2.7 %collective-permute-done.1 = f32[56,16,256]{2,1,0:T(8,128)} collective-permute-done((f32[56,16,256]{2,1,0:T(8,128)}, f32[56,16,256]{2,1,0:T(8,128)}, u32[]{:S(2)}, u32[]{:S(2)}) %collective-permute-start.1) | collective-permute-done | bytes 917536 | tf_op jit(solution)/shard_map/ppermute | solution.py:80
  34.5 2.4 %reshape.169 = f32[224,4,256]{2,1,0:T(4,128)} reshape(f32[56,16,256]{2,1,0:T(8,128)} %collective-permute-done.1) | data formatting | bytes 1835008 | tf_op jit(solution)/shard_map/reshape | solution.py:80
  36.8 2.5 %copy.8 = f32[224,4,256]{0,2,1:T(8,128)} copy(f32[224,4,256]{2,1,0:T(4,128)} %reshape.169) | data formatting | bytes 1835008 | tf_op jit(solution)/shard_map/reshape | solution.py:80
  41.5 1.5 %collective-permute-start.3 = (f32[8,4,224]{2,1,0:T(4,128)S(1)}, f32[8,4,224]{2,1,0:T(4,128)S(1)}, u32[]{:S(2)}, u32[]{:S(2)}) collective-permute-start(f32[8,4,224]{2,1,0:T(4,128)S(1)} %get-tuple-element.17), channel_id=1, source_target_pairs={{1,0},{2,1},{3,2},{4,3},{5,4},{6,5},{7,6},{9,8},{10,9},{11,10},{12... | collective-permute-start | bytes 86024 | tf_op jit(solution)/shard_map/ppermute | solution.py:109
  43.0 3.3 %collective-permute-done.3 = f32[8,4,224]{2,1,0:T(4,128)S(1)} collective-permute-done((f32[8,4,224]{2,1,0:T(4,128)S(1)}, f32[8,4,224]{2,1,0:T(4,128)S(1)}, u32[]{:S(2)}, u32[]{:S(2)}) %collective-permute-start.3) | collective-permute-done | bytes 28704 | tf_op jit(solution)/shard_map/ppermute | solution.py:109
  46.3 1.8 %maximum_maximum_fusion = f32[16,264,224]{2,1,0:T(8,128)S(1)} fusion(f32[4,4,224]{2,1,0:T(4,128)S(1)} %get-tuple-element.23, f32[4,256,224]{2,1,0:T(8,128)} %bitcast.23, f32[4,4,224]{2,1,0:T(4,128)S(1)} %get-tuple-element.21, f32[8,4,224]{2,1,0:T(4,128)S(1)} %collective-permute-done.5, f32[8,256,224]{2,1,0:T(8,128)S(1)} %bitcast.19, ...), kind=kLoop, calls=%fused_computation | loop fusion | flops 7569408 | bytes 7569408 | tf_op jit(solution)/shard_map/concatenate | solution.py:110
  49.4 1.4 %broadcast_multiply_fusion.1 = (f32[15,263,224]{2,1,0:T(8,128)S(1)}, f32[15,263,224]{2,1,0:T(8,128)S(1)}) fusion(f32[15,263]{1,0:T(8,128)S(1)} %add_rsqrt_fusion.3, f32[16,264,224]{2,1,0:T(8,128)S(1)} %maximum_maximum_fusion), kind=kLoop, calls=%fused_computation.46 | loop fusion | flops 3534720 | bytes 17689380 | tf_op jit(solution)/shard_map/mul | solution.py:132
  50.8 2.6 %fusion.3 = f32[14,262,224]{2,1,0:T(8,128)S(1)} fusion(f32[15,263,224]{2,1,0:T(8,128)S(1)} %get-tuple-element.7, f32[15,263,224]{2,1,0:T(8,128)S(1)} %get-tuple-element.6, f32[16,264,224]{2,1,0:T(8,128)S(1)} %maximum_maximum_fusion, pred[14,262]{1,0:T(8,128)(4,1)S(1)} %broadcast_and_fusion), kind=kLoop, calls=%fused_computation.8 | loop fusion | flops 7394688 | bytes 19722836 | tf_op jit(solution)/shard_map/jit(_where)/select_n | solution.py:137
  55.8 2.4 %fusion.6 = f32[12,260,224]{2,1,0:T(8,128)S(1)} fusion(f32[16,264,224]{2,1,0:T(8,128)S(1)} %maximum_maximum_fusion, f32[13,261,224]{2,1,0:T(8,128)S(1)} %get-tuple-element.9, f32[13,261,224]{2,1,0:T(8,128)S(1)} %get-tuple-element.8, f32[14,262,224]{2,1,0:T(8,128)S(1)} %fusion.3, pred[12,260]{1,0:T(8,128)(4,1)S(1)} %broadcast_and_fusion.1), kind=kLoop, calls=%fused_computation.17 | loop fusion | flops 6289920 | bytes 19571760 | tf_op jit(solution)/shard_map/jit(_where)/select_n | solution.py:137
  60.1 2.4 %fusion.11 = f32[10,258,224]{2,1,0:T(8,128)S(1)} fusion(f32[16,264,224]{2,1,0:T(8,128)S(1)} %maximum_maximum_fusion, f32[11,259,224]{2,1,0:T(8,128)S(1)} %get-tuple-element.11, f32[11,259,224]{2,1,0:T(8,128)S(1)} %get-tuple-element.10, f32[12,260,224]{2,1,0:T(8,128)S(1)} %fusion.6, pred[10,258]{1,0:T(8,128)(4,1)S(1)} %broadcast_and_fusion.2), kind=kLoop, calls=%fused_computation.29 | loop fusion | flops 5201280 | bytes 16184340 | tf_op jit(solution)/shard_map/jit(_where)/select_n | solution.py:137
  65.0 1.5 %fusion.17 = f32[8,256,224]{2,1,0:T(8,128)S(1)} fusion(f32[9,257,224]{2,1,0:T(8,128)S(1)} %get-tuple-element.13, f32[9,257,224]{2,1,0:T(8,128)S(1)} %get-tuple-element.12, f32[10,258,224]{2,1,0:T(8,128)S(1)} %fusion.11, pred[8,256]{1,0:T(8,128)(4,1)S(1)} %broadcast_and_fusion.3, f32[224,8,256]{0,2,1:T(8,128)S(1)} %copy-done.1), kind=kLoop, calls=%fused_computation.42 | loop fusion | flops 4128768 | bytes 12847104 | tf_op jit(solution)/shard_map/jit(_where)/select_n | solution.py:137
  66.5 3.5 %convolution_bitcast_fusion = f32[224,224]{1,0:T(8,128)S(1)} fusion(f32[8,256,224]{2,1,0:T(8,128)S(1)} %fusion.17), kind=kOutput, calls=%fused_computation.53 | convolution fusion | flops 1233125376 | bytes 2035712 | tf_op jit(solution)/shard_map/dot_general | solution.py:225
  70.0 2.7 %collective-permute-start.6 = (f32[112,224]{1,0:T(8,128)S(1)}, f32[112,224]{1,0:T(8,128)S(1)}, u32[]{:S(2)}, u32[]{:S(2)}) collective-permute-start(f32[112,224]{1,0:T(8,128)S(1)} %slice_select_fusion), channel_id=1, source_target_pairs={{0,1},{1,0},{2,3},{3,2},{4,5},{5,4},{6,7},{7,6},{8,9},{9,8},{10,11... | collective-permute-start | bytes 301064 | tf_op jit(solution)/shard_map/ppermute | solution.py:44
  73.7 2.5 %collective-permute-start.7 = (f32[112,224]{1,0:T(8,128)S(1)}, f32[112,224]{1,0:T(8,128)S(1)}, u32[]{:S(2)}, u32[]{:S(2)}) collective-permute-start(f32[112,224]{1,0:T(8,128)S(1)} %select_add_fusion), channel_id=1, source_target_pairs={{0,2},{1,3},{2,0},{3,1},{4,6},{5,7},{6,4},{7,5},{8,10},{9,11},{10,... | collective-permute-start | bytes 301064 | tf_op jit(solution)/shard_map/ppermute | solution.py:27
  76.2 3.7 %collective-permute-done.7 = f32[112,224]{1,0:T(8,128)S(1)} collective-permute-done((f32[112,224]{1,0:T(8,128)S(1)}, f32[112,224]{1,0:T(8,128)S(1)}, u32[]{:S(2)}, u32[]{:S(2)}) %collective-permute-start.7) | collective-permute-done | bytes 100384 | tf_op jit(solution)/shard_map/ppermute | solution.py:27
  80.8 4.0 %collective-permute-done.8 = f32[112,224]{1,0:T(8,128)S(1)} collective-permute-done((f32[112,224]{1,0:T(8,128)S(1)}, f32[112,224]{1,0:T(8,128)S(1)}, u32[]{:S(2)}, u32[]{:S(2)}) %collective-permute-start.8) | collective-permute-done | bytes 100384 | tf_op jit(solution)/shard_map/ppermute | solution.py:27
  85.5 4.2 %collective-permute-done.9 = f32[112,224]{1,0:T(8,128)S(1)} collective-permute-done((f32[112,224]{1,0:T(8,128)S(1)}, f32[112,224]{1,0:T(8,128)S(1)}, u32[]{:S(2)}, u32[]{:S(2)}) %collective-permute-start.9) | collective-permute-done | bytes 100384 | tf_op jit(solution)/shard_map/ppermute | solution.py:27
  89.7 1.7 %collective-permute-start.10 = (f32[112,224]{1,0:T(8,128)S(1)}, f32[112,224]{1,0:T(8,128)S(1)}, u32[]{:S(2)}, u32[]{:S(2)}) collective-permute-start(f32[112,224]{1,0:T(8,128)S(1)} %add.141), channel_id=1, source_target_pairs={{0,16},{8,24},{16,0},{24,8},{1,17},{9,25},{17,1},{25,9},{2,18},{10... | collective-permute-start | bytes 301064 | tf_op jit(solution)/shard_map/ppermute | solution.py:27
  91.4 5.3 %collective-permute-done.10 = f32[112,224]{1,0:T(8,128)S(1)} collective-permute-done((f32[112,224]{1,0:T(8,128)S(1)}, f32[112,224]{1,0:T(8,128)S(1)}, u32[]{:S(2)}, u32[]{:S(2)}) %collective-permute-start.10) | collective-permute-done | bytes 100384 | tf_op jit(solution)/shard_map/ppermute | solution.py:27
  97.5 1.8 %copy.11 = f32[224,8,256]{2,1,0:T(8,128)} copy(f32[224,8,256]{0,2,1:T(8,128)S(1)} %bitcast.16) | data formatting | bytes 3670016
  100.0 11.1 %shard_map.41 = f32[224,16]{1,0:T(8,128)} custom-call(f32[224,224]{1,0:T(8,128)} %maximum_select_fusion.gram_ref, f32[224,16]{1,0:T(8,128)} %copy.10.basis_ref), custom_call_target="tpu_custom_call" | custom-call | flops 45875200 | bytes 229376 | tf_op jit(solution)/shard_map/pallas_call | solution.py:182
  111.1 2.8 %fusion.25 = f32[2048,16]{1,0:T(8,128)S(1)} fusion(f32[2048,224]{1,0:T(8,128)S(1)} %bitcast.17, f32[224,16]{1,0:T(8,128)} %shard_map.41), kind=kOutput, calls=%fused_computation.76 | convolution fusion | flops 88080384 | bytes 1980416 | tf_op jit(solution)/shard_map/dot_general | solution.py:235
  113.8 1.6 %fusion.26 = f32[224,2048]{1,0:T(8,128)S(1)} fusion(f32[224,16]{1,0:T(8,128)S(1)} %copy-done.2, f32[2048,16]{1,0:T(8,128)S(1)} %fusion.25), kind=kOutput, calls=%fused_computation.77 | convolution fusion | flops 88080384 | bytes 1980416 | tf_op jit(solution)/shard_map/dot_general | solution.py:236
  115.5 2.0 %copy.12 = f32[28,8,8,256]{3,2,1,0:T(8,128)} copy(f32[28,8,8,256]{3,1,2,0:T(8,128)S(1)} %bitcast.24) | data formatting | bytes 3670016
  (57 shorter events, 18.0 us)
Async XLA Ops:
  3.3 24.5 %collective-permute-start = (f32[56,16,256]{2,1,0:T(8,128)S(1)}, f32[56,16,256]{2,1,0:T(8,128)}, u32[]{:S(2)}, u32[]{:S(2)}) collective-permute-start(f32[56,16,256]{2,1,0:T(8,128)S(1)} %reshape.166), channel_id=1, source_target_pairs={{0,8},{8,16},{16,24},{1,9},{9,17},{17,25},{2,10},{10,18},{18,26},{... | collective-permute-start | bytes 2752520 | tf_op jit(solution)/shard_map/ppermute | solution.py:80
  10.4 24.0 %collective-permute-start.1 = (f32[56,16,256]{2,1,0:T(8,128)}, f32[56,16,256]{2,1,0:T(8,128)}, u32[]{:S(2)}, u32[]{:S(2)}) collective-permute-start(f32[56,16,256]{2,1,0:T(8,128)} %reshape.168), channel_id=1, source_target_pairs={{8,0},{16,8},{24,16},{9,1},{17,9},{25,17},{10,2},{18,10},{26,18},{... | collective-permute-start | bytes 2752520 | tf_op jit(solution)/shard_map/ppermute | solution.py:80
  13.6 32.7 %copy-start = (f32[224,8,256]{0,2,1:T(8,128)}, f32[224,8,256]{0,2,1:T(8,128)S(1)}, u32[]{:S(2)}) copy-start(f32[224,8,256]{0,2,1:T(8,128)S(1)} %copy.9) | copy-start | bytes 5505028
  13.7 32.6 %collective-permute-start.4 = (f32[8,4,224]{2,1,0:T(4,128)S(1)}, f32[8,4,224]{2,1,0:T(4,128)S(1)}, u32[]{:S(2)}, u32[]{:S(2)}) collective-permute-start(f32[8,4,224]{2,1,0:T(4,128)S(1)} %get-tuple-element.14), channel_id=1, source_target_pairs={{0,1},{1,2},{2,3},{3,4},{4,5},{5,6},{6,7},{8,9},{9,10},{10,11},{11... | collective-permute-start | bytes 86024 | tf_op jit(solution)/shard_map/ppermute | solution.py:105
  15.1 31.2 %collective-permute-start.5 = (f32[8,4,224]{2,1,0:T(4,128)S(1)}, f32[8,4,224]{2,1,0:T(4,128)S(1)}, u32[]{:S(2)}, u32[]{:S(2)}) collective-permute-start(f32[8,4,224]{2,1,0:T(4,128)S(1)} %get-tuple-element.15), channel_id=1, source_target_pairs={{1,0},{2,1},{3,2},{4,3},{5,4},{6,5},{7,6},{9,8},{10,9},{11,10},{12... | collective-permute-start | bytes 86024 | tf_op jit(solution)/shard_map/ppermute | solution.py:106
  40.1 2.8 %collective-permute-start.2 = (f32[8,4,224]{2,1,0:T(4,128)S(1)}, f32[8,4,224]{2,1,0:T(4,128)S(1)}, u32[]{:S(2)}, u32[]{:S(2)}) collective-permute-start(f32[8,4,224]{2,1,0:T(4,128)S(1)} %get-tuple-element.16), channel_id=1, source_target_pairs={{0,1},{1,2},{2,3},{3,4},{4,5},{5,6},{6,7},{8,9},{9,10},{10,11},{11... | collective-permute-start | bytes 86024 | tf_op jit(solution)/shard_map/ppermute | solution.py:108
  41.5 4.8 %collective-permute-start.3 = (f32[8,4,224]{2,1,0:T(4,128)S(1)}, f32[8,4,224]{2,1,0:T(4,128)S(1)}, u32[]{:S(2)}, u32[]{:S(2)}) collective-permute-start(f32[8,4,224]{2,1,0:T(4,128)S(1)} %get-tuple-element.17), channel_id=1, source_target_pairs={{1,0},{2,1},{3,2},{4,3},{5,4},{6,5},{7,6},{9,8},{10,9},{11,10},{12... | collective-permute-start | bytes 86024 | tf_op jit(solution)/shard_map/ppermute | solution.py:109
  63.4 1.6 %copy-start.1 = (f32[224,8,256]{0,2,1:T(8,128)S(1)}, f32[224,8,256]{0,2,1:T(8,128)}, u32[]{:S(2)}) copy-start(f32[224,8,256]{0,2,1:T(8,128)} %copy-done) | copy-start | bytes 5505028
  66.5 30.2 %copy-start.3 = (f32[224,16]{0,1:T(8,128)S(1)}, f32[224,16]{0,1:T(8,128)}, u32[]{:S(2)}) copy-start(f32[224,16]{0,1:T(8,128)} %param.3) | copy-start | bytes 43012
  70.0 3.7 %collective-permute-start.6 = (f32[112,224]{1,0:T(8,128)S(1)}, f32[112,224]{1,0:T(8,128)S(1)}, u32[]{:S(2)}, u32[]{:S(2)}) collective-permute-start(f32[112,224]{1,0:T(8,128)S(1)} %slice_select_fusion), channel_id=1, source_target_pairs={{0,1},{1,0},{2,3},{3,2},{4,5},{5,4},{6,7},{7,6},{8,9},{9,8},{10,11... | collective-permute-start | bytes 301064 | tf_op jit(solution)/shard_map/ppermute | solution.py:44
  73.7 6.1 %collective-permute-start.7 = (f32[112,224]{1,0:T(8,128)S(1)}, f32[112,224]{1,0:T(8,128)S(1)}, u32[]{:S(2)}, u32[]{:S(2)}) collective-permute-start(f32[112,224]{1,0:T(8,128)S(1)} %select_add_fusion), channel_id=1, source_target_pairs={{0,2},{1,3},{2,0},{3,1},{4,6},{5,7},{6,4},{7,5},{8,10},{9,11},{10,... | collective-permute-start | bytes 301064 | tf_op jit(solution)/shard_map/ppermute | solution.py:27
  79.9 4.9 %collective-permute-start.8 = (f32[112,224]{1,0:T(8,128)S(1)}, f32[112,224]{1,0:T(8,128)S(1)}, u32[]{:S(2)}, u32[]{:S(2)}) collective-permute-start(f32[112,224]{1,0:T(8,128)S(1)} %add.139), channel_id=1, source_target_pairs={{0,4},{1,5},{2,6},{3,7},{4,0},{5,1},{6,2},{7,3},{8,12},{9,13},{10,... | collective-permute-start | bytes 301064 | tf_op jit(solution)/shard_map/ppermute | solution.py:27
  84.8 4.9 %collective-permute-start.9 = (f32[112,224]{1,0:T(8,128)S(1)}, f32[112,224]{1,0:T(8,128)S(1)}, u32[]{:S(2)}, u32[]{:S(2)}) collective-permute-start(f32[112,224]{1,0:T(8,128)S(1)} %add.140), channel_id=1, source_target_pairs={{0,8},{8,0},{16,24},{24,16},{1,9},{9,1},{17,25},{25,17},{2,10},{10... | collective-permute-start | bytes 301064 | tf_op jit(solution)/shard_map/ppermute | solution.py:27
  89.7 7.0 %collective-permute-start.10 = (f32[112,224]{1,0:T(8,128)S(1)}, f32[112,224]{1,0:T(8,128)S(1)}, u32[]{:S(2)}, u32[]{:S(2)}) collective-permute-start(f32[112,224]{1,0:T(8,128)S(1)} %add.141), channel_id=1, source_target_pairs={{0,16},{8,24},{16,0},{24,8},{1,17},{9,25},{17,1},{25,9},{2,18},{10... | collective-permute-start | bytes 301064 | tf_op jit(solution)/shard_map/ppermute | solution.py:27
  96.7 2.6 %collective-permute-start.11 = (f32[112,224]{1,0:T(8,128)S(1)}, f32[112,224]{1,0:T(8,128)S(1)}, u32[]{:S(2)}, u32[]{:S(2)}) collective-permute-start(f32[112,224]{1,0:T(8,128)S(1)} %add.142), channel_id=1, source_target_pairs={{0,1},{1,0},{2,3},{3,2},{4,5},{5,4},{6,7},{7,6},{8,9},{9,8},{10,11... | collective-permute-start | bytes 301064 | tf_op jit(solution)/shard_map/ppermute | solution.py:46
  111.0 2.8 %copy-start.2 = (f32[224,16]{1,0:T(8,128)S(1)}, f32[224,16]{1,0:T(8,128)}, u32[]{:S(2)}) copy-start(f32[224,16]{1,0:T(8,128)} %shard_map.41) | copy-start | bytes 43012

commit v15 on v13

--- a/solution.py
+++ b/solution.py
@@ -122,10 +122,12 @@
     diff_row = field[1:, :-1] - field[:-1, :-1]
     energy_sum = jnp.sum(diff_col * diff_col + diff_row * diff_row, axis=-1, keepdims=True)
     weight = 1.0 / jnp.sqrt(1.0 + energy_sum / field.shape[-1])
-    flux_col = weight * diff_col
-    flux_row = weight * diff_row
-    spread = flux_col[1:, 1:] - flux_col[1:, :-1] + flux_row[1:, 1:] - flux_row[:-1, 1:]
     centre = field[1:-1, 1:-1]
+    col_here = weight[1:, 1:] * (field[1:-1, 2:] - centre)
+    col_left = weight[1:, :-1] * (centre - field[1:-1, :-2])
+    row_here = weight[1:, 1:] * (field[2:, 1:-1] - centre)
+    row_up = weight[:-1, 1:] * (centre - field[:-2, 1:-1])
+    spread = col_here - col_left + row_here - row_up
     new = centre + tau_step * spread + tau_step * fidelity * (source - centre)
     return jnp.where(keep, new, 0.0)
 

time: 115 us -> 113 us (0.983)
  other arithmetic: 21 us -> 19.6 us
    mul x4 -> x0, other arithmetic: 4.17 us -> none  [sweep(): flux_col = weight * diff_col]
    select_n x4, other arithmetic: 8.95 us -> 11.7 us  [sweep(): return jnp.where(keep, new, 0.0)]
where the time goes in v15:
time: 113 us
  waiting for transfers between devices  41.6 us (37%)
  starting transfers between devices  21.9 us (19%)
  other arithmetic  19.6 us (17%)
  Pallas kernels  11.1 us (10%)
  local copies, waits for them, and re-layouts  9.63 us (9%)
  matrix products  7.86 us (7%)
    ppermute x2, waiting for transfers between devices, flat_permute(): return lax.ppermute(flat, axis, pairs).reshape(block.shape)  21.9 us
    ppermute x4, waiting for transfers between devices, butterfly_sum(): partner = lax.ppermute(value, axis, [(i, i ^ step) for i in range(count)])  15.3 us
    select_n x4, other arithmetic, sweep(): return jnp.where(keep, new, 0.0)  11.7 us
    pallas_call x1, Pallas kernels, subspace_step(): pl.pallas_call(subspace_kernel, out_shape=jax.ShapeDtypeStruct(basis.shap...  11.1 us
    ppermute x4, starting transfers between devices, butterfly_sum(): partner = lax.ppermute(value, axis, [(i, i ^ step) for i in range(count)])  7.57 us
    unnamed x12, local copies, waits for them, and re-layouts  7.09 us
    ppermute x2, starting transfers between devices, flat_permute(): return lax.ppermute(flat, axis, pairs).reshape(block.shape)  6.27 us
    reduce_sum x4, other arithmetic, sweep(): jnp.sum(diff_col * diff_col + diff_row * diff_row, axis=-1, keepdims=True)  4.09 us
  transfers between devices with their start and end apart: 12, of which 8 were waited for; matrix products, arithmetic and copies ran while one was open for 4% of the time, Pallas kernels for 0%

profile of v15, /device:TPU:0, one launch (start us, length us, event | category | flops | bytes accessed | tf_op | source)
XLA Modules:
  0.0 112.7 jit_solution(3671869609945439039)
XLA Ops:
  0.6 1.9 %copy.4 = f32[224,8,256]{0,2,1:T(8,128)S(1)} copy(f32[224,8,256]{2,1,0:T(8,128)} %param.2) | data formatting | bytes 3670016 | tf_op args[0]
  2.5 1.6 %fusion.66 = (f32[4,256,224]{2,1,0:T(8,128)}, f32[4,256,224]{2,1,0:T(8,128)}) fusion(f32[8,256,224]{2,1,0:T(8,128)S(1)} %bitcast.52), kind=kLoop, calls=%fused_computation.121 | loop fusion | bytes 3670016 | tf_op jit(solution)/shard_map/slice | solution.py:96
  4.1 5.0 %collective-permute-start = (f32[16,64,224]{2,1,0:T(8,128)}, f32[16,64,224]{2,1,0:T(8,128)S(1)}, u32[]{:S(2)}, u32[]{:S(2)}) collective-permute-start(f32[16,64,224]{2,1,0:T(8,128)} %bitcast.1), channel_id=1, source_target_pairs={{0,8},{8,16},{16,24},{1,9},{9,17},{17,25},{2,10},{10,18},{18,26},{... | collective-permute-start | bytes 2752520 | tf_op jit(solution)/shard_map/ppermute | solution.py:71
  9.1 1.3 %collective-permute-start.1 = (f32[16,64,224]{2,1,0:T(8,128)}, f32[16,64,224]{2,1,0:T(8,128)}, u32[]{:S(2)}, u32[]{:S(2)}) collective-permute-start(f32[16,64,224]{2,1,0:T(8,128)} %bitcast.3), channel_id=1, source_target_pairs={{8,0},{16,8},{24,16},{9,1},{17,9},{25,17},{10,2},{18,10},{26,18},{... | collective-permute-start | bytes 2752520 | tf_op jit(solution)/shard_map/ppermute | solution.py:71
  10.5 1.5 %collective-permute-start.4 = (f32[8,4,224]{2,1,0:T(4,128)S(1)}, f32[8,4,224]{2,1,0:T(4,128)S(1)}, u32[]{:S(2)}, u32[]{:S(2)}) collective-permute-start(f32[8,4,224]{2,1,0:T(4,128)S(1)} %get-tuple-element.4), channel_id=1, source_target_pairs={{0,1},{1,2},{2,3},{3,4},{4,5},{5,6},{6,7},{8,9},{9,10},{10,11},{11... | collective-permute-start | bytes 86024 | tf_op jit(solution)/shard_map/ppermute | solution.py:98
  11.9 1.3 %collective-permute-start.5 = (f32[8,4,224]{2,1,0:T(4,128)S(1)}, f32[8,4,224]{2,1,0:T(4,128)S(1)}, u32[]{:S(2)}, u32[]{:S(2)}) collective-permute-start(f32[8,4,224]{2,1,0:T(4,128)S(1)} %get-tuple-element.5), channel_id=1, source_target_pairs={{1,0},{2,1},{3,2},{4,3},{5,4},{6,5},{7,6},{9,8},{10,9},{11,10},{12... | collective-permute-start | bytes 86024 | tf_op jit(solution)/shard_map/ppermute | solution.py:99
  14.1 17.7 %collective-permute-done = f32[16,64,224]{2,1,0:T(8,128)S(1)} collective-permute-done((f32[16,64,224]{2,1,0:T(8,128)}, f32[16,64,224]{2,1,0:T(8,128)S(1)}, u32[]{:S(2)}, u32[]{:S(2)}) %collective-permute-start) | collective-permute-done | bytes 917536 | tf_op jit(solution)/shard_map/ppermute | solution.py:71
  31.8 4.2 %collective-permute-done.1 = f32[16,64,224]{2,1,0:T(8,128)} collective-permute-done((f32[16,64,224]{2,1,0:T(8,128)}, f32[16,64,224]{2,1,0:T(8,128)}, u32[]{:S(2)}, u32[]{:S(2)}) %collective-permute-start.1) | collective-permute-done | bytes 917536 | tf_op jit(solution)/shard_map/ppermute | solution.py:71
  36.8 1.3 %collective-permute-start.2 = (f32[8,4,224]{2,1,0:T(4,128)S(1)}, f32[8,4,224]{2,1,0:T(4,128)S(1)}, u32[]{:S(2)}, u32[]{:S(2)}) collective-permute-start(f32[8,4,224]{2,1,0:T(4,128)S(1)} %get-tuple-element.6), channel_id=1, source_target_pairs={{0,1},{1,2},{2,3},{3,4},{4,5},{5,6},{6,7},{8,9},{9,10},{10,11},{11... | collective-permute-start | bytes 86024 | tf_op jit(solution)/shard_map/ppermute | solution.py:101
  38.1 1.3 %collective-permute-start.3 = (f32[8,4,224]{2,1,0:T(4,128)S(1)}, f32[8,4,224]{2,1,0:T(4,128)S(1)}, u32[]{:S(2)}, u32[]{:S(2)}) collective-permute-start(f32[8,4,224]{2,1,0:T(4,128)S(1)} %get-tuple-element.7), channel_id=1, source_target_pairs={{1,0},{2,1},{3,2},{4,3},{5,4},{6,5},{7,6},{9,8},{10,9},{11,10},{12... | collective-permute-start | bytes 86024 | tf_op jit(solution)/shard_map/ppermute | solution.py:102
  39.4 3.5 %collective-permute-done.3 = f32[8,4,224]{2,1,0:T(4,128)S(1)} collective-permute-done((f32[8,4,224]{2,1,0:T(4,128)S(1)}, f32[8,4,224]{2,1,0:T(4,128)S(1)}, u32[]{:S(2)}, u32[]{:S(2)}) %collective-permute-start.3) | collective-permute-done | bytes 28704 | tf_op jit(solution)/shard_map/ppermute | solution.py:102
  43.0 1.8 %maximum_maximum_fusion = f32[16,264,224]{2,1,0:T(8,128)S(1)} fusion(f32[4,4,224]{2,1,0:T(4,128)S(1)} %get-tuple-element.13, f32[4,256,224]{2,1,0:T(8,128)} %bitcast.4, f32[4,4,224]{2,1,0:T(4,128)S(1)} %get-tuple-element.11, f32[8,4,224]{2,1,0:T(4,128)S(1)} %collective-permute-done.5, f32[8,256,224]{2,1,0:T(8,128)S(1)} %bitcast.54, ...), kind=kLoop, calls=%fused_computation | loop fusion | flops 7569408 | bytes 7569408 | tf_op jit(solution)/shard_map/concatenate | solution.py:103
  44.8 1.3 %fusion.2 = f32[15,263]{1,0:T(8,128)S(1)} fusion(f32[16,264,224]{2,1,0:T(8,128)S(1)} %maximum_maximum_fusion), kind=kLoop, calls=%fused_computation.4 | loop fusion | flops 5298135 | bytes 10619940 | tf_op jit(solution)/shard_map/reduce_sum | solution.py:123
  46.2 3.6 %fusion.9 = f32[14,262,224]{2,1,0:T(8,128)S(1)} fusion(f32[16,264,224]{2,1,0:T(8,128)S(1)} %maximum_maximum_fusion, f32[14,262]{1,0:T(8,128)S(1)} %get-tuple-element.24, f32[14,262]{1,0:T(8,128)S(1)} %get-tuple-element.25, f32[14,262]{1,0:T(8,128)S(1)} %get-tuple-element.23, pred[14,262]{1,0:T(8,128)(4,1)S(1)} %broadcast_and_fusion), kind=kLoop, calls=%fused_computation.13 | loop fusion | flops 13967744 | bytes 19766852 | tf_op jit(solution)/shard_map/jit(_where)/select_n | solution.py:132
  49.8 1.1 fusion.17
  51.0 3.4 %fusion.21 = f32[12,260,224]{2,1,0:T(8,128)S(1)} fusion(f32[16,264,224]{2,1,0:T(8,128)S(1)} %maximum_maximum_fusion, f32[14,262,224]{2,1,0:T(8,128)S(1)} %fusion.9, f32[12,260]{1,0:T(8,128)S(1)} %get-tuple-element.21, f32[12,260]{1,0:T(8,128)S(1)} %get-tuple-element.22, f32[12,260]{1,0:T(8,128)S(1)} %get-tuple-element.20, ...), kind=kLoop, calls=%fused_computation.31 | loop fusion | flops 11880960 | bytes 19609200 | tf_op jit(solution)/shard_map/jit(_where)/select_n | solution.py:132
  55.4 2.7 %fusion.37 = f32[10,258,224]{2,1,0:T(8,128)S(1)} fusion(f32[16,264,224]{2,1,0:T(8,128)S(1)} %maximum_maximum_fusion, f32[12,260,224]{2,1,0:T(8,128)S(1)} %fusion.21, f32[10,258]{1,0:T(8,128)S(1)} %get-tuple-element.18, f32[10,258]{1,0:T(8,128)S(1)} %get-tuple-element.19, f32[10,258]{1,0:T(8,128)S(1)} %get-tuple-element.17, ...), kind=kLoop, calls=%fused_computation.54 | loop fusion | flops 9824640 | bytes 16215300 | tf_op jit(solution)/shard_map/jit(_where)/select_n | solution.py:132
  59.7 2.0 %fusion.56 = f32[8,256,224]{2,1,0:T(8,128)S(1)} fusion(f32[10,258,224]{2,1,0:T(8,128)S(1)} %fusion.37, f32[8,256]{1,0:T(8,128)S(1)} %get-tuple-element.15, f32[8,256]{1,0:T(8,128)S(1)} %get-tuple-element.16, f32[8,256]{1,0:T(8,128)S(1)} %get-tuple-element.14, pred[8,256]{1,0:T(8,128)(4,1)S(1)} %broadcast_and_fusion.3, f32[224,8,256]{0,2,1:T(8,128)S(1)} %copy-done.1), kind=kLoop, calls=%fused_computation.80 | loop fusion | flops 7798784 | bytes 12871680 | tf_op jit(solution)/shard_map/jit(_where)/select_n | solution.py:132
  61.7 3.5 %convolution_bitcast_fusion = f32[224,224]{1,0:T(8,128)S(1)} fusion(f32[8,256,224]{2,1,0:T(8,128)S(1)} %fusion.56), kind=kOutput, calls=%fused_computation.89 | convolution fusion | flops 1233125376 | bytes 2035712 | tf_op jit(solution)/shard_map/dot_general | solution.py:212
  65.2 2.7 %collective-permute-start.6 = (f32[112,224]{1,0:T(8,128)S(1)}, f32[112,224]{1,0:T(8,128)S(1)}, u32[]{:S(2)}, u32[]{:S(2)}) collective-permute-start(f32[112,224]{1,0:T(8,128)S(1)} %slice_select_fusion), channel_id=1, source_target_pairs={{0,1},{1,0},{2,3},{3,2},{4,5},{5,4},{6,7},{7,6},{8,9},{9,8},{10,11... | collective-permute-start | bytes 301064 | tf_op jit(solution)/shard_map/ppermute | solution.py:44
  68.9 2.5 %collective-permute-start.7 = (f32[112,224]{1,0:T(8,128)S(1)}, f32[112,224]{1,0:T(8,128)S(1)}, u32[]{:S(2)}, u32[]{:S(2)}) collective-permute-start(f32[112,224]{1,0:T(8,128)S(1)} %select_add_fusion), channel_id=1, source_target_pairs={{0,2},{1,3},{2,0},{3,1},{4,6},{5,7},{6,4},{7,5},{8,10},{9,11},{10,... | collective-permute-start | bytes 301064 | tf_op jit(solution)/shard_map/ppermute | solution.py:27
  71.4 3.7 %collective-permute-done.7 = f32[112,224]{1,0:T(8,128)S(1)} collective-permute-done((f32[112,224]{1,0:T(8,128)S(1)}, f32[112,224]{1,0:T(8,128)S(1)}, u32[]{:S(2)}, u32[]{:S(2)}) %collective-permute-start.7) | collective-permute-done | bytes 100384 | tf_op jit(solution)/shard_map/ppermute | solution.py:27
  76.0 4.0 %collective-permute-done.8 = f32[112,224]{1,0:T(8,128)S(1)} collective-permute-done((f32[112,224]{1,0:T(8,128)S(1)}, f32[112,224]{1,0:T(8,128)S(1)}, u32[]{:S(2)}, u32[]{:S(2)}) %collective-permute-start.8) | collective-permute-done | bytes 100384 | tf_op jit(solution)/shard_map/ppermute | solution.py:27
  80.0 1.6 %collective-permute-start.9 = (f32[112,224]{1,0:T(8,128)S(1)}, f32[112,224]{1,0:T(8,128)S(1)}, u32[]{:S(2)}, u32[]{:S(2)}) collective-permute-start(f32[112,224]{1,0:T(8,128)S(1)} %add.156), channel_id=1, source_target_pairs={{0,8},{8,0},{16,24},{24,16},{1,9},{9,1},{17,25},{25,17},{2,10},{10... | collective-permute-start | bytes 301064 | tf_op jit(solution)/shard_map/ppermute | solution.py:27
  81.6 3.3 %collective-permute-done.9 = f32[112,224]{1,0:T(8,128)S(1)} collective-permute-done((f32[112,224]{1,0:T(8,128)S(1)}, f32[112,224]{1,0:T(8,128)S(1)}, u32[]{:S(2)}, u32[]{:S(2)}) %collective-permute-start.9) | collective-permute-done | bytes 100384 | tf_op jit(solution)/shard_map/ppermute | solution.py:27
  84.9 2.6 %collective-permute-start.10 = (f32[112,224]{1,0:T(8,128)S(1)}, f32[112,224]{1,0:T(8,128)S(1)}, u32[]{:S(2)}, u32[]{:S(2)}) collective-permute-start(f32[112,224]{1,0:T(8,128)S(1)} %add.157), channel_id=1, source_target_pairs={{0,16},{8,24},{16,0},{24,8},{1,17},{9,25},{17,1},{25,9},{2,18},{10... | collective-permute-start | bytes 301064 | tf_op jit(solution)/shard_map/ppermute | solution.py:27
  87.5 4.4 %collective-permute-done.10 = f32[112,224]{1,0:T(8,128)S(1)} collective-permute-done((f32[112,224]{1,0:T(8,128)S(1)}, f32[112,224]{1,0:T(8,128)S(1)}, u32[]{:S(2)}, u32[]{:S(2)}) %collective-permute-start.10) | collective-permute-done | bytes 100384 | tf_op jit(solution)/shard_map/ppermute | solution.py:27
  92.7 1.8 %copy.6 = f32[224,8,256]{2,1,0:T(8,128)} copy(f32[224,8,256]{0,2,1:T(8,128)S(1)} %bitcast.50) | data formatting | bytes 3670016
  95.2 11.1 %shard_map.41 = f32[224,16]{1,0:T(8,128)} custom-call(f32[224,224]{1,0:T(8,128)} %maximum_select_fusion.gram_ref, f32[224,16]{1,0:T(8,128)} %copy.5.basis_ref), custom_call_target="tpu_custom_call" | custom-call | flops 45875200 | bytes 229376 | tf_op jit(solution)/shard_map/pallas_call | solution.py:177
  106.3 2.8 %fusion.69 = f32[2048,16]{1,0:T(8,128)S(1)} fusion(f32[2048,224]{1,0:T(8,128)S(1)} %bitcast.51, f32[224,16]{1,0:T(8,128)} %shard_map.41), kind=kOutput, calls=%fused_computation.124 | convolution fusion | flops 88080384 | bytes 1980416 | tf_op jit(solution)/shard_map/dot_general | solution.py:222
  109.0 1.6 %fusion.70 = f32[224,2048]{1,0:T(8,128)S(1)} fusion(f32[224,16]{1,0:T(8,128)S(1)} %copy-done.2, f32[2048,16]{1,0:T(8,128)S(1)} %fusion.69), kind=kOutput, calls=%fused_computation.125 | convolution fusion | flops 88080384 | bytes 1980416 | tf_op jit(solution)/shard_map/dot_general | solution.py:223
  110.7 2.0 %copy.7 = f32[28,8,8,256]{3,2,1,0:T(8,128)} copy(f32[28,8,8,256]{3,1,2,0:T(8,128)S(1)} %bitcast.55) | data formatting | bytes 3670016
  (51 shorter events, 8.1 us)
Async XLA Ops:
  2.5 40.4 %copy-start = (f32[224,8,256]{0,2,1:T(8,128)}, f32[224,8,256]{0,2,1:T(8,128)S(1)}, u32[]{:S(2)}) copy-start(f32[224,8,256]{0,2,1:T(8,128)S(1)} %copy.4) | copy-start | bytes 5505028
  4.1 27.6 %collective-permute-start = (f32[16,64,224]{2,1,0:T(8,128)}, f32[16,64,224]{2,1,0:T(8,128)S(1)}, u32[]{:S(2)}, u32[]{:S(2)}) collective-permute-start(f32[16,64,224]{2,1,0:T(8,128)} %bitcast.1), channel_id=1, source_target_pairs={{0,8},{8,16},{16,24},{1,9},{9,17},{17,25},{2,10},{10,18},{18,26},{... | collective-permute-start | bytes 2752520 | tf_op jit(solution)/shard_map/ppermute | solution.py:71
  9.1 26.8 %collective-permute-start.1 = (f32[16,64,224]{2,1,0:T(8,128)}, f32[16,64,224]{2,1,0:T(8,128)}, u32[]{:S(2)}, u32[]{:S(2)}) collective-permute-start(f32[16,64,224]{2,1,0:T(8,128)} %bitcast.3), channel_id=1, source_target_pairs={{8,0},{16,8},{24,16},{9,1},{17,9},{25,17},{10,2},{18,10},{26,18},{... | collective-permute-start | bytes 2752520 | tf_op jit(solution)/shard_map/ppermute | solution.py:71
  10.5 32.5 %collective-permute-start.4 = (f32[8,4,224]{2,1,0:T(4,128)S(1)}, f32[8,4,224]{2,1,0:T(4,128)S(1)}, u32[]{:S(2)}, u32[]{:S(2)}) collective-permute-start(f32[8,4,224]{2,1,0:T(4,128)S(1)} %get-tuple-element.4), channel_id=1, source_target_pairs={{0,1},{1,2},{2,3},{3,4},{4,5},{5,6},{6,7},{8,9},{9,10},{10,11},{11... | collective-permute-start | bytes 86024 | tf_op jit(solution)/shard_map/ppermute | solution.py:98
  11.9 31.0 %collective-permute-start.5 = (f32[8,4,224]{2,1,0:T(4,128)S(1)}, f32[8,4,224]{2,1,0:T(4,128)S(1)}, u32[]{:S(2)}, u32[]{:S(2)}) collective-permute-start(f32[8,4,224]{2,1,0:T(4,128)S(1)} %get-tuple-element.5), channel_id=1, source_target_pairs={{1,0},{2,1},{3,2},{4,3},{5,4},{6,5},{7,6},{9,8},{10,9},{11,10},{12... | collective-permute-start | bytes 86024 | tf_op jit(solution)/shard_map/ppermute | solution.py:99
  36.8 2.7 %collective-permute-start.2 = (f32[8,4,224]{2,1,0:T(4,128)S(1)}, f32[8,4,224]{2,1,0:T(4,128)S(1)}, u32[]{:S(2)}, u32[]{:S(2)}) collective-permute-start(f32[8,4,224]{2,1,0:T(4,128)S(1)} %get-tuple-element.6), channel_id=1, source_target_pairs={{0,1},{1,2},{2,3},{3,4},{4,5},{5,6},{6,7},{8,9},{9,10},{10,11},{11... | collective-permute-start | bytes 86024 | tf_op jit(solution)/shard_map/ppermute | solution.py:101
  38.1 4.8 %collective-permute-start.3 = (f32[8,4,224]{2,1,0:T(4,128)S(1)}, f32[8,4,224]{2,1,0:T(4,128)S(1)}, u32[]{:S(2)}, u32[]{:S(2)}) collective-permute-start(f32[8,4,224]{2,1,0:T(4,128)S(1)} %get-tuple-element.7), channel_id=1, source_target_pairs={{1,0},{2,1},{3,2},{4,3},{5,4},{6,5},{7,6},{9,8},{10,9},{11,10},{12... | collective-permute-start | bytes 86024 | tf_op jit(solution)/shard_map/ppermute | solution.py:102
  58.1 1.6 %copy-start.1 = (f32[224,8,256]{0,2,1:T(8,128)S(1)}, f32[224,8,256]{0,2,1:T(8,128)}, u32[]{:S(2)}) copy-start(f32[224,8,256]{0,2,1:T(8,128)} %copy-done) | copy-start | bytes 5505028
  61.7 30.2 %copy-start.3 = (f32[224,16]{0,1:T(8,128)S(1)}, f32[224,16]{0,1:T(8,128)}, u32[]{:S(2)}) copy-start(f32[224,16]{0,1:T(8,128)} %param.3) | copy-start | bytes 43012
  65.2 3.7 %collective-permute-start.6 = (f32[112,224]{1,0:T(8,128)S(1)}, f32[112,224]{1,0:T(8,128)S(1)}, u32[]{:S(2)}, u32[]{:S(2)}) collective-permute-start(f32[112,224]{1,0:T(8,128)S(1)} %slice_select_fusion), channel_id=1, source_target_pairs={{0,1},{1,0},{2,3},{3,2},{4,5},{5,4},{6,7},{7,6},{8,9},{9,8},{10,11... | collective-permute-start | bytes 301064 | tf_op jit(solution)/shard_map/ppermute | solution.py:44
  68.9 6.1 %collective-permute-start.7 = (f32[112,224]{1,0:T(8,128)S(1)}, f32[112,224]{1,0:T(8,128)S(1)}, u32[]{:S(2)}, u32[]{:S(2)}) collective-permute-start(f32[112,224]{1,0:T(8,128)S(1)} %select_add_fusion), channel_id=1, source_target_pairs={{0,2},{1,3},{2,0},{3,1},{4,6},{5,7},{6,4},{7,5},{8,10},{9,11},{10,... | collective-permute-start | bytes 301064 | tf_op jit(solution)/shard_map/ppermute | solution.py:27
  75.1 4.9 %collective-permute-start.8 = (f32[112,224]{1,0:T(8,128)S(1)}, f32[112,224]{1,0:T(8,128)S(1)}, u32[]{:S(2)}, u32[]{:S(2)}) collective-permute-start(f32[112,224]{1,0:T(8,128)S(1)} %add.155), channel_id=1, source_target_pairs={{0,4},{1,5},{2,6},{3,7},{4,0},{5,1},{6,2},{7,3},{8,12},{9,13},{10,... | collective-permute-start | bytes 301064 | tf_op jit(solution)/shard_map/ppermute | solution.py:27
  80.0 4.9 %collective-permute-start.9 = (f32[112,224]{1,0:T(8,128)S(1)}, f32[112,224]{1,0:T(8,128)S(1)}, u32[]{:S(2)}, u32[]{:S(2)}) collective-permute-start(f32[112,224]{1,0:T(8,128)S(1)} %add.156), channel_id=1, source_target_pairs={{0,8},{8,0},{16,24},{24,16},{1,9},{9,1},{17,25},{25,17},{2,10},{10... | collective-permute-start | bytes 301064 | tf_op jit(solution)/shard_map/ppermute | solution.py:27
  84.9 7.0 %collective-permute-start.10 = (f32[112,224]{1,0:T(8,128)S(1)}, f32[112,224]{1,0:T(8,128)S(1)}, u32[]{:S(2)}, u32[]{:S(2)}) collective-permute-start(f32[112,224]{1,0:T(8,128)S(1)} %add.157), channel_id=1, source_target_pairs={{0,16},{8,24},{16,0},{24,8},{1,17},{9,25},{17,1},{25,9},{2,18},{10... | collective-permute-start | bytes 301064 | tf_op jit(solution)/shard_map/ppermute | solution.py:27
  91.9 2.6 %collective-permute-start.11 = (f32[112,224]{1,0:T(8,128)S(1)}, f32[112,224]{1,0:T(8,128)S(1)}, u32[]{:S(2)}, u32[]{:S(2)}) collective-permute-start(f32[112,224]{1,0:T(8,128)S(1)} %add.158), channel_id=1, source_target_pairs={{0,1},{1,0},{2,3},{3,2},{4,5},{5,4},{6,7},{7,6},{8,9},{9,8},{10,11... | collective-permute-start | bytes 301064 | tf_op jit(solution)/shard_map/ppermute | solution.py:46
  106.3 2.8 %copy-start.2 = (f32[224,16]{1,0:T(8,128)S(1)}, f32[224,16]{1,0:T(8,128)}, u32[]{:S(2)}) copy-start(f32[224,16]{1,0:T(8,128)} %shard_map.41) | copy-start | bytes 43012

commit v16 on v15

--- a/solution.py
+++ b/solution.py
@@ -219,14 +219,21 @@
     gram_full = paired_sum(local_gram, order)
     basis_now = start_basis
     basis_now = subspace_step(gram_full, basis_now)
-    coeffs = jnp.dot(flat_cells, basis_now, precision=lax.Precision.HIGHEST)
+    coeffs = lax.dot_general(
+        basis_now,
+        smoothed,
+        (((0,), (0,)), ((), ())),
+        precision=lax.Precision.HIGHEST,
+        preferred_element_type=jnp.float32,
+    )
     lowrank = lax.dot_general(
         basis_now,
         coeffs,
-        (((1,), (1,)), ((), ())),
+        (((1,), (0,)), ((), ())),
         precision=lax.Precision.HIGHEST,
-    )
-    return (smoothed, lowrank.reshape(band_count, tile_rows, tile_cols))
+        preferred_element_type=jnp.float32,
+    )
+    return (smoothed, lowrank)
 
 
 def solution(mesh):

time: 113 us -> 114 us (level)
    unnamed x12 -> x10, local copies, waits for them, and re-layouts: 7.09 us -> 7.4 us
where the time goes in v16:
time: 114 us
  waiting for transfers between devices  41.6 us (36%)
  starting transfers between devices  21.9 us (19%)
  other arithmetic  19.6 us (17%)
  Pallas kernels  11.1 us (10%)
  local copies, waits for them, and re-layouts  9.94 us (9%)
  matrix products  8.69 us (8%)
    ppermute x2, waiting for transfers between devices, flat_permute(): return lax.ppermute(flat, axis, pairs).reshape(block.shape)  21.9 us
    ppermute x4, waiting for transfers between devices, butterfly_sum(): partner = lax.ppermute(value, axis, [(i, i ^ step) for i in range(count)])  15.3 us
    select_n x4, other arithmetic, sweep(): return jnp.where(keep, new, 0.0)  11.7 us
    pallas_call x1, Pallas kernels, subspace_step(): pl.pallas_call(subspace_kernel, out_shape=jax.ShapeDtypeStruct(basis.shap...  11.1 us
    ppermute x4, starting transfers between devices, butterfly_sum(): partner = lax.ppermute(value, axis, [(i, i ^ step) for i in range(count)])  7.57 us
    unnamed x10, local copies, waits for them, and re-layouts  7.4 us
    ppermute x2, starting transfers between devices, flat_permute(): return lax.ppermute(flat, axis, pairs).reshape(block.shape)  6.27 us
    reduce_sum x4, other arithmetic, sweep(): jnp.sum(diff_col * diff_col + diff_row * diff_row, axis=-1, keepdims=True)  4.09 us
  transfers between devices with their start and end apart: 12, of which 8 were waited for; matrix products, arithmetic and copies ran while one was open for 4% of the time, Pallas kernels for 0%

profile of v16, /device:TPU:0, one launch (start us, length us, event | category | flops | bytes accessed | tf_op | source)
XLA Modules:
  0.0 113.8 jit_solution(4466656596950792167)
XLA Ops:
  0.6 1.9 %copy.4 = f32[224,8,256]{0,2,1:T(8,128)S(1)} copy(f32[224,8,256]{2,1,0:T(8,128)} %param.2) | data formatting | bytes 3670016 | tf_op args[0]
  2.5 1.6 %fusion.71 = (f32[4,256,224]{2,1,0:T(8,128)}, f32[4,256,224]{2,1,0:T(8,128)}) fusion(f32[8,256,224]{2,1,0:T(8,128)S(1)} %bitcast.53), kind=kLoop, calls=%fused_computation.126 | loop fusion | bytes 3670016 | tf_op jit(solution)/shard_map/slice | solution.py:96
  4.1 5.0 %collective-permute-start = (f32[16,64,224]{2,1,0:T(8,128)}, f32[16,64,224]{2,1,0:T(8,128)S(1)}, u32[]{:S(2)}, u32[]{:S(2)}) collective-permute-start(f32[16,64,224]{2,1,0:T(8,128)} %bitcast.1), channel_id=1, source_target_pairs={{0,8},{8,16},{16,24},{1,9},{9,17},{17,25},{2,10},{10,18},{18,26},{... | collective-permute-start | bytes 2752520 | tf_op jit(solution)/shard_map/ppermute | solution.py:71
  9.1 1.3 %collective-permute-start.1 = (f32[16,64,224]{2,1,0:T(8,128)}, f32[16,64,224]{2,1,0:T(8,128)}, u32[]{:S(2)}, u32[]{:S(2)}) collective-permute-start(f32[16,64,224]{2,1,0:T(8,128)} %bitcast.3), channel_id=1, source_target_pairs={{8,0},{16,8},{24,16},{9,1},{17,9},{25,17},{10,2},{18,10},{26,18},{... | collective-permute-start | bytes 2752520 | tf_op jit(solution)/shard_map/ppermute | solution.py:71
  10.5 1.5 %collective-permute-start.4 = (f32[8,4,224]{2,1,0:T(4,128)S(1)}, f32[8,4,224]{2,1,0:T(4,128)S(1)}, u32[]{:S(2)}, u32[]{:S(2)}) collective-permute-start(f32[8,4,224]{2,1,0:T(4,128)S(1)} %get-tuple-element.4), channel_id=1, source_target_pairs={{0,1},{1,2},{2,3},{3,4},{4,5},{5,6},{6,7},{8,9},{9,10},{10,11},{11... | collective-permute-start | bytes 86024 | tf_op jit(solution)/shard_map/ppermute | solution.py:98
  11.9 1.3 %collective-permute-start.5 = (f32[8,4,224]{2,1,0:T(4,128)S(1)}, f32[8,4,224]{2,1,0:T(4,128)S(1)}, u32[]{:S(2)}, u32[]{:S(2)}) collective-permute-start(f32[8,4,224]{2,1,0:T(4,128)S(1)} %get-tuple-element.5), channel_id=1, source_target_pairs={{1,0},{2,1},{3,2},{4,3},{5,4},{6,5},{7,6},{9,8},{10,9},{11,10},{12... | collective-permute-start | bytes 86024 | tf_op jit(solution)/shard_map/ppermute | solution.py:99
  14.1 17.7 %collective-permute-done = f32[16,64,224]{2,1,0:T(8,128)S(1)} collective-permute-done((f32[16,64,224]{2,1,0:T(8,128)}, f32[16,64,224]{2,1,0:T(8,128)S(1)}, u32[]{:S(2)}, u32[]{:S(2)}) %collective-permute-start) | collective-permute-done | bytes 917536 | tf_op jit(solution)/shard_map/ppermute | solution.py:71
  31.8 4.2 %collective-permute-done.1 = f32[16,64,224]{2,1,0:T(8,128)} collective-permute-done((f32[16,64,224]{2,1,0:T(8,128)}, f32[16,64,224]{2,1,0:T(8,128)}, u32[]{:S(2)}, u32[]{:S(2)}) %collective-permute-start.1) | collective-permute-done | bytes 917536 | tf_op jit(solution)/shard_map/ppermute | solution.py:71
  36.8 1.3 %collective-permute-start.2 = (f32[8,4,224]{2,1,0:T(4,128)S(1)}, f32[8,4,224]{2,1,0:T(4,128)S(1)}, u32[]{:S(2)}, u32[]{:S(2)}) collective-permute-start(f32[8,4,224]{2,1,0:T(4,128)S(1)} %get-tuple-element.6), channel_id=1, source_target_pairs={{0,1},{1,2},{2,3},{3,4},{4,5},{5,6},{6,7},{8,9},{9,10},{10,11},{11... | collective-permute-start | bytes 86024 | tf_op jit(solution)/shard_map/ppermute | solution.py:101
  38.1 1.3 %collective-permute-start.3 = (f32[8,4,224]{2,1,0:T(4,128)S(1)}, f32[8,4,224]{2,1,0:T(4,128)S(1)}, u32[]{:S(2)}, u32[]{:S(2)}) collective-permute-start(f32[8,4,224]{2,1,0:T(4,128)S(1)} %get-tuple-element.7), channel_id=1, source_target_pairs={{1,0},{2,1},{3,2},{4,3},{5,4},{6,5},{7,6},{9,8},{10,9},{11,10},{12... | collective-permute-start | bytes 86024 | tf_op jit(solution)/shard_map/ppermute | solution.py:102
  39.4 3.5 %collective-permute-done.3 = f32[8,4,224]{2,1,0:T(4,128)S(1)} collective-permute-done((f32[8,4,224]{2,1,0:T(4,128)S(1)}, f32[8,4,224]{2,1,0:T(4,128)S(1)}, u32[]{:S(2)}, u32[]{:S(2)}) %collective-permute-start.3) | collective-permute-done | bytes 28704 | tf_op jit(solution)/shard_map/ppermute | solution.py:102
  43.0 1.8 %maximum_maximum_fusion = f32[16,264,224]{2,1,0:T(8,128)S(1)} fusion(f32[4,4,224]{2,1,0:T(4,128)S(1)} %get-tuple-element.13, f32[4,256,224]{2,1,0:T(8,128)} %bitcast.4, f32[4,4,224]{2,1,0:T(4,128)S(1)} %get-tuple-element.11, f32[8,4,224]{2,1,0:T(4,128)S(1)} %collective-permute-done.5, f32[8,256,224]{2,1,0:T(8,128)S(1)} %bitcast.55, ...), kind=kLoop, calls=%fused_computation | loop fusion | flops 7569408 | bytes 7569408 | tf_op jit(solution)/shard_map/concatenate | solution.py:103
  44.8 1.3 %fusion.2 = f32[15,263]{1,0:T(8,128)S(1)} fusion(f32[16,264,224]{2,1,0:T(8,128)S(1)} %maximum_maximum_fusion), kind=kLoop, calls=%fused_computation.4 | loop fusion | flops 5298135 | bytes 10619940 | tf_op jit(solution)/shard_map/reduce_sum | solution.py:123
  46.2 3.6 %fusion.9 = f32[14,262,224]{2,1,0:T(8,128)S(1)} fusion(f32[16,264,224]{2,1,0:T(8,128)S(1)} %maximum_maximum_fusion, f32[14,262]{1,0:T(8,128)S(1)} %get-tuple-element.24, f32[14,262]{1,0:T(8,128)S(1)} %get-tuple-element.25, f32[14,262]{1,0:T(8,128)S(1)} %get-tuple-element.23, pred[14,262]{1,0:T(8,128)(4,1)S(1)} %broadcast_and_fusion), kind=kLoop, calls=%fused_computation.13 | loop fusion | flops 13967744 | bytes 19766852 | tf_op jit(solution)/shard_map/jit(_where)/select_n | solution.py:132
  49.8 1.1 fusion.17
  51.0 3.4 %fusion.21 = f32[12,260,224]{2,1,0:T(8,128)S(1)} fusion(f32[16,264,224]{2,1,0:T(8,128)S(1)} %maximum_maximum_fusion, f32[14,262,224]{2,1,0:T(8,128)S(1)} %fusion.9, f32[12,260]{1,0:T(8,128)S(1)} %get-tuple-element.21, f32[12,260]{1,0:T(8,128)S(1)} %get-tuple-element.22, f32[12,260]{1,0:T(8,128)S(1)} %get-tuple-element.20, ...), kind=kLoop, calls=%fused_computation.31 | loop fusion | flops 11880960 | bytes 19609200 | tf_op jit(solution)/shard_map/jit(_where)/select_n | solution.py:132
  55.4 2.7 %fusion.37 = f32[10,258,224]{2,1,0:T(8,128)S(1)} fusion(f32[16,264,224]{2,1,0:T(8,128)S(1)} %maximum_maximum_fusion, f32[12,260,224]{2,1,0:T(8,128)S(1)} %fusion.21, f32[10,258]{1,0:T(8,128)S(1)} %get-tuple-element.18, f32[10,258]{1,0:T(8,128)S(1)} %get-tuple-element.19, f32[10,258]{1,0:T(8,128)S(1)} %get-tuple-element.17, ...), kind=kLoop, calls=%fused_computation.54 | loop fusion | flops 9824640 | bytes 16215300 | tf_op jit(solution)/shard_map/jit(_where)/select_n | solution.py:132
  59.7 2.0 %fusion.56 = f32[8,256,224]{2,1,0:T(8,128)S(1)} fusion(f32[10,258,224]{2,1,0:T(8,128)S(1)} %fusion.37, f32[8,256]{1,0:T(8,128)S(1)} %get-tuple-element.15, f32[8,256]{1,0:T(8,128)S(1)} %get-tuple-element.16, f32[8,256]{1,0:T(8,128)S(1)} %get-tuple-element.14, pred[8,256]{1,0:T(8,128)(4,1)S(1)} %broadcast_and_fusion.3, f32[224,8,256]{0,2,1:T(8,128)S(1)} %copy-done.1), kind=kLoop, calls=%fused_computation.80 | loop fusion | flops 7798784 | bytes 12871680 | tf_op jit(solution)/shard_map/jit(_where)/select_n | solution.py:132
  61.7 3.5 %convolution_bitcast_fusion = f32[224,224]{1,0:T(8,128)S(1)} fusion(f32[8,256,224]{2,1,0:T(8,128)S(1)} %fusion.56), kind=kOutput, calls=%fused_computation.89 | convolution fusion | flops 1233125376 | bytes 2035712 | tf_op jit(solution)/shard_map/dot_general | solution.py:212
  65.2 2.7 %collective-permute-start.6 = (f32[112,224]{1,0:T(8,128)S(1)}, f32[112,224]{1,0:T(8,128)S(1)}, u32[]{:S(2)}, u32[]{:S(2)}) collective-permute-start(f32[112,224]{1,0:T(8,128)S(1)} %slice_select_fusion), channel_id=1, source_target_pairs={{0,1},{1,0},{2,3},{3,2},{4,5},{5,4},{6,7},{7,6},{8,9},{9,8},{10,11... | collective-permute-start | bytes 301064 | tf_op jit(solution)/shard_map/ppermute | solution.py:44
  68.9 2.5 %collective-permute-start.7 = (f32[112,224]{1,0:T(8,128)S(1)}, f32[112,224]{1,0:T(8,128)S(1)}, u32[]{:S(2)}, u32[]{:S(2)}) collective-permute-start(f32[112,224]{1,0:T(8,128)S(1)} %select_add_fusion), channel_id=1, source_target_pairs={{0,2},{1,3},{2,0},{3,1},{4,6},{5,7},{6,4},{7,5},{8,10},{9,11},{10,... | collective-permute-start | bytes 301064 | tf_op jit(solution)/shard_map/ppermute | solution.py:27
  71.4 3.7 %collective-permute-done.7 = f32[112,224]{1,0:T(8,128)S(1)} collective-permute-done((f32[112,224]{1,0:T(8,128)S(1)}, f32[112,224]{1,0:T(8,128)S(1)}, u32[]{:S(2)}, u32[]{:S(2)}) %collective-permute-start.7) | collective-permute-done | bytes 100384 | tf_op jit(solution)/shard_map/ppermute | solution.py:27
  76.0 4.0 %collective-permute-done.8 = f32[112,224]{1,0:T(8,128)S(1)} collective-permute-done((f32[112,224]{1,0:T(8,128)S(1)}, f32[112,224]{1,0:T(8,128)S(1)}, u32[]{:S(2)}, u32[]{:S(2)}) %collective-permute-start.8) | collective-permute-done | bytes 100384 | tf_op jit(solution)/shard_map/ppermute | solution.py:27
  80.0 1.6 %collective-permute-start.9 = (f32[112,224]{1,0:T(8,128)S(1)}, f32[112,224]{1,0:T(8,128)S(1)}, u32[]{:S(2)}, u32[]{:S(2)}) collective-permute-start(f32[112,224]{1,0:T(8,128)S(1)} %add.156), channel_id=1, source_target_pairs={{0,8},{8,0},{16,24},{24,16},{1,9},{9,1},{17,25},{25,17},{2,10},{10... | collective-permute-start | bytes 301064 | tf_op jit(solution)/shard_map/ppermute | solution.py:27
  81.6 3.3 %collective-permute-done.9 = f32[112,224]{1,0:T(8,128)S(1)} collective-permute-done((f32[112,224]{1,0:T(8,128)S(1)}, f32[112,224]{1,0:T(8,128)S(1)}, u32[]{:S(2)}, u32[]{:S(2)}) %collective-permute-start.9) | collective-permute-done | bytes 100384 | tf_op jit(solution)/shard_map/ppermute | solution.py:27
  84.9 2.6 %collective-permute-start.10 = (f32[112,224]{1,0:T(8,128)S(1)}, f32[112,224]{1,0:T(8,128)S(1)}, u32[]{:S(2)}, u32[]{:S(2)}) collective-permute-start(f32[112,224]{1,0:T(8,128)S(1)} %add.157), channel_id=1, source_target_pairs={{0,16},{8,24},{16,0},{24,8},{1,17},{9,25},{17,1},{25,9},{2,18},{10... | collective-permute-start | bytes 301064 | tf_op jit(solution)/shard_map/ppermute | solution.py:27
  87.5 4.4 %collective-permute-done.10 = f32[112,224]{1,0:T(8,128)S(1)} collective-permute-done((f32[112,224]{1,0:T(8,128)S(1)}, f32[112,224]{1,0:T(8,128)S(1)}, u32[]{:S(2)}, u32[]{:S(2)}) %collective-permute-start.10) | collective-permute-done | bytes 100384 | tf_op jit(solution)/shard_map/ppermute | solution.py:27
  92.7 1.8 %copy.7 = f32[224,8,256]{2,1,0:T(8,128)} copy(f32[224,8,256]{0,2,1:T(8,128)S(1)} %bitcast.52) | data formatting | bytes 3670016
  95.2 11.1 %shard_map.41 = f32[224,16]{1,0:T(8,128)} custom-call(f32[224,224]{1,0:T(8,128)} %maximum_select_fusion.gram_ref, f32[224,16]{1,0:T(8,128)} %copy.5.basis_ref), custom_call_target="tpu_custom_call" | custom-call | flops 45875200 | bytes 229376 | tf_op jit(solution)/shard_map/pallas_call | solution.py:177
  106.3 2.7 %fusion.62 = f32[16,8,256]{2,0,1:T(8,128)S(1)} fusion(f32[224,16]{1,0:T(8,128)} %shard_map.41, f32[8,256,224]{2,1,0:T(8,128)S(1)} %fusion.56), kind=kOutput, calls=%fused_computation.91 | convolution fusion | flops 88080384 | bytes 1980416 | tf_op jit(solution)/shard_map/dot_general | solution.py:222
  109.0 2.5 %fusion.64 = f32[224,8,256]{2,0,1:T(8,128)S(1)} fusion(f32[16,8,256]{2,0,1:T(8,128)S(1)} %fusion.62, f32[224,16]{1,0:T(8,128)} %shard_map.41), kind=kOutput, calls=%fused_computation.93 | convolution fusion | flops 88080384 | bytes 1980416 | tf_op jit(solution)/shard_map/dot_general | solution.py:229
  111.5 2.3 %copy.8 = f32[224,8,256]{2,1,0:T(8,128)} copy(f32[224,8,256]{2,0,1:T(8,128)S(1)} %fusion.64) | data formatting | bytes 3670016
  (49 shorter events, 8.1 us)
Async XLA Ops:
  2.5 40.4 %copy-start = (f32[224,8,256]{0,2,1:T(8,128)}, f32[224,8,256]{0,2,1:T(8,128)S(1)}, u32[]{:S(2)}) copy-start(f32[224,8,256]{0,2,1:T(8,128)S(1)} %copy.4) | copy-start | bytes 5505028
  4.1 27.6 %collective-permute-start = (f32[16,64,224]{2,1,0:T(8,128)}, f32[16,64,224]{2,1,0:T(8,128)S(1)}, u32[]{:S(2)}, u32[]{:S(2)}) collective-permute-start(f32[16,64,224]{2,1,0:T(8,128)} %bitcast.1), channel_id=1, source_target_pairs={{0,8},{8,16},{16,24},{1,9},{9,17},{17,25},{2,10},{10,18},{18,26},{... | collective-permute-start | bytes 2752520 | tf_op jit(solution)/shard_map/ppermute | solution.py:71
  9.1 26.8 %collective-permute-start.1 = (f32[16,64,224]{2,1,0:T(8,128)}, f32[16,64,224]{2,1,0:T(8,128)}, u32[]{:S(2)}, u32[]{:S(2)}) collective-permute-start(f32[16,64,224]{2,1,0:T(8,128)} %bitcast.3), channel_id=1, source_target_pairs={{8,0},{16,8},{24,16},{9,1},{17,9},{25,17},{10,2},{18,10},{26,18},{... | collective-permute-start | bytes 2752520 | tf_op jit(solution)/shard_map/ppermute | solution.py:71
  10.5 32.5 %collective-permute-start.4 = (f32[8,4,224]{2,1,0:T(4,128)S(1)}, f32[8,4,224]{2,1,0:T(4,128)S(1)}, u32[]{:S(2)}, u32[]{:S(2)}) collective-permute-start(f32[8,4,224]{2,1,0:T(4,128)S(1)} %get-tuple-element.4), channel_id=1, source_target_pairs={{0,1},{1,2},{2,3},{3,4},{4,5},{5,6},{6,7},{8,9},{9,10},{10,11},{11... | collective-permute-start | bytes 86024 | tf_op jit(solution)/shard_map/ppermute | solution.py:98
  11.9 31.0 %collective-permute-start.5 = (f32[8,4,224]{2,1,0:T(4,128)S(1)}, f32[8,4,224]{2,1,0:T(4,128)S(1)}, u32[]{:S(2)}, u32[]{:S(2)}) collective-permute-start(f32[8,4,224]{2,1,0:T(4,128)S(1)} %get-tuple-element.5), channel_id=1, source_target_pairs={{1,0},{2,1},{3,2},{4,3},{5,4},{6,5},{7,6},{9,8},{10,9},{11,10},{12... | collective-permute-start | bytes 86024 | tf_op jit(solution)/shard_map/ppermute | solution.py:99
  36.8 2.7 %collective-permute-start.2 = (f32[8,4,224]{2,1,0:T(4,128)S(1)}, f32[8,4,224]{2,1,0:T(4,128)S(1)}, u32[]{:S(2)}, u32[]{:S(2)}) collective-permute-start(f32[8,4,224]{2,1,0:T(4,128)S(1)} %get-tuple-element.6), channel_id=1, source_target_pairs={{0,1},{1,2},{2,3},{3,4},{4,5},{5,6},{6,7},{8,9},{9,10},{10,11},{11... | collective-permute-start | bytes 86024 | tf_op jit(solution)/shard_map/ppermute | solution.py:101
  38.1 4.8 %collective-permute-start.3 = (f32[8,4,224]{2,1,0:T(4,128)S(1)}, f32[8,4,224]{2,1,0:T(4,128)S(1)}, u32[]{:S(2)}, u32[]{:S(2)}) collective-permute-start(f32[8,4,224]{2,1,0:T(4,128)S(1)} %get-tuple-element.7), channel_id=1, source_target_pairs={{1,0},{2,1},{3,2},{4,3},{5,4},{6,5},{7,6},{9,8},{10,9},{11,10},{12... | collective-permute-start | bytes 86024 | tf_op jit(solution)/shard_map/ppermute | solution.py:102
  58.1 1.6 %copy-start.1 = (f32[224,8,256]{0,2,1:T(8,128)S(1)}, f32[224,8,256]{0,2,1:T(8,128)}, u32[]{:S(2)}) copy-start(f32[224,8,256]{0,2,1:T(8,128)} %copy-done) | copy-start | bytes 5505028
  61.7 30.2 %copy-start.2 = (f32[224,16]{0,1:T(8,128)S(1)}, f32[224,16]{0,1:T(8,128)}, u32[]{:S(2)}) copy-start(f32[224,16]{0,1:T(8,128)} %param.3) | copy-start | bytes 43012
  65.2 3.7 %collective-permute-start.6 = (f32[112,224]{1,0:T(8,128)S(1)}, f32[112,224]{1,0:T(8,128)S(1)}, u32[]{:S(2)}, u32[]{:S(2)}) collective-permute-start(f32[112,224]{1,0:T(8,128)S(1)} %slice_select_fusion), channel_id=1, source_target_pairs={{0,1},{1,0},{2,3},{3,2},{4,5},{5,4},{6,7},{7,6},{8,9},{9,8},{10,11... | collective-permute-start | bytes 301064 | tf_op jit(solution)/shard_map/ppermute | solution.py:44
  68.9 6.1 %collective-permute-start.7 = (f32[112,224]{1,0:T(8,128)S(1)}, f32[112,224]{1,0:T(8,128)S(1)}, u32[]{:S(2)}, u32[]{:S(2)}) collective-permute-start(f32[112,224]{1,0:T(8,128)S(1)} %select_add_fusion), channel_id=1, source_target_pairs={{0,2},{1,3},{2,0},{3,1},{4,6},{5,7},{6,4},{7,5},{8,10},{9,11},{10,... | collective-permute-start | bytes 301064 | tf_op jit(solution)/shard_map/ppermute | solution.py:27
  75.1 4.9 %collective-permute-start.8 = (f32[112,224]{1,0:T(8,128)S(1)}, f32[112,224]{1,0:T(8,128)S(1)}, u32[]{:S(2)}, u32[]{:S(2)}) collective-permute-start(f32[112,224]{1,0:T(8,128)S(1)} %add.155), channel_id=1, source_target_pairs={{0,4},{1,5},{2,6},{3,7},{4,0},{5,1},{6,2},{7,3},{8,12},{9,13},{10,... | collective-permute-start | bytes 301064 | tf_op jit(solution)/shard_map/ppermute | solution.py:27
  80.0 4.9 %collective-permute-start.9 = (f32[112,224]{1,0:T(8,128)S(1)}, f32[112,224]{1,0:T(8,128)S(1)}, u32[]{:S(2)}, u32[]{:S(2)}) collective-permute-start(f32[112,224]{1,0:T(8,128)S(1)} %add.156), channel_id=1, source_target_pairs={{0,8},{8,0},{16,24},{24,16},{1,9},{9,1},{17,25},{25,17},{2,10},{10... | collective-permute-start | bytes 301064 | tf_op jit(solution)/shard_map/ppermute | solution.py:27
  84.9 7.0 %collective-permute-start.10 = (f32[112,224]{1,0:T(8,128)S(1)}, f32[112,224]{1,0:T(8,128)S(1)}, u32[]{:S(2)}, u32[]{:S(2)}) collective-permute-start(f32[112,224]{1,0:T(8,128)S(1)} %add.157), channel_id=1, source_target_pairs={{0,16},{8,24},{16,0},{24,8},{1,17},{9,25},{17,1},{25,9},{2,18},{10... | collective-permute-start | bytes 301064 | tf_op jit(solution)/shard_map/ppermute | solution.py:27
  91.9 2.6 %collective-permute-start.11 = (f32[112,224]{1,0:T(8,128)S(1)}, f32[112,224]{1,0:T(8,128)S(1)}, u32[]{:S(2)}, u32[]{:S(2)}) collective-permute-start(f32[112,224]{1,0:T(8,128)S(1)} %add.158), channel_id=1, source_target_pairs={{0,1},{1,0},{2,3},{3,2},{4,5},{5,4},{6,7},{7,6},{8,9},{9,8},{10,11... | collective-permute-start | bytes 301064 | tf_op jit(solution)/shard_map/ppermute | solution.py:46

commit v17 on v15

--- a/solution.py
+++ b/solution.py
@@ -213,18 +213,18 @@
         flat_cells,
         flat_cells,
         (((0,), (0,)), ((), ())),
-        precision=lax.Precision.HIGHEST,
+        precision=lax.Precision.HIGH,
         preferred_element_type=jnp.float32,
     )
     gram_full = paired_sum(local_gram, order)
     basis_now = start_basis
     basis_now = subspace_step(gram_full, basis_now)
-    coeffs = jnp.dot(flat_cells, basis_now, precision=lax.Precision.HIGHEST)
+    coeffs = jnp.dot(flat_cells, basis_now, precision=lax.Precision.HIGH)
     lowrank = lax.dot_general(
         basis_now,
         coeffs,
         (((1,), (1,)), ((), ())),
-        precision=lax.Precision.HIGHEST,
+        precision=lax.Precision.HIGH,
     )
     return (smoothed, lowrank.reshape(band_count, tile_rows, tile_cols))
 

time: 113 us -> 110 us (0.973)
  matrix products: 7.86 us -> 4.64 us
    dot_general x1, matrix products: 3.47 us -> 1.8 us  [shards(): lax.dot_general(flat_cells, flat_cells, (((0,), (0,)), ((), ())), precisi...]
where the time goes in v17:
time: 110 us; the launch traced here: 109 us
  waiting for transfers between devices  41.6 us (38%)
  starting transfers between devices  21.9 us (20%)
  other arithmetic  19.6 us (18%)
  Pallas kernels  11.1 us (10%)
  local copies, waits for them, and re-layouts  9.63 us (9%)
  matrix products  4.64 us (4%)
    ppermute x2, waiting for transfers between devices, flat_permute(): return lax.ppermute(flat, axis, pairs).reshape(block.shape)  21.9 us
    ppermute x4, waiting for transfers between devices, butterfly_sum(): partner = lax.ppermute(value, axis, [(i, i ^ step) for i in range(count)])  15.3 us
    select_n x4, other arithmetic, sweep(): return jnp.where(keep, new, 0.0)  11.7 us
    pallas_call x1, Pallas kernels, subspace_step(): pl.pallas_call(subspace_kernel, out_shape=jax.ShapeDtypeStruct(basis.shap...  11.1 us
    ppermute x4, starting transfers between devices, butterfly_sum(): partner = lax.ppermute(value, axis, [(i, i ^ step) for i in range(count)])  7.57 us
    unnamed x12, local copies, waits for them, and re-layouts  7.09 us
    ppermute x2, starting transfers between devices, flat_permute(): return lax.ppermute(flat, axis, pairs).reshape(block.shape)  6.27 us
    reduce_sum x4, other arithmetic, sweep(): jnp.sum(diff_col * diff_col + diff_row * diff_row, axis=-1, keepdims=True)  4.09 us
  transfers between devices with their start and end apart: 12, of which 8 were waited for; matrix products, arithmetic and copies ran while one was open for 4% of the time, Pallas kernels for 0%

profile of v17, /device:TPU:0, one launch (start us, length us, event | category | flops | bytes accessed | tf_op | source)
XLA Modules:
  0.0 109.4 jit_solution(2276623540440631714)
XLA Ops:
  0.6 1.9 %copy.4 = f32[224,8,256]{0,2,1:T(8,128)S(1)} copy(f32[224,8,256]{2,1,0:T(8,128)} %param.2) | data formatting | bytes 3670016 | tf_op args[0]
  2.5 1.6 %fusion.66 = (f32[4,256,224]{2,1,0:T(8,128)}, f32[4,256,224]{2,1,0:T(8,128)}) fusion(f32[8,256,224]{2,1,0:T(8,128)S(1)} %bitcast.52), kind=kLoop, calls=%fused_computation.121 | loop fusion | bytes 3670016 | tf_op jit(solution)/shard_map/slice | solution.py:96
  4.1 5.0 %collective-permute-start = (f32[16,64,224]{2,1,0:T(8,128)}, f32[16,64,224]{2,1,0:T(8,128)S(1)}, u32[]{:S(2)}, u32[]{:S(2)}) collective-permute-start(f32[16,64,224]{2,1,0:T(8,128)} %bitcast.1), channel_id=1, source_target_pairs={{0,8},{8,16},{16,24},{1,9},{9,17},{17,25},{2,10},{10,18},{18,26},{... | collective-permute-start | bytes 2752520 | tf_op jit(solution)/shard_map/ppermute | solution.py:71
  9.1 1.3 %collective-permute-start.1 = (f32[16,64,224]{2,1,0:T(8,128)}, f32[16,64,224]{2,1,0:T(8,128)}, u32[]{:S(2)}, u32[]{:S(2)}) collective-permute-start(f32[16,64,224]{2,1,0:T(8,128)} %bitcast.3), channel_id=1, source_target_pairs={{8,0},{16,8},{24,16},{9,1},{17,9},{25,17},{10,2},{18,10},{26,18},{... | collective-permute-start | bytes 2752520 | tf_op jit(solution)/shard_map/ppermute | solution.py:71
  10.5 1.5 %collective-permute-start.4 = (f32[8,4,224]{2,1,0:T(4,128)S(1)}, f32[8,4,224]{2,1,0:T(4,128)S(1)}, u32[]{:S(2)}, u32[]{:S(2)}) collective-permute-start(f32[8,4,224]{2,1,0:T(4,128)S(1)} %get-tuple-element.4), channel_id=1, source_target_pairs={{0,1},{1,2},{2,3},{3,4},{4,5},{5,6},{6,7},{8,9},{9,10},{10,11},{11... | collective-permute-start | bytes 86024 | tf_op jit(solution)/shard_map/ppermute | solution.py:98
  11.9 1.3 %collective-permute-start.5 = (f32[8,4,224]{2,1,0:T(4,128)S(1)}, f32[8,4,224]{2,1,0:T(4,128)S(1)}, u32[]{:S(2)}, u32[]{:S(2)}) collective-permute-start(f32[8,4,224]{2,1,0:T(4,128)S(1)} %get-tuple-element.5), channel_id=1, source_target_pairs={{1,0},{2,1},{3,2},{4,3},{5,4},{6,5},{7,6},{9,8},{10,9},{11,10},{12... | collective-permute-start | bytes 86024 | tf_op jit(solution)/shard_map/ppermute | solution.py:99
  14.1 17.7 %collective-permute-done = f32[16,64,224]{2,1,0:T(8,128)S(1)} collective-permute-done((f32[16,64,224]{2,1,0:T(8,128)}, f32[16,64,224]{2,1,0:T(8,128)S(1)}, u32[]{:S(2)}, u32[]{:S(2)}) %collective-permute-start) | collective-permute-done | bytes 917536 | tf_op jit(solution)/shard_map/ppermute | solution.py:71
  31.8 4.2 %collective-permute-done.1 = f32[16,64,224]{2,1,0:T(8,128)} collective-permute-done((f32[16,64,224]{2,1,0:T(8,128)}, f32[16,64,224]{2,1,0:T(8,128)}, u32[]{:S(2)}, u32[]{:S(2)}) %collective-permute-start.1) | collective-permute-done | bytes 917536 | tf_op jit(solution)/shard_map/ppermute | solution.py:71
  36.8 1.3 %collective-permute-start.2 = (f32[8,4,224]{2,1,0:T(4,128)S(1)}, f32[8,4,224]{2,1,0:T(4,128)S(1)}, u32[]{:S(2)}, u32[]{:S(2)}) collective-permute-start(f32[8,4,224]{2,1,0:T(4,128)S(1)} %get-tuple-element.6), channel_id=1, source_target_pairs={{0,1},{1,2},{2,3},{3,4},{4,5},{5,6},{6,7},{8,9},{9,10},{10,11},{11... | collective-permute-start | bytes 86024 | tf_op jit(solution)/shard_map/ppermute | solution.py:101
  38.1 1.3 %collective-permute-start.3 = (f32[8,4,224]{2,1,0:T(4,128)S(1)}, f32[8,4,224]{2,1,0:T(4,128)S(1)}, u32[]{:S(2)}, u32[]{:S(2)}) collective-permute-start(f32[8,4,224]{2,1,0:T(4,128)S(1)} %get-tuple-element.7), channel_id=1, source_target_pairs={{1,0},{2,1},{3,2},{4,3},{5,4},{6,5},{7,6},{9,8},{10,9},{11,10},{12... | collective-permute-start | bytes 86024 | tf_op jit(solution)/shard_map/ppermute | solution.py:102
  39.4 3.5 %collective-permute-done.3 = f32[8,4,224]{2,1,0:T(4,128)S(1)} collective-permute-done((f32[8,4,224]{2,1,0:T(4,128)S(1)}, f32[8,4,224]{2,1,0:T(4,128)S(1)}, u32[]{:S(2)}, u32[]{:S(2)}) %collective-permute-start.3) | collective-permute-done | bytes 28704 | tf_op jit(solution)/shard_map/ppermute | solution.py:102
  43.0 1.8 %maximum_maximum_fusion = f32[16,264,224]{2,1,0:T(8,128)S(1)} fusion(f32[4,4,224]{2,1,0:T(4,128)S(1)} %get-tuple-element.13, f32[4,256,224]{2,1,0:T(8,128)} %bitcast.4, f32[4,4,224]{2,1,0:T(4,128)S(1)} %get-tuple-element.11, f32[8,4,224]{2,1,0:T(4,128)S(1)} %collective-permute-done.5, f32[8,256,224]{2,1,0:T(8,128)S(1)} %bitcast.54, ...), kind=kLoop, calls=%fused_computation | loop fusion | flops 7569408 | bytes 7569408 | tf_op jit(solution)/shard_map/concatenate | solution.py:103
  44.8 1.3 %fusion.2 = f32[15,263]{1,0:T(8,128)S(1)} fusion(f32[16,264,224]{2,1,0:T(8,128)S(1)} %maximum_maximum_fusion), kind=kLoop, calls=%fused_computation.4 | loop fusion | flops 5298135 | bytes 10619940 | tf_op jit(solution)/shard_map/reduce_sum | solution.py:123
  46.2 3.6 %fusion.9 = f32[14,262,224]{2,1,0:T(8,128)S(1)} fusion(f32[16,264,224]{2,1,0:T(8,128)S(1)} %maximum_maximum_fusion, f32[14,262]{1,0:T(8,128)S(1)} %get-tuple-element.24, f32[14,262]{1,0:T(8,128)S(1)} %get-tuple-element.25, f32[14,262]{1,0:T(8,128)S(1)} %get-tuple-element.23, pred[14,262]{1,0:T(8,128)(4,1)S(1)} %broadcast_and_fusion), kind=kLoop, calls=%fused_computation.13 | loop fusion | flops 13967744 | bytes 19766852 | tf_op jit(solution)/shard_map/jit(_where)/select_n | solution.py:132
  49.8 1.1 %fusion.17 = f32[13,261]{1,0:T(8,128)S(1)} fusion(f32[14,262,224]{2,1,0:T(8,128)S(1)} %fusion.9), kind=kLoop, calls=%fused_computation.25 | loop fusion | flops 4556799 | bytes 9133956 | tf_op jit(solution)/shard_map/reduce_sum | solution.py:123
  51.0 3.4 %fusion.21 = f32[12,260,224]{2,1,0:T(8,128)S(1)} fusion(f32[16,264,224]{2,1,0:T(8,128)S(1)} %maximum_maximum_fusion, f32[14,262,224]{2,1,0:T(8,128)S(1)} %fusion.9, f32[12,260]{1,0:T(8,128)S(1)} %get-tuple-element.21, f32[12,260]{1,0:T(8,128)S(1)} %get-tuple-element.22, f32[12,260]{1,0:T(8,128)S(1)} %get-tuple-element.20, ...), kind=kLoop, calls=%fused_computation.31 | loop fusion | flops 11880960 | bytes 19609200 | tf_op jit(solution)/shard_map/jit(_where)/select_n | solution.py:132
  55.4 2.7 %fusion.37 = f32[10,258,224]{2,1,0:T(8,128)S(1)} fusion(f32[16,264,224]{2,1,0:T(8,128)S(1)} %maximum_maximum_fusion, f32[12,260,224]{2,1,0:T(8,128)S(1)} %fusion.21, f32[10,258]{1,0:T(8,128)S(1)} %get-tuple-element.18, f32[10,258]{1,0:T(8,128)S(1)} %get-tuple-element.19, f32[10,258]{1,0:T(8,128)S(1)} %get-tuple-element.17, ...), kind=kLoop, calls=%fused_computation.54 | loop fusion | flops 9824640 | bytes 16215300 | tf_op jit(solution)/shard_map/jit(_where)/select_n | solution.py:132
  59.7 2.0 %fusion.56 = f32[8,256,224]{2,1,0:T(8,128)S(1)} fusion(f32[10,258,224]{2,1,0:T(8,128)S(1)} %fusion.37, f32[8,256]{1,0:T(8,128)S(1)} %get-tuple-element.15, f32[8,256]{1,0:T(8,128)S(1)} %get-tuple-element.16, f32[8,256]{1,0:T(8,128)S(1)} %get-tuple-element.14, pred[8,256]{1,0:T(8,128)(4,1)S(1)} %broadcast_and_fusion.3, f32[224,8,256]{0,2,1:T(8,128)S(1)} %copy-done.1), kind=kLoop, calls=%fused_computation.80 | loop fusion | flops 7798784 | bytes 12871680 | tf_op jit(solution)/shard_map/jit(_where)/select_n | solution.py:132
  61.7 1.8 %convolution_bitcast_fusion = f32[224,224]{1,0:T(8,128)S(1)} fusion(f32[8,256,224]{2,1,0:T(8,128)S(1)} %fusion.56), kind=kOutput, calls=%fused_computation.89 | convolution fusion | flops 616562688 | bytes 2035712 | tf_op jit(solution)/shard_map/dot_general | solution.py:212
  63.6 2.7 %collective-permute-start.6 = (f32[112,224]{1,0:T(8,128)S(1)}, f32[112,224]{1,0:T(8,128)S(1)}, u32[]{:S(2)}, u32[]{:S(2)}) collective-permute-start(f32[112,224]{1,0:T(8,128)S(1)} %slice_select_fusion), channel_id=1, source_target_pairs={{0,1},{1,0},{2,3},{3,2},{4,5},{5,4},{6,7},{7,6},{8,9},{9,8},{10,11... | collective-permute-start | bytes 301064 | tf_op jit(solution)/shard_map/ppermute | solution.py:44
  66.3 1.0 collective-permute-done.6
  67.3 2.5 %collective-permute-start.7 = (f32[112,224]{1,0:T(8,128)S(1)}, f32[112,224]{1,0:T(8,128)S(1)}, u32[]{:S(2)}, u32[]{:S(2)}) collective-permute-start(f32[112,224]{1,0:T(8,128)S(1)} %select_add_fusion), channel_id=1, source_target_pairs={{0,2},{1,3},{2,0},{3,1},{4,6},{5,7},{6,4},{7,5},{8,10},{9,11},{10,... | collective-permute-start | bytes 301064 | tf_op jit(solution)/shard_map/ppermute | solution.py:27
  69.7 3.7 %collective-permute-done.7 = f32[112,224]{1,0:T(8,128)S(1)} collective-permute-done((f32[112,224]{1,0:T(8,128)S(1)}, f32[112,224]{1,0:T(8,128)S(1)}, u32[]{:S(2)}, u32[]{:S(2)}) %collective-permute-start.7) | collective-permute-done | bytes 100384 | tf_op jit(solution)/shard_map/ppermute | solution.py:27
  74.3 4.0 %collective-permute-done.8 = f32[112,224]{1,0:T(8,128)S(1)} collective-permute-done((f32[112,224]{1,0:T(8,128)S(1)}, f32[112,224]{1,0:T(8,128)S(1)}, u32[]{:S(2)}, u32[]{:S(2)}) %collective-permute-start.8) | collective-permute-done | bytes 100384 | tf_op jit(solution)/shard_map/ppermute | solution.py:27
  78.3 1.6 %collective-permute-start.9 = (f32[112,224]{1,0:T(8,128)S(1)}, f32[112,224]{1,0:T(8,128)S(1)}, u32[]{:S(2)}, u32[]{:S(2)}) collective-permute-start(f32[112,224]{1,0:T(8,128)S(1)} %add.156), channel_id=1, source_target_pairs={{0,8},{8,0},{16,24},{24,16},{1,9},{9,1},{17,25},{25,17},{2,10},{10... | collective-permute-start | bytes 301064 | tf_op jit(solution)/shard_map/ppermute | solution.py:27
  79.9 3.3 %collective-permute-done.9 = f32[112,224]{1,0:T(8,128)S(1)} collective-permute-done((f32[112,224]{1,0:T(8,128)S(1)}, f32[112,224]{1,0:T(8,128)S(1)}, u32[]{:S(2)}, u32[]{:S(2)}) %collective-permute-start.9) | collective-permute-done | bytes 100384 | tf_op jit(solution)/shard_map/ppermute | solution.py:27
  83.2 2.6 %collective-permute-start.10 = (f32[112,224]{1,0:T(8,128)S(1)}, f32[112,224]{1,0:T(8,128)S(1)}, u32[]{:S(2)}, u32[]{:S(2)}) collective-permute-start(f32[112,224]{1,0:T(8,128)S(1)} %add.157), channel_id=1, source_target_pairs={{0,16},{8,24},{16,0},{24,8},{1,17},{9,25},{17,1},{25,9},{2,18},{10... | collective-permute-start | bytes 301064 | tf_op jit(solution)/shard_map/ppermute | solution.py:27
  85.8 4.4 %collective-permute-done.10 = f32[112,224]{1,0:T(8,128)S(1)} collective-permute-done((f32[112,224]{1,0:T(8,128)S(1)}, f32[112,224]{1,0:T(8,128)S(1)}, u32[]{:S(2)}, u32[]{:S(2)}) %collective-permute-start.10) | collective-permute-done | bytes 100384 | tf_op jit(solution)/shard_map/ppermute | solution.py:27
  91.0 1.8 %copy.6 = f32[224,8,256]{2,1,0:T(8,128)} copy(f32[224,8,256]{0,2,1:T(8,128)S(1)} %bitcast.50) | data formatting | bytes 3670016
  93.5 11.1 %shard_map.41 = f32[224,16]{1,0:T(8,128)} custom-call(f32[224,224]{1,0:T(8,128)} %maximum_select_fusion.gram_ref, f32[224,16]{1,0:T(8,128)} %copy.5.basis_ref), custom_call_target="tpu_custom_call" | custom-call | flops 45875200 | bytes 229376 | tf_op jit(solution)/shard_map/pallas_call | solution.py:177
  104.6 2.0 %fusion.69 = f32[2048,16]{1,0:T(8,128)S(1)} fusion(f32[2048,224]{1,0:T(8,128)S(1)} %bitcast.51, f32[224,16]{1,0:T(8,128)} %shard_map.41), kind=kOutput, calls=%fused_computation.124 | convolution fusion | flops 44040192 | bytes 1980416 | tf_op jit(solution)/shard_map/dot_general | solution.py:222
  107.5 2.0 %copy.7 = f32[28,8,8,256]{3,2,1,0:T(8,128)} copy(f32[28,8,8,256]{3,1,2,0:T(8,128)S(1)} %bitcast.55) | data formatting | bytes 3670016
  (51 shorter events, 8.0 us)
Async XLA Ops:
  2.5 40.4 %copy-start = (f32[224,8,256]{0,2,1:T(8,128)}, f32[224,8,256]{0,2,1:T(8,128)S(1)}, u32[]{:S(2)}) copy-start(f32[224,8,256]{0,2,1:T(8,128)S(1)} %copy.4) | copy-start | bytes 5505028
  4.1 27.6 %collective-permute-start = (f32[16,64,224]{2,1,0:T(8,128)}, f32[16,64,224]{2,1,0:T(8,128)S(1)}, u32[]{:S(2)}, u32[]{:S(2)}) collective-permute-start(f32[16,64,224]{2,1,0:T(8,128)} %bitcast.1), channel_id=1, source_target_pairs={{0,8},{8,16},{16,24},{1,9},{9,17},{17,25},{2,10},{10,18},{18,26},{... | collective-permute-start | bytes 2752520 | tf_op jit(solution)/shard_map/ppermute | solution.py:71
  9.1 26.8 %collective-permute-start.1 = (f32[16,64,224]{2,1,0:T(8,128)}, f32[16,64,224]{2,1,0:T(8,128)}, u32[]{:S(2)}, u32[]{:S(2)}) collective-permute-start(f32[16,64,224]{2,1,0:T(8,128)} %bitcast.3), channel_id=1, source_target_pairs={{8,0},{16,8},{24,16},{9,1},{17,9},{25,17},{10,2},{18,10},{26,18},{... | collective-permute-start | bytes 2752520 | tf_op jit(solution)/shard_map/ppermute | solution.py:71
  10.5 32.5 %collective-permute-start.4 = (f32[8,4,224]{2,1,0:T(4,128)S(1)}, f32[8,4,224]{2,1,0:T(4,128)S(1)}, u32[]{:S(2)}, u32[]{:S(2)}) collective-permute-start(f32[8,4,224]{2,1,0:T(4,128)S(1)} %get-tuple-element.4), channel_id=1, source_target_pairs={{0,1},{1,2},{2,3},{3,4},{4,5},{5,6},{6,7},{8,9},{9,10},{10,11},{11... | collective-permute-start | bytes 86024 | tf_op jit(solution)/shard_map/ppermute | solution.py:98
  11.9 31.0 %collective-permute-start.5 = (f32[8,4,224]{2,1,0:T(4,128)S(1)}, f32[8,4,224]{2,1,0:T(4,128)S(1)}, u32[]{:S(2)}, u32[]{:S(2)}) collective-permute-start(f32[8,4,224]{2,1,0:T(4,128)S(1)} %get-tuple-element.5), channel_id=1, source_target_pairs={{1,0},{2,1},{3,2},{4,3},{5,4},{6,5},{7,6},{9,8},{10,9},{11,10},{12... | collective-permute-start | bytes 86024 | tf_op jit(solution)/shard_map/ppermute | solution.py:99
  36.8 2.7 %collective-permute-start.2 = (f32[8,4,224]{2,1,0:T(4,128)S(1)}, f32[8,4,224]{2,1,0:T(4,128)S(1)}, u32[]{:S(2)}, u32[]{:S(2)}) collective-permute-start(f32[8,4,224]{2,1,0:T(4,128)S(1)} %get-tuple-element.6), channel_id=1, source_target_pairs={{0,1},{1,2},{2,3},{3,4},{4,5},{5,6},{6,7},{8,9},{9,10},{10,11},{11... | collective-permute-start | bytes 86024 | tf_op jit(solution)/shard_map/ppermute | solution.py:101
  38.1 4.8 %collective-permute-start.3 = (f32[8,4,224]{2,1,0:T(4,128)S(1)}, f32[8,4,224]{2,1,0:T(4,128)S(1)}, u32[]{:S(2)}, u32[]{:S(2)}) collective-permute-start(f32[8,4,224]{2,1,0:T(4,128)S(1)} %get-tuple-element.7), channel_id=1, source_target_pairs={{1,0},{2,1},{3,2},{4,3},{5,4},{6,5},{7,6},{9,8},{10,9},{11,10},{12... | collective-permute-start | bytes 86024 | tf_op jit(solution)/shard_map/ppermute | solution.py:102
  58.1 1.6 %copy-start.1 = (f32[224,8,256]{0,2,1:T(8,128)S(1)}, f32[224,8,256]{0,2,1:T(8,128)}, u32[]{:S(2)}) copy-start(f32[224,8,256]{0,2,1:T(8,128)} %copy-done) | copy-start | bytes 5505028
  61.7 28.6 %copy-start.3 = (f32[224,16]{0,1:T(8,128)S(1)}, f32[224,16]{0,1:T(8,128)}, u32[]{:S(2)}) copy-start(f32[224,16]{0,1:T(8,128)} %param.3) | copy-start | bytes 43012
  63.6 3.7 %collective-permute-start.6 = (f32[112,224]{1,0:T(8,128)S(1)}, f32[112,224]{1,0:T(8,128)S(1)}, u32[]{:S(2)}, u32[]{:S(2)}) collective-permute-start(f32[112,224]{1,0:T(8,128)S(1)} %slice_select_fusion), channel_id=1, source_target_pairs={{0,1},{1,0},{2,3},{3,2},{4,5},{5,4},{6,7},{7,6},{8,9},{9,8},{10,11... | collective-permute-start | bytes 301064 | tf_op jit(solution)/shard_map/ppermute | solution.py:44
  67.3 6.1 %collective-permute-start.7 = (f32[112,224]{1,0:T(8,128)S(1)}, f32[112,224]{1,0:T(8,128)S(1)}, u32[]{:S(2)}, u32[]{:S(2)}) collective-permute-start(f32[112,224]{1,0:T(8,128)S(1)} %select_add_fusion), channel_id=1, source_target_pairs={{0,2},{1,3},{2,0},{3,1},{4,6},{5,7},{6,4},{7,5},{8,10},{9,11},{10,... | collective-permute-start | bytes 301064 | tf_op jit(solution)/shard_map/ppermute | solution.py:27
  73.4 4.9 %collective-permute-start.8 = (f32[112,224]{1,0:T(8,128)S(1)}, f32[112,224]{1,0:T(8,128)S(1)}, u32[]{:S(2)}, u32[]{:S(2)}) collective-permute-start(f32[112,224]{1,0:T(8,128)S(1)} %add.155), channel_id=1, source_target_pairs={{0,4},{1,5},{2,6},{3,7},{4,0},{5,1},{6,2},{7,3},{8,12},{9,13},{10,... | collective-permute-start | bytes 301064 | tf_op jit(solution)/shard_map/ppermute | solution.py:27
  78.3 4.9 %collective-permute-start.9 = (f32[112,224]{1,0:T(8,128)S(1)}, f32[112,224]{1,0:T(8,128)S(1)}, u32[]{:S(2)}, u32[]{:S(2)}) collective-permute-start(f32[112,224]{1,0:T(8,128)S(1)} %add.156), channel_id=1, source_target_pairs={{0,8},{8,0},{16,24},{24,16},{1,9},{9,1},{17,25},{25,17},{2,10},{10... | collective-permute-start | bytes 301064 | tf_op jit(solution)/shard_map/ppermute | solution.py:27
  83.2 7.0 %collective-permute-start.10 = (f32[112,224]{1,0:T(8,128)S(1)}, f32[112,224]{1,0:T(8,128)S(1)}, u32[]{:S(2)}, u32[]{:S(2)}) collective-permute-start(f32[112,224]{1,0:T(8,128)S(1)} %add.157), channel_id=1, source_target_pairs={{0,16},{8,24},{16,0},{24,8},{1,17},{9,25},{17,1},{25,9},{2,18},{10... | collective-permute-start | bytes 301064 | tf_op jit(solution)/shard_map/ppermute | solution.py:27
  90.2 2.6 %collective-permute-start.11 = (f32[112,224]{1,0:T(8,128)S(1)}, f32[112,224]{1,0:T(8,128)S(1)}, u32[]{:S(2)}, u32[]{:S(2)}) collective-permute-start(f32[112,224]{1,0:T(8,128)S(1)} %add.158), channel_id=1, source_target_pairs={{0,1},{1,0},{2,3},{3,2},{4,5},{5,4},{6,7},{7,6},{8,9},{9,8},{10,11... | collective-permute-start | bytes 301064 | tf_op jit(solution)/shard_map/ppermute | solution.py:46
  104.6 2.0 %copy-start.2 = (f32[224,16]{1,0:T(8,128)S(1)}, f32[224,16]{1,0:T(8,128)}, u32[]{:S(2)}) copy-start(f32[224,16]{1,0:T(8,128)} %shard_map.41) | copy-start | bytes 43012

commit v18 on v17

--- a/solution.py
+++ b/solution.py
@@ -213,7 +213,7 @@
         flat_cells,
         flat_cells,
         (((0,), (0,)), ((), ())),
-        precision=lax.Precision.HIGH,
+        precision=lax.Precision.HIGHEST,
         preferred_element_type=jnp.float32,
     )
     gram_full = paired_sum(local_gram, order)

time: 110 us -> 112 us (1.018)
  matrix products: 4.64 us -> 6.32 us
    dot_general x1, matrix products: 1.8 us -> 3.47 us  [shards(): lax.dot_general(flat_cells, flat_cells, (((0,), (0,)), ((), ())), precisi...]
where the time goes in v18:
time: 112 us; the launch traced here: 111 us
  waiting for transfers between devices  41.6 us (37%)
  starting transfers between devices  21.9 us (20%)
  other arithmetic  19.6 us (18%)
  Pallas kernels  11.1 us (10%)
  local copies, waits for them, and re-layouts  9.63 us (9%)
  matrix products  6.32 us (6%)
    ppermute x2, waiting for transfers between devices, flat_permute(): return lax.ppermute(flat, axis, pairs).reshape(block.shape)  21.9 us
    ppermute x4, waiting for transfers between devices, butterfly_sum(): partner = lax.ppermute(value, axis, [(i, i ^ step) for i in range(count)])  15.3 us
    select_n x4, other arithmetic, sweep(): return jnp.where(keep, new, 0.0)  11.7 us
    pallas_call x1, Pallas kernels, subspace_step(): pl.pallas_call(subspace_kernel, out_shape=jax.ShapeDtypeStruct(basis.shap...  11.1 us
    ppermute x4, starting transfers between devices, butterfly_sum(): partner = lax.ppermute(value, axis, [(i, i ^ step) for i in range(count)])  7.57 us
    unnamed x12, local copies, waits for them, and re-layouts  7.09 us
    ppermute x2, starting transfers between devices, flat_permute(): return lax.ppermute(flat, axis, pairs).reshape(block.shape)  6.27 us
    reduce_sum x4, other arithmetic, sweep(): jnp.sum(diff_col * diff_col + diff_row * diff_row, axis=-1, keepdims=True)  4.09 us
  transfers between devices with their start and end apart: 12, of which 8 were waited for; matrix products, arithmetic and copies ran while one was open for 4% of the time, Pallas kernels for 0%

profile of v18, /device:TPU:0, one launch (start us, length us, event | category | flops | bytes accessed | tf_op | source)
XLA Modules:
  0.0 111.1 jit_solution(6867613976426772921)
XLA Ops:
  0.6 1.9 %copy.4 = f32[224,8,256]{0,2,1:T(8,128)S(1)} copy(f32[224,8,256]{2,1,0:T(8,128)} %param.2) | data formatting | bytes 3670016 | tf_op args[0]
  2.5 1.6 %fusion.66 = (f32[4,256,224]{2,1,0:T(8,128)}, f32[4,256,224]{2,1,0:T(8,128)}) fusion(f32[8,256,224]{2,1,0:T(8,128)S(1)} %bitcast.52), kind=kLoop, calls=%fused_computation.121 | loop fusion | bytes 3670016 | tf_op jit(solution)/shard_map/slice | solution.py:96
  4.1 5.0 %collective-permute-start = (f32[16,64,224]{2,1,0:T(8,128)}, f32[16,64,224]{2,1,0:T(8,128)S(1)}, u32[]{:S(2)}, u32[]{:S(2)}) collective-permute-start(f32[16,64,224]{2,1,0:T(8,128)} %bitcast.1), channel_id=1, source_target_pairs={{0,8},{8,16},{16,24},{1,9},{9,17},{17,25},{2,10},{10,18},{18,26},{... | collective-permute-start | bytes 2752520 | tf_op jit(solution)/shard_map/ppermute | solution.py:71
  9.1 1.3 %collective-permute-start.1 = (f32[16,64,224]{2,1,0:T(8,128)}, f32[16,64,224]{2,1,0:T(8,128)}, u32[]{:S(2)}, u32[]{:S(2)}) collective-permute-start(f32[16,64,224]{2,1,0:T(8,128)} %bitcast.3), channel_id=1, source_target_pairs={{8,0},{16,8},{24,16},{9,1},{17,9},{25,17},{10,2},{18,10},{26,18},{... | collective-permute-start | bytes 2752520 | tf_op jit(solution)/shard_map/ppermute | solution.py:71
  10.5 1.5 %collective-permute-start.4 = (f32[8,4,224]{2,1,0:T(4,128)S(1)}, f32[8,4,224]{2,1,0:T(4,128)S(1)}, u32[]{:S(2)}, u32[]{:S(2)}) collective-permute-start(f32[8,4,224]{2,1,0:T(4,128)S(1)} %get-tuple-element.4), channel_id=1, source_target_pairs={{0,1},{1,2},{2,3},{3,4},{4,5},{5,6},{6,7},{8,9},{9,10},{10,11},{11... | collective-permute-start | bytes 86024 | tf_op jit(solution)/shard_map/ppermute | solution.py:98
  11.9 1.3 %collective-permute-start.5 = (f32[8,4,224]{2,1,0:T(4,128)S(1)}, f32[8,4,224]{2,1,0:T(4,128)S(1)}, u32[]{:S(2)}, u32[]{:S(2)}) collective-permute-start(f32[8,4,224]{2,1,0:T(4,128)S(1)} %get-tuple-element.5), channel_id=1, source_target_pairs={{1,0},{2,1},{3,2},{4,3},{5,4},{6,5},{7,6},{9,8},{10,9},{11,10},{12... | collective-permute-start | bytes 86024 | tf_op jit(solution)/shard_map/ppermute | solution.py:99
  14.1 17.7 %collective-permute-done = f32[16,64,224]{2,1,0:T(8,128)S(1)} collective-permute-done((f32[16,64,224]{2,1,0:T(8,128)}, f32[16,64,224]{2,1,0:T(8,128)S(1)}, u32[]{:S(2)}, u32[]{:S(2)}) %collective-permute-start) | collective-permute-done | bytes 917536 | tf_op jit(solution)/shard_map/ppermute | solution.py:71
  31.8 4.2 %collective-permute-done.1 = f32[16,64,224]{2,1,0:T(8,128)} collective-permute-done((f32[16,64,224]{2,1,0:T(8,128)}, f32[16,64,224]{2,1,0:T(8,128)}, u32[]{:S(2)}, u32[]{:S(2)}) %collective-permute-start.1) | collective-permute-done | bytes 917536 | tf_op jit(solution)/shard_map/ppermute | solution.py:71
  36.8 1.3 %collective-permute-start.2 = (f32[8,4,224]{2,1,0:T(4,128)S(1)}, f32[8,4,224]{2,1,0:T(4,128)S(1)}, u32[]{:S(2)}, u32[]{:S(2)}) collective-permute-start(f32[8,4,224]{2,1,0:T(4,128)S(1)} %get-tuple-element.6), channel_id=1, source_target_pairs={{0,1},{1,2},{2,3},{3,4},{4,5},{5,6},{6,7},{8,9},{9,10},{10,11},{11... | collective-permute-start | bytes 86024 | tf_op jit(solution)/shard_map/ppermute | solution.py:101
  38.1 1.3 %collective-permute-start.3 = (f32[8,4,224]{2,1,0:T(4,128)S(1)}, f32[8,4,224]{2,1,0:T(4,128)S(1)}, u32[]{:S(2)}, u32[]{:S(2)}) collective-permute-start(f32[8,4,224]{2,1,0:T(4,128)S(1)} %get-tuple-element.7), channel_id=1, source_target_pairs={{1,0},{2,1},{3,2},{4,3},{5,4},{6,5},{7,6},{9,8},{10,9},{11,10},{12... | collective-permute-start | bytes 86024 | tf_op jit(solution)/shard_map/ppermute | solution.py:102
  39.4 3.5 %collective-permute-done.3 = f32[8,4,224]{2,1,0:T(4,128)S(1)} collective-permute-done((f32[8,4,224]{2,1,0:T(4,128)S(1)}, f32[8,4,224]{2,1,0:T(4,128)S(1)}, u32[]{:S(2)}, u32[]{:S(2)}) %collective-permute-start.3) | collective-permute-done | bytes 28704 | tf_op jit(solution)/shard_map/ppermute | solution.py:102
  43.0 1.8 %maximum_maximum_fusion = f32[16,264,224]{2,1,0:T(8,128)S(1)} fusion(f32[4,4,224]{2,1,0:T(4,128)S(1)} %get-tuple-element.13, f32[4,256,224]{2,1,0:T(8,128)} %bitcast.4, f32[4,4,224]{2,1,0:T(4,128)S(1)} %get-tuple-element.11, f32[8,4,224]{2,1,0:T(4,128)S(1)} %collective-permute-done.5, f32[8,256,224]{2,1,0:T(8,128)S(1)} %bitcast.54, ...), kind=kLoop, calls=%fused_computation | loop fusion | flops 7569408 | bytes 7569408 | tf_op jit(solution)/shard_map/concatenate | solution.py:103
  44.8 1.3 %fusion.2 = f32[15,263]{1,0:T(8,128)S(1)} fusion(f32[16,264,224]{2,1,0:T(8,128)S(1)} %maximum_maximum_fusion), kind=kLoop, calls=%fused_computation.4 | loop fusion | flops 5298135 | bytes 10619940 | tf_op jit(solution)/shard_map/reduce_sum | solution.py:123
  46.2 3.6 %fusion.9 = f32[14,262,224]{2,1,0:T(8,128)S(1)} fusion(f32[16,264,224]{2,1,0:T(8,128)S(1)} %maximum_maximum_fusion, f32[14,262]{1,0:T(8,128)S(1)} %get-tuple-element.24, f32[14,262]{1,0:T(8,128)S(1)} %get-tuple-element.25, f32[14,262]{1,0:T(8,128)S(1)} %get-tuple-element.23, pred[14,262]{1,0:T(8,128)(4,1)S(1)} %broadcast_and_fusion), kind=kLoop, calls=%fused_computation.13 | loop fusion | flops 13967744 | bytes 19766852 | tf_op jit(solution)/shard_map/jit(_where)/select_n | solution.py:132
  49.8 1.1 fusion.17
  51.0 3.4 %fusion.21 = f32[12,260,224]{2,1,0:T(8,128)S(1)} fusion(f32[16,264,224]{2,1,0:T(8,128)S(1)} %maximum_maximum_fusion, f32[14,262,224]{2,1,0:T(8,128)S(1)} %fusion.9, f32[12,260]{1,0:T(8,128)S(1)} %get-tuple-element.21, f32[12,260]{1,0:T(8,128)S(1)} %get-tuple-element.22, f32[12,260]{1,0:T(8,128)S(1)} %get-tuple-element.20, ...), kind=kLoop, calls=%fused_computation.31 | loop fusion | flops 11880960 | bytes 19609200 | tf_op jit(solution)/shard_map/jit(_where)/select_n | solution.py:132
  55.4 2.7 %fusion.37 = f32[10,258,224]{2,1,0:T(8,128)S(1)} fusion(f32[16,264,224]{2,1,0:T(8,128)S(1)} %maximum_maximum_fusion, f32[12,260,224]{2,1,0:T(8,128)S(1)} %fusion.21, f32[10,258]{1,0:T(8,128)S(1)} %get-tuple-element.18, f32[10,258]{1,0:T(8,128)S(1)} %get-tuple-element.19, f32[10,258]{1,0:T(8,128)S(1)} %get-tuple-element.17, ...), kind=kLoop, calls=%fused_computation.54 | loop fusion | flops 9824640 | bytes 16215300 | tf_op jit(solution)/shard_map/jit(_where)/select_n | solution.py:132
  59.7 2.0 %fusion.56 = f32[8,256,224]{2,1,0:T(8,128)S(1)} fusion(f32[10,258,224]{2,1,0:T(8,128)S(1)} %fusion.37, f32[8,256]{1,0:T(8,128)S(1)} %get-tuple-element.15, f32[8,256]{1,0:T(8,128)S(1)} %get-tuple-element.16, f32[8,256]{1,0:T(8,128)S(1)} %get-tuple-element.14, pred[8,256]{1,0:T(8,128)(4,1)S(1)} %broadcast_and_fusion.3, f32[224,8,256]{0,2,1:T(8,128)S(1)} %copy-done.1), kind=kLoop, calls=%fused_computation.80 | loop fusion | flops 7798784 | bytes 12871680 | tf_op jit(solution)/shard_map/jit(_where)/select_n | solution.py:132
  61.7 3.5 %convolution_bitcast_fusion = f32[224,224]{1,0:T(8,128)S(1)} fusion(f32[8,256,224]{2,1,0:T(8,128)S(1)} %fusion.56), kind=kOutput, calls=%fused_computation.89 | convolution fusion | flops 1233125376 | bytes 2035712 | tf_op jit(solution)/shard_map/dot_general | solution.py:212
  65.2 2.7 %collective-permute-start.6 = (f32[112,224]{1,0:T(8,128)S(1)}, f32[112,224]{1,0:T(8,128)S(1)}, u32[]{:S(2)}, u32[]{:S(2)}) collective-permute-start(f32[112,224]{1,0:T(8,128)S(1)} %slice_select_fusion), channel_id=1, source_target_pairs={{0,1},{1,0},{2,3},{3,2},{4,5},{5,4},{6,7},{7,6},{8,9},{9,8},{10,11... | collective-permute-start | bytes 301064 | tf_op jit(solution)/shard_map/ppermute | solution.py:44
  67.9 1.0 collective-permute-done.6
  68.9 2.5 %collective-permute-start.7 = (f32[112,224]{1,0:T(8,128)S(1)}, f32[112,224]{1,0:T(8,128)S(1)}, u32[]{:S(2)}, u32[]{:S(2)}) collective-permute-start(f32[112,224]{1,0:T(8,128)S(1)} %select_add_fusion), channel_id=1, source_target_pairs={{0,2},{1,3},{2,0},{3,1},{4,6},{5,7},{6,4},{7,5},{8,10},{9,11},{10,... | collective-permute-start | bytes 301064 | tf_op jit(solution)/shard_map/ppermute | solution.py:27
  71.4 3.7 %collective-permute-done.7 = f32[112,224]{1,0:T(8,128)S(1)} collective-permute-done((f32[112,224]{1,0:T(8,128)S(1)}, f32[112,224]{1,0:T(8,128)S(1)}, u32[]{:S(2)}, u32[]{:S(2)}) %collective-permute-start.7) | collective-permute-done | bytes 100384 | tf_op jit(solution)/shard_map/ppermute | solution.py:27
  76.0 4.0 %collective-permute-done.8 = f32[112,224]{1,0:T(8,128)S(1)} collective-permute-done((f32[112,224]{1,0:T(8,128)S(1)}, f32[112,224]{1,0:T(8,128)S(1)}, u32[]{:S(2)}, u32[]{:S(2)}) %collective-permute-start.8) | collective-permute-done | bytes 100384 | tf_op jit(solution)/shard_map/ppermute | solution.py:27
  80.0 1.6 %collective-permute-start.9 = (f32[112,224]{1,0:T(8,128)S(1)}, f32[112,224]{1,0:T(8,128)S(1)}, u32[]{:S(2)}, u32[]{:S(2)}) collective-permute-start(f32[112,224]{1,0:T(8,128)S(1)} %add.156), channel_id=1, source_target_pairs={{0,8},{8,0},{16,24},{24,16},{1,9},{9,1},{17,25},{25,17},{2,10},{10... | collective-permute-start | bytes 301064 | tf_op jit(solution)/shard_map/ppermute | solution.py:27
  81.6 3.3 %collective-permute-done.9 = f32[112,224]{1,0:T(8,128)S(1)} collective-permute-done((f32[112,224]{1,0:T(8,128)S(1)}, f32[112,224]{1,0:T(8,128)S(1)}, u32[]{:S(2)}, u32[]{:S(2)}) %collective-permute-start.9) | collective-permute-done | bytes 100384 | tf_op jit(solution)/shard_map/ppermute | solution.py:27
  84.9 2.6 %collective-permute-start.10 = (f32[112,224]{1,0:T(8,128)S(1)}, f32[112,224]{1,0:T(8,128)S(1)}, u32[]{:S(2)}, u32[]{:S(2)}) collective-permute-start(f32[112,224]{1,0:T(8,128)S(1)} %add.157), channel_id=1, source_target_pairs={{0,16},{8,24},{16,0},{24,8},{1,17},{9,25},{17,1},{25,9},{2,18},{10... | collective-permute-start | bytes 301064 | tf_op jit(solution)/shard_map/ppermute | solution.py:27
  87.5 4.4 %collective-permute-done.10 = f32[112,224]{1,0:T(8,128)S(1)} collective-permute-done((f32[112,224]{1,0:T(8,128)S(1)}, f32[112,224]{1,0:T(8,128)S(1)}, u32[]{:S(2)}, u32[]{:S(2)}) %collective-permute-start.10) | collective-permute-done | bytes 100384 | tf_op jit(solution)/shard_map/ppermute | solution.py:27
  92.7 1.8 %copy.6 = f32[224,8,256]{2,1,0:T(8,128)} copy(f32[224,8,256]{0,2,1:T(8,128)S(1)} %bitcast.50) | data formatting | bytes 3670016
  95.2 11.1 %shard_map.41 = f32[224,16]{1,0:T(8,128)} custom-call(f32[224,224]{1,0:T(8,128)} %maximum_select_fusion.gram_ref, f32[224,16]{1,0:T(8,128)} %copy.5.basis_ref), custom_call_target="tpu_custom_call" | custom-call | flops 45875200 | bytes 229376 | tf_op jit(solution)/shard_map/pallas_call | solution.py:177
  106.3 2.0 %fusion.69 = f32[2048,16]{1,0:T(8,128)S(1)} fusion(f32[2048,224]{1,0:T(8,128)S(1)} %bitcast.51, f32[224,16]{1,0:T(8,128)} %shard_map.41), kind=kOutput, calls=%fused_computation.124 | convolution fusion | flops 44040192 | bytes 1980416 | tf_op jit(solution)/shard_map/dot_general | solution.py:222
  109.1 2.0 %copy.7 = f32[28,8,8,256]{3,2,1,0:T(8,128)} copy(f32[28,8,8,256]{3,1,2,0:T(8,128)S(1)} %bitcast.55) | data formatting | bytes 3670016
  (51 shorter events, 8.0 us)
Async XLA Ops:
  2.5 40.4 %copy-start = (f32[224,8,256]{0,2,1:T(8,128)}, f32[224,8,256]{0,2,1:T(8,128)S(1)}, u32[]{:S(2)}) copy-start(f32[224,8,256]{0,2,1:T(8,128)S(1)} %copy.4) | copy-start | bytes 5505028
  4.1 27.6 %collective-permute-start = (f32[16,64,224]{2,1,0:T(8,128)}, f32[16,64,224]{2,1,0:T(8,128)S(1)}, u32[]{:S(2)}, u32[]{:S(2)}) collective-permute-start(f32[16,64,224]{2,1,0:T(8,128)} %bitcast.1), channel_id=1, source_target_pairs={{0,8},{8,16},{16,24},{1,9},{9,17},{17,25},{2,10},{10,18},{18,26},{... | collective-permute-start | bytes 2752520 | tf_op jit(solution)/shard_map/ppermute | solution.py:71
  9.1 26.8 %collective-permute-start.1 = (f32[16,64,224]{2,1,0:T(8,128)}, f32[16,64,224]{2,1,0:T(8,128)}, u32[]{:S(2)}, u32[]{:S(2)}) collective-permute-start(f32[16,64,224]{2,1,0:T(8,128)} %bitcast.3), channel_id=1, source_target_pairs={{8,0},{16,8},{24,16},{9,1},{17,9},{25,17},{10,2},{18,10},{26,18},{... | collective-permute-start | bytes 2752520 | tf_op jit(solution)/shard_map/ppermute | solution.py:71
  10.5 32.5 %collective-permute-start.4 = (f32[8,4,224]{2,1,0:T(4,128)S(1)}, f32[8,4,224]{2,1,0:T(4,128)S(1)}, u32[]{:S(2)}, u32[]{:S(2)}) collective-permute-start(f32[8,4,224]{2,1,0:T(4,128)S(1)} %get-tuple-element.4), channel_id=1, source_target_pairs={{0,1},{1,2},{2,3},{3,4},{4,5},{5,6},{6,7},{8,9},{9,10},{10,11},{11... | collective-permute-start | bytes 86024 | tf_op jit(solution)/shard_map/ppermute | solution.py:98
  11.9 31.0 %collective-permute-start.5 = (f32[8,4,224]{2,1,0:T(4,128)S(1)}, f32[8,4,224]{2,1,0:T(4,128)S(1)}, u32[]{:S(2)}, u32[]{:S(2)}) collective-permute-start(f32[8,4,224]{2,1,0:T(4,128)S(1)} %get-tuple-element.5), channel_id=1, source_target_pairs={{1,0},{2,1},{3,2},{4,3},{5,4},{6,5},{7,6},{9,8},{10,9},{11,10},{12... | collective-permute-start | bytes 86024 | tf_op jit(solution)/shard_map/ppermute | solution.py:99
  36.8 2.7 %collective-permute-start.2 = (f32[8,4,224]{2,1,0:T(4,128)S(1)}, f32[8,4,224]{2,1,0:T(4,128)S(1)}, u32[]{:S(2)}, u32[]{:S(2)}) collective-permute-start(f32[8,4,224]{2,1,0:T(4,128)S(1)} %get-tuple-element.6), channel_id=1, source_target_pairs={{0,1},{1,2},{2,3},{3,4},{4,5},{5,6},{6,7},{8,9},{9,10},{10,11},{11... | collective-permute-start | bytes 86024 | tf_op jit(solution)/shard_map/ppermute | solution.py:101
  38.1 4.8 %collective-permute-start.3 = (f32[8,4,224]{2,1,0:T(4,128)S(1)}, f32[8,4,224]{2,1,0:T(4,128)S(1)}, u32[]{:S(2)}, u32[]{:S(2)}) collective-permute-start(f32[8,4,224]{2,1,0:T(4,128)S(1)} %get-tuple-element.7), channel_id=1, source_target_pairs={{1,0},{2,1},{3,2},{4,3},{5,4},{6,5},{7,6},{9,8},{10,9},{11,10},{12... | collective-permute-start | bytes 86024 | tf_op jit(solution)/shard_map/ppermute | solution.py:102
  58.1 1.6 %copy-start.1 = (f32[224,8,256]{0,2,1:T(8,128)S(1)}, f32[224,8,256]{0,2,1:T(8,128)}, u32[]{:S(2)}) copy-start(f32[224,8,256]{0,2,1:T(8,128)} %copy-done) | copy-start | bytes 5505028
  61.7 30.2 %copy-start.3 = (f32[224,16]{0,1:T(8,128)S(1)}, f32[224,16]{0,1:T(8,128)}, u32[]{:S(2)}) copy-start(f32[224,16]{0,1:T(8,128)} %param.3) | copy-start | bytes 43012
  65.2 3.7 %collective-permute-start.6 = (f32[112,224]{1,0:T(8,128)S(1)}, f32[112,224]{1,0:T(8,128)S(1)}, u32[]{:S(2)}, u32[]{:S(2)}) collective-permute-start(f32[112,224]{1,0:T(8,128)S(1)} %slice_select_fusion), channel_id=1, source_target_pairs={{0,1},{1,0},{2,3},{3,2},{4,5},{5,4},{6,7},{7,6},{8,9},{9,8},{10,11... | collective-permute-start | bytes 301064 | tf_op jit(solution)/shard_map/ppermute | solution.py:44
  68.9 6.1 %collective-permute-start.7 = (f32[112,224]{1,0:T(8,128)S(1)}, f32[112,224]{1,0:T(8,128)S(1)}, u32[]{:S(2)}, u32[]{:S(2)}) collective-permute-start(f32[112,224]{1,0:T(8,128)S(1)} %select_add_fusion), channel_id=1, source_target_pairs={{0,2},{1,3},{2,0},{3,1},{4,6},{5,7},{6,4},{7,5},{8,10},{9,11},{10,... | collective-permute-start | bytes 301064 | tf_op jit(solution)/shard_map/ppermute | solution.py:27
  75.1 4.9 %collective-permute-start.8 = (f32[112,224]{1,0:T(8,128)S(1)}, f32[112,224]{1,0:T(8,128)S(1)}, u32[]{:S(2)}, u32[]{:S(2)}) collective-permute-start(f32[112,224]{1,0:T(8,128)S(1)} %add.155), channel_id=1, source_target_pairs={{0,4},{1,5},{2,6},{3,7},{4,0},{5,1},{6,2},{7,3},{8,12},{9,13},{10,... | collective-permute-start | bytes 301064 | tf_op jit(solution)/shard_map/ppermute | solution.py:27
  80.0 4.9 %collective-permute-start.9 = (f32[112,224]{1,0:T(8,128)S(1)}, f32[112,224]{1,0:T(8,128)S(1)}, u32[]{:S(2)}, u32[]{:S(2)}) collective-permute-start(f32[112,224]{1,0:T(8,128)S(1)} %add.156), channel_id=1, source_target_pairs={{0,8},{8,0},{16,24},{24,16},{1,9},{9,1},{17,25},{25,17},{2,10},{10... | collective-permute-start | bytes 301064 | tf_op jit(solution)/shard_map/ppermute | solution.py:27
  84.9 7.0 %collective-permute-start.10 = (f32[112,224]{1,0:T(8,128)S(1)}, f32[112,224]{1,0:T(8,128)S(1)}, u32[]{:S(2)}, u32[]{:S(2)}) collective-permute-start(f32[112,224]{1,0:T(8,128)S(1)} %add.157), channel_id=1, source_target_pairs={{0,16},{8,24},{16,0},{24,8},{1,17},{9,25},{17,1},{25,9},{2,18},{10... | collective-permute-start | bytes 301064 | tf_op jit(solution)/shard_map/ppermute | solution.py:27
  91.9 2.6 %collective-permute-start.11 = (f32[112,224]{1,0:T(8,128)S(1)}, f32[112,224]{1,0:T(8,128)S(1)}, u32[]{:S(2)}, u32[]{:S(2)}) collective-permute-start(f32[112,224]{1,0:T(8,128)S(1)} %add.158), channel_id=1, source_target_pairs={{0,1},{1,0},{2,3},{3,2},{4,5},{5,4},{6,7},{7,6},{8,9},{9,8},{10,11... | collective-permute-start | bytes 301064 | tf_op jit(solution)/shard_map/ppermute | solution.py:46
  106.3 2.0 %copy-start.2 = (f32[224,16]{1,0:T(8,128)S(1)}, f32[224,16]{1,0:T(8,128)}, u32[]{:S(2)}) copy-start(f32[224,16]{1,0:T(8,128)} %shard_map.41) | copy-start | bytes 43012

commit v19 on v18

--- a/solution.py
+++ b/solution.py
@@ -219,13 +219,14 @@
     gram_full = paired_sum(local_gram, order)
     basis_now = start_basis
     basis_now = subspace_step(gram_full, basis_now)
-    coeffs = jnp.dot(flat_cells, basis_now, precision=lax.Precision.HIGH)
-    lowrank = lax.dot_general(
+    coeffs = lax.dot_general(
         basis_now,
-        coeffs,
-        (((1,), (1,)), ((), ())),
+        flat_cells,
+        (((0,), (1,)), ((), ())),
         precision=lax.Precision.HIGH,
-    )
+        preferred_element_type=jnp.float32,
+    )
+    lowrank = jnp.dot(basis_now, coeffs, precision=lax.Precision.HIGH)
     return (smoothed, lowrank.reshape(band_count, tile_rows, tile_cols))
 
 

time: 112 us -> 112 us (level)
    unnamed x12 -> x10, local copies, waits for them, and re-layouts: 7.09 us -> 7.07 us
where the time goes in v19:
time: 112 us
  waiting for transfers between devices  41.6 us (37%)
  starting transfers between devices  21.9 us (20%)
  other arithmetic  19.6 us (18%)
  Pallas kernels  11.1 us (10%)
  local copies, waits for them, and re-layouts  9.61 us (9%)
  matrix products  7.08 us (6%)
    ppermute x2, waiting for transfers between devices, flat_permute(): return lax.ppermute(flat, axis, pairs).reshape(block.shape)  21.9 us
    ppermute x4, waiting for transfers between devices, butterfly_sum(): partner = lax.ppermute(value, axis, [(i, i ^ step) for i in range(count)])  15.3 us
    select_n x4, other arithmetic, sweep(): return jnp.where(keep, new, 0.0)  11.7 us
    pallas_call x1, Pallas kernels, subspace_step(): pl.pallas_call(subspace_kernel, out_shape=jax.ShapeDtypeStruct(basis.shap...  11.1 us
    ppermute x4, starting transfers between devices, butterfly_sum(): partner = lax.ppermute(value, axis, [(i, i ^ step) for i in range(count)])  7.57 us
    unnamed x10, local copies, waits for them, and re-layouts  7.07 us
    ppermute x2, starting transfers between devices, flat_permute(): return lax.ppermute(flat, axis, pairs).reshape(block.shape)  6.27 us
    reduce_sum x4, other arithmetic, sweep(): jnp.sum(diff_col * diff_col + diff_row * diff_row, axis=-1, keepdims=True)  4.09 us
  transfers between devices with their start and end apart: 12, of which 8 were waited for; matrix products, arithmetic and copies ran while one was open for 4% of the time, Pallas kernels for 0%

profile of v19, /device:TPU:0, one launch (start us, length us, event | category | flops | bytes accessed | tf_op | source)
XLA Modules:
  0.0 111.8 jit_solution(9271955540004618421)
XLA Ops:
  0.6 1.9 %copy.4 = f32[224,8,256]{0,2,1:T(8,128)S(1)} copy(f32[224,8,256]{2,1,0:T(8,128)} %param.2) | data formatting | bytes 3670016 | tf_op args[0]
  2.5 1.6 %fusion.66 = (f32[4,256,224]{2,1,0:T(8,128)}, f32[4,256,224]{2,1,0:T(8,128)}) fusion(f32[8,256,224]{2,1,0:T(8,128)S(1)} %bitcast.52), kind=kLoop, calls=%fused_computation.121 | loop fusion | bytes 3670016 | tf_op jit(solution)/shard_map/slice | solution.py:96
  4.1 5.0 %collective-permute-start = (f32[16,64,224]{2,1,0:T(8,128)}, f32[16,64,224]{2,1,0:T(8,128)S(1)}, u32[]{:S(2)}, u32[]{:S(2)}) collective-permute-start(f32[16,64,224]{2,1,0:T(8,128)} %bitcast.1), channel_id=1, source_target_pairs={{0,8},{8,16},{16,24},{1,9},{9,17},{17,25},{2,10},{10,18},{18,26},{... | collective-permute-start | bytes 2752520 | tf_op jit(solution)/shard_map/ppermute | solution.py:71
  9.1 1.3 %collective-permute-start.1 = (f32[16,64,224]{2,1,0:T(8,128)}, f32[16,64,224]{2,1,0:T(8,128)}, u32[]{:S(2)}, u32[]{:S(2)}) collective-permute-start(f32[16,64,224]{2,1,0:T(8,128)} %bitcast.3), channel_id=1, source_target_pairs={{8,0},{16,8},{24,16},{9,1},{17,9},{25,17},{10,2},{18,10},{26,18},{... | collective-permute-start | bytes 2752520 | tf_op jit(solution)/shard_map/ppermute | solution.py:71
  10.5 1.5 %collective-permute-start.4 = (f32[8,4,224]{2,1,0:T(4,128)S(1)}, f32[8,4,224]{2,1,0:T(4,128)S(1)}, u32[]{:S(2)}, u32[]{:S(2)}) collective-permute-start(f32[8,4,224]{2,1,0:T(4,128)S(1)} %get-tuple-element.4), channel_id=1, source_target_pairs={{0,1},{1,2},{2,3},{3,4},{4,5},{5,6},{6,7},{8,9},{9,10},{10,11},{11... | collective-permute-start | bytes 86024 | tf_op jit(solution)/shard_map/ppermute | solution.py:98
  11.9 1.3 %collective-permute-start.5 = (f32[8,4,224]{2,1,0:T(4,128)S(1)}, f32[8,4,224]{2,1,0:T(4,128)S(1)}, u32[]{:S(2)}, u32[]{:S(2)}) collective-permute-start(f32[8,4,224]{2,1,0:T(4,128)S(1)} %get-tuple-element.5), channel_id=1, source_target_pairs={{1,0},{2,1},{3,2},{4,3},{5,4},{6,5},{7,6},{9,8},{10,9},{11,10},{12... | collective-permute-start | bytes 86024 | tf_op jit(solution)/shard_map/ppermute | solution.py:99
  14.1 17.7 %collective-permute-done = f32[16,64,224]{2,1,0:T(8,128)S(1)} collective-permute-done((f32[16,64,224]{2,1,0:T(8,128)}, f32[16,64,224]{2,1,0:T(8,128)S(1)}, u32[]{:S(2)}, u32[]{:S(2)}) %collective-permute-start) | collective-permute-done | bytes 917536 | tf_op jit(solution)/shard_map/ppermute | solution.py:71
  31.8 4.2 %collective-permute-done.1 = f32[16,64,224]{2,1,0:T(8,128)} collective-permute-done((f32[16,64,224]{2,1,0:T(8,128)}, f32[16,64,224]{2,1,0:T(8,128)}, u32[]{:S(2)}, u32[]{:S(2)}) %collective-permute-start.1) | collective-permute-done | bytes 917536 | tf_op jit(solution)/shard_map/ppermute | solution.py:71
  36.8 1.3 %collective-permute-start.2 = (f32[8,4,224]{2,1,0:T(4,128)S(1)}, f32[8,4,224]{2,1,0:T(4,128)S(1)}, u32[]{:S(2)}, u32[]{:S(2)}) collective-permute-start(f32[8,4,224]{2,1,0:T(4,128)S(1)} %get-tuple-element.6), channel_id=1, source_target_pairs={{0,1},{1,2},{2,3},{3,4},{4,5},{5,6},{6,7},{8,9},{9,10},{10,11},{11... | collective-permute-start | bytes 86024 | tf_op jit(solution)/shard_map/ppermute | solution.py:101
  38.1 1.3 %collective-permute-start.3 = (f32[8,4,224]{2,1,0:T(4,128)S(1)}, f32[8,4,224]{2,1,0:T(4,128)S(1)}, u32[]{:S(2)}, u32[]{:S(2)}) collective-permute-start(f32[8,4,224]{2,1,0:T(4,128)S(1)} %get-tuple-element.7), channel_id=1, source_target_pairs={{1,0},{2,1},{3,2},{4,3},{5,4},{6,5},{7,6},{9,8},{10,9},{11,10},{12... | collective-permute-start | bytes 86024 | tf_op jit(solution)/shard_map/ppermute | solution.py:102
  39.4 3.5 %collective-permute-done.3 = f32[8,4,224]{2,1,0:T(4,128)S(1)} collective-permute-done((f32[8,4,224]{2,1,0:T(4,128)S(1)}, f32[8,4,224]{2,1,0:T(4,128)S(1)}, u32[]{:S(2)}, u32[]{:S(2)}) %collective-permute-start.3) | collective-permute-done | bytes 28704 | tf_op jit(solution)/shard_map/ppermute | solution.py:102
  43.0 1.8 %maximum_maximum_fusion = f32[16,264,224]{2,1,0:T(8,128)S(1)} fusion(f32[4,4,224]{2,1,0:T(4,128)S(1)} %get-tuple-element.13, f32[4,256,224]{2,1,0:T(8,128)} %bitcast.4, f32[4,4,224]{2,1,0:T(4,128)S(1)} %get-tuple-element.11, f32[8,4,224]{2,1,0:T(4,128)S(1)} %collective-permute-done.5, f32[8,256,224]{2,1,0:T(8,128)S(1)} %bitcast.54, ...), kind=kLoop, calls=%fused_computation | loop fusion | flops 7569408 | bytes 7569408 | tf_op jit(solution)/shard_map/concatenate | solution.py:103
  44.8 1.3 %fusion.2 = f32[15,263]{1,0:T(8,128)S(1)} fusion(f32[16,264,224]{2,1,0:T(8,128)S(1)} %maximum_maximum_fusion), kind=kLoop, calls=%fused_computation.4 | loop fusion | flops 5298135 | bytes 10619940 | tf_op jit(solution)/shard_map/reduce_sum | solution.py:123
  46.2 3.6 %fusion.9 = f32[14,262,224]{2,1,0:T(8,128)S(1)} fusion(f32[16,264,224]{2,1,0:T(8,128)S(1)} %maximum_maximum_fusion, f32[14,262]{1,0:T(8,128)S(1)} %get-tuple-element.24, f32[14,262]{1,0:T(8,128)S(1)} %get-tuple-element.25, f32[14,262]{1,0:T(8,128)S(1)} %get-tuple-element.23, pred[14,262]{1,0:T(8,128)(4,1)S(1)} %broadcast_and_fusion), kind=kLoop, calls=%fused_computation.13 | loop fusion | flops 13967744 | bytes 19766852 | tf_op jit(solution)/shard_map/jit(_where)/select_n | solution.py:132
  49.8 1.1 fusion.17
  51.0 3.4 %fusion.21 = f32[12,260,224]{2,1,0:T(8,128)S(1)} fusion(f32[16,264,224]{2,1,0:T(8,128)S(1)} %maximum_maximum_fusion, f32[14,262,224]{2,1,0:T(8,128)S(1)} %fusion.9, f32[12,260]{1,0:T(8,128)S(1)} %get-tuple-element.21, f32[12,260]{1,0:T(8,128)S(1)} %get-tuple-element.22, f32[12,260]{1,0:T(8,128)S(1)} %get-tuple-element.20, ...), kind=kLoop, calls=%fused_computation.31 | loop fusion | flops 11880960 | bytes 19609200 | tf_op jit(solution)/shard_map/jit(_where)/select_n | solution.py:132
  55.4 2.7 %fusion.37 = f32[10,258,224]{2,1,0:T(8,128)S(1)} fusion(f32[16,264,224]{2,1,0:T(8,128)S(1)} %maximum_maximum_fusion, f32[12,260,224]{2,1,0:T(8,128)S(1)} %fusion.21, f32[10,258]{1,0:T(8,128)S(1)} %get-tuple-element.18, f32[10,258]{1,0:T(8,128)S(1)} %get-tuple-element.19, f32[10,258]{1,0:T(8,128)S(1)} %get-tuple-element.17, ...), kind=kLoop, calls=%fused_computation.54 | loop fusion | flops 9824640 | bytes 16215300 | tf_op jit(solution)/shard_map/jit(_where)/select_n | solution.py:132
  59.7 2.0 %fusion.56 = f32[8,256,224]{2,1,0:T(8,128)S(1)} fusion(f32[10,258,224]{2,1,0:T(8,128)S(1)} %fusion.37, f32[8,256]{1,0:T(8,128)S(1)} %get-tuple-element.15, f32[8,256]{1,0:T(8,128)S(1)} %get-tuple-element.16, f32[8,256]{1,0:T(8,128)S(1)} %get-tuple-element.14, pred[8,256]{1,0:T(8,128)(4,1)S(1)} %broadcast_and_fusion.3, f32[224,8,256]{0,2,1:T(8,128)S(1)} %copy-done.1), kind=kLoop, calls=%fused_computation.80 | loop fusion | flops 7798784 | bytes 12871680 | tf_op jit(solution)/shard_map/jit(_where)/select_n | solution.py:132
  61.7 3.5 %convolution_bitcast_fusion = f32[224,224]{1,0:T(8,128)S(1)} fusion(f32[8,256,224]{2,1,0:T(8,128)S(1)} %fusion.56), kind=kOutput, calls=%fused_computation.89 | convolution fusion | flops 1233125376 | bytes 2035712 | tf_op jit(solution)/shard_map/dot_general | solution.py:212
  65.2 2.7 %collective-permute-start.6 = (f32[112,224]{1,0:T(8,128)S(1)}, f32[112,224]{1,0:T(8,128)S(1)}, u32[]{:S(2)}, u32[]{:S(2)}) collective-permute-start(f32[112,224]{1,0:T(8,128)S(1)} %slice_select_fusion), channel_id=1, source_target_pairs={{0,1},{1,0},{2,3},{3,2},{4,5},{5,4},{6,7},{7,6},{8,9},{9,8},{10,11... | collective-permute-start | bytes 301064 | tf_op jit(solution)/shard_map/ppermute | solution.py:44
  68.9 2.5 %collective-permute-start.7 = (f32[112,224]{1,0:T(8,128)S(1)}, f32[112,224]{1,0:T(8,128)S(1)}, u32[]{:S(2)}, u32[]{:S(2)}) collective-permute-start(f32[112,224]{1,0:T(8,128)S(1)} %select_add_fusion), channel_id=1, source_target_pairs={{0,2},{1,3},{2,0},{3,1},{4,6},{5,7},{6,4},{7,5},{8,10},{9,11},{10,... | collective-permute-start | bytes 301064 | tf_op jit(solution)/shard_map/ppermute | solution.py:27
  71.4 3.7 %collective-permute-done.7 = f32[112,224]{1,0:T(8,128)S(1)} collective-permute-done((f32[112,224]{1,0:T(8,128)S(1)}, f32[112,224]{1,0:T(8,128)S(1)}, u32[]{:S(2)}, u32[]{:S(2)}) %collective-permute-start.7) | collective-permute-done | bytes 100384 | tf_op jit(solution)/shard_map/ppermute | solution.py:27
  76.0 4.0 %collective-permute-done.8 = f32[112,224]{1,0:T(8,128)S(1)} collective-permute-done((f32[112,224]{1,0:T(8,128)S(1)}, f32[112,224]{1,0:T(8,128)S(1)}, u32[]{:S(2)}, u32[]{:S(2)}) %collective-permute-start.8) | collective-permute-done | bytes 100384 | tf_op jit(solution)/shard_map/ppermute | solution.py:27
  80.0 1.6 %collective-permute-start.9 = (f32[112,224]{1,0:T(8,128)S(1)}, f32[112,224]{1,0:T(8,128)S(1)}, u32[]{:S(2)}, u32[]{:S(2)}) collective-permute-start(f32[112,224]{1,0:T(8,128)S(1)} %add.156), channel_id=1, source_target_pairs={{0,8},{8,0},{16,24},{24,16},{1,9},{9,1},{17,25},{25,17},{2,10},{10... | collective-permute-start | bytes 301064 | tf_op jit(solution)/shard_map/ppermute | solution.py:27
  81.6 3.3 %collective-permute-done.9 = f32[112,224]{1,0:T(8,128)S(1)} collective-permute-done((f32[112,224]{1,0:T(8,128)S(1)}, f32[112,224]{1,0:T(8,128)S(1)}, u32[]{:S(2)}, u32[]{:S(2)}) %collective-permute-start.9) | collective-permute-done | bytes 100384 | tf_op jit(solution)/shard_map/ppermute | solution.py:27
  84.9 2.6 %collective-permute-start.10 = (f32[112,224]{1,0:T(8,128)S(1)}, f32[112,224]{1,0:T(8,128)S(1)}, u32[]{:S(2)}, u32[]{:S(2)}) collective-permute-start(f32[112,224]{1,0:T(8,128)S(1)} %add.157), channel_id=1, source_target_pairs={{0,16},{8,24},{16,0},{24,8},{1,17},{9,25},{17,1},{25,9},{2,18},{10... | collective-permute-start | bytes 301064 | tf_op jit(solution)/shard_map/ppermute | solution.py:27
  87.5 4.4 %collective-permute-done.10 = f32[112,224]{1,0:T(8,128)S(1)} collective-permute-done((f32[112,224]{1,0:T(8,128)S(1)}, f32[112,224]{1,0:T(8,128)S(1)}, u32[]{:S(2)}, u32[]{:S(2)}) %collective-permute-start.10) | collective-permute-done | bytes 100384 | tf_op jit(solution)/shard_map/ppermute | solution.py:27
  92.7 1.8 %copy.6 = f32[224,8,256]{2,1,0:T(8,128)} copy(f32[224,8,256]{0,2,1:T(8,128)S(1)} %bitcast.50) | data formatting | bytes 3670016
  95.2 11.1 %shard_map.41 = f32[224,16]{1,0:T(8,128)} custom-call(f32[224,224]{1,0:T(8,128)} %maximum_select_fusion.gram_ref, f32[224,16]{1,0:T(8,128)} %copy.5.basis_ref), custom_call_target="tpu_custom_call" | custom-call | flops 45875200 | bytes 229376 | tf_op jit(solution)/shard_map/pallas_call | solution.py:177
  106.3 1.8 %fusion.69 = f32[16,2048]{1,0:T(8,128)S(1)} fusion(f32[224,16]{1,0:T(8,128)} %shard_map.41, f32[2048,224]{1,0:T(8,128)S(1)} %bitcast.51), kind=kOutput, calls=%fused_computation.124 | convolution fusion | flops 44040192 | bytes 1980416 | tf_op jit(solution)/shard_map/dot_general | solution.py:222
  108.1 1.8 %fusion.70 = f32[224,2048]{1,0:T(8,128)S(1)} fusion(f32[224,16]{1,0:T(8,128)} %shard_map.41, f32[16,2048]{1,0:T(8,128)S(1)} %fusion.69), kind=kOutput, calls=%fused_computation.125 | convolution fusion | flops 44040192 | bytes 1980416 | tf_op jit(solution)/shard_map/dot_general | solution.py:229
  109.9 2.0 %copy.7 = f32[28,8,8,256]{3,2,1,0:T(8,128)} copy(f32[28,8,8,256]{3,1,2,0:T(8,128)S(1)} %bitcast.55) | data formatting | bytes 3670016
  (49 shorter events, 8.1 us)
Async XLA Ops:
  2.5 40.4 %copy-start = (f32[224,8,256]{0,2,1:T(8,128)}, f32[224,8,256]{0,2,1:T(8,128)S(1)}, u32[]{:S(2)}) copy-start(f32[224,8,256]{0,2,1:T(8,128)S(1)} %copy.4) | copy-start | bytes 5505028
  4.1 27.6 %collective-permute-start = (f32[16,64,224]{2,1,0:T(8,128)}, f32[16,64,224]{2,1,0:T(8,128)S(1)}, u32[]{:S(2)}, u32[]{:S(2)}) collective-permute-start(f32[16,64,224]{2,1,0:T(8,128)} %bitcast.1), channel_id=1, source_target_pairs={{0,8},{8,16},{16,24},{1,9},{9,17},{17,25},{2,10},{10,18},{18,26},{... | collective-permute-start | bytes 2752520 | tf_op jit(solution)/shard_map/ppermute | solution.py:71
  9.1 26.8 %collective-permute-start.1 = (f32[16,64,224]{2,1,0:T(8,128)}, f32[16,64,224]{2,1,0:T(8,128)}, u32[]{:S(2)}, u32[]{:S(2)}) collective-permute-start(f32[16,64,224]{2,1,0:T(8,128)} %bitcast.3), channel_id=1, source_target_pairs={{8,0},{16,8},{24,16},{9,1},{17,9},{25,17},{10,2},{18,10},{26,18},{... | collective-permute-start | bytes 2752520 | tf_op jit(solution)/shard_map/ppermute | solution.py:71
  10.5 32.5 %collective-permute-start.4 = (f32[8,4,224]{2,1,0:T(4,128)S(1)}, f32[8,4,224]{2,1,0:T(4,128)S(1)}, u32[]{:S(2)}, u32[]{:S(2)}) collective-permute-start(f32[8,4,224]{2,1,0:T(4,128)S(1)} %get-tuple-element.4), channel_id=1, source_target_pairs={{0,1},{1,2},{2,3},{3,4},{4,5},{5,6},{6,7},{8,9},{9,10},{10,11},{11... | collective-permute-start | bytes 86024 | tf_op jit(solution)/shard_map/ppermute | solution.py:98
  11.9 31.0 %collective-permute-start.5 = (f32[8,4,224]{2,1,0:T(4,128)S(1)}, f32[8,4,224]{2,1,0:T(4,128)S(1)}, u32[]{:S(2)}, u32[]{:S(2)}) collective-permute-start(f32[8,4,224]{2,1,0:T(4,128)S(1)} %get-tuple-element.5), channel_id=1, source_target_pairs={{1,0},{2,1},{3,2},{4,3},{5,4},{6,5},{7,6},{9,8},{10,9},{11,10},{12... | collective-permute-start | bytes 86024 | tf_op jit(solution)/shard_map/ppermute | solution.py:99
  36.8 2.7 %collective-permute-start.2 = (f32[8,4,224]{2,1,0:T(4,128)S(1)}, f32[8,4,224]{2,1,0:T(4,128)S(1)}, u32[]{:S(2)}, u32[]{:S(2)}) collective-permute-start(f32[8,4,224]{2,1,0:T(4,128)S(1)} %get-tuple-element.6), channel_id=1, source_target_pairs={{0,1},{1,2},{2,3},{3,4},{4,5},{5,6},{6,7},{8,9},{9,10},{10,11},{11... | collective-permute-start | bytes 86024 | tf_op jit(solution)/shard_map/ppermute | solution.py:101
  38.1 4.8 %collective-permute-start.3 = (f32[8,4,224]{2,1,0:T(4,128)S(1)}, f32[8,4,224]{2,1,0:T(4,128)S(1)}, u32[]{:S(2)}, u32[]{:S(2)}) collective-permute-start(f32[8,4,224]{2,1,0:T(4,128)S(1)} %get-tuple-element.7), channel_id=1, source_target_pairs={{1,0},{2,1},{3,2},{4,3},{5,4},{6,5},{7,6},{9,8},{10,9},{11,10},{12... | collective-permute-start | bytes 86024 | tf_op jit(solution)/shard_map/ppermute | solution.py:102
  58.1 1.6 %copy-start.1 = (f32[224,8,256]{0,2,1:T(8,128)S(1)}, f32[224,8,256]{0,2,1:T(8,128)}, u32[]{:S(2)}) copy-start(f32[224,8,256]{0,2,1:T(8,128)} %copy-done) | copy-start | bytes 5505028
  61.7 30.2 %copy-start.2 = (f32[224,16]{0,1:T(8,128)S(1)}, f32[224,16]{0,1:T(8,128)}, u32[]{:S(2)}) copy-start(f32[224,16]{0,1:T(8,128)} %param.3) | copy-start | bytes 43012
  65.2 3.7 %collective-permute-start.6 = (f32[112,224]{1,0:T(8,128)S(1)}, f32[112,224]{1,0:T(8,128)S(1)}, u32[]{:S(2)}, u32[]{:S(2)}) collective-permute-start(f32[112,224]{1,0:T(8,128)S(1)} %slice_select_fusion), channel_id=1, source_target_pairs={{0,1},{1,0},{2,3},{3,2},{4,5},{5,4},{6,7},{7,6},{8,9},{9,8},{10,11... | collective-permute-start | bytes 301064 | tf_op jit(solution)/shard_map/ppermute | solution.py:44
  68.9 6.1 %collective-permute-start.7 = (f32[112,224]{1,0:T(8,128)S(1)}, f32[112,224]{1,0:T(8,128)S(1)}, u32[]{:S(2)}, u32[]{:S(2)}) collective-permute-start(f32[112,224]{1,0:T(8,128)S(1)} %select_add_fusion), channel_id=1, source_target_pairs={{0,2},{1,3},{2,0},{3,1},{4,6},{5,7},{6,4},{7,5},{8,10},{9,11},{10,... | collective-permute-start | bytes 301064 | tf_op jit(solution)/shard_map/ppermute | solution.py:27
  75.1 4.9 %collective-permute-start.8 = (f32[112,224]{1,0:T(8,128)S(1)}, f32[112,224]{1,0:T(8,128)S(1)}, u32[]{:S(2)}, u32[]{:S(2)}) collective-permute-start(f32[112,224]{1,0:T(8,128)S(1)} %add.155), channel_id=1, source_target_pairs={{0,4},{1,5},{2,6},{3,7},{4,0},{5,1},{6,2},{7,3},{8,12},{9,13},{10,... | collective-permute-start | bytes 301064 | tf_op jit(solution)/shard_map/ppermute | solution.py:27
  80.0 4.9 %collective-permute-start.9 = (f32[112,224]{1,0:T(8,128)S(1)}, f32[112,224]{1,0:T(8,128)S(1)}, u32[]{:S(2)}, u32[]{:S(2)}) collective-permute-start(f32[112,224]{1,0:T(8,128)S(1)} %add.156), channel_id=1, source_target_pairs={{0,8},{8,0},{16,24},{24,16},{1,9},{9,1},{17,25},{25,17},{2,10},{10... | collective-permute-start | bytes 301064 | tf_op jit(solution)/shard_map/ppermute | solution.py:27
  84.9 7.0 %collective-permute-start.10 = (f32[112,224]{1,0:T(8,128)S(1)}, f32[112,224]{1,0:T(8,128)S(1)}, u32[]{:S(2)}, u32[]{:S(2)}) collective-permute-start(f32[112,224]{1,0:T(8,128)S(1)} %add.157), channel_id=1, source_target_pairs={{0,16},{8,24},{16,0},{24,8},{1,17},{9,25},{17,1},{25,9},{2,18},{10... | collective-permute-start | bytes 301064 | tf_op jit(solution)/shard_map/ppermute | solution.py:27
  91.9 2.6 %collective-permute-start.11 = (f32[112,224]{1,0:T(8,128)S(1)}, f32[112,224]{1,0:T(8,128)S(1)}, u32[]{:S(2)}, u32[]{:S(2)}) collective-permute-start(f32[112,224]{1,0:T(8,128)S(1)} %add.158), channel_id=1, source_target_pairs={{0,1},{1,0},{2,3},{3,2},{4,5},{5,4},{6,7},{7,6},{8,9},{9,8},{10,11... | collective-permute-start | bytes 301064 | tf_op jit(solution)/shard_map/ppermute | solution.py:46

commit v20 on v18

--- a/solution.py
+++ b/solution.py
@@ -35,7 +35,8 @@
     count = lax.axis_size(first)
     half = value.shape[0] // 2
     if count < 2 or count & (count - 1) or value.shape[0] % 2:
-        return butterfly_sum(value, axes)
+        total = butterfly_sum(value, axes)
+        return total[:half], total[half:], jnp.ones((1, 1), jnp.float32)
     pairs = [(i, i ^ 1) for i in range(count)]
     low = lax.axis_index(first) % 2 == 0
     top, bottom = value[:half], value[half:]
@@ -44,7 +45,7 @@
     part = keep + lax.ppermute(give, first, pairs)
     part = butterfly_sum(part, axes, start=2)
     other = lax.ppermute(part, first, pairs)
-    return jnp.where(low, jnp.concatenate([part, other]), jnp.concatenate([other, part]))
+    return part, other, jnp.where(low, 1.0, 0.0).reshape(1, 1).astype(jnp.float32)
 
 
 def core_first(mesh):
@@ -162,27 +163,36 @@
     )
 
 
-def subspace_kernel(gram_ref, basis_ref, out_ref):
+def subspace_kernel(mine_ref, theirs_ref, low_ref, basis_ref, out_ref):
+    mine = mine_ref[...]
+    theirs = theirs_ref[...]
+    if mine.shape == theirs.shape:
+        low = low_ref[...] > 0.5
+        gram = jnp.concatenate([jnp.where(low, mine, theirs), jnp.where(low, theirs, mine)], axis=0)
+    else:
+        gram = jnp.concatenate([mine, theirs], axis=0)
     basis = basis_ref[...]
     for turn in range(SUBIT):
         product = jnp.dot(
-            gram_ref[...], basis,
+            gram, basis,
             precision=lax.Precision.HIGHEST, preferred_element_type=jnp.float32,
         )
         basis = cholesky_qr(cholesky_qr(product))
     out_ref[...] = basis
 
 
-def subspace_step(gram_full, basis):
+def subspace_step(halves, basis):
+    mine, theirs, low = halves
+    bands = mine.shape[0] + theirs.shape[0]
     return pl.pallas_call(
         subspace_kernel,
         out_shape=jax.ShapeDtypeStruct(basis.shape, jnp.float32),
         cost_estimate=pl.CostEstimate(
-            flops=SUBIT * (2 * gram_full.shape[0] * gram_full.size + 8 * basis.size * basis.shape[1]),
+            flops=SUBIT * (2 * bands * bands * basis.shape[1] + 8 * basis.size * basis.shape[1]),
             transcendentals=SUBIT * 2 * basis.shape[1],
-            bytes_accessed=4 * (gram_full.size + 2 * basis.size),
+            bytes_accessed=4 * (bands * bands + 2 * basis.size),
         ),
-    )(gram_full, basis)
+    )(mine, theirs, low, basis)
 
 
 def orthonormal(block):
@@ -216,9 +226,9 @@
         precision=lax.Precision.HIGHEST,
         preferred_element_type=jnp.float32,
     )
-    gram_full = paired_sum(local_gram, order)
+    gram_halves = paired_sum(local_gram, order)
     basis_now = start_basis
-    basis_now = subspace_step(gram_full, basis_now)
+    basis_now = subspace_step(gram_halves, basis_now)
     coeffs = jnp.dot(flat_cells, basis_now, precision=lax.Precision.HIGH)
     lowrank = lax.dot_general(
         basis_now,

time: 112 us -> 112 us (level)
    unnamed x12 -> x16, local copies, waits for them, and re-layouts: 7.09 us -> 7.73 us
where the time goes in v20:
time: 112 us; the launch traced here: 111 us
  waiting for transfers between devices  41.6 us (37%)
  starting transfers between devices  21.9 us (20%)
  other arithmetic  18.9 us (17%)
  Pallas kernels  11.2 us (10%)
  local copies, waits for them, and re-layouts  10.3 us (9%)
  matrix products  6.32 us (6%)
    ppermute x2, waiting for transfers between devices, flat_permute(): return lax.ppermute(flat, axis, pairs).reshape(block.shape)  21.9 us
    ppermute x4, waiting for transfers between devices, butterfly_sum(): partner = lax.ppermute(value, axis, [(i, i ^ step) for i in range(count)])  15.3 us
    select_n x4, other arithmetic, sweep(): return jnp.where(keep, new, 0.0)  11.7 us
    pallas_call x1, Pallas kernels, subspace_step(): pl.pallas_call(subspace_kernel, out_shape=jax.ShapeDtypeStruct(basis.shap...  11.2 us
    unnamed x16, local copies, waits for them, and re-layouts  7.73 us
    ppermute x4, starting transfers between devices, butterfly_sum(): partner = lax.ppermute(value, axis, [(i, i ^ step) for i in range(count)])  7.57 us
    ppermute x2, starting transfers between devices, flat_permute(): return lax.ppermute(flat, axis, pairs).reshape(block.shape)  6.27 us
    reduce_sum x4, other arithmetic, sweep(): jnp.sum(diff_col * diff_col + diff_row * diff_row, axis=-1, keepdims=True)  4.09 us
  transfers between devices with their start and end apart: 12, of which 8 were waited for; matrix products, arithmetic and copies ran while one was open for 4% of the time, Pallas kernels for 0%

profile of v20, /device:TPU:0, one launch (start us, length us, event | category | flops | bytes accessed | tf_op | source)
XLA Modules:
  0.0 111.1 jit_solution(10972255714558072953)
XLA Ops:
  0.6 1.9 %copy.4 = f32[224,8,256]{0,2,1:T(8,128)S(1)} copy(f32[224,8,256]{2,1,0:T(8,128)} %param.2) | data formatting | bytes 3670016 | tf_op args[0]
  2.5 1.6 %fusion.66 = (f32[4,256,224]{2,1,0:T(8,128)}, f32[4,256,224]{2,1,0:T(8,128)}) fusion(f32[8,256,224]{2,1,0:T(8,128)S(1)} %bitcast.53), kind=kLoop, calls=%fused_computation.120 | loop fusion | bytes 3670016 | tf_op jit(solution)/shard_map/slice | solution.py:97
  4.1 5.0 %collective-permute-start = (f32[16,64,224]{2,1,0:T(8,128)}, f32[16,64,224]{2,1,0:T(8,128)S(1)}, u32[]{:S(2)}, u32[]{:S(2)}) collective-permute-start(f32[16,64,224]{2,1,0:T(8,128)} %bitcast.1), channel_id=1, source_target_pairs={{0,8},{8,16},{16,24},{1,9},{9,17},{17,25},{2,10},{10,18},{18,26},{... | collective-permute-start | bytes 2752520 | tf_op jit(solution)/shard_map/ppermute | solution.py:72
  9.1 1.3 %collective-permute-start.1 = (f32[16,64,224]{2,1,0:T(8,128)}, f32[16,64,224]{2,1,0:T(8,128)}, u32[]{:S(2)}, u32[]{:S(2)}) collective-permute-start(f32[16,64,224]{2,1,0:T(8,128)} %bitcast.3), channel_id=1, source_target_pairs={{8,0},{16,8},{24,16},{9,1},{17,9},{25,17},{10,2},{18,10},{26,18},{... | collective-permute-start | bytes 2752520 | tf_op jit(solution)/shard_map/ppermute | solution.py:72
  10.5 1.5 %collective-permute-start.4 = (f32[8,4,224]{2,1,0:T(4,128)S(1)}, f32[8,4,224]{2,1,0:T(4,128)S(1)}, u32[]{:S(2)}, u32[]{:S(2)}) collective-permute-start(f32[8,4,224]{2,1,0:T(4,128)S(1)} %get-tuple-element.4), channel_id=1, source_target_pairs={{0,1},{1,2},{2,3},{3,4},{4,5},{5,6},{6,7},{8,9},{9,10},{10,11},{11... | collective-permute-start | bytes 86024 | tf_op jit(solution)/shard_map/ppermute | solution.py:99
  11.9 1.3 %collective-permute-start.5 = (f32[8,4,224]{2,1,0:T(4,128)S(1)}, f32[8,4,224]{2,1,0:T(4,128)S(1)}, u32[]{:S(2)}, u32[]{:S(2)}) collective-permute-start(f32[8,4,224]{2,1,0:T(4,128)S(1)} %get-tuple-element.5), channel_id=1, source_target_pairs={{1,0},{2,1},{3,2},{4,3},{5,4},{6,5},{7,6},{9,8},{10,9},{11,10},{12... | collective-permute-start | bytes 86024 | tf_op jit(solution)/shard_map/ppermute | solution.py:100
  14.1 17.7 %collective-permute-done = f32[16,64,224]{2,1,0:T(8,128)S(1)} collective-permute-done((f32[16,64,224]{2,1,0:T(8,128)}, f32[16,64,224]{2,1,0:T(8,128)S(1)}, u32[]{:S(2)}, u32[]{:S(2)}) %collective-permute-start) | collective-permute-done | bytes 917536 | tf_op jit(solution)/shard_map/ppermute | solution.py:72
  31.8 4.2 %collective-permute-done.1 = f32[16,64,224]{2,1,0:T(8,128)} collective-permute-done((f32[16,64,224]{2,1,0:T(8,128)}, f32[16,64,224]{2,1,0:T(8,128)}, u32[]{:S(2)}, u32[]{:S(2)}) %collective-permute-start.1) | collective-permute-done | bytes 917536 | tf_op jit(solution)/shard_map/ppermute | solution.py:72
  36.8 1.3 %collective-permute-start.2 = (f32[8,4,224]{2,1,0:T(4,128)S(1)}, f32[8,4,224]{2,1,0:T(4,128)S(1)}, u32[]{:S(2)}, u32[]{:S(2)}) collective-permute-start(f32[8,4,224]{2,1,0:T(4,128)S(1)} %get-tuple-element.6), channel_id=1, source_target_pairs={{0,1},{1,2},{2,3},{3,4},{4,5},{5,6},{6,7},{8,9},{9,10},{10,11},{11... | collective-permute-start | bytes 86024 | tf_op jit(solution)/shard_map/ppermute | solution.py:102
  38.1 1.3 %collective-permute-start.3 = (f32[8,4,224]{2,1,0:T(4,128)S(1)}, f32[8,4,224]{2,1,0:T(4,128)S(1)}, u32[]{:S(2)}, u32[]{:S(2)}) collective-permute-start(f32[8,4,224]{2,1,0:T(4,128)S(1)} %get-tuple-element.7), channel_id=1, source_target_pairs={{1,0},{2,1},{3,2},{4,3},{5,4},{6,5},{7,6},{9,8},{10,9},{11,10},{12... | collective-permute-start | bytes 86024 | tf_op jit(solution)/shard_map/ppermute | solution.py:103
  39.4 3.5 %collective-permute-done.3 = f32[8,4,224]{2,1,0:T(4,128)S(1)} collective-permute-done((f32[8,4,224]{2,1,0:T(4,128)S(1)}, f32[8,4,224]{2,1,0:T(4,128)S(1)}, u32[]{:S(2)}, u32[]{:S(2)}) %collective-permute-start.3) | collective-permute-done | bytes 28704 | tf_op jit(solution)/shard_map/ppermute | solution.py:103
  43.0 1.8 %maximum_maximum_fusion = f32[16,264,224]{2,1,0:T(8,128)S(1)} fusion(f32[4,4,224]{2,1,0:T(4,128)S(1)} %get-tuple-element.13, f32[4,256,224]{2,1,0:T(8,128)} %bitcast.4, f32[4,4,224]{2,1,0:T(4,128)S(1)} %get-tuple-element.11, f32[8,4,224]{2,1,0:T(4,128)S(1)} %collective-permute-done.5, f32[8,256,224]{2,1,0:T(8,128)S(1)} %bitcast.55, ...), kind=kLoop, calls=%fused_computation | loop fusion | flops 7569408 | bytes 7569408 | tf_op jit(solution)/shard_map/concatenate | solution.py:104
  44.8 1.3 %fusion.2 = f32[15,263]{1,0:T(8,128)S(1)} fusion(f32[16,264,224]{2,1,0:T(8,128)S(1)} %maximum_maximum_fusion), kind=kLoop, calls=%fused_computation.4 | loop fusion | flops 5298135 | bytes 10619940 | tf_op jit(solution)/shard_map/reduce_sum | solution.py:124
  46.2 3.6 %fusion.9 = f32[14,262,224]{2,1,0:T(8,128)S(1)} fusion(f32[16,264,224]{2,1,0:T(8,128)S(1)} %maximum_maximum_fusion, f32[14,262]{1,0:T(8,128)S(1)} %get-tuple-element.24, f32[14,262]{1,0:T(8,128)S(1)} %get-tuple-element.25, f32[14,262]{1,0:T(8,128)S(1)} %get-tuple-element.23, pred[14,262]{1,0:T(8,128)(4,1)S(1)} %broadcast_and_fusion), kind=kLoop, calls=%fused_computation.13 | loop fusion | flops 13967744 | bytes 19766852 | tf_op jit(solution)/shard_map/jit(_where)/select_n | solution.py:133
  49.8 1.1 fusion.17
  51.0 3.4 %fusion.21 = f32[12,260,224]{2,1,0:T(8,128)S(1)} fusion(f32[16,264,224]{2,1,0:T(8,128)S(1)} %maximum_maximum_fusion, f32[14,262,224]{2,1,0:T(8,128)S(1)} %fusion.9, f32[12,260]{1,0:T(8,128)S(1)} %get-tuple-element.21, f32[12,260]{1,0:T(8,128)S(1)} %get-tuple-element.22, f32[12,260]{1,0:T(8,128)S(1)} %get-tuple-element.20, ...), kind=kLoop, calls=%fused_computation.31 | loop fusion | flops 11880960 | bytes 19609200 | tf_op jit(solution)/shard_map/jit(_where)/select_n | solution.py:133
  55.4 2.7 %fusion.37 = f32[10,258,224]{2,1,0:T(8,128)S(1)} fusion(f32[16,264,224]{2,1,0:T(8,128)S(1)} %maximum_maximum_fusion, f32[12,260,224]{2,1,0:T(8,128)S(1)} %fusion.21, f32[10,258]{1,0:T(8,128)S(1)} %get-tuple-element.18, f32[10,258]{1,0:T(8,128)S(1)} %get-tuple-element.19, f32[10,258]{1,0:T(8,128)S(1)} %get-tuple-element.17, ...), kind=kLoop, calls=%fused_computation.54 | loop fusion | flops 9824640 | bytes 16215300 | tf_op jit(solution)/shard_map/jit(_where)/select_n | solution.py:133
  59.7 2.0 %fusion.56 = f32[8,256,224]{2,1,0:T(8,128)S(1)} fusion(f32[10,258,224]{2,1,0:T(8,128)S(1)} %fusion.37, f32[8,256]{1,0:T(8,128)S(1)} %get-tuple-element.15, f32[8,256]{1,0:T(8,128)S(1)} %get-tuple-element.16, f32[8,256]{1,0:T(8,128)S(1)} %get-tuple-element.14, pred[8,256]{1,0:T(8,128)(4,1)S(1)} %broadcast_and_fusion.3, f32[224,8,256]{0,2,1:T(8,128)S(1)} %copy-done.1), kind=kLoop, calls=%fused_computation.80 | loop fusion | flops 7798784 | bytes 12871680 | tf_op jit(solution)/shard_map/jit(_where)/select_n | solution.py:133
  61.7 3.5 %convolution_bitcast_fusion = f32[224,224]{1,0:T(8,128)S(1)} fusion(f32[8,256,224]{2,1,0:T(8,128)S(1)} %fusion.56), kind=kOutput, calls=%fused_computation.89 | convolution fusion | flops 1233125376 | bytes 2035712 | tf_op jit(solution)/shard_map/dot_general | solution.py:222
  65.2 2.7 %collective-permute-start.6 = (f32[112,224]{1,0:T(8,128)S(1)}, f32[112,224]{1,0:T(8,128)S(1)}, u32[]{:S(2)}, u32[]{:S(2)}) collective-permute-start(f32[112,224]{1,0:T(8,128)S(1)} %slice_select_fusion), channel_id=1, source_target_pairs={{0,1},{1,0},{2,3},{3,2},{4,5},{5,4},{6,7},{7,6},{8,9},{9,8},{10,11... | collective-permute-start | bytes 301064 | tf_op jit(solution)/shard_map/ppermute | solution.py:45
  67.9 1.0 collective-permute-done.6
  68.9 2.5 %collective-permute-start.7 = (f32[112,224]{1,0:T(8,128)S(1)}, f32[112,224]{1,0:T(8,128)S(1)}, u32[]{:S(2)}, u32[]{:S(2)}) collective-permute-start(f32[112,224]{1,0:T(8,128)S(1)} %select_add_fusion), channel_id=1, source_target_pairs={{0,2},{1,3},{2,0},{3,1},{4,6},{5,7},{6,4},{7,5},{8,10},{9,11},{10,... | collective-permute-start | bytes 301064 | tf_op jit(solution)/shard_map/ppermute | solution.py:27
  71.4 3.7 %collective-permute-done.7 = f32[112,224]{1,0:T(8,128)S(1)} collective-permute-done((f32[112,224]{1,0:T(8,128)S(1)}, f32[112,224]{1,0:T(8,128)S(1)}, u32[]{:S(2)}, u32[]{:S(2)}) %collective-permute-start.7) | collective-permute-done | bytes 100384 | tf_op jit(solution)/shard_map/ppermute | solution.py:27
  76.0 4.0 %collective-permute-done.8 = f32[112,224]{1,0:T(8,128)S(1)} collective-permute-done((f32[112,224]{1,0:T(8,128)S(1)}, f32[112,224]{1,0:T(8,128)S(1)}, u32[]{:S(2)}, u32[]{:S(2)}) %collective-permute-start.8) | collective-permute-done | bytes 100384 | tf_op jit(solution)/shard_map/ppermute | solution.py:27
  80.0 1.6 %collective-permute-start.9 = (f32[112,224]{1,0:T(8,128)S(1)}, f32[112,224]{1,0:T(8,128)S(1)}, u32[]{:S(2)}, u32[]{:S(2)}) collective-permute-start(f32[112,224]{1,0:T(8,128)S(1)} %add.156), channel_id=1, source_target_pairs={{0,8},{8,0},{16,24},{24,16},{1,9},{9,1},{17,25},{25,17},{2,10},{10... | collective-permute-start | bytes 301064 | tf_op jit(solution)/shard_map/ppermute | solution.py:27
  81.6 3.3 %collective-permute-done.9 = f32[112,224]{1,0:T(8,128)S(1)} collective-permute-done((f32[112,224]{1,0:T(8,128)S(1)}, f32[112,224]{1,0:T(8,128)S(1)}, u32[]{:S(2)}, u32[]{:S(2)}) %collective-permute-start.9) | collective-permute-done | bytes 100384 | tf_op jit(solution)/shard_map/ppermute | solution.py:27
  84.9 2.6 %collective-permute-start.10 = (f32[112,224]{1,0:T(8,128)S(1)}, f32[112,224]{1,0:T(8,128)S(1)}, u32[]{:S(2)}, u32[]{:S(2)}) collective-permute-start(f32[112,224]{1,0:T(8,128)S(1)} %add.157), channel_id=1, source_target_pairs={{0,16},{8,24},{16,0},{24,8},{1,17},{9,25},{17,1},{25,9},{2,18},{10... | collective-permute-start | bytes 301064 | tf_op jit(solution)/shard_map/ppermute | solution.py:27
  87.5 4.4 %collective-permute-done.10 = f32[112,224]{1,0:T(8,128)S(1)} collective-permute-done((f32[112,224]{1,0:T(8,128)S(1)}, f32[112,224]{1,0:T(8,128)S(1)}, u32[]{:S(2)}, u32[]{:S(2)}) %collective-permute-start.10) | collective-permute-done | bytes 100384 | tf_op jit(solution)/shard_map/ppermute | solution.py:27
  92.7 1.8 %copy.6 = f32[224,8,256]{2,1,0:T(8,128)} copy(f32[224,8,256]{0,2,1:T(8,128)S(1)} %bitcast.51) | data formatting | bytes 3670016
  95.1 11.2 %shard_map.41 = f32[224,16]{1,0:T(8,128)} custom-call(f32[112,224]{1,0:T(8,128)} %copy-done.3, f32[112,224]{1,0:T(8,128)} %copy-done.4, f32[1,1]{1,0:T(1,128)} %bitcast.23.low_ref, f32[224,16]{1,0:T(8,128)} %copy.5.basis_ref), custom_call_target="tpu_custom_call" | custom-call | flops 4128768 | bytes 229376 | tf_op jit(solution)/shard_map/pallas_call | solution.py:187
  106.3 2.0 %fusion.69 = f32[2048,16]{1,0:T(8,128)S(1)} fusion(f32[2048,224]{1,0:T(8,128)S(1)} %bitcast.52, f32[224,16]{1,0:T(8,128)} %shard_map.41), kind=kOutput, calls=%fused_computation.123 | convolution fusion | flops 44040192 | bytes 1980416 | tf_op jit(solution)/shard_map/dot_general | solution.py:232
  109.2 2.0 %copy.7 = f32[28,8,8,256]{3,2,1,0:T(8,128)} copy(f32[28,8,8,256]{3,1,2,0:T(8,128)S(1)} %bitcast.56) | data formatting | bytes 3670016
  (54 shorter events, 7.9 us)
Async XLA Ops:
  2.5 40.4 %copy-start = (f32[224,8,256]{0,2,1:T(8,128)}, f32[224,8,256]{0,2,1:T(8,128)S(1)}, u32[]{:S(2)}) copy-start(f32[224,8,256]{0,2,1:T(8,128)S(1)} %copy.4) | copy-start | bytes 5505028
  4.1 27.6 %collective-permute-start = (f32[16,64,224]{2,1,0:T(8,128)}, f32[16,64,224]{2,1,0:T(8,128)S(1)}, u32[]{:S(2)}, u32[]{:S(2)}) collective-permute-start(f32[16,64,224]{2,1,0:T(8,128)} %bitcast.1), channel_id=1, source_target_pairs={{0,8},{8,16},{16,24},{1,9},{9,17},{17,25},{2,10},{10,18},{18,26},{... | collective-permute-start | bytes 2752520 | tf_op jit(solution)/shard_map/ppermute | solution.py:72
  9.1 26.8 %collective-permute-start.1 = (f32[16,64,224]{2,1,0:T(8,128)}, f32[16,64,224]{2,1,0:T(8,128)}, u32[]{:S(2)}, u32[]{:S(2)}) collective-permute-start(f32[16,64,224]{2,1,0:T(8,128)} %bitcast.3), channel_id=1, source_target_pairs={{8,0},{16,8},{24,16},{9,1},{17,9},{25,17},{10,2},{18,10},{26,18},{... | collective-permute-start | bytes 2752520 | tf_op jit(solution)/shard_map/ppermute | solution.py:72
  10.5 32.5 %collective-permute-start.4 = (f32[8,4,224]{2,1,0:T(4,128)S(1)}, f32[8,4,224]{2,1,0:T(4,128)S(1)}, u32[]{:S(2)}, u32[]{:S(2)}) collective-permute-start(f32[8,4,224]{2,1,0:T(4,128)S(1)} %get-tuple-element.4), channel_id=1, source_target_pairs={{0,1},{1,2},{2,3},{3,4},{4,5},{5,6},{6,7},{8,9},{9,10},{10,11},{11... | collective-permute-start | bytes 86024 | tf_op jit(solution)/shard_map/ppermute | solution.py:99
  11.9 31.0 %collective-permute-start.5 = (f32[8,4,224]{2,1,0:T(4,128)S(1)}, f32[8,4,224]{2,1,0:T(4,128)S(1)}, u32[]{:S(2)}, u32[]{:S(2)}) collective-permute-start(f32[8,4,224]{2,1,0:T(4,128)S(1)} %get-tuple-element.5), channel_id=1, source_target_pairs={{1,0},{2,1},{3,2},{4,3},{5,4},{6,5},{7,6},{9,8},{10,9},{11,10},{12... | collective-permute-start | bytes 86024 | tf_op jit(solution)/shard_map/ppermute | solution.py:100
  36.8 2.7 %collective-permute-start.2 = (f32[8,4,224]{2,1,0:T(4,128)S(1)}, f32[8,4,224]{2,1,0:T(4,128)S(1)}, u32[]{:S(2)}, u32[]{:S(2)}) collective-permute-start(f32[8,4,224]{2,1,0:T(4,128)S(1)} %get-tuple-element.6), channel_id=1, source_target_pairs={{0,1},{1,2},{2,3},{3,4},{4,5},{5,6},{6,7},{8,9},{9,10},{10,11},{11... | collective-permute-start | bytes 86024 | tf_op jit(solution)/shard_map/ppermute | solution.py:102
  38.1 4.8 %collective-permute-start.3 = (f32[8,4,224]{2,1,0:T(4,128)S(1)}, f32[8,4,224]{2,1,0:T(4,128)S(1)}, u32[]{:S(2)}, u32[]{:S(2)}) collective-permute-start(f32[8,4,224]{2,1,0:T(4,128)S(1)} %get-tuple-element.7), channel_id=1, source_target_pairs={{1,0},{2,1},{3,2},{4,3},{5,4},{6,5},{7,6},{9,8},{10,9},{11,10},{12... | collective-permute-start | bytes 86024 | tf_op jit(solution)/shard_map/ppermute | solution.py:103
  58.1 1.6 %copy-start.1 = (f32[224,8,256]{0,2,1:T(8,128)S(1)}, f32[224,8,256]{0,2,1:T(8,128)}, u32[]{:S(2)}) copy-start(f32[224,8,256]{0,2,1:T(8,128)} %copy-done) | copy-start | bytes 5505028
  61.7 30.2 %copy-start.5 = (f32[224,16]{0,1:T(8,128)S(1)}, f32[224,16]{0,1:T(8,128)}, u32[]{:S(2)}) copy-start(f32[224,16]{0,1:T(8,128)} %param.3) | copy-start | bytes 43012
  65.2 3.7 %collective-permute-start.6 = (f32[112,224]{1,0:T(8,128)S(1)}, f32[112,224]{1,0:T(8,128)S(1)}, u32[]{:S(2)}, u32[]{:S(2)}) collective-permute-start(f32[112,224]{1,0:T(8,128)S(1)} %slice_select_fusion), channel_id=1, source_target_pairs={{0,1},{1,0},{2,3},{3,2},{4,5},{5,4},{6,7},{7,6},{8,9},{9,8},{10,11... | collective-permute-start | bytes 301064 | tf_op jit(solution)/shard_map/ppermute | solution.py:45
  68.9 6.1 %collective-permute-start.7 = (f32[112,224]{1,0:T(8,128)S(1)}, f32[112,224]{1,0:T(8,128)S(1)}, u32[]{:S(2)}, u32[]{:S(2)}) collective-permute-start(f32[112,224]{1,0:T(8,128)S(1)} %select_add_fusion), channel_id=1, source_target_pairs={{0,2},{1,3},{2,0},{3,1},{4,6},{5,7},{6,4},{7,5},{8,10},{9,11},{10,... | collective-permute-start | bytes 301064 | tf_op jit(solution)/shard_map/ppermute | solution.py:27
  75.1 4.9 %collective-permute-start.8 = (f32[112,224]{1,0:T(8,128)S(1)}, f32[112,224]{1,0:T(8,128)S(1)}, u32[]{:S(2)}, u32[]{:S(2)}) collective-permute-start(f32[112,224]{1,0:T(8,128)S(1)} %add.155), channel_id=1, source_target_pairs={{0,4},{1,5},{2,6},{3,7},{4,0},{5,1},{6,2},{7,3},{8,12},{9,13},{10,... | collective-permute-start | bytes 301064 | tf_op jit(solution)/shard_map/ppermute | solution.py:27
  80.0 4.9 %collective-permute-start.9 = (f32[112,224]{1,0:T(8,128)S(1)}, f32[112,224]{1,0:T(8,128)S(1)}, u32[]{:S(2)}, u32[]{:S(2)}) collective-permute-start(f32[112,224]{1,0:T(8,128)S(1)} %add.156), channel_id=1, source_target_pairs={{0,8},{8,0},{16,24},{24,16},{1,9},{9,1},{17,25},{25,17},{2,10},{10... | collective-permute-start | bytes 301064 | tf_op jit(solution)/shard_map/ppermute | solution.py:27
  84.9 7.0 %collective-permute-start.10 = (f32[112,224]{1,0:T(8,128)S(1)}, f32[112,224]{1,0:T(8,128)S(1)}, u32[]{:S(2)}, u32[]{:S(2)}) collective-permute-start(f32[112,224]{1,0:T(8,128)S(1)} %add.157), channel_id=1, source_target_pairs={{0,16},{8,24},{16,0},{24,8},{1,17},{9,25},{17,1},{25,9},{2,18},{10... | collective-permute-start | bytes 301064 | tf_op jit(solution)/shard_map/ppermute | solution.py:27
  91.9 2.6 %copy-start.3 = (f32[112,224]{1,0:T(8,128)}, f32[112,224]{1,0:T(8,128)S(1)}, u32[]{:S(2)}) copy-start(f32[112,224]{1,0:T(8,128)S(1)} %add.158.mine_ref) | copy-start | bytes 301060
  91.9 2.6 %collective-permute-start.11 = (f32[112,224]{1,0:T(8,128)S(1)}, f32[112,224]{1,0:T(8,128)S(1)}, u32[]{:S(2)}, u32[]{:S(2)}) collective-permute-start(f32[112,224]{1,0:T(8,128)S(1)} %add.158.mine_ref), channel_id=1, source_target_pairs={{0,1},{1,0},{2,3},{3,2},{4,5},{5,4},{6,7},{7,6},{8,9},{9,8},{10,11... | collective-permute-start | bytes 301064 | tf_op jit(solution)/shard_map/ppermute | solution.py:47
  94.5 0.6 copy-start.4
  106.3 2.0 %copy-start.2 = (f32[224,16]{1,0:T(8,128)S(1)}, f32[224,16]{1,0:T(8,128)}, u32[]{:S(2)}) copy-start(f32[224,16]{1,0:T(8,128)} %shard_map.41) | copy-start | bytes 43012

commit v21 on v20

--- a/solution.py
+++ b/solution.py
@@ -130,7 +130,7 @@
     row_up = weight[:-1, 1:] * (centre - field[:-2, 1:-1])
     spread = col_here - col_left + row_here - row_up
     new = centre + tau_step * spread + tau_step * fidelity * (source - centre)
-    return jnp.where(keep, new, 0.0)
+    return new if keep is None else jnp.where(keep, new, 0.0)
 
 
 def cholesky_qr(block):
@@ -214,6 +214,9 @@
         lo = sweep_no + 1
         nr = tile_rows + 2 * left
         nc = tile_cols + 2 * left
+        if left == 0:
+            field = pinned(sweep(field, cells, None))
+            continue
         source = ext[lo:lo + nr, lo:lo + nc]
         keep = (row_in[lo:lo + nr, None] & col_in[None, lo:lo + nc])[:, :, None]
         field = pinned(sweep(field, source, keep))

time: 112 us -> 112 us (level)
    select_n x4 -> x3, other arithmetic: 11.7 us -> 9.71 us  [sweep(): return new if keep is None else jnp.where(keep, new, 0.0)]
    add x0 -> x1, other arithmetic: none -> 1.83 us  [sweep(): new = centre + tau_step * spread + tau_step * fidelity * (source - centre)]
where the time goes in v21:
time: 112 us; the launch traced here: 111 us
  waiting for transfers between devices  41.9 us (37%)
  starting transfers between devices  21.9 us (20%)
  other arithmetic  18.7 us (17%)
  Pallas kernels  11.2 us (10%)
  local copies, waits for them, and re-layouts  10.3 us (9%)
  matrix products  6.32 us (6%)
    ppermute x2, waiting for transfers between devices, flat_permute(): return lax.ppermute(flat, axis, pairs).reshape(block.shape)  22.1 us
    ppermute x4, waiting for transfers between devices, butterfly_sum(): partner = lax.ppermute(value, axis, [(i, i ^ step) for i in range(count)])  15.3 us
    pallas_call x1, Pallas kernels, subspace_step(): pl.pallas_call(subspace_kernel, out_shape=jax.ShapeDtypeStruct(basis.shap...  11.2 us
    select_n x3, other arithmetic, sweep(): return new if keep is None else jnp.where(keep, new, 0.0)  9.71 us
    unnamed x16, local copies, waits for them, and re-layouts  7.73 us
    ppermute x4, starting transfers between devices, butterfly_sum(): partner = lax.ppermute(value, axis, [(i, i ^ step) for i in range(count)])  7.57 us
    ppermute x2, starting transfers between devices, flat_permute(): return lax.ppermute(flat, axis, pairs).reshape(block.shape)  6.27 us
    reduce_sum x4, other arithmetic, sweep(): jnp.sum(diff_col * diff_col + diff_row * diff_row, axis=-1, keepdims=True)  4.09 us
  transfers between devices with their start and end apart: 12, of which 8 were waited for; matrix products, arithmetic and copies ran while one was open for 4% of the time, Pallas kernels for 0%

profile of v21, /device:TPU:0, one launch (start us, length us, event | category | flops | bytes accessed | tf_op | source)
XLA Modules:
  0.0 111.1 jit_solution(4707321111703540353)
XLA Ops:
  0.6 1.9 %copy.4 = f32[224,8,256]{0,2,1:T(8,128)S(1)} copy(f32[224,8,256]{2,1,0:T(8,128)} %param.2) | data formatting | bytes 3670016 | tf_op args[0]
  2.5 1.8 %fusion.65 = (f32[4,256,224]{2,1,0:T(8,128)}, f32[4,256,224]{2,1,0:T(8,128)}) fusion(f32[8,256,224]{2,1,0:T(8,128)S(1)} %bitcast.53), kind=kLoop, calls=%fused_computation.118 | loop fusion | bytes 3670016 | tf_op jit(solution)/shard_map/slice | solution.py:97
  4.3 5.0 %collective-permute-start = (f32[16,64,224]{2,1,0:T(8,128)}, f32[16,64,224]{2,1,0:T(8,128)S(1)}, u32[]{:S(2)}, u32[]{:S(2)}) collective-permute-start(f32[16,64,224]{2,1,0:T(8,128)} %bitcast.1), channel_id=1, source_target_pairs={{0,8},{8,16},{16,24},{1,9},{9,17},{17,25},{2,10},{10,18},{18,26},{... | collective-permute-start | bytes 2752520 | tf_op jit(solution)/shard_map/ppermute | solution.py:72
  9.3 1.3 %collective-permute-start.1 = (f32[16,64,224]{2,1,0:T(8,128)}, f32[16,64,224]{2,1,0:T(8,128)}, u32[]{:S(2)}, u32[]{:S(2)}) collective-permute-start(f32[16,64,224]{2,1,0:T(8,128)} %bitcast.3), channel_id=1, source_target_pairs={{8,0},{16,8},{24,16},{9,1},{17,9},{25,17},{10,2},{18,10},{26,18},{... | collective-permute-start | bytes 2752520 | tf_op jit(solution)/shard_map/ppermute | solution.py:72
  10.6 1.5 %collective-permute-start.4 = (f32[8,4,224]{2,1,0:T(4,128)S(1)}, f32[8,4,224]{2,1,0:T(4,128)S(1)}, u32[]{:S(2)}, u32[]{:S(2)}) collective-permute-start(f32[8,4,224]{2,1,0:T(4,128)S(1)} %get-tuple-element.4), channel_id=1, source_target_pairs={{0,1},{1,2},{2,3},{3,4},{4,5},{5,6},{6,7},{8,9},{9,10},{10,11},{11... | collective-permute-start | bytes 86024 | tf_op jit(solution)/shard_map/ppermute | solution.py:99
  12.1 1.3 %collective-permute-start.5 = (f32[8,4,224]{2,1,0:T(4,128)S(1)}, f32[8,4,224]{2,1,0:T(4,128)S(1)}, u32[]{:S(2)}, u32[]{:S(2)}) collective-permute-start(f32[8,4,224]{2,1,0:T(4,128)S(1)} %get-tuple-element.5), channel_id=1, source_target_pairs={{1,0},{2,1},{3,2},{4,3},{5,4},{6,5},{7,6},{9,8},{10,9},{11,10},{12... | collective-permute-start | bytes 86024 | tf_op jit(solution)/shard_map/ppermute | solution.py:100
  14.0 17.9 %collective-permute-done = f32[16,64,224]{2,1,0:T(8,128)S(1)} collective-permute-done((f32[16,64,224]{2,1,0:T(8,128)}, f32[16,64,224]{2,1,0:T(8,128)S(1)}, u32[]{:S(2)}, u32[]{:S(2)}) %collective-permute-start) | collective-permute-done | bytes 917536 | tf_op jit(solution)/shard_map/ppermute | solution.py:72
  31.9 4.2 %collective-permute-done.1 = f32[16,64,224]{2,1,0:T(8,128)} collective-permute-done((f32[16,64,224]{2,1,0:T(8,128)}, f32[16,64,224]{2,1,0:T(8,128)}, u32[]{:S(2)}, u32[]{:S(2)}) %collective-permute-start.1) | collective-permute-done | bytes 917536 | tf_op jit(solution)/shard_map/ppermute | solution.py:72
  36.9 1.3 %collective-permute-start.2 = (f32[8,4,224]{2,1,0:T(4,128)S(1)}, f32[8,4,224]{2,1,0:T(4,128)S(1)}, u32[]{:S(2)}, u32[]{:S(2)}) collective-permute-start(f32[8,4,224]{2,1,0:T(4,128)S(1)} %get-tuple-element.6), channel_id=1, source_target_pairs={{0,1},{1,2},{2,3},{3,4},{4,5},{5,6},{6,7},{8,9},{9,10},{10,11},{11... | collective-permute-start | bytes 86024 | tf_op jit(solution)/shard_map/ppermute | solution.py:102
  38.3 1.3 %collective-permute-start.3 = (f32[8,4,224]{2,1,0:T(4,128)S(1)}, f32[8,4,224]{2,1,0:T(4,128)S(1)}, u32[]{:S(2)}, u32[]{:S(2)}) collective-permute-start(f32[8,4,224]{2,1,0:T(4,128)S(1)} %get-tuple-element.7), channel_id=1, source_target_pairs={{1,0},{2,1},{3,2},{4,3},{5,4},{6,5},{7,6},{9,8},{10,9},{11,10},{12... | collective-permute-start | bytes 86024 | tf_op jit(solution)/shard_map/ppermute | solution.py:103
  39.6 3.5 %collective-permute-done.3 = f32[8,4,224]{2,1,0:T(4,128)S(1)} collective-permute-done((f32[8,4,224]{2,1,0:T(4,128)S(1)}, f32[8,4,224]{2,1,0:T(4,128)S(1)}, u32[]{:S(2)}, u32[]{:S(2)}) %collective-permute-start.3) | collective-permute-done | bytes 28704 | tf_op jit(solution)/shard_map/ppermute | solution.py:103
  43.1 1.8 %maximum_maximum_fusion = f32[16,264,224]{2,1,0:T(8,128)S(1)} fusion(f32[4,4,224]{2,1,0:T(4,128)S(1)} %get-tuple-element.13, f32[4,256,224]{2,1,0:T(8,128)} %bitcast.4, f32[4,4,224]{2,1,0:T(4,128)S(1)} %get-tuple-element.11, f32[8,4,224]{2,1,0:T(4,128)S(1)} %collective-permute-done.5, f32[8,256,224]{2,1,0:T(8,128)S(1)} %bitcast.55, ...), kind=kLoop, calls=%fused_computation | loop fusion | flops 7569408 | bytes 7569408 | tf_op jit(solution)/shard_map/concatenate | solution.py:104
  45.0 1.3 %fusion.2 = f32[15,263]{1,0:T(8,128)S(1)} fusion(f32[16,264,224]{2,1,0:T(8,128)S(1)} %maximum_maximum_fusion), kind=kLoop, calls=%fused_computation.4 | loop fusion | flops 5298135 | bytes 10619940 | tf_op jit(solution)/shard_map/reduce_sum | solution.py:124
  46.3 3.6 %fusion.9 = f32[14,262,224]{2,1,0:T(8,128)S(1)} fusion(f32[16,264,224]{2,1,0:T(8,128)S(1)} %maximum_maximum_fusion, f32[14,262]{1,0:T(8,128)S(1)} %get-tuple-element.24, f32[14,262]{1,0:T(8,128)S(1)} %get-tuple-element.25, f32[14,262]{1,0:T(8,128)S(1)} %get-tuple-element.23, pred[14,262]{1,0:T(8,128)(4,1)S(1)} %broadcast_and_fusion), kind=kLoop, calls=%fused_computation.13 | loop fusion | flops 13967744 | bytes 19766852 | tf_op jit(solution)/shard_map/jit(_where)/select_n | solution.py:133
  49.9 1.1 fusion.17
  51.1 3.4 %fusion.21 = f32[12,260,224]{2,1,0:T(8,128)S(1)} fusion(f32[16,264,224]{2,1,0:T(8,128)S(1)} %maximum_maximum_fusion, f32[14,262,224]{2,1,0:T(8,128)S(1)} %fusion.9, f32[12,260]{1,0:T(8,128)S(1)} %get-tuple-element.21, f32[12,260]{1,0:T(8,128)S(1)} %get-tuple-element.22, f32[12,260]{1,0:T(8,128)S(1)} %get-tuple-element.20, ...), kind=kLoop, calls=%fused_computation.31 | loop fusion | flops 11880960 | bytes 19609200 | tf_op jit(solution)/shard_map/jit(_where)/select_n | solution.py:133
  55.6 2.7 %fusion.37 = f32[10,258,224]{2,1,0:T(8,128)S(1)} fusion(f32[16,264,224]{2,1,0:T(8,128)S(1)} %maximum_maximum_fusion, f32[12,260,224]{2,1,0:T(8,128)S(1)} %fusion.21, f32[10,258]{1,0:T(8,128)S(1)} %get-tuple-element.18, f32[10,258]{1,0:T(8,128)S(1)} %get-tuple-element.19, f32[10,258]{1,0:T(8,128)S(1)} %get-tuple-element.17, ...), kind=kLoop, calls=%fused_computation.54 | loop fusion | flops 9824640 | bytes 16215300 | tf_op jit(solution)/shard_map/jit(_where)/select_n | solution.py:133
  59.9 1.8 %fusion.55 = f32[8,256,224]{2,1,0:T(8,128)S(1)} fusion(f32[10,258,224]{2,1,0:T(8,128)S(1)} %fusion.37, f32[8,256]{1,0:T(8,128)S(1)} %get-tuple-element.15, f32[8,256]{1,0:T(8,128)S(1)} %get-tuple-element.16, f32[8,256]{1,0:T(8,128)S(1)} %get-tuple-element.14, f32[224,8,256]{0,2,1:T(8,128)S(1)} %copy-done.1), kind=kLoop, calls=%fused_computation.79 | loop fusion | flops 7340032 | bytes 12869632 | tf_op jit(solution)/shard_map/add | solution.py:132
  61.7 3.5 %convolution_bitcast_fusion = f32[224,224]{1,0:T(8,128)S(1)} fusion(f32[8,256,224]{2,1,0:T(8,128)S(1)} %fusion.55), kind=kOutput, calls=%fused_computation.88 | convolution fusion | flops 1233125376 | bytes 2035712 | tf_op jit(solution)/shard_map/dot_general | solution.py:225
  65.2 2.7 %collective-permute-start.6 = (f32[112,224]{1,0:T(8,128)S(1)}, f32[112,224]{1,0:T(8,128)S(1)}, u32[]{:S(2)}, u32[]{:S(2)}) collective-permute-start(f32[112,224]{1,0:T(8,128)S(1)} %slice_select_fusion), channel_id=1, source_target_pairs={{0,1},{1,0},{2,3},{3,2},{4,5},{5,4},{6,7},{7,6},{8,9},{9,8},{10,11... | collective-permute-start | bytes 301064 | tf_op jit(solution)/shard_map/ppermute | solution.py:45
  67.9 1.0 collective-permute-done.6
  68.9 2.5 %collective-permute-start.7 = (f32[112,224]{1,0:T(8,128)S(1)}, f32[112,224]{1,0:T(8,128)S(1)}, u32[]{:S(2)}, u32[]{:S(2)}) collective-permute-start(f32[112,224]{1,0:T(8,128)S(1)} %select_add_fusion), channel_id=1, source_target_pairs={{0,2},{1,3},{2,0},{3,1},{4,6},{5,7},{6,4},{7,5},{8,10},{9,11},{10,... | collective-permute-start | bytes 301064 | tf_op jit(solution)/shard_map/ppermute | solution.py:27
  71.4 3.7 %collective-permute-done.7 = f32[112,224]{1,0:T(8,128)S(1)} collective-permute-done((f32[112,224]{1,0:T(8,128)S(1)}, f32[112,224]{1,0:T(8,128)S(1)}, u32[]{:S(2)}, u32[]{:S(2)}) %collective-permute-start.7) | collective-permute-done | bytes 100384 | tf_op jit(solution)/shard_map/ppermute | solution.py:27
  76.0 4.0 %collective-permute-done.8 = f32[112,224]{1,0:T(8,128)S(1)} collective-permute-done((f32[112,224]{1,0:T(8,128)S(1)}, f32[112,224]{1,0:T(8,128)S(1)}, u32[]{:S(2)}, u32[]{:S(2)}) %collective-permute-start.8) | collective-permute-done | bytes 100384 | tf_op jit(solution)/shard_map/ppermute | solution.py:27
  80.0 1.6 %collective-permute-start.9 = (f32[112,224]{1,0:T(8,128)S(1)}, f32[112,224]{1,0:T(8,128)S(1)}, u32[]{:S(2)}, u32[]{:S(2)}) collective-permute-start(f32[112,224]{1,0:T(8,128)S(1)} %add.156), channel_id=1, source_target_pairs={{0,8},{8,0},{16,24},{24,16},{1,9},{9,1},{17,25},{25,17},{2,10},{10... | collective-permute-start | bytes 301064 | tf_op jit(solution)/shard_map/ppermute | solution.py:27
  81.6 3.3 %collective-permute-done.9 = f32[112,224]{1,0:T(8,128)S(1)} collective-permute-done((f32[112,224]{1,0:T(8,128)S(1)}, f32[112,224]{1,0:T(8,128)S(1)}, u32[]{:S(2)}, u32[]{:S(2)}) %collective-permute-start.9) | collective-permute-done | bytes 100384 | tf_op jit(solution)/shard_map/ppermute | solution.py:27
  84.9 2.6 %collective-permute-start.10 = (f32[112,224]{1,0:T(8,128)S(1)}, f32[112,224]{1,0:T(8,128)S(1)}, u32[]{:S(2)}, u32[]{:S(2)}) collective-permute-start(f32[112,224]{1,0:T(8,128)S(1)} %add.157), channel_id=1, source_target_pairs={{0,16},{8,24},{16,0},{24,8},{1,17},{9,25},{17,1},{25,9},{2,18},{10... | collective-permute-start | bytes 301064 | tf_op jit(solution)/shard_map/ppermute | solution.py:27
  87.5 4.4 %collective-permute-done.10 = f32[112,224]{1,0:T(8,128)S(1)} collective-permute-done((f32[112,224]{1,0:T(8,128)S(1)}, f32[112,224]{1,0:T(8,128)S(1)}, u32[]{:S(2)}, u32[]{:S(2)}) %collective-permute-start.10) | collective-permute-done | bytes 100384 | tf_op jit(solution)/shard_map/ppermute | solution.py:27
  92.7 1.8 %copy.6 = f32[224,8,256]{2,1,0:T(8,128)} copy(f32[224,8,256]{0,2,1:T(8,128)S(1)} %bitcast.51) | data formatting | bytes 3670016
  95.1 11.2 %shard_map.41 = f32[224,16]{1,0:T(8,128)} custom-call(f32[112,224]{1,0:T(8,128)} %copy-done.3, f32[112,224]{1,0:T(8,128)} %copy-done.4, f32[1,1]{1,0:T(1,128)} %bitcast.23.low_ref, f32[224,16]{1,0:T(8,128)} %copy.5.basis_ref), custom_call_target="tpu_custom_call" | custom-call | flops 4128768 | bytes 229376 | tf_op jit(solution)/shard_map/pallas_call | solution.py:187
  106.3 2.0 %fusion.68 = f32[2048,16]{1,0:T(8,128)S(1)} fusion(f32[2048,224]{1,0:T(8,128)S(1)} %bitcast.52, f32[224,16]{1,0:T(8,128)} %shard_map.41), kind=kOutput, calls=%fused_computation.121 | convolution fusion | flops 44040192 | bytes 1980416 | tf_op jit(solution)/shard_map/dot_general | solution.py:235
  109.2 2.0 %copy.7 = f32[28,8,8,256]{3,2,1,0:T(8,128)} copy(f32[28,8,8,256]{3,1,2,0:T(8,128)S(1)} %bitcast.56) | data formatting | bytes 3670016
  (51 shorter events, 7.7 us)
Async XLA Ops:
  2.5 40.6 %copy-start = (f32[224,8,256]{0,2,1:T(8,128)}, f32[224,8,256]{0,2,1:T(8,128)S(1)}, u32[]{:S(2)}) copy-start(f32[224,8,256]{0,2,1:T(8,128)S(1)} %copy.4) | copy-start | bytes 5505028
  4.3 27.6 %collective-permute-start = (f32[16,64,224]{2,1,0:T(8,128)}, f32[16,64,224]{2,1,0:T(8,128)S(1)}, u32[]{:S(2)}, u32[]{:S(2)}) collective-permute-start(f32[16,64,224]{2,1,0:T(8,128)} %bitcast.1), channel_id=1, source_target_pairs={{0,8},{8,16},{16,24},{1,9},{9,17},{17,25},{2,10},{10,18},{18,26},{... | collective-permute-start | bytes 2752520 | tf_op jit(solution)/shard_map/ppermute | solution.py:72
  9.3 26.8 %collective-permute-start.1 = (f32[16,64,224]{2,1,0:T(8,128)}, f32[16,64,224]{2,1,0:T(8,128)}, u32[]{:S(2)}, u32[]{:S(2)}) collective-permute-start(f32[16,64,224]{2,1,0:T(8,128)} %bitcast.3), channel_id=1, source_target_pairs={{8,0},{16,8},{24,16},{9,1},{17,9},{25,17},{10,2},{18,10},{26,18},{... | collective-permute-start | bytes 2752520 | tf_op jit(solution)/shard_map/ppermute | solution.py:72
  10.6 32.5 %collective-permute-start.4 = (f32[8,4,224]{2,1,0:T(4,128)S(1)}, f32[8,4,224]{2,1,0:T(4,128)S(1)}, u32[]{:S(2)}, u32[]{:S(2)}) collective-permute-start(f32[8,4,224]{2,1,0:T(4,128)S(1)} %get-tuple-element.4), channel_id=1, source_target_pairs={{0,1},{1,2},{2,3},{3,4},{4,5},{5,6},{6,7},{8,9},{9,10},{10,11},{11... | collective-permute-start | bytes 86024 | tf_op jit(solution)/shard_map/ppermute | solution.py:99
  12.1 31.0 %collective-permute-start.5 = (f32[8,4,224]{2,1,0:T(4,128)S(1)}, f32[8,4,224]{2,1,0:T(4,128)S(1)}, u32[]{:S(2)}, u32[]{:S(2)}) collective-permute-start(f32[8,4,224]{2,1,0:T(4,128)S(1)} %get-tuple-element.5), channel_id=1, source_target_pairs={{1,0},{2,1},{3,2},{4,3},{5,4},{6,5},{7,6},{9,8},{10,9},{11,10},{12... | collective-permute-start | bytes 86024 | tf_op jit(solution)/shard_map/ppermute | solution.py:100
  36.9 2.7 %collective-permute-start.2 = (f32[8,4,224]{2,1,0:T(4,128)S(1)}, f32[8,4,224]{2,1,0:T(4,128)S(1)}, u32[]{:S(2)}, u32[]{:S(2)}) collective-permute-start(f32[8,4,224]{2,1,0:T(4,128)S(1)} %get-tuple-element.6), channel_id=1, source_target_pairs={{0,1},{1,2},{2,3},{3,4},{4,5},{5,6},{6,7},{8,9},{9,10},{10,11},{11... | collective-permute-start | bytes 86024 | tf_op jit(solution)/shard_map/ppermute | solution.py:102
  38.3 4.8 %collective-permute-start.3 = (f32[8,4,224]{2,1,0:T(4,128)S(1)}, f32[8,4,224]{2,1,0:T(4,128)S(1)}, u32[]{:S(2)}, u32[]{:S(2)}) collective-permute-start(f32[8,4,224]{2,1,0:T(4,128)S(1)} %get-tuple-element.7), channel_id=1, source_target_pairs={{1,0},{2,1},{3,2},{4,3},{5,4},{6,5},{7,6},{9,8},{10,9},{11,10},{12... | collective-permute-start | bytes 86024 | tf_op jit(solution)/shard_map/ppermute | solution.py:103
  58.3 1.6 %copy-start.1 = (f32[224,8,256]{0,2,1:T(8,128)S(1)}, f32[224,8,256]{0,2,1:T(8,128)}, u32[]{:S(2)}) copy-start(f32[224,8,256]{0,2,1:T(8,128)} %copy-done) | copy-start | bytes 5505028
  61.7 30.2 %copy-start.5 = (f32[224,16]{0,1:T(8,128)S(1)}, f32[224,16]{0,1:T(8,128)}, u32[]{:S(2)}) copy-start(f32[224,16]{0,1:T(8,128)} %param.3) | copy-start | bytes 43012
  65.2 3.7 %collective-permute-start.6 = (f32[112,224]{1,0:T(8,128)S(1)}, f32[112,224]{1,0:T(8,128)S(1)}, u32[]{:S(2)}, u32[]{:S(2)}) collective-permute-start(f32[112,224]{1,0:T(8,128)S(1)} %slice_select_fusion), channel_id=1, source_target_pairs={{0,1},{1,0},{2,3},{3,2},{4,5},{5,4},{6,7},{7,6},{8,9},{9,8},{10,11... | collective-permute-start | bytes 301064 | tf_op jit(solution)/shard_map/ppermute | solution.py:45
  68.9 6.1 %collective-permute-start.7 = (f32[112,224]{1,0:T(8,128)S(1)}, f32[112,224]{1,0:T(8,128)S(1)}, u32[]{:S(2)}, u32[]{:S(2)}) collective-permute-start(f32[112,224]{1,0:T(8,128)S(1)} %select_add_fusion), channel_id=1, source_target_pairs={{0,2},{1,3},{2,0},{3,1},{4,6},{5,7},{6,4},{7,5},{8,10},{9,11},{10,... | collective-permute-start | bytes 301064 | tf_op jit(solution)/shard_map/ppermute | solution.py:27
  75.1 4.9 %collective-permute-start.8 = (f32[112,224]{1,0:T(8,128)S(1)}, f32[112,224]{1,0:T(8,128)S(1)}, u32[]{:S(2)}, u32[]{:S(2)}) collective-permute-start(f32[112,224]{1,0:T(8,128)S(1)} %add.155), channel_id=1, source_target_pairs={{0,4},{1,5},{2,6},{3,7},{4,0},{5,1},{6,2},{7,3},{8,12},{9,13},{10,... | collective-permute-start | bytes 301064 | tf_op jit(solution)/shard_map/ppermute | solution.py:27
  80.0 4.9 %collective-permute-start.9 = (f32[112,224]{1,0:T(8,128)S(1)}, f32[112,224]{1,0:T(8,128)S(1)}, u32[]{:S(2)}, u32[]{:S(2)}) collective-permute-start(f32[112,224]{1,0:T(8,128)S(1)} %add.156), channel_id=1, source_target_pairs={{0,8},{8,0},{16,24},{24,16},{1,9},{9,1},{17,25},{25,17},{2,10},{10... | collective-permute-start | bytes 301064 | tf_op jit(solution)/shard_map/ppermute | solution.py:27
  84.9 7.0 %collective-permute-start.10 = (f32[112,224]{1,0:T(8,128)S(1)}, f32[112,224]{1,0:T(8,128)S(1)}, u32[]{:S(2)}, u32[]{:S(2)}) collective-permute-start(f32[112,224]{1,0:T(8,128)S(1)} %add.157), channel_id=1, source_target_pairs={{0,16},{8,24},{16,0},{24,8},{1,17},{9,25},{17,1},{25,9},{2,18},{10... | collective-permute-start | bytes 301064 | tf_op jit(solution)/shard_map/ppermute | solution.py:27
  91.9 2.6 %copy-start.3 = (f32[112,224]{1,0:T(8,128)}, f32[112,224]{1,0:T(8,128)S(1)}, u32[]{:S(2)}) copy-start(f32[112,224]{1,0:T(8,128)S(1)} %add.158.mine_ref) | copy-start | bytes 301060
  91.9 2.6 %collective-permute-start.11 = (f32[112,224]{1,0:T(8,128)S(1)}, f32[112,224]{1,0:T(8,128)S(1)}, u32[]{:S(2)}, u32[]{:S(2)}) collective-permute-start(f32[112,224]{1,0:T(8,128)S(1)} %add.158.mine_ref), channel_id=1, source_target_pairs={{0,1},{1,0},{2,3},{3,2},{4,5},{5,4},{6,7},{7,6},{8,9},{9,8},{10,11... | collective-permute-start | bytes 301064 | tf_op jit(solution)/shard_map/ppermute | solution.py:47
  94.5 0.6 copy-start.4
  106.3 2.0 %copy-start.2 = (f32[224,16]{1,0:T(8,128)S(1)}, f32[224,16]{1,0:T(8,128)}, u32[]{:S(2)}) copy-start(f32[224,16]{1,0:T(8,128)} %shard_map.41) | copy-start | bytes 43012

commit v22 on v20

--- a/solution.py
+++ b/solution.py
@@ -147,16 +147,15 @@
     for j in range(size):
         col = rest[:, j:j + 1]
         row = rest[j:j + 1, :]
-        pivot = jnp.sqrt(rest[j:j + 1, j:j + 1])
-        col = jnp.where(sub[:, :1] >= j, col / pivot, 0.0)
-        row = jnp.where(lane[:1] >= j, row / pivot, 0.0)
+        scale = 1.0 / jnp.sqrt(rest[j:j + 1, j:j + 1])
+        col = jnp.where(sub[:, :1] >= j, col * scale, 0.0)
+        row = jnp.where(lane[:1] >= j, row * scale, 0.0)
         upper = upper + jnp.where(sub == j, row, 0.0)
         rest = rest - col * row
         coef = upper[:, j:j + 1]
-        diag = upper[j:j + 1, j:j + 1]
         acc = jnp.sum(jnp.where(sub[:, :1] < j, coef, 0.0) * inverse, axis=0, keepdims=True)
         unit = jnp.where(lane[:1] == j, 1.0, 0.0)
-        inverse = inverse + jnp.where(sub == j, (unit - acc) / diag, 0.0)
+        inverse = inverse + jnp.where(sub == j, (unit - acc) * scale, 0.0)
     return lax.dot_general(
         block, inverse, (((1,), (1,)), ((), ())),
         precision=lax.Precision.HIGHEST, preferred_element_type=jnp.float32,

time: 112 us -> 112 us (level)
  no operation moved by 1% of the time
where the time goes in v22:
time: 112 us; the launch traced here: 111 us
  waiting for transfers between devices  41.6 us (37%)
  starting transfers between devices  21.9 us (20%)
  other arithmetic  18.9 us (17%)
  Pallas kernels  11.2 us (10%)
  local copies, waits for them, and re-layouts  10.3 us (9%)
  matrix products  6.32 us (6%)
    ppermute x2, waiting for transfers between devices, flat_permute(): return lax.ppermute(flat, axis, pairs).reshape(block.shape)  21.9 us
    ppermute x4, waiting for transfers between devices, butterfly_sum(): partner = lax.ppermute(value, axis, [(i, i ^ step) for i in range(count)])  15.3 us
    select_n x4, other arithmetic, sweep(): return jnp.where(keep, new, 0.0)  11.7 us
    pallas_call x1, Pallas kernels, subspace_step(): pl.pallas_call(subspace_kernel, out_shape=jax.ShapeDtypeStruct(basis.shap...  11.2 us
    unnamed x16, local copies, waits for them, and re-layouts  7.73 us
    ppermute x4, starting transfers between devices, butterfly_sum(): partner = lax.ppermute(value, axis, [(i, i ^ step) for i in range(count)])  7.57 us
    ppermute x2, starting transfers between devices, flat_permute(): return lax.ppermute(flat, axis, pairs).reshape(block.shape)  6.27 us
    reduce_sum x4, other arithmetic, sweep(): jnp.sum(diff_col * diff_col + diff_row * diff_row, axis=-1, keepdims=True)  4.09 us
  transfers between devices with their start and end apart: 12, of which 8 were waited for; matrix products, arithmetic and copies ran while one was open for 4% of the time, Pallas kernels for 0%

profile of v22, /device:TPU:0, one launch (start us, length us, event | category | flops | bytes accessed | tf_op | source)
XLA Modules:
  0.0 111.1 jit_solution(2155188619126650621)
XLA Ops:
  0.6 1.9 %copy.4 = f32[224,8,256]{0,2,1:T(8,128)S(1)} copy(f32[224,8,256]{2,1,0:T(8,128)} %param.2) | data formatting | bytes 3670016 | tf_op args[0]
  2.5 1.6 %fusion.66 = (f32[4,256,224]{2,1,0:T(8,128)}, f32[4,256,224]{2,1,0:T(8,128)}) fusion(f32[8,256,224]{2,1,0:T(8,128)S(1)} %bitcast.53), kind=kLoop, calls=%fused_computation.120 | loop fusion | bytes 3670016 | tf_op jit(solution)/shard_map/slice | solution.py:97
  4.1 5.0 %collective-permute-start = (f32[16,64,224]{2,1,0:T(8,128)}, f32[16,64,224]{2,1,0:T(8,128)S(1)}, u32[]{:S(2)}, u32[]{:S(2)}) collective-permute-start(f32[16,64,224]{2,1,0:T(8,128)} %bitcast.1), channel_id=1, source_target_pairs={{0,8},{8,16},{16,24},{1,9},{9,17},{17,25},{2,10},{10,18},{18,26},{... | collective-permute-start | bytes 2752520 | tf_op jit(solution)/shard_map/ppermute | solution.py:72
  9.1 1.3 %collective-permute-start.1 = (f32[16,64,224]{2,1,0:T(8,128)}, f32[16,64,224]{2,1,0:T(8,128)}, u32[]{:S(2)}, u32[]{:S(2)}) collective-permute-start(f32[16,64,224]{2,1,0:T(8,128)} %bitcast.3), channel_id=1, source_target_pairs={{8,0},{16,8},{24,16},{9,1},{17,9},{25,17},{10,2},{18,10},{26,18},{... | collective-permute-start | bytes 2752520 | tf_op jit(solution)/shard_map/ppermute | solution.py:72
  10.5 1.5 %collective-permute-start.4 = (f32[8,4,224]{2,1,0:T(4,128)S(1)}, f32[8,4,224]{2,1,0:T(4,128)S(1)}, u32[]{:S(2)}, u32[]{:S(2)}) collective-permute-start(f32[8,4,224]{2,1,0:T(4,128)S(1)} %get-tuple-element.4), channel_id=1, source_target_pairs={{0,1},{1,2},{2,3},{3,4},{4,5},{5,6},{6,7},{8,9},{9,10},{10,11},{11... | collective-permute-start | bytes 86024 | tf_op jit(solution)/shard_map/ppermute | solution.py:99
  11.9 1.3 %collective-permute-start.5 = (f32[8,4,224]{2,1,0:T(4,128)S(1)}, f32[8,4,224]{2,1,0:T(4,128)S(1)}, u32[]{:S(2)}, u32[]{:S(2)}) collective-permute-start(f32[8,4,224]{2,1,0:T(4,128)S(1)} %get-tuple-element.5), channel_id=1, source_target_pairs={{1,0},{2,1},{3,2},{4,3},{5,4},{6,5},{7,6},{9,8},{10,9},{11,10},{12... | collective-permute-start | bytes 86024 | tf_op jit(solution)/shard_map/ppermute | solution.py:100
  14.1 17.7 %collective-permute-done = f32[16,64,224]{2,1,0:T(8,128)S(1)} collective-permute-done((f32[16,64,224]{2,1,0:T(8,128)}, f32[16,64,224]{2,1,0:T(8,128)S(1)}, u32[]{:S(2)}, u32[]{:S(2)}) %collective-permute-start) | collective-permute-done | bytes 917536 | tf_op jit(solution)/shard_map/ppermute | solution.py:72
  31.8 4.2 %collective-permute-done.1 = f32[16,64,224]{2,1,0:T(8,128)} collective-permute-done((f32[16,64,224]{2,1,0:T(8,128)}, f32[16,64,224]{2,1,0:T(8,128)}, u32[]{:S(2)}, u32[]{:S(2)}) %collective-permute-start.1) | collective-permute-done | bytes 917536 | tf_op jit(solution)/shard_map/ppermute | solution.py:72
  36.8 1.3 %collective-permute-start.2 = (f32[8,4,224]{2,1,0:T(4,128)S(1)}, f32[8,4,224]{2,1,0:T(4,128)S(1)}, u32[]{:S(2)}, u32[]{:S(2)}) collective-permute-start(f32[8,4,224]{2,1,0:T(4,128)S(1)} %get-tuple-element.6), channel_id=1, source_target_pairs={{0,1},{1,2},{2,3},{3,4},{4,5},{5,6},{6,7},{8,9},{9,10},{10,11},{11... | collective-permute-start | bytes 86024 | tf_op jit(solution)/shard_map/ppermute | solution.py:102
  38.1 1.3 %collective-permute-start.3 = (f32[8,4,224]{2,1,0:T(4,128)S(1)}, f32[8,4,224]{2,1,0:T(4,128)S(1)}, u32[]{:S(2)}, u32[]{:S(2)}) collective-permute-start(f32[8,4,224]{2,1,0:T(4,128)S(1)} %get-tuple-element.7), channel_id=1, source_target_pairs={{1,0},{2,1},{3,2},{4,3},{5,4},{6,5},{7,6},{9,8},{10,9},{11,10},{12... | collective-permute-start | bytes 86024 | tf_op jit(solution)/shard_map/ppermute | solution.py:103
  39.4 3.5 %collective-permute-done.3 = f32[8,4,224]{2,1,0:T(4,128)S(1)} collective-permute-done((f32[8,4,224]{2,1,0:T(4,128)S(1)}, f32[8,4,224]{2,1,0:T(4,128)S(1)}, u32[]{:S(2)}, u32[]{:S(2)}) %collective-permute-start.3) | collective-permute-done | bytes 28704 | tf_op jit(solution)/shard_map/ppermute | solution.py:103
  43.0 1.8 %maximum_maximum_fusion = f32[16,264,224]{2,1,0:T(8,128)S(1)} fusion(f32[4,4,224]{2,1,0:T(4,128)S(1)} %get-tuple-element.13, f32[4,256,224]{2,1,0:T(8,128)} %bitcast.4, f32[4,4,224]{2,1,0:T(4,128)S(1)} %get-tuple-element.11, f32[8,4,224]{2,1,0:T(4,128)S(1)} %collective-permute-done.5, f32[8,256,224]{2,1,0:T(8,128)S(1)} %bitcast.55, ...), kind=kLoop, calls=%fused_computation | loop fusion | flops 7569408 | bytes 7569408 | tf_op jit(solution)/shard_map/concatenate | solution.py:104
  44.8 1.3 %fusion.2 = f32[15,263]{1,0:T(8,128)S(1)} fusion(f32[16,264,224]{2,1,0:T(8,128)S(1)} %maximum_maximum_fusion), kind=kLoop, calls=%fused_computation.4 | loop fusion | flops 5298135 | bytes 10619940 | tf_op jit(solution)/shard_map/reduce_sum | solution.py:124
  46.2 3.6 %fusion.9 = f32[14,262,224]{2,1,0:T(8,128)S(1)} fusion(f32[16,264,224]{2,1,0:T(8,128)S(1)} %maximum_maximum_fusion, f32[14,262]{1,0:T(8,128)S(1)} %get-tuple-element.24, f32[14,262]{1,0:T(8,128)S(1)} %get-tuple-element.25, f32[14,262]{1,0:T(8,128)S(1)} %get-tuple-element.23, pred[14,262]{1,0:T(8,128)(4,1)S(1)} %broadcast_and_fusion), kind=kLoop, calls=%fused_computation.13 | loop fusion | flops 13967744 | bytes 19766852 | tf_op jit(solution)/shard_map/jit(_where)/select_n | solution.py:133
  49.8 1.1 fusion.17
  51.0 3.4 %fusion.21 = f32[12,260,224]{2,1,0:T(8,128)S(1)} fusion(f32[16,264,224]{2,1,0:T(8,128)S(1)} %maximum_maximum_fusion, f32[14,262,224]{2,1,0:T(8,128)S(1)} %fusion.9, f32[12,260]{1,0:T(8,128)S(1)} %get-tuple-element.21, f32[12,260]{1,0:T(8,128)S(1)} %get-tuple-element.22, f32[12,260]{1,0:T(8,128)S(1)} %get-tuple-element.20, ...), kind=kLoop, calls=%fused_computation.31 | loop fusion | flops 11880960 | bytes 19609200 | tf_op jit(solution)/shard_map/jit(_where)/select_n | solution.py:133
  55.4 2.7 %fusion.37 = f32[10,258,224]{2,1,0:T(8,128)S(1)} fusion(f32[16,264,224]{2,1,0:T(8,128)S(1)} %maximum_maximum_fusion, f32[12,260,224]{2,1,0:T(8,128)S(1)} %fusion.21, f32[10,258]{1,0:T(8,128)S(1)} %get-tuple-element.18, f32[10,258]{1,0:T(8,128)S(1)} %get-tuple-element.19, f32[10,258]{1,0:T(8,128)S(1)} %get-tuple-element.17, ...), kind=kLoop, calls=%fused_computation.54 | loop fusion | flops 9824640 | bytes 16215300 | tf_op jit(solution)/shard_map/jit(_where)/select_n | solution.py:133
  59.7 2.0 %fusion.56 = f32[8,256,224]{2,1,0:T(8,128)S(1)} fusion(f32[10,258,224]{2,1,0:T(8,128)S(1)} %fusion.37, f32[8,256]{1,0:T(8,128)S(1)} %get-tuple-element.15, f32[8,256]{1,0:T(8,128)S(1)} %get-tuple-element.16, f32[8,256]{1,0:T(8,128)S(1)} %get-tuple-element.14, pred[8,256]{1,0:T(8,128)(4,1)S(1)} %broadcast_and_fusion.3, f32[224,8,256]{0,2,1:T(8,128)S(1)} %copy-done.1), kind=kLoop, calls=%fused_computation.80 | loop fusion | flops 7798784 | bytes 12871680 | tf_op jit(solution)/shard_map/jit(_where)/select_n | solution.py:133
  61.7 3.5 %convolution_bitcast_fusion = f32[224,224]{1,0:T(8,128)S(1)} fusion(f32[8,256,224]{2,1,0:T(8,128)S(1)} %fusion.56), kind=kOutput, calls=%fused_computation.89 | convolution fusion | flops 1233125376 | bytes 2035712 | tf_op jit(solution)/shard_map/dot_general | solution.py:221
  65.2 2.7 %collective-permute-start.6 = (f32[112,224]{1,0:T(8,128)S(1)}, f32[112,224]{1,0:T(8,128)S(1)}, u32[]{:S(2)}, u32[]{:S(2)}) collective-permute-start(f32[112,224]{1,0:T(8,128)S(1)} %slice_select_fusion), channel_id=1, source_target_pairs={{0,1},{1,0},{2,3},{3,2},{4,5},{5,4},{6,7},{7,6},{8,9},{9,8},{10,11... | collective-permute-start | bytes 301064 | tf_op jit(solution)/shard_map/ppermute | solution.py:45
  67.9 1.0 collective-permute-done.6
  68.9 2.5 %collective-permute-start.7 = (f32[112,224]{1,0:T(8,128)S(1)}, f32[112,224]{1,0:T(8,128)S(1)}, u32[]{:S(2)}, u32[]{:S(2)}) collective-permute-start(f32[112,224]{1,0:T(8,128)S(1)} %select_add_fusion), channel_id=1, source_target_pairs={{0,2},{1,3},{2,0},{3,1},{4,6},{5,7},{6,4},{7,5},{8,10},{9,11},{10,... | collective-permute-start | bytes 301064 | tf_op jit(solution)/shard_map/ppermute | solution.py:27
  71.4 3.7 %collective-permute-done.7 = f32[112,224]{1,0:T(8,128)S(1)} collective-permute-done((f32[112,224]{1,0:T(8,128)S(1)}, f32[112,224]{1,0:T(8,128)S(1)}, u32[]{:S(2)}, u32[]{:S(2)}) %collective-permute-start.7) | collective-permute-done | bytes 100384 | tf_op jit(solution)/shard_map/ppermute | solution.py:27
  76.0 4.0 %collective-permute-done.8 = f32[112,224]{1,0:T(8,128)S(1)} collective-permute-done((f32[112,224]{1,0:T(8,128)S(1)}, f32[112,224]{1,0:T(8,128)S(1)}, u32[]{:S(2)}, u32[]{:S(2)}) %collective-permute-start.8) | collective-permute-done | bytes 100384 | tf_op jit(solution)/shard_map/ppermute | solution.py:27
  80.0 1.6 %collective-permute-start.9 = (f32[112,224]{1,0:T(8,128)S(1)}, f32[112,224]{1,0:T(8,128)S(1)}, u32[]{:S(2)}, u32[]{:S(2)}) collective-permute-start(f32[112,224]{1,0:T(8,128)S(1)} %add.156), channel_id=1, source_target_pairs={{0,8},{8,0},{16,24},{24,16},{1,9},{9,1},{17,25},{25,17},{2,10},{10... | collective-permute-start | bytes 301064 | tf_op jit(solution)/shard_map/ppermute | solution.py:27
  81.6 3.3 %collective-permute-done.9 = f32[112,224]{1,0:T(8,128)S(1)} collective-permute-done((f32[112,224]{1,0:T(8,128)S(1)}, f32[112,224]{1,0:T(8,128)S(1)}, u32[]{:S(2)}, u32[]{:S(2)}) %collective-permute-start.9) | collective-permute-done | bytes 100384 | tf_op jit(solution)/shard_map/ppermute | solution.py:27
  84.9 2.6 %collective-permute-start.10 = (f32[112,224]{1,0:T(8,128)S(1)}, f32[112,224]{1,0:T(8,128)S(1)}, u32[]{:S(2)}, u32[]{:S(2)}) collective-permute-start(f32[112,224]{1,0:T(8,128)S(1)} %add.157), channel_id=1, source_target_pairs={{0,16},{8,24},{16,0},{24,8},{1,17},{9,25},{17,1},{25,9},{2,18},{10... | collective-permute-start | bytes 301064 | tf_op jit(solution)/shard_map/ppermute | solution.py:27
  87.5 4.4 %collective-permute-done.10 = f32[112,224]{1,0:T(8,128)S(1)} collective-permute-done((f32[112,224]{1,0:T(8,128)S(1)}, f32[112,224]{1,0:T(8,128)S(1)}, u32[]{:S(2)}, u32[]{:S(2)}) %collective-permute-start.10) | collective-permute-done | bytes 100384 | tf_op jit(solution)/shard_map/ppermute | solution.py:27
  92.7 1.8 %copy.6 = f32[224,8,256]{2,1,0:T(8,128)} copy(f32[224,8,256]{0,2,1:T(8,128)S(1)} %bitcast.51) | data formatting | bytes 3670016
  95.1 11.2 %shard_map.41 = f32[224,16]{1,0:T(8,128)} custom-call(f32[112,224]{1,0:T(8,128)} %copy-done.3, f32[112,224]{1,0:T(8,128)} %copy-done.4, f32[1,1]{1,0:T(1,128)} %bitcast.23.low_ref, f32[224,16]{1,0:T(8,128)} %copy.5.basis_ref), custom_call_target="tpu_custom_call" | custom-call | flops 4128768 | bytes 229376 | tf_op jit(solution)/shard_map/pallas_call | solution.py:186
  106.3 2.0 %fusion.69 = f32[2048,16]{1,0:T(8,128)S(1)} fusion(f32[2048,224]{1,0:T(8,128)S(1)} %bitcast.52, f32[224,16]{1,0:T(8,128)} %shard_map.41), kind=kOutput, calls=%fused_computation.123 | convolution fusion | flops 44040192 | bytes 1980416 | tf_op jit(solution)/shard_map/dot_general | solution.py:231
  109.1 2.0 %copy.7 = f32[28,8,8,256]{3,2,1,0:T(8,128)} copy(f32[28,8,8,256]{3,1,2,0:T(8,128)S(1)} %bitcast.56) | data formatting | bytes 3670016
  (54 shorter events, 7.9 us)
Async XLA Ops:
  2.5 40.4 %copy-start = (f32[224,8,256]{0,2,1:T(8,128)}, f32[224,8,256]{0,2,1:T(8,128)S(1)}, u32[]{:S(2)}) copy-start(f32[224,8,256]{0,2,1:T(8,128)S(1)} %copy.4) | copy-start | bytes 5505028
  4.1 27.6 %collective-permute-start = (f32[16,64,224]{2,1,0:T(8,128)}, f32[16,64,224]{2,1,0:T(8,128)S(1)}, u32[]{:S(2)}, u32[]{:S(2)}) collective-permute-start(f32[16,64,224]{2,1,0:T(8,128)} %bitcast.1), channel_id=1, source_target_pairs={{0,8},{8,16},{16,24},{1,9},{9,17},{17,25},{2,10},{10,18},{18,26},{... | collective-permute-start | bytes 2752520 | tf_op jit(solution)/shard_map/ppermute | solution.py:72
  9.1 26.8 %collective-permute-start.1 = (f32[16,64,224]{2,1,0:T(8,128)}, f32[16,64,224]{2,1,0:T(8,128)}, u32[]{:S(2)}, u32[]{:S(2)}) collective-permute-start(f32[16,64,224]{2,1,0:T(8,128)} %bitcast.3), channel_id=1, source_target_pairs={{8,0},{16,8},{24,16},{9,1},{17,9},{25,17},{10,2},{18,10},{26,18},{... | collective-permute-start | bytes 2752520 | tf_op jit(solution)/shard_map/ppermute | solution.py:72
  10.5 32.5 %collective-permute-start.4 = (f32[8,4,224]{2,1,0:T(4,128)S(1)}, f32[8,4,224]{2,1,0:T(4,128)S(1)}, u32[]{:S(2)}, u32[]{:S(2)}) collective-permute-start(f32[8,4,224]{2,1,0:T(4,128)S(1)} %get-tuple-element.4), channel_id=1, source_target_pairs={{0,1},{1,2},{2,3},{3,4},{4,5},{5,6},{6,7},{8,9},{9,10},{10,11},{11... | collective-permute-start | bytes 86024 | tf_op jit(solution)/shard_map/ppermute | solution.py:99
  11.9 31.0 %collective-permute-start.5 = (f32[8,4,224]{2,1,0:T(4,128)S(1)}, f32[8,4,224]{2,1,0:T(4,128)S(1)}, u32[]{:S(2)}, u32[]{:S(2)}) collective-permute-start(f32[8,4,224]{2,1,0:T(4,128)S(1)} %get-tuple-element.5), channel_id=1, source_target_pairs={{1,0},{2,1},{3,2},{4,3},{5,4},{6,5},{7,6},{9,8},{10,9},{11,10},{12... | collective-permute-start | bytes 86024 | tf_op jit(solution)/shard_map/ppermute | solution.py:100
  36.8 2.7 %collective-permute-start.2 = (f32[8,4,224]{2,1,0:T(4,128)S(1)}, f32[8,4,224]{2,1,0:T(4,128)S(1)}, u32[]{:S(2)}, u32[]{:S(2)}) collective-permute-start(f32[8,4,224]{2,1,0:T(4,128)S(1)} %get-tuple-element.6), channel_id=1, source_target_pairs={{0,1},{1,2},{2,3},{3,4},{4,5},{5,6},{6,7},{8,9},{9,10},{10,11},{11... | collective-permute-start | bytes 86024 | tf_op jit(solution)/shard_map/ppermute | solution.py:102
  38.1 4.8 %collective-permute-start.3 = (f32[8,4,224]{2,1,0:T(4,128)S(1)}, f32[8,4,224]{2,1,0:T(4,128)S(1)}, u32[]{:S(2)}, u32[]{:S(2)}) collective-permute-start(f32[8,4,224]{2,1,0:T(4,128)S(1)} %get-tuple-element.7), channel_id=1, source_target_pairs={{1,0},{2,1},{3,2},{4,3},{5,4},{6,5},{7,6},{9,8},{10,9},{11,10},{12... | collective-permute-start | bytes 86024 | tf_op jit(solution)/shard_map/ppermute | solution.py:103
  58.1 1.6 %copy-start.1 = (f32[224,8,256]{0,2,1:T(8,128)S(1)}, f32[224,8,256]{0,2,1:T(8,128)}, u32[]{:S(2)}) copy-start(f32[224,8,256]{0,2,1:T(8,128)} %copy-done) | copy-start | bytes 5505028
  61.7 30.2 %copy-start.5 = (f32[224,16]{0,1:T(8,128)S(1)}, f32[224,16]{0,1:T(8,128)}, u32[]{:S(2)}) copy-start(f32[224,16]{0,1:T(8,128)} %param.3) | copy-start | bytes 43012
  65.2 3.7 %collective-permute-start.6 = (f32[112,224]{1,0:T(8,128)S(1)}, f32[112,224]{1,0:T(8,128)S(1)}, u32[]{:S(2)}, u32[]{:S(2)}) collective-permute-start(f32[112,224]{1,0:T(8,128)S(1)} %slice_select_fusion), channel_id=1, source_target_pairs={{0,1},{1,0},{2,3},{3,2},{4,5},{5,4},{6,7},{7,6},{8,9},{9,8},{10,11... | collective-permute-start | bytes 301064 | tf_op jit(solution)/shard_map/ppermute | solution.py:45
  68.9 6.1 %collective-permute-start.7 = (f32[112,224]{1,0:T(8,128)S(1)}, f32[112,224]{1,0:T(8,128)S(1)}, u32[]{:S(2)}, u32[]{:S(2)}) collective-permute-start(f32[112,224]{1,0:T(8,128)S(1)} %select_add_fusion), channel_id=1, source_target_pairs={{0,2},{1,3},{2,0},{3,1},{4,6},{5,7},{6,4},{7,5},{8,10},{9,11},{10,... | collective-permute-start | bytes 301064 | tf_op jit(solution)/shard_map/ppermute | solution.py:27
  75.1 4.9 %collective-permute-start.8 = (f32[112,224]{1,0:T(8,128)S(1)}, f32[112,224]{1,0:T(8,128)S(1)}, u32[]{:S(2)}, u32[]{:S(2)}) collective-permute-start(f32[112,224]{1,0:T(8,128)S(1)} %add.155), channel_id=1, source_target_pairs={{0,4},{1,5},{2,6},{3,7},{4,0},{5,1},{6,2},{7,3},{8,12},{9,13},{10,... | collective-permute-start | bytes 301064 | tf_op jit(solution)/shard_map/ppermute | solution.py:27
  80.0 4.9 %collective-permute-start.9 = (f32[112,224]{1,0:T(8,128)S(1)}, f32[112,224]{1,0:T(8,128)S(1)}, u32[]{:S(2)}, u32[]{:S(2)}) collective-permute-start(f32[112,224]{1,0:T(8,128)S(1)} %add.156), channel_id=1, source_target_pairs={{0,8},{8,0},{16,24},{24,16},{1,9},{9,1},{17,25},{25,17},{2,10},{10... | collective-permute-start | bytes 301064 | tf_op jit(solution)/shard_map/ppermute | solution.py:27
  84.9 7.0 %collective-permute-start.10 = (f32[112,224]{1,0:T(8,128)S(1)}, f32[112,224]{1,0:T(8,128)S(1)}, u32[]{:S(2)}, u32[]{:S(2)}) collective-permute-start(f32[112,224]{1,0:T(8,128)S(1)} %add.157), channel_id=1, source_target_pairs={{0,16},{8,24},{16,0},{24,8},{1,17},{9,25},{17,1},{25,9},{2,18},{10... | collective-permute-start | bytes 301064 | tf_op jit(solution)/shard_map/ppermute | solution.py:27
  91.9 2.6 %copy-start.3 = (f32[112,224]{1,0:T(8,128)}, f32[112,224]{1,0:T(8,128)S(1)}, u32[]{:S(2)}) copy-start(f32[112,224]{1,0:T(8,128)S(1)} %add.158.mine_ref) | copy-start | bytes 301060
  91.9 2.6 %collective-permute-start.11 = (f32[112,224]{1,0:T(8,128)S(1)}, f32[112,224]{1,0:T(8,128)S(1)}, u32[]{:S(2)}, u32[]{:S(2)}) collective-permute-start(f32[112,224]{1,0:T(8,128)S(1)} %add.158.mine_ref), channel_id=1, source_target_pairs={{0,1},{1,0},{2,3},{3,2},{4,5},{5,4},{6,7},{7,6},{8,9},{9,8},{10,11... | collective-permute-start | bytes 301064 | tf_op jit(solution)/shard_map/ppermute | solution.py:47
  94.5 0.6 copy-start.4
  106.3 2.0 %copy-start.2 = (f32[224,16]{1,0:T(8,128)S(1)}, f32[224,16]{1,0:T(8,128)}, u32[]{:S(2)}) copy-start(f32[224,16]{1,0:T(8,128)} %shard_map.41) | copy-start | bytes 43012
